TPU v7x, 512 devices: a whole 4x8x8 slice. The times are simulated.
512 devices in a mesh: section: 8 (over z_lo, x), fsdp: 64 (over z_hi, y, core).
Axes of the slice: x: 4, y: 8, z: 8 (z_hi: 4, z_lo: 2; z = z_hi * 2 + z_lo), core: 2. Of those that a mesh axis runs over, the one named last changes fastest.
Arguments:
- activations: bfloat16 [10240, 6144], P('fsdp'), may hold values from -36 to 36
- keep: int32 [10240], P('fsdp'), may hold values from 0 to 1, as said below
- gains: bfloat16 [8, 6144], P('section'), may hold values from 0.099609375 to 1.8984375
- up_rows: int32 [8, 192, 2], P('section'), may hold values from 0 to 95
- up_blocks: bfloat16 [8, 384, 4096], P('section', 'fsdp'), may hold values from -0.5 to 0.5
- down_rows: int32 [8, 96, 2], P('section'), may hold values from 0 to 191
- down_blocks: bfloat16 [8, 192, 4096], P('section', 'fsdp'), may hold values from -0.5 to 0.5
Outputs:
- section_out: bfloat16 [8, 10240, 6144], P('section', 'fsdp')
Inputs may be any that keep to these rules, and one draw needn't show every extreme that they name: `keep`: each aligned block of 160 tokens (the tokens of one index of fsdp) holds exactly 128 ones.
All inputs are finite; a program needn't handle non-finite values.
Results may differ from a plain program's by a relative error of at most 0.012.
Values may be sent and summed in bfloat16 or wider, within the bound.
No kernel may reach another device: no remote copies, remote signals or barrier semaphores. Data moves between devices by JAX's collectives and lax.ppermute only.
A program may use at most 128 MiB of HBM per device.

v0:
```python
import jax
import jax.numpy as jnp
from jax import lax
from jax.sharding import PartitionSpec as P

BLK = 64
UP_DEPTH = 2
DOWN_DEPTH = 2
KEEP_DEV = 128


def from_behind(value, axis, steps):
    count = lax.axis_size(axis)
    initial, last = (max(0, -steps), min(count, count - steps))
    return lax.ppermute(value, axis, [(source, source + steps) for source in range(initial, last)])


def make_layer(gain, up_index, up_values, down_index, down_values):
    width = gain.shape[0]
    hidden_width = up_values.shape[0] // UP_DEPTH * BLK
    blocks_in = width // BLK
    blocks_hid = hidden_width // BLK
    weights_up = up_values.reshape(blocks_hid, UP_DEPTH * BLK, BLK)
    weights_down = down_values.reshape(blocks_in, DOWN_DEPTH * BLK, BLK)
    gain_wide = gain.astype(jnp.float32)

    def layer(block):
        count = block.shape[0]
        wide = block.astype(jnp.float32)
        meansq = jnp.mean(wide * wide, axis=-1, keepdims=True)
        normed = (wide * lax.rsqrt(meansq + 1e-05) * gain_wide).astype(jnp.bfloat16)
        picked = normed.reshape(count, blocks_in, BLK)[:, up_index, :]
        picked = picked.reshape(count, blocks_hid, UP_DEPTH * BLK)
        up_sums = jnp.einsum("ncr,crj->ncj", picked, weights_up, preferred_element_type=jnp.float32)
        hidden = jax.nn.gelu(up_sums, approximate=True).astype(jnp.bfloat16)
        second = hidden[:, down_index, :].reshape(count, blocks_in, DOWN_DEPTH * BLK)
        down_sums = jnp.einsum(
            "ncr,crj->ncj", second, weights_down, preferred_element_type=jnp.float32
        )
        return (wide + down_sums.reshape(count, width)).astype(jnp.bfloat16)

    return layer


def per_device(activations, keep, gains, up_rows, up_blocks, down_rows, down_blocks):
    up_all, down_all = (
        lax.all_gather(up_blocks, "fsdp", axis=1, tiled=True),
        lax.all_gather(down_blocks, "fsdp", axis=1, tiled=True),
    )
    apply = make_layer(
        gains[0], up_rows[0].reshape(-1), up_all[0], down_rows[0].reshape(-1), down_all[0]
    )
    places = jnp.cumsum(keep) - 1
    target = jnp.where(keep == 1, places, KEEP_DEV)
    chosen = (
        jnp.zeros((KEEP_DEV + 1,), jnp.int32)
        .at[target]
        .set(jnp.arange(keep.shape[0], dtype=jnp.int32))[:KEEP_DEV]
    )
    selected = activations[chosen]
    width = selected.shape[1]
    section = lax.axis_index("section")
    sections = lax.axis_size("section")
    pieces = 8
    group_rows = selected.shape[0] // pieces
    split = selected.reshape(pieces, group_rows, width)

    def advance(turn, held, record):
        offset = turn - section
        entry = jnp.where(section == 0, split[jnp.minimum(turn, pieces - 1)], held)
        active = (offset >= 0) & (offset < pieces)
        result = lax.cond(active, apply, jnp.zeros_like, entry)
        slot = jnp.clip(offset, 0, pieces - 1)
        current = lax.dynamic_index_in_dim(record, slot, 0, keepdims=False)
        updated = jnp.where(active, result, current)
        record = lax.dynamic_update_index_in_dim(record, updated, slot, 0)
        return (result, record)

    def turn_step(turn, carry):
        held, record = carry
        result, record = advance(turn, held, record)
        held = from_behind(result, "section", 1)
        return (held, record)

    final_turn = sections + pieces - 2
    held, record = lax.fori_loop(0, final_turn, turn_step, (split[0], split))
    result, record = advance(final_turn, held, record)
    final = record.reshape(selected.shape[0], width)
    merged = activations.at[chosen].set(final)
    return merged[None]


def solution(mesh):
    return jax.shard_map(
        per_device,
        mesh=mesh,
        in_specs=(
            P("fsdp", None),
            P("fsdp"),
            P("section", None),
            P("section", None, None),
            P("section", "fsdp", None),
            P("section", None, None),
            P("section", "fsdp", None),
        ),
        out_specs=P("section", "fsdp", None),
        check_vma=False,
    )
```

profile of v0, /device:TPU:86, one launch (start us, length us, event | category | flops | bytes accessed | tf_op | source)
XLA Modules:
  0.0 659.5 jit_solution(10641447543679874243)
XLA Ops:
  11.4 2.6 gather_fusion.4
  15.0 2.7 copy.61
  18.9 80.8 %all-gather.5.cloned.1.call-done = bf16[1,192,4096]{2,0,1:T(2,128)(2,1)} async-done(((bf16[1,3,4096]{2,0,1:T(2,128)(2,1)}), bf16[1,192,4096]{2,0,1:T(2,128)(2,1)}) %all-gather.5.cloned.1.call-update) | async-done | bytes 1572880 | tf_op jit(solution)/shard_map/all_gather | solution.py:48
  99.7 12.3 %reduce.2 = bf16[192,4096]{1,0:T(8,128)(2,1)} reduce(bf16[1,192,4096]{2,0,1:T(2,128)(2,1)} %all-gather.5.cloned.1.call-done, bf16[]{:T(256)} %constant.162), dimensions={0}, to_apply=%all_gather.7.reduce_sub_computation | reduce | bytes 3145730 | tf_op jit(solution)/shard_map/all_gather | solution.py:48
  112.0 5.6 reshape_squeeze.15
  117.5 4.3 copy.43
  121.8 70.4 %all-gather.3.cloned.1.call-done = bf16[1,384,4096]{2,0,1:T(2,128)(2,1)} async-done(((bf16[1,6,4096]{2,0,1:T(2,128)(2,1)}), bf16[1,384,4096]{2,0,1:T(2,128)(2,1)}) %all-gather.3.cloned.1.call-update) | async-done | bytes 3145744 | tf_op jit(solution)/shard_map/all_gather | solution.py:47
  192.2 20.4 %reduce.1 = bf16[384,4096]{1,0:T(8,128)(2,1)} reduce(bf16[1,384,4096]{2,0,1:T(2,128)(2,1)} %all-gather.3.cloned.1.call-done, bf16[]{:T(256)} %constant.162), dimensions={0}, to_apply=%all_gather.6.reduce_sub_computation | reduce | bytes 6291458 | tf_op jit(solution)/shard_map/all_gather | solution.py:47
  212.6 9.7 %reshape_squeeze.13 = bf16[192,128,64]{2,1,0:T(8,128)(2,1)} reshape(bf16[384,4096]{1,0:T(8,128)(2,1)} %reduce.1) | data formatting | bytes 6291456 | tf_op jit(solution)/shard_map/reshape;squeeze | solution.py:23
  222.3 6.7 %copy.42 = bf16[192,128,64]{1,2,0:T(8,128)(2,1)} copy(bf16[192,128,64]{2,1,0:T(8,128)(2,1)} %reshape_squeeze.13) | data formatting | bytes 6291456 | tf_op jit(solution)/shard_map/while | solution.py:86
  229.0 377.3 %while.16 = (s32[]{:T(128)}, bf16[16,6144]{1,0:T(8,128)(2,1)S(1)}, bf16[8,16,6144]{2,1,0:T(8,128)(2,1)}, s32[]{:T(128)}, pred[]{:T(512)}, /*index=5*/bf16[8,16,6...) while((s32[]{:T(128)}, bf16[16,6144]{1,0:T(8,128)(2,1)S(1)}, ...), condition=%wide.region_7.8_spmd, body=%wide.region_3.0_spmd.sunk | while | flops 78450392 | bytes 21276344 | solution.py:86
  232.7 6.1 collective-permute-done
  242.5 5.3 collective-permute-done
  251.5 4.8 collective-permute-done
  259.9 4.8 collective-permute-done
  268.5 6.3 collective-permute-done
  278.5 6.7 %collective-permute-done = bf16[16,6144]{1,0:T(8,128)(2,1)S(1)} collective-permute-done((bf16[16,6144]{1,0:T(8,128)(2,1)}, bf16[16,6144]{1,0:T(8,128)(2,1)S(1)}, u32[]{:S(2)}, u32[]{:S(2)}) %collective-permute-start) | collective-permute-done | bytes 196640 | tf_op jit(solution)/shard_map/while/body/eval_jaxpr/ppermute | solution.py:15
  288.8 120.1 %collective-permute-done = bf16[16,6144]{1,0:T(8,128)(2,1)S(1)} collective-permute-done((bf16[16,6144]{1,0:T(8,128)(2,1)}, bf16[16,6144]{1,0:T(8,128)(2,1)S(1)}, u32[]{:S(2)}, u32[]{:S(2)}) %collective-permute-start) | collective-permute-done | bytes 196640 | tf_op jit(solution)/shard_map/while/body/eval_jaxpr/ppermute | solution.py:15
  408.9 18.3 %conditional.4 = (bf16[16,6144]{1,0:T(8,128)(2,1)}) conditional(s32[]{:T(128)} %convert_element_type.82, () %tuple.59, (pred[]{:T(512)}, s32[]{:T(128)}, bf16[8,16,6144]{2,1,0:T(8,128)(2,1)}, bf16[16,6144]{1,0:T(8,128)(2,1)S(1)}, f32[6144]{0:T(1024)}, /*index=5*/s32[384]{0:T(512)S(1)}, bf16[192,128,64]{1,2,0:T(8,128)(2,1)}, s32[192]{0:T(256)S(1)}, ...), branch_computations={%region_4.4_spmd, %region_5.6_spmd} | conditional | flops 78352080 | bytes 19506548 | solution.py:72
  412.1 2.5 gather_fusion
  418.0 3.9 fusion.7
  423.2 2.3 convolution_bitcast_fusion
  431.1 6.0 collective-permute-done
  437.1 18.3 %conditional.4 = (bf16[16,6144]{1,0:T(8,128)(2,1)}) conditional(s32[]{:T(128)} %convert_element_type.82, () %tuple.59, (pred[]{:T(512)}, s32[]{:T(128)}, bf16[8,16,6144]{2,1,0:T(8,128)(2,1)}, bf16[16,6144]{1,0:T(8,128)(2,1)S(1)}, f32[6144]{0:T(1024)}, /*index=5*/s32[384]{0:T(512)S(1)}, bf16[192,128,64]{1,2,0:T(8,128)(2,1)}, s32[192]{0:T(256)S(1)}, ...), branch_computations={%region_4.4_spmd, %region_5.6_spmd} | conditional | flops 78352080 | bytes 19506548 | solution.py:72
  440.3 2.5 gather_fusion
  446.2 3.9 fusion.7
  451.4 2.3 convolution_bitcast_fusion
  459.3 6.0 collective-permute-done
  465.3 18.3 %conditional.4 = (bf16[16,6144]{1,0:T(8,128)(2,1)}) conditional(s32[]{:T(128)} %convert_element_type.82, () %tuple.59, (pred[]{:T(512)}, s32[]{:T(128)}, bf16[8,16,6144]{2,1,0:T(8,128)(2,1)}, bf16[16,6144]{1,0:T(8,128)(2,1)S(1)}, f32[6144]{0:T(1024)}, /*index=5*/s32[384]{0:T(512)S(1)}, bf16[192,128,64]{1,2,0:T(8,128)(2,1)}, s32[192]{0:T(256)S(1)}, ...), branch_computations={%region_4.4_spmd, %region_5.6_spmd} | conditional | flops 78352080 | bytes 19506548 | solution.py:72
  468.5 2.5 gather_fusion
  474.4 3.9 fusion.7
  479.6 2.3 convolution_bitcast_fusion
  487.5 6.0 collective-permute-done
  493.5 18.3 %conditional.4 = (bf16[16,6144]{1,0:T(8,128)(2,1)}) conditional(s32[]{:T(128)} %convert_element_type.82, () %tuple.59, (pred[]{:T(512)}, s32[]{:T(128)}, bf16[8,16,6144]{2,1,0:T(8,128)(2,1)}, bf16[16,6144]{1,0:T(8,128)(2,1)S(1)}, f32[6144]{0:T(1024)}, /*index=5*/s32[384]{0:T(512)S(1)}, bf16[192,128,64]{1,2,0:T(8,128)(2,1)}, s32[192]{0:T(256)S(1)}, ...), branch_computations={%region_4.4_spmd, %region_5.6_spmd} | conditional | flops 78352080 | bytes 19506548 | solution.py:72
  496.7 2.5 gather_fusion
  502.6 3.9 fusion.7
  507.9 2.3 convolution_bitcast_fusion
  515.7 6.0 collective-permute-done
  521.7 18.3 %conditional.4 = (bf16[16,6144]{1,0:T(8,128)(2,1)}) conditional(s32[]{:T(128)} %convert_element_type.82, () %tuple.59, (pred[]{:T(512)}, s32[]{:T(128)}, bf16[8,16,6144]{2,1,0:T(8,128)(2,1)}, bf16[16,6144]{1,0:T(8,128)(2,1)S(1)}, f32[6144]{0:T(1024)}, /*index=5*/s32[384]{0:T(512)S(1)}, bf16[192,128,64]{1,2,0:T(8,128)(2,1)}, s32[192]{0:T(256)S(1)}, ...), branch_computations={%region_4.4_spmd, %region_5.6_spmd} | conditional | flops 78352080 | bytes 19506548 | solution.py:72
  524.9 2.5 gather_fusion
  530.8 3.9 fusion.7
  536.1 2.3 convolution_bitcast_fusion
  544.0 6.0 collective-permute-done
  549.9 18.3 %conditional.4 = (bf16[16,6144]{1,0:T(8,128)(2,1)}) conditional(s32[]{:T(128)} %convert_element_type.82, () %tuple.59, (pred[]{:T(512)}, s32[]{:T(128)}, bf16[8,16,6144]{2,1,0:T(8,128)(2,1)}, bf16[16,6144]{1,0:T(8,128)(2,1)S(1)}, f32[6144]{0:T(1024)}, /*index=5*/s32[384]{0:T(512)S(1)}, bf16[192,128,64]{1,2,0:T(8,128)(2,1)}, s32[192]{0:T(256)S(1)}, ...), branch_computations={%region_4.4_spmd, %region_5.6_spmd} | conditional | flops 78352080 | bytes 19506548 | solution.py:72
  553.1 2.5 gather_fusion
  559.0 3.9 fusion.7
  564.3 2.3 convolution_bitcast_fusion
  572.2 6.0 collective-permute-done
  578.1 18.3 %conditional.4 = (bf16[16,6144]{1,0:T(8,128)(2,1)}) conditional(s32[]{:T(128)} %convert_element_type.82, () %tuple.59, (pred[]{:T(512)}, s32[]{:T(128)}, bf16[8,16,6144]{2,1,0:T(8,128)(2,1)}, bf16[16,6144]{1,0:T(8,128)(2,1)S(1)}, f32[6144]{0:T(1024)}, /*index=5*/s32[384]{0:T(512)S(1)}, bf16[192,128,64]{1,2,0:T(8,128)(2,1)}, s32[192]{0:T(256)S(1)}, ...), branch_computations={%region_4.4_spmd, %region_5.6_spmd} | conditional | flops 78352080 | bytes 19506548 | solution.py:72
  581.3 2.5 gather_fusion
  587.2 3.9 fusion.7
  592.5 2.3 convolution_bitcast_fusion
  600.4 6.0 collective-permute-done
  608.6 38.0 %conditional.2 = (bf16[16,6144]{1,0:T(8,128)(2,1)}) conditional(s32[]{:T(128)} %convert_element_type.51, () %tuple.41, (pred[]{:T(512)}, bf16[128,6144]{1,0:T(8,128)(2,1)}, bf16[16,6144]{1,0:T(8,128)(2,1)}, f32[6144]{0:T(1024)}, s32[384]{0:T(512)S(1)}, /*index=5*/bf16[192,128,64]{2,1,0:T(8,128)(2,1)}, s32[192]{0:T(256)S(1)}, ...), branch_computations={%region_8.9_spmd, %region_9.11_spmd} | conditional | flops 78352080 | bytes 18720036 | solution.py:72
  616.2 3.1 gather_fusion.2
  619.3 3.0 copy.33
  622.2 3.3 reshape.70
  625.6 5.7 fusion.21
  631.3 2.8 gather_fusion.3
  634.1 2.2 copy.35
  636.3 2.3 reshape.71
  638.6 2.9 convolution_bitcast_fusion.1
  642.7 2.2 reshape.72
  647.7 3.7 scatter_fusion
  (260 shorter events, 145.8 us)
Async XLA Ops:
  6.5 3.1 copy-start.9
  6.5 2.3 copy-start.6
  6.5 1.6 copy-start.7
  6.5 93.1 %all-gather.5.cloned.1.call-start = ((), (), s32[]{:S(2)}) async-start(), calls=%async_computation.1 | async-start | bytes 3194880 | tf_op jit(solution)/shard_map/all_gather | solution.py:48
  8.8 183.4 %all-gather.3.cloned.1.call-start = ((), (), s32[]{:S(2)}) async-start(), calls=%async_computation | async-start | bytes 6389760 | tf_op jit(solution)/shard_map/all_gather | solution.py:47
  15.0 2.7 copy-start.10
  15.0 3.0 copy-start.11
  15.0 3.2 copy-start.8
  229.7 9.1 %collective-permute-start = (bf16[16,6144]{1,0:T(8,128)(2,1)}, bf16[16,6144]{1,0:T(8,128)(2,1)S(1)}, u32[]{:S(2)}, u32[]{:S(2)}) collective-permute-start(bf16[16,6144]{1,0:T(8,128)(2,1)} %get-tuple-element.529), channel_id=1, source_target_pairs={{0,64},{64,128},{128,192},{192,256},{256,320},{320,384},{384,448},... | collective-permute-start | bytes 589832 | tf_op jit(solution)/shard_map/while/body/eval_jaxpr/ppermute | solution.py:15
  239.5 8.3 %collective-permute-start = (bf16[16,6144]{1,0:T(8,128)(2,1)}, bf16[16,6144]{1,0:T(8,128)(2,1)S(1)}, u32[]{:S(2)}, u32[]{:S(2)}) collective-permute-start(bf16[16,6144]{1,0:T(8,128)(2,1)} %get-tuple-element.529), channel_id=1, source_target_pairs={{0,64},{64,128},{128,192},{192,256},{256,320},{320,384},{384,448},... | collective-permute-start | bytes 589832 | tf_op jit(solution)/shard_map/while/body/eval_jaxpr/ppermute | solution.py:15
  248.5 7.8 %collective-permute-start = (bf16[16,6144]{1,0:T(8,128)(2,1)}, bf16[16,6144]{1,0:T(8,128)(2,1)S(1)}, u32[]{:S(2)}, u32[]{:S(2)}) collective-permute-start(bf16[16,6144]{1,0:T(8,128)(2,1)} %get-tuple-element.529), channel_id=1, source_target_pairs={{0,64},{64,128},{128,192},{192,256},{256,320},{320,384},{384,448},... | collective-permute-start | bytes 589832 | tf_op jit(solution)/shard_map/while/body/eval_jaxpr/ppermute | solution.py:15
  256.9 7.8 %collective-permute-start = (bf16[16,6144]{1,0:T(8,128)(2,1)}, bf16[16,6144]{1,0:T(8,128)(2,1)S(1)}, u32[]{:S(2)}, u32[]{:S(2)}) collective-permute-start(bf16[16,6144]{1,0:T(8,128)(2,1)} %get-tuple-element.529), channel_id=1, source_target_pairs={{0,64},{64,128},{128,192},{192,256},{256,320},{320,384},{384,448},... | collective-permute-start | bytes 589832 | tf_op jit(solution)/shard_map/while/body/eval_jaxpr/ppermute | solution.py:15
  265.5 9.3 %collective-permute-start = (bf16[16,6144]{1,0:T(8,128)(2,1)}, bf16[16,6144]{1,0:T(8,128)(2,1)S(1)}, u32[]{:S(2)}, u32[]{:S(2)}) collective-permute-start(bf16[16,6144]{1,0:T(8,128)(2,1)} %get-tuple-element.529), channel_id=1, source_target_pairs={{0,64},{64,128},{128,192},{192,256},{256,320},{320,384},{384,448},... | collective-permute-start | bytes 589832 | tf_op jit(solution)/shard_map/while/body/eval_jaxpr/ppermute | solution.py:15
  275.5 9.7 %collective-permute-start = (bf16[16,6144]{1,0:T(8,128)(2,1)}, bf16[16,6144]{1,0:T(8,128)(2,1)S(1)}, u32[]{:S(2)}, u32[]{:S(2)}) collective-permute-start(bf16[16,6144]{1,0:T(8,128)(2,1)} %get-tuple-element.529), channel_id=1, source_target_pairs={{0,64},{64,128},{128,192},{192,256},{256,320},{320,384},{384,448},... | collective-permute-start | bytes 589832 | tf_op jit(solution)/shard_map/while/body/eval_jaxpr/ppermute | solution.py:15
  285.8 123.1 %collective-permute-start = (bf16[16,6144]{1,0:T(8,128)(2,1)}, bf16[16,6144]{1,0:T(8,128)(2,1)S(1)}, u32[]{:S(2)}, u32[]{:S(2)}) collective-permute-start(bf16[16,6144]{1,0:T(8,128)(2,1)} %get-tuple-element.529), channel_id=1, source_target_pairs={{0,64},{64,128},{128,192},{192,256},{256,320},{320,384},{384,448},... | collective-permute-start | bytes 589832 | tf_op jit(solution)/shard_map/while/body/eval_jaxpr/ppermute | solution.py:15
  410.0 0.7 copy-start.1
  425.6 0.9 copy-start.2
  427.2 9.9 %collective-permute-start = (bf16[16,6144]{1,0:T(8,128)(2,1)}, bf16[16,6144]{1,0:T(8,128)(2,1)S(1)}, u32[]{:S(2)}, u32[]{:S(2)}) collective-permute-start(bf16[16,6144]{1,0:T(8,128)(2,1)} %get-tuple-element.529), channel_id=1, source_target_pairs={{0,64},{64,128},{128,192},{192,256},{256,320},{320,384},{384,448},... | collective-permute-start | bytes 589832 | tf_op jit(solution)/shard_map/while/body/eval_jaxpr/ppermute | solution.py:15
  438.2 0.7 copy-start.1
  453.8 0.9 copy-start.2
  455.4 9.9 %collective-permute-start = (bf16[16,6144]{1,0:T(8,128)(2,1)}, bf16[16,6144]{1,0:T(8,128)(2,1)S(1)}, u32[]{:S(2)}, u32[]{:S(2)}) collective-permute-start(bf16[16,6144]{1,0:T(8,128)(2,1)} %get-tuple-element.529), channel_id=1, source_target_pairs={{0,64},{64,128},{128,192},{192,256},{256,320},{320,384},{384,448},... | collective-permute-start | bytes 589832 | tf_op jit(solution)/shard_map/while/body/eval_jaxpr/ppermute | solution.py:15
  466.4 0.7 copy-start.1
  482.0 0.9 copy-start.2
  483.6 9.9 %collective-permute-start = (bf16[16,6144]{1,0:T(8,128)(2,1)}, bf16[16,6144]{1,0:T(8,128)(2,1)S(1)}, u32[]{:S(2)}, u32[]{:S(2)}) collective-permute-start(bf16[16,6144]{1,0:T(8,128)(2,1)} %get-tuple-element.529), channel_id=1, source_target_pairs={{0,64},{64,128},{128,192},{192,256},{256,320},{320,384},{384,448},... | collective-permute-start | bytes 589832 | tf_op jit(solution)/shard_map/while/body/eval_jaxpr/ppermute | solution.py:15
  494.6 0.7 copy-start.1
  510.2 0.9 copy-start.2
  511.8 9.9 %collective-permute-start = (bf16[16,6144]{1,0:T(8,128)(2,1)}, bf16[16,6144]{1,0:T(8,128)(2,1)S(1)}, u32[]{:S(2)}, u32[]{:S(2)}) collective-permute-start(bf16[16,6144]{1,0:T(8,128)(2,1)} %get-tuple-element.529), channel_id=1, source_target_pairs={{0,64},{64,128},{128,192},{192,256},{256,320},{320,384},{384,448},... | collective-permute-start | bytes 589832 | tf_op jit(solution)/shard_map/while/body/eval_jaxpr/ppermute | solution.py:15
  522.8 0.7 copy-start.1
  538.4 0.9 copy-start.2
  540.0 9.9 %collective-permute-start = (bf16[16,6144]{1,0:T(8,128)(2,1)}, bf16[16,6144]{1,0:T(8,128)(2,1)S(1)}, u32[]{:S(2)}, u32[]{:S(2)}) collective-permute-start(bf16[16,6144]{1,0:T(8,128)(2,1)} %get-tuple-element.529), channel_id=1, source_target_pairs={{0,64},{64,128},{128,192},{192,256},{256,320},{320,384},{384,448},... | collective-permute-start | bytes 589832 | tf_op jit(solution)/shard_map/while/body/eval_jaxpr/ppermute | solution.py:15
  551.0 0.7 copy-start.1
  566.6 0.9 copy-start.2
  568.3 9.9 %collective-permute-start = (bf16[16,6144]{1,0:T(8,128)(2,1)}, bf16[16,6144]{1,0:T(8,128)(2,1)S(1)}, u32[]{:S(2)}, u32[]{:S(2)}) collective-permute-start(bf16[16,6144]{1,0:T(8,128)(2,1)} %get-tuple-element.529), channel_id=1, source_target_pairs={{0,64},{64,128},{128,192},{192,256},{256,320},{320,384},{384,448},... | collective-permute-start | bytes 589832 | tf_op jit(solution)/shard_map/while/body/eval_jaxpr/ppermute | solution.py:15
  579.2 0.7 copy-start.1
  594.8 0.9 copy-start.2
  596.5 9.9 %collective-permute-start = (bf16[16,6144]{1,0:T(8,128)(2,1)}, bf16[16,6144]{1,0:T(8,128)(2,1)S(1)}, u32[]{:S(2)}, u32[]{:S(2)}) collective-permute-start(bf16[16,6144]{1,0:T(8,128)(2,1)} %get-tuple-element.529), channel_id=1, source_target_pairs={{0,64},{64,128},{128,192},{192,256},{256,320},{320,384},{384,448},... | collective-permute-start | bytes 589832 | tf_op jit(solution)/shard_map/while/body/eval_jaxpr/ppermute | solution.py:15
  606.3 0.7 copy-start.4
  608.6 38.0 %copy-start.3 = (bf16[8,16,6144]{2,1,0:T(8,128)(2,1)S(1)}, bf16[8,16,6144]{2,1,0:T(8,128)(2,1)}, u32[]{:S(2)}) copy-start(bf16[8,16,6144]{2,1,0:T(8,128)(2,1)} %get-tuple-element.350) | copy-start | bytes 4718596
  609.9 0.7 copy-start.5
  651.4 1.3 copy-start
Sparse Core Ops, SparseCore 0:
  10.6 88.9 all-gather.4
  103.0 89.2 all-gather.2
where the time goes:
time: 663 us; the launch traced here: 659 us
  waiting for transfers between devices  347 us (52%)
  local copies, waits for them, and re-layouts  152 us (23%)
  other arithmetic  75.2 us (11%)
  matrix products  52.2 us (8%)
  starting transfers between devices  18 us (3%)
  between operations  13.5 us (2%)
    ppermute x14, waiting for transfers between devices, from_behind(): lax.ppermute(value, axis, [(source, source + steps) for source in range(i...  196 us
    all_gather x1, waiting for transfers between devices, per_device(): lax.all_gather(down_blocks, 'fsdp', axis=1, tiled=True)  80.8 us
    all_gather x1, waiting for transfers between devices, per_device(): lax.all_gather(up_blocks, 'fsdp', axis=1, tiled=True)  70.4 us
    gather x16, local copies, waits for them, and re-layouts, layer(): picked = normed.reshape(count, blocks_in, BLK)[:, up_index, :]  36.6 us
    dot_general x8, matrix products, layer(): jnp.einsum('ncr,crj->ncj', picked, weights_up, preferred_element_type=jnp...  33 us
    all_gather x1, other arithmetic, per_device(): lax.all_gather(up_blocks, 'fsdp', axis=1, tiled=True)  20.4 us
    dot_general x8, matrix products, layer(): jnp.einsum('ncr,crj->ncj', second, weights_down, preferred_element_type=j...  19.2 us
    ppermute x14, starting transfers between devices, from_behind(): lax.ppermute(value, axis, [(source, source + steps) for source in range(i...  17.9 us
  transfers between devices with their start and end apart: 16, of which 16 were waited for; matrix products, arithmetic and copies ran while one was open for 9% of the time, Pallas kernels for 0%

commit v1 on v0

--- a/solution.py
+++ b/solution.py
@@ -1,6 +1,7 @@
 import jax
 import jax.numpy as jnp
 from jax import lax
+from jax.sharding import Mesh
 from jax.sharding import PartitionSpec as P
 
 BLK = 64
@@ -8,11 +9,25 @@
 DOWN_DEPTH = 2
 KEEP_DEV = 128
 
+SEC = ("zl", "x")
+FS = ("zh", "y", "c")
+
 
 def from_behind(value, axis, steps):
     count = lax.axis_size(axis)
     initial, last = (max(0, -steps), min(count, count - steps))
     return lax.ppermute(value, axis, [(source, source + steps) for source in range(initial, last)])
+
+
+def gather_blocks(shard):
+    n = shard.shape[1]
+    rows = shard.reshape(n * 32, 128)
+    rows = lax.all_gather(rows, "zh", axis=0, tiled=True)
+    rows = lax.all_gather(rows, ("y", "c"), axis=0, tiled=True)
+    zh = lax.axis_size("zh")
+    yc = rows.shape[0] // (zh * n * 32)
+    rows = rows.reshape(yc, zh, n * 32, 128).transpose(1, 0, 2, 3)
+    return rows.reshape(zh * yc * n, 4096)
 
 
 def make_layer(gain, up_index, up_values, down_index, down_values):
@@ -43,12 +58,10 @@
 
 
 def per_device(activations, keep, gains, up_rows, up_blocks, down_rows, down_blocks):
-    up_all, down_all = (
-        lax.all_gather(up_blocks, "fsdp", axis=1, tiled=True),
-        lax.all_gather(down_blocks, "fsdp", axis=1, tiled=True),
-    )
+    up_all = gather_blocks(up_blocks)
+    down_all = gather_blocks(down_blocks)
     apply = make_layer(
-        gains[0], up_rows[0].reshape(-1), up_all[0], down_rows[0].reshape(-1), down_all[0]
+        gains[0], up_rows[0].reshape(-1), up_all, down_rows[0].reshape(-1), down_all
     )
     places = jnp.cumsum(keep) - 1
     target = jnp.where(keep == 1, places, KEEP_DEV)
@@ -59,8 +72,8 @@
     )
     selected = activations[chosen]
     width = selected.shape[1]
-    section = lax.axis_index("section")
-    sections = lax.axis_size("section")
+    section = lax.axis_index(SEC)
+    sections = lax.axis_size(SEC)
     pieces = 8
     group_rows = selected.shape[0] // pieces
     split = selected.reshape(pieces, group_rows, width)
@@ -79,7 +92,7 @@
     def turn_step(turn, carry):
         held, record = carry
         result, record = advance(turn, held, record)
-        held = from_behind(result, "section", 1)
+        held = from_behind(result, SEC, 1)
         return (held, record)
 
     final_turn = sections + pieces - 2
@@ -91,18 +104,24 @@
 
 
 def solution(mesh):
+    zh = 4
+    yc = mesh.shape["fsdp"] // zh
+    zl = 2
+    xs = mesh.shape["section"] // zl
+    devices = mesh.devices.reshape(zl, xs, zh, yc // 2, 2)
+    fine = Mesh(devices, ("zl", "x", "zh", "y", "c"))
     return jax.shard_map(
         per_device,
-        mesh=mesh,
+        mesh=fine,
         in_specs=(
-            P("fsdp", None),
-            P("fsdp"),
-            P("section", None),
-            P("section", None, None),
-            P("section", "fsdp", None),
-            P("section", None, None),
-            P("section", "fsdp", None),
+            P(FS, None),
+            P(FS),
+            P(SEC, None),
+            P(SEC, None, None),
+            P(SEC, FS, None),
+            P(SEC, None, None),
+            P(SEC, FS, None),
         ),
-        out_specs=P("section", "fsdp", None),
+        out_specs=P(SEC, FS, None),
         check_vma=False,
     )

time: 663 us -> 563 us (0.85)
  the two profiles are of different devices: /device:TPU:86 before, /device:TPU:70 now
where the time goes in v1:
time: 563 us; the launch traced here: 559 us
  waiting for transfers between devices  242 us (43%)
  local copies, waits for them, and re-layouts  156 us (28%)
  matrix products  52.2 us (9%)
  other arithmetic  42.4 us (8%)
  blocking collectives  34.2 us (6%)
  starting transfers between devices  18 us (3%)
  between operations  13.5 us (2%)
    ppermute x14, waiting for transfers between devices, from_behind(): lax.ppermute(value, axis, [(source, source + steps) for source in range(i...  193 us
    all_gather x2, waiting for transfers between devices, gather_blocks(): rows = lax.all_gather(rows, ('y', 'c'), axis=0, tiled=True)  48.3 us
    gather x16, local copies, waits for them, and re-layouts, layer(): picked = normed.reshape(count, blocks_in, BLK)[:, up_index, :]  36.5 us
    all_gather x2, blocking collectives, gather_blocks(): rows = lax.all_gather(rows, 'zh', axis=0, tiled=True)  34.2 us
    dot_general x8, matrix products, layer(): jnp.einsum('ncr,crj->ncj', picked, weights_up, preferred_element_type=jnp...  33 us
    dot_general x8, matrix products, layer(): jnp.einsum('ncr,crj->ncj', second, weights_down, preferred_element_type=j...  19.2 us
    ppermute x14, starting transfers between devices, from_behind(): lax.ppermute(value, axis, [(source, source + steps) for source in range(i...  17.9 us
    dynamic_update_slice x15, other arithmetic, advance(): record = lax.dynamic_update_index_in_dim(record, updated, slot, 0)  17.9 us
  transfers between devices with their start and end apart: 16, of which 16 were waited for; matrix products, arithmetic and copies ran while one was open for 9% of the time, Pallas kernels for 0%

profile of v1, /device:TPU:70, one launch (start us, length us, event | category | flops | bytes accessed | tf_op | source)
XLA Modules:
  0.0 559.4 jit_solution(17447083865191138212)
XLA Ops:
  8.2 19.2 %all_gather.14 = bf16[384,128]{1,0:T(8,128)(2,1)} all-gather(bf16[96,128]{1,0:T(8,128)(2,1)S(1)} %reshape.94), channel_id=1, replica_groups=mesh['zl'=2,'x'=4,'zh'=4,'y'=8,'c'=2] {'zh'}, dimensions={0}, use_global_device_ids=true | all-gather | bytes 122880 | tf_op jit(solution)/shard_map/all_gather | solution.py:25
  27.6 15.0 %all_gather.12 = bf16[768,128]{1,0:T(8,128)(2,1)} all-gather(bf16[192,128]{1,0:T(8,128)(2,1)S(1)} %reshape.92), channel_id=1, replica_groups=mesh['zl'=2,'x'=4,'zh'=4,'y'=8,'c'=2] {'zh'}, dimensions={0}, use_global_device_ids=true | all-gather | bytes 245760 | tf_op jit(solution)/shard_map/all_gather | solution.py:25
  44.4 2.6 gather_fusion.4
  48.0 2.7 copy.61
  51.9 16.2 %all-gather.5.cloned.1.call-done = bf16[6144,128]{1,0:T(8,128)(2,1)} async-done(((bf16[384,128]{1,0:T(8,128)(2,1)}), bf16[6144,128]{1,0:T(8,128)(2,1)}) %all-gather.5.cloned.1.call-update) | async-done | bytes 1572880 | tf_op jit(solution)/shard_map/all_gather | solution.py:26
  68.1 2.7 copy.41
  70.8 5.1 reshape_reshape.7
  76.0 4.3 copy.43
  80.2 32.2 %all-gather.3.cloned.1.call-done = bf16[12288,128]{1,0:T(8,128)(2,1)} async-done(((bf16[768,128]{1,0:T(8,128)(2,1)}), bf16[12288,128]{1,0:T(8,128)(2,1)}) %all-gather.3.cloned.1.call-update) | async-done | bytes 3145744 | tf_op jit(solution)/shard_map/all_gather | solution.py:26
  112.4 3.8 copy.39
  116.2 8.8 %reshape_reshape.6 = bf16[192,128,64]{2,1,0:T(8,128)(2,1)} reshape(bf16[4,16,192,128]{3,2,1,0:T(8,128)(2,1)} %copy.39) | data formatting | bytes 6291456 | tf_op jit(solution)/shard_map/reshape;reshape | solution.py:38
  125.0 6.7 %copy.42 = bf16[192,128,64]{1,2,0:T(8,128)(2,1)} copy(bf16[192,128,64]{2,1,0:T(8,128)(2,1)} %reshape_reshape.6) | data formatting | bytes 6291456 | tf_op jit(solution)/shard_map/while | solution.py:99
  131.7 374.5 %while.16 = (s32[]{:T(128)}, bf16[16,6144]{1,0:T(8,128)(2,1)S(1)}, bf16[8,16,6144]{2,1,0:T(8,128)(2,1)}, s32[]{:T(128)}, pred[]{:T(512)}, /*index=5*/bf16[8,16,6...) while((s32[]{:T(128)}, bf16[16,6144]{1,0:T(8,128)(2,1)S(1)}, ...), condition=%wide.region_7.8_spmd, body=%wide.region_3.0_spmd.sunk | while | flops 78450392 | bytes 21276344 | solution.py:99
  135.4 6.1 %collective-permute-done = bf16[16,6144]{1,0:T(8,128)(2,1)S(1)} collective-permute-done((bf16[16,6144]{1,0:T(8,128)(2,1)}, bf16[16,6144]{1,0:T(8,128)(2,1)S(1)}, u32[]{:S(2)}, u32[]{:S(2)}) %collective-permute-start) | collective-permute-done | bytes 196640 | tf_op jit(solution)/shard_map/while/body/eval_jaxpr/ppermute | solution.py:19
  145.2 5.3 collective-permute-done
  154.2 4.8 collective-permute-done
  162.6 4.8 collective-permute-done
  171.0 4.9 collective-permute-done
  179.6 6.9 %collective-permute-done = bf16[16,6144]{1,0:T(8,128)(2,1)S(1)} collective-permute-done((bf16[16,6144]{1,0:T(8,128)(2,1)}, bf16[16,6144]{1,0:T(8,128)(2,1)S(1)}, u32[]{:S(2)}, u32[]{:S(2)}) %collective-permute-start) | collective-permute-done | bytes 196640 | tf_op jit(solution)/shard_map/while/body/eval_jaxpr/ppermute | solution.py:19
  190.2 118.9 %collective-permute-done = bf16[16,6144]{1,0:T(8,128)(2,1)S(1)} collective-permute-done((bf16[16,6144]{1,0:T(8,128)(2,1)}, bf16[16,6144]{1,0:T(8,128)(2,1)S(1)}, u32[]{:S(2)}, u32[]{:S(2)}) %collective-permute-start) | collective-permute-done | bytes 196640 | tf_op jit(solution)/shard_map/while/body/eval_jaxpr/ppermute | solution.py:19
  309.1 18.3 %conditional.4 = (bf16[16,6144]{1,0:T(8,128)(2,1)}) conditional(s32[]{:T(128)} %convert_element_type.82, () %tuple.59, (pred[]{:T(512)}, s32[]{:T(128)}, bf16[8,16,6144]{2,1,0:T(8,128)(2,1)}, bf16[16,6144]{1,0:T(8,128)(2,1)S(1)}, f32[6144]{0:T(1024)}, /*index=5*/s32[384]{0:T(512)S(1)}, bf16[192,128,64]{1,2,0:T(8,128)(2,1)}, s32[192]{0:T(256)S(1)}, ...), branch_computations={%region_4.4_spmd, %region_5.6_spmd} | conditional | flops 78352080 | bytes 19506548 | solution.py:85
  312.3 2.5 gather_fusion
  318.1 3.9 fusion.7
  323.4 2.3 convolution_bitcast_fusion
  331.3 6.0 %collective-permute-done = bf16[16,6144]{1,0:T(8,128)(2,1)S(1)} collective-permute-done((bf16[16,6144]{1,0:T(8,128)(2,1)}, bf16[16,6144]{1,0:T(8,128)(2,1)S(1)}, u32[]{:S(2)}, u32[]{:S(2)}) %collective-permute-start) | collective-permute-done | bytes 196640 | tf_op jit(solution)/shard_map/while/body/eval_jaxpr/ppermute | solution.py:19
  337.2 18.3 %conditional.4 = (bf16[16,6144]{1,0:T(8,128)(2,1)}) conditional(s32[]{:T(128)} %convert_element_type.82, () %tuple.59, (pred[]{:T(512)}, s32[]{:T(128)}, bf16[8,16,6144]{2,1,0:T(8,128)(2,1)}, bf16[16,6144]{1,0:T(8,128)(2,1)S(1)}, f32[6144]{0:T(1024)}, /*index=5*/s32[384]{0:T(512)S(1)}, bf16[192,128,64]{1,2,0:T(8,128)(2,1)}, s32[192]{0:T(256)S(1)}, ...), branch_computations={%region_4.4_spmd, %region_5.6_spmd} | conditional | flops 78352080 | bytes 19506548 | solution.py:85
  340.4 2.5 gather_fusion
  346.3 3.9 fusion.7
  351.6 2.3 convolution_bitcast_fusion
  359.5 5.9 %collective-permute-done = bf16[16,6144]{1,0:T(8,128)(2,1)S(1)} collective-permute-done((bf16[16,6144]{1,0:T(8,128)(2,1)}, bf16[16,6144]{1,0:T(8,128)(2,1)S(1)}, u32[]{:S(2)}, u32[]{:S(2)}) %collective-permute-start) | collective-permute-done | bytes 196640 | tf_op jit(solution)/shard_map/while/body/eval_jaxpr/ppermute | solution.py:19
  365.4 18.3 %conditional.4 = (bf16[16,6144]{1,0:T(8,128)(2,1)}) conditional(s32[]{:T(128)} %convert_element_type.82, () %tuple.59, (pred[]{:T(512)}, s32[]{:T(128)}, bf16[8,16,6144]{2,1,0:T(8,128)(2,1)}, bf16[16,6144]{1,0:T(8,128)(2,1)S(1)}, f32[6144]{0:T(1024)}, /*index=5*/s32[384]{0:T(512)S(1)}, bf16[192,128,64]{1,2,0:T(8,128)(2,1)}, s32[192]{0:T(256)S(1)}, ...), branch_computations={%region_4.4_spmd, %region_5.6_spmd} | conditional | flops 78352080 | bytes 19506548 | solution.py:85
  368.6 2.5 gather_fusion
  374.4 3.9 fusion.7
  379.7 2.3 convolution_bitcast_fusion
  387.6 6.0 %collective-permute-done = bf16[16,6144]{1,0:T(8,128)(2,1)S(1)} collective-permute-done((bf16[16,6144]{1,0:T(8,128)(2,1)}, bf16[16,6144]{1,0:T(8,128)(2,1)S(1)}, u32[]{:S(2)}, u32[]{:S(2)}) %collective-permute-start) | collective-permute-done | bytes 196640 | tf_op jit(solution)/shard_map/while/body/eval_jaxpr/ppermute | solution.py:19
  393.6 18.3 %conditional.4 = (bf16[16,6144]{1,0:T(8,128)(2,1)}) conditional(s32[]{:T(128)} %convert_element_type.82, () %tuple.59, (pred[]{:T(512)}, s32[]{:T(128)}, bf16[8,16,6144]{2,1,0:T(8,128)(2,1)}, bf16[16,6144]{1,0:T(8,128)(2,1)S(1)}, f32[6144]{0:T(1024)}, /*index=5*/s32[384]{0:T(512)S(1)}, bf16[192,128,64]{1,2,0:T(8,128)(2,1)}, s32[192]{0:T(256)S(1)}, ...), branch_computations={%region_4.4_spmd, %region_5.6_spmd} | conditional | flops 78352080 | bytes 19506548 | solution.py:85
  396.8 2.5 gather_fusion
  402.6 3.9 fusion.7
  407.9 2.3 convolution_bitcast_fusion
  415.8 5.9 %collective-permute-done = bf16[16,6144]{1,0:T(8,128)(2,1)S(1)} collective-permute-done((bf16[16,6144]{1,0:T(8,128)(2,1)}, bf16[16,6144]{1,0:T(8,128)(2,1)S(1)}, u32[]{:S(2)}, u32[]{:S(2)}) %collective-permute-start) | collective-permute-done | bytes 196640 | tf_op jit(solution)/shard_map/while/body/eval_jaxpr/ppermute | solution.py:19
  421.7 18.3 %conditional.4 = (bf16[16,6144]{1,0:T(8,128)(2,1)}) conditional(s32[]{:T(128)} %convert_element_type.82, () %tuple.59, (pred[]{:T(512)}, s32[]{:T(128)}, bf16[8,16,6144]{2,1,0:T(8,128)(2,1)}, bf16[16,6144]{1,0:T(8,128)(2,1)S(1)}, f32[6144]{0:T(1024)}, /*index=5*/s32[384]{0:T(512)S(1)}, bf16[192,128,64]{1,2,0:T(8,128)(2,1)}, s32[192]{0:T(256)S(1)}, ...), branch_computations={%region_4.4_spmd, %region_5.6_spmd} | conditional | flops 78352080 | bytes 19506548 | solution.py:85
  425.0 2.5 gather_fusion
  430.8 3.9 fusion.7
  436.1 2.3 convolution_bitcast_fusion
  444.0 6.0 %collective-permute-done = bf16[16,6144]{1,0:T(8,128)(2,1)S(1)} collective-permute-done((bf16[16,6144]{1,0:T(8,128)(2,1)}, bf16[16,6144]{1,0:T(8,128)(2,1)S(1)}, u32[]{:S(2)}, u32[]{:S(2)}) %collective-permute-start) | collective-permute-done | bytes 196640 | tf_op jit(solution)/shard_map/while/body/eval_jaxpr/ppermute | solution.py:19
  449.9 18.3 %conditional.4 = (bf16[16,6144]{1,0:T(8,128)(2,1)}) conditional(s32[]{:T(128)} %convert_element_type.82, () %tuple.59, (pred[]{:T(512)}, s32[]{:T(128)}, bf16[8,16,6144]{2,1,0:T(8,128)(2,1)}, bf16[16,6144]{1,0:T(8,128)(2,1)S(1)}, f32[6144]{0:T(1024)}, /*index=5*/s32[384]{0:T(512)S(1)}, bf16[192,128,64]{1,2,0:T(8,128)(2,1)}, s32[192]{0:T(256)S(1)}, ...), branch_computations={%region_4.4_spmd, %region_5.6_spmd} | conditional | flops 78352080 | bytes 19506548 | solution.py:85
  453.1 2.5 gather_fusion
  459.0 3.9 fusion.7
  464.2 2.3 convolution_bitcast_fusion
  472.1 5.9 %collective-permute-done = bf16[16,6144]{1,0:T(8,128)(2,1)S(1)} collective-permute-done((bf16[16,6144]{1,0:T(8,128)(2,1)}, bf16[16,6144]{1,0:T(8,128)(2,1)S(1)}, u32[]{:S(2)}, u32[]{:S(2)}) %collective-permute-start) | collective-permute-done | bytes 196640 | tf_op jit(solution)/shard_map/while/body/eval_jaxpr/ppermute | solution.py:19
  478.1 18.3 %conditional.4 = (bf16[16,6144]{1,0:T(8,128)(2,1)}) conditional(s32[]{:T(128)} %convert_element_type.82, () %tuple.59, (pred[]{:T(512)}, s32[]{:T(128)}, bf16[8,16,6144]{2,1,0:T(8,128)(2,1)}, bf16[16,6144]{1,0:T(8,128)(2,1)S(1)}, f32[6144]{0:T(1024)}, /*index=5*/s32[384]{0:T(512)S(1)}, bf16[192,128,64]{1,2,0:T(8,128)(2,1)}, s32[192]{0:T(256)S(1)}, ...), branch_computations={%region_4.4_spmd, %region_5.6_spmd} | conditional | flops 78352080 | bytes 19506548 | solution.py:85
  481.3 2.5 gather_fusion
  487.1 3.9 fusion.7
  492.4 2.3 convolution_bitcast_fusion
  500.3 6.0 %collective-permute-done = bf16[16,6144]{1,0:T(8,128)(2,1)S(1)} collective-permute-done((bf16[16,6144]{1,0:T(8,128)(2,1)}, bf16[16,6144]{1,0:T(8,128)(2,1)S(1)}, u32[]{:S(2)}, u32[]{:S(2)}) %collective-permute-start) | collective-permute-done | bytes 196640 | tf_op jit(solution)/shard_map/while/body/eval_jaxpr/ppermute | solution.py:19
  508.6 38.0 %conditional.2 = (bf16[16,6144]{1,0:T(8,128)(2,1)}) conditional(s32[]{:T(128)} %convert_element_type.51, () %tuple.41, (pred[]{:T(512)}, bf16[128,6144]{1,0:T(8,128)(2,1)}, bf16[16,6144]{1,0:T(8,128)(2,1)}, f32[6144]{0:T(1024)}, s32[384]{0:T(512)S(1)}, /*index=5*/bf16[192,128,64]{2,1,0:T(8,128)(2,1)}, s32[192]{0:T(256)S(1)}, ...), branch_computations={%region_8.9_spmd, %region_9.11_spmd} | conditional | flops 78352080 | bytes 18720036 | solution.py:85
  516.1 3.1 gather_fusion.2
  519.2 3.0 copy.33
  522.2 3.3 reshape.78
  525.5 5.7 %fusion.21 = bf16[16,192,64]{2,0,1:T(8,128)(2,1)} fusion(bf16[192,128,64]{2,1,0:T(8,128)(2,1)} %get-tuple-element.387, bf16[16,192,128]{2,1,0:T(8,128)(2,1)} %reshape.78), kind=kOutput, calls=%fused_computation.43 | convolution fusion | flops 52101120 | bytes 4325376 | tf_op jit(solution)/shard_map/cond/branch_1_fun/ncr,crj->ncj/dot_general | solution.py:49
  531.3 2.8 gather_fusion.3
  536.3 2.3 reshape.79
  538.6 2.9 convolution_bitcast_fusion.1
  547.6 3.7 scatter_fusion
  (262 shorter events, 148.8 us)
Async XLA Ops:
  6.5 36.1 %copy-start.9 = (s32[160]{0:T(256)S(1)}, s32[160]{0:T(256)}, u32[]{:S(2)}) copy-start(s32[160]{0:T(256)} %param.14) | copy-start | bytes 1924
  6.5 20.9 %copy-start.6 = (bf16[1,6,4096]{2,1,0:T(8,128)(2,1)S(1)}, bf16[1,6,4096]{2,1,0:T(8,128)(2,1)}, u32[]{:S(2)}) copy-start(bf16[1,6,4096]{2,1,0:T(8,128)(2,1)} %param.17) | copy-start | bytes 147460
  6.5 1.6 copy-start.7
  6.5 61.5 %all-gather.5.cloned.1.call-start = ((), (), s32[]{:S(2)}) async-start(), calls=%async_computation.1 | async-start | bytes 1671168 | tf_op jit(solution)/shard_map/all_gather | solution.py:26
  27.4 85.0 %all-gather.3.cloned.1.call-start = ((), (), s32[]{:S(2)}) async-start(), calls=%async_computation | async-start | bytes 3342336 | tf_op jit(solution)/shard_map/all_gather | solution.py:26
  48.0 2.8 copy-start.10
  48.0 3.0 copy-start.11
  48.0 3.3 copy-start.8
  132.4 9.1 %collective-permute-start = (bf16[16,6144]{1,0:T(8,128)(2,1)}, bf16[16,6144]{1,0:T(8,128)(2,1)S(1)}, u32[]{:S(2)}, u32[]{:S(2)}) collective-permute-start(bf16[16,6144]{1,0:T(8,128)(2,1)} %get-tuple-element.529), channel_id=1, source_target_pairs={{0,64},{64,128},{128,192},{192,256},{256,320},{320,384},{384,448},... | collective-permute-start | bytes 589832 | tf_op jit(solution)/shard_map/while/body/eval_jaxpr/ppermute | solution.py:19
  142.2 8.3 %collective-permute-start = (bf16[16,6144]{1,0:T(8,128)(2,1)}, bf16[16,6144]{1,0:T(8,128)(2,1)S(1)}, u32[]{:S(2)}, u32[]{:S(2)}) collective-permute-start(bf16[16,6144]{1,0:T(8,128)(2,1)} %get-tuple-element.529), channel_id=1, source_target_pairs={{0,64},{64,128},{128,192},{192,256},{256,320},{320,384},{384,448},... | collective-permute-start | bytes 589832 | tf_op jit(solution)/shard_map/while/body/eval_jaxpr/ppermute | solution.py:19
  151.2 7.8 %collective-permute-start = (bf16[16,6144]{1,0:T(8,128)(2,1)}, bf16[16,6144]{1,0:T(8,128)(2,1)S(1)}, u32[]{:S(2)}, u32[]{:S(2)}) collective-permute-start(bf16[16,6144]{1,0:T(8,128)(2,1)} %get-tuple-element.529), channel_id=1, source_target_pairs={{0,64},{64,128},{128,192},{192,256},{256,320},{320,384},{384,448},... | collective-permute-start | bytes 589832 | tf_op jit(solution)/shard_map/while/body/eval_jaxpr/ppermute | solution.py:19
  159.6 7.8 %collective-permute-start = (bf16[16,6144]{1,0:T(8,128)(2,1)}, bf16[16,6144]{1,0:T(8,128)(2,1)S(1)}, u32[]{:S(2)}, u32[]{:S(2)}) collective-permute-start(bf16[16,6144]{1,0:T(8,128)(2,1)} %get-tuple-element.529), channel_id=1, source_target_pairs={{0,64},{64,128},{128,192},{192,256},{256,320},{320,384},{384,448},... | collective-permute-start | bytes 589832 | tf_op jit(solution)/shard_map/while/body/eval_jaxpr/ppermute | solution.py:19
  168.1 7.9 %collective-permute-start = (bf16[16,6144]{1,0:T(8,128)(2,1)}, bf16[16,6144]{1,0:T(8,128)(2,1)S(1)}, u32[]{:S(2)}, u32[]{:S(2)}) collective-permute-start(bf16[16,6144]{1,0:T(8,128)(2,1)} %get-tuple-element.529), channel_id=1, source_target_pairs={{0,64},{64,128},{128,192},{192,256},{256,320},{320,384},{384,448},... | collective-permute-start | bytes 589832 | tf_op jit(solution)/shard_map/while/body/eval_jaxpr/ppermute | solution.py:19
  176.7 9.9 %collective-permute-start = (bf16[16,6144]{1,0:T(8,128)(2,1)}, bf16[16,6144]{1,0:T(8,128)(2,1)S(1)}, u32[]{:S(2)}, u32[]{:S(2)}) collective-permute-start(bf16[16,6144]{1,0:T(8,128)(2,1)} %get-tuple-element.529), channel_id=1, source_target_pairs={{0,64},{64,128},{128,192},{192,256},{256,320},{320,384},{384,448},... | collective-permute-start | bytes 589832 | tf_op jit(solution)/shard_map/while/body/eval_jaxpr/ppermute | solution.py:19
  187.2 121.8 %collective-permute-start = (bf16[16,6144]{1,0:T(8,128)(2,1)}, bf16[16,6144]{1,0:T(8,128)(2,1)S(1)}, u32[]{:S(2)}, u32[]{:S(2)}) collective-permute-start(bf16[16,6144]{1,0:T(8,128)(2,1)} %get-tuple-element.529), channel_id=1, source_target_pairs={{0,64},{64,128},{128,192},{192,256},{256,320},{320,384},{384,448},... | collective-permute-start | bytes 589832 | tf_op jit(solution)/shard_map/while/body/eval_jaxpr/ppermute | solution.py:19
  310.2 0.7 copy-start.1
  325.7 0.9 copy-start.2
  327.4 9.9 %collective-permute-start = (bf16[16,6144]{1,0:T(8,128)(2,1)}, bf16[16,6144]{1,0:T(8,128)(2,1)S(1)}, u32[]{:S(2)}, u32[]{:S(2)}) collective-permute-start(bf16[16,6144]{1,0:T(8,128)(2,1)} %get-tuple-element.529), channel_id=1, source_target_pairs={{0,64},{64,128},{128,192},{192,256},{256,320},{320,384},{384,448},... | collective-permute-start | bytes 589832 | tf_op jit(solution)/shard_map/while/body/eval_jaxpr/ppermute | solution.py:19
  338.3 0.7 copy-start.1
  353.9 0.9 copy-start.2
  355.5 9.9 %collective-permute-start = (bf16[16,6144]{1,0:T(8,128)(2,1)}, bf16[16,6144]{1,0:T(8,128)(2,1)S(1)}, u32[]{:S(2)}, u32[]{:S(2)}) collective-permute-start(bf16[16,6144]{1,0:T(8,128)(2,1)} %get-tuple-element.529), channel_id=1, source_target_pairs={{0,64},{64,128},{128,192},{192,256},{256,320},{320,384},{384,448},... | collective-permute-start | bytes 589832 | tf_op jit(solution)/shard_map/while/body/eval_jaxpr/ppermute | solution.py:19
  366.5 0.7 copy-start.1
  382.0 0.9 copy-start.2
  383.7 9.9 %collective-permute-start = (bf16[16,6144]{1,0:T(8,128)(2,1)}, bf16[16,6144]{1,0:T(8,128)(2,1)S(1)}, u32[]{:S(2)}, u32[]{:S(2)}) collective-permute-start(bf16[16,6144]{1,0:T(8,128)(2,1)} %get-tuple-element.529), channel_id=1, source_target_pairs={{0,64},{64,128},{128,192},{192,256},{256,320},{320,384},{384,448},... | collective-permute-start | bytes 589832 | tf_op jit(solution)/shard_map/while/body/eval_jaxpr/ppermute | solution.py:19
  394.7 0.7 copy-start.1
  410.2 0.9 copy-start.2
  411.9 9.9 %collective-permute-start = (bf16[16,6144]{1,0:T(8,128)(2,1)}, bf16[16,6144]{1,0:T(8,128)(2,1)S(1)}, u32[]{:S(2)}, u32[]{:S(2)}) collective-permute-start(bf16[16,6144]{1,0:T(8,128)(2,1)} %get-tuple-element.529), channel_id=1, source_target_pairs={{0,64},{64,128},{128,192},{192,256},{256,320},{320,384},{384,448},... | collective-permute-start | bytes 589832 | tf_op jit(solution)/shard_map/while/body/eval_jaxpr/ppermute | solution.py:19
  422.9 0.7 copy-start.1
  438.4 0.9 copy-start.2
  440.1 9.9 %collective-permute-start = (bf16[16,6144]{1,0:T(8,128)(2,1)}, bf16[16,6144]{1,0:T(8,128)(2,1)S(1)}, u32[]{:S(2)}, u32[]{:S(2)}) collective-permute-start(bf16[16,6144]{1,0:T(8,128)(2,1)} %get-tuple-element.529), channel_id=1, source_target_pairs={{0,64},{64,128},{128,192},{192,256},{256,320},{320,384},{384,448},... | collective-permute-start | bytes 589832 | tf_op jit(solution)/shard_map/while/body/eval_jaxpr/ppermute | solution.py:19
  451.0 0.7 copy-start.1
  466.6 0.9 copy-start.2
  468.2 9.9 %collective-permute-start = (bf16[16,6144]{1,0:T(8,128)(2,1)}, bf16[16,6144]{1,0:T(8,128)(2,1)S(1)}, u32[]{:S(2)}, u32[]{:S(2)}) collective-permute-start(bf16[16,6144]{1,0:T(8,128)(2,1)} %get-tuple-element.529), channel_id=1, source_target_pairs={{0,64},{64,128},{128,192},{192,256},{256,320},{320,384},{384,448},... | collective-permute-start | bytes 589832 | tf_op jit(solution)/shard_map/while/body/eval_jaxpr/ppermute | solution.py:19
  479.2 0.7 copy-start.1
  494.7 0.9 copy-start.2
  496.4 9.9 %collective-permute-start = (bf16[16,6144]{1,0:T(8,128)(2,1)}, bf16[16,6144]{1,0:T(8,128)(2,1)S(1)}, u32[]{:S(2)}, u32[]{:S(2)}) collective-permute-start(bf16[16,6144]{1,0:T(8,128)(2,1)} %get-tuple-element.529), channel_id=1, source_target_pairs={{0,64},{64,128},{128,192},{192,256},{256,320},{320,384},{384,448},... | collective-permute-start | bytes 589832 | tf_op jit(solution)/shard_map/while/body/eval_jaxpr/ppermute | solution.py:19
  506.3 0.7 copy-start.4
  508.6 38.0 %copy-start.3 = (bf16[8,16,6144]{2,1,0:T(8,128)(2,1)S(1)}, bf16[8,16,6144]{2,1,0:T(8,128)(2,1)}, u32[]{:S(2)}) copy-start(bf16[8,16,6144]{2,1,0:T(8,128)(2,1)} %get-tuple-element.350) | copy-start | bytes 4718596
  509.9 0.7 copy-start.5
  551.3 1.3 copy-start
Sparse Core Ops, SparseCore 0:
  27.6 40.4 all-gather.4
  70.2 42.1 all-gather.2

commit v2 on v1

--- a/solution.py
+++ b/solution.py
@@ -19,23 +19,40 @@
     return lax.ppermute(value, axis, [(source, source + steps) for source in range(initial, last)])
 
 
-def gather_blocks(shard):
+def exchange_zh(part):
+    count = lax.axis_size("zh")
+    own = lax.axis_index("zh")
+    got = [part]
+    for shift in range(1, count):
+        got.append(lax.ppermute(part, "zh", [(i, (i + shift) % count) for i in range(count)]))
+    stacked = jnp.stack(got)
+    order = (own - jnp.arange(count, dtype=jnp.int32)) % count
+    return jnp.take(stacked, order, axis=0)
+
+
+def gather_up(shard):
+    cols = shard.shape[1] // UP_DEPTH
+    part = shard.reshape(cols, UP_DEPTH, BLK, BLK).transpose(0, 3, 1, 2)
+    part = part.reshape(cols, BLK, UP_DEPTH * BLK)
+    full = exchange_zh(part)
+    full = lax.all_gather(full, ("y", "c"), axis=1, tiled=True)
+    return full.reshape(-1, BLK, UP_DEPTH * BLK)
+
+
+def gather_rows(shard):
     n = shard.shape[1]
-    rows = shard.reshape(n * 32, 128)
-    rows = lax.all_gather(rows, "zh", axis=0, tiled=True)
-    rows = lax.all_gather(rows, ("y", "c"), axis=0, tiled=True)
-    zh = lax.axis_size("zh")
-    yc = rows.shape[0] // (zh * n * 32)
-    rows = rows.reshape(yc, zh, n * 32, 128).transpose(1, 0, 2, 3)
-    return rows.reshape(zh * yc * n, 4096)
+    part = shard.reshape(n * 32, 128)
+    full = exchange_zh(part)
+    full = lax.all_gather(full, ("y", "c"), axis=1, tiled=True)
+    return full.reshape(-1, 4096)
 
 
 def make_layer(gain, up_index, up_values, down_index, down_values):
     width = gain.shape[0]
-    hidden_width = up_values.shape[0] // UP_DEPTH * BLK
+    hidden_width = up_values.shape[0] * BLK
     blocks_in = width // BLK
     blocks_hid = hidden_width // BLK
-    weights_up = up_values.reshape(blocks_hid, UP_DEPTH * BLK, BLK)
+    weights_up = up_values
     weights_down = down_values.reshape(blocks_in, DOWN_DEPTH * BLK, BLK)
     gain_wide = gain.astype(jnp.float32)
 
@@ -46,7 +63,7 @@
         normed = (wide * lax.rsqrt(meansq + 1e-05) * gain_wide).astype(jnp.bfloat16)
         picked = normed.reshape(count, blocks_in, BLK)[:, up_index, :]
         picked = picked.reshape(count, blocks_hid, UP_DEPTH * BLK)
-        up_sums = jnp.einsum("ncr,crj->ncj", picked, weights_up, preferred_element_type=jnp.float32)
+        up_sums = jnp.einsum("ncr,cjr->ncj", picked, weights_up, preferred_element_type=jnp.float32)
         hidden = jax.nn.gelu(up_sums, approximate=True).astype(jnp.bfloat16)
         second = hidden[:, down_index, :].reshape(count, blocks_in, DOWN_DEPTH * BLK)
         down_sums = jnp.einsum(
@@ -58,8 +75,8 @@
 
 
 def per_device(activations, keep, gains, up_rows, up_blocks, down_rows, down_blocks):
-    up_all = gather_blocks(up_blocks)
-    down_all = gather_blocks(down_blocks)
+    up_all = gather_up(up_blocks)
+    down_all = gather_rows(down_blocks)
     apply = make_layer(
         gains[0], up_rows[0].reshape(-1), up_all, down_rows[0].reshape(-1), down_all
     )
@@ -95,9 +112,8 @@
         held = from_behind(result, SEC, 1)
         return (held, record)
 
-    final_turn = sections + pieces - 2
-    held, record = lax.fori_loop(0, final_turn, turn_step, (split[0], split))
-    result, record = advance(final_turn, held, record)
+    turns = sections + pieces - 1
+    held, record = lax.fori_loop(0, turns, turn_step, (split[0], split))
     final = record.reshape(selected.shape[0], width)
     merged = activations.at[chosen].set(final)
     return merged[None]

time: 563 us -> 519 us (0.922)
  local copies, waits for them, and re-layouts: 156 us -> 116 us
  blocking collectives: 34.2 us -> 0 us
  starting transfers between devices: 18 us -> 48.6 us
  waiting for transfers between devices: 242 us -> 257 us
  other arithmetic: 42.4 us -> 29.9 us
    all_gather x2 -> x0, blocking collectives: 34.2 us -> none  [gather_blocks(): rows = lax.all_gather(rows, 'zh', axis=0, tiled=True)]
    ppermute x0 -> x6, starting transfers between devices: none -> 29.2 us  [exchange_zh(): lax.ppermute(part, 'zh', [(i, (i + shift) % count) for i in range(count)])]
    another operation x9 -> x10, local copies, waits for them, and re-layouts: 13.7 us -> 0.38 us  [the longest x1 8.79 us: make_layer(): weights_up = up_values.reshape(blocks_hid, UP_DEPTH * BLK, BLK)]
    ppermute x14 -> x15, waiting for transfers between devices: 193 us -> 202 us  [from_behind(): lax.ppermute(value, axis, [(source, source + steps) for source in range(i...]
    ppermute x0 -> x6, waiting for transfers between devices: none -> 7.53 us  [exchange_zh(): lax.ppermute(part, 'zh', [(i, (i + shift) % count) for i in range(count)])]
    dynamic_update_slice x15, other arithmetic: 17.9 us -> 11.1 us  [advance(): record = lax.dynamic_update_index_in_dim(record, updated, slot, 0)]
    while x2 -> x1, local copies, waits for them, and re-layouts: 11 us -> 4.28 us  [per_device(): held, record = lax.fori_loop(0, turns, turn_step, (split[0], split))]
    transpose x2 -> x0, local copies, waits for them, and re-layouts: 6.52 us -> none  [gather_blocks(): rows = rows.reshape(yc, zh, n * 32, 128).transpose(1, 0, 2, 3)]
  transfers between devices with their start and end apart: 16 -> 23, of which waited for: 16 -> 20; matrix products, arithmetic and copies ran while one was open for 9% -> 9% of each run, Pallas kernels for 0% -> 0%
where the time goes in v2:
time: 519 us; the launch traced here: 516 us
  waiting for transfers between devices  257 us (50%)
  local copies, waits for them, and re-layouts  116 us (22%)
  matrix products  49.8 us (10%)
  starting transfers between devices  48.6 us (9%)
  other arithmetic  29.9 us (6%)
  between operations  13.7 us (3%)
    ppermute x15, waiting for transfers between devices, from_behind(): lax.ppermute(value, axis, [(source, source + steps) for source in range(i...  202 us
    gather x16, local copies, waits for them, and re-layouts, layer(): picked = normed.reshape(count, blocks_in, BLK)[:, up_index, :]  35 us
    all_gather x1, waiting for transfers between devices, gather_up(): full = lax.all_gather(full, ('y', 'c'), axis=1, tiled=True)  34.8 us
    dot_general x8, matrix products, layer(): jnp.einsum('ncr,cjr->ncj', picked, weights_up, preferred_element_type=jnp...  31.2 us
    ppermute x6, starting transfers between devices, exchange_zh(): lax.ppermute(part, 'zh', [(i, (i + shift) % count) for i in range(count)])  29.2 us
    ppermute x15, starting transfers between devices, from_behind(): lax.ppermute(value, axis, [(source, source + steps) for source in range(i...  19.4 us
    dot_general x8, matrix products, layer(): jnp.einsum('ncr,crj->ncj', second, weights_down, preferred_element_type=j...  18.6 us
    dynamic_slice x15, local copies, waits for them, and re-layouts, advance(): current = lax.dynamic_index_in_dim(record, slot, 0, keepdims=False)  14.2 us
  transfers between devices with their start and end apart: 23, of which 20 were waited for; matrix products, arithmetic and copies ran while one was open for 9% of the time, Pallas kernels for 0%

profile of v2, /device:TPU:70, one launch (start us, length us, event | category | flops | bytes accessed | tf_op | source)
XLA Modules:
  0.0 516.3 jit_solution(16447429242946423552)
XLA Ops:
  8.2 6.1 %collective-permute-start.4 = (bf16[96,128]{1,0:T(8,128)(2,1)S(1)}, bf16[96,128]{1,0:T(8,128)(2,1)S(1)}, u32[]{:S(2)}, u32[]{:S(2)}) collective-permute-start(bf16[96,128]{1,0:T(8,128)(2,1)S(1)} %reshape.126), channel_id=1, source_target_pairs={{0,16},{16,32},{32,48},{48,0},{1,17},{17,33},{33,49},{49,1},{2,18}... | collective-permute-start | bytes 73736 | tf_op jit(solution)/shard_map/ppermute | solution.py:27
  14.3 8.2 %collective-permute-start.5 = (bf16[96,128]{1,0:T(8,128)(2,1)S(1)}, bf16[96,128]{1,0:T(8,128)(2,1)S(1)}, u32[]{:S(2)}, u32[]{:S(2)}) collective-permute-start(bf16[96,128]{1,0:T(8,128)(2,1)S(1)} %reshape.126), channel_id=1, source_target_pairs={{0,32},{16,48},{32,0},{48,16},{1,33},{17,49},{33,1},{49,17},{2,34}... | collective-permute-start | bytes 73736 | tf_op jit(solution)/shard_map/ppermute | solution.py:27
  22.5 3.7 collective-permute-start.6
  26.3 2.8 collective-permute-done.6
  30.9 3.1 collective-permute-start.1
  34.0 6.0 %collective-permute-start.2 = (bf16[3,64,128]{2,1,0:T(8,128)(2,1)S(1)}, bf16[3,64,128]{2,1,0:T(8,128)(2,1)S(1)}, u32[]{:S(2)}, u32[]{:S(2)}) collective-permute-start(bf16[3,64,128]{2,1,0:T(8,128)(2,1)S(1)} %reshape.124), channel_id=1, source_target_pairs={{0,32},{16,48},{32,0},{48,16},{1,33},{17,49},{33,1},{49,17},{2,34}... | collective-permute-start | bytes 147464 | tf_op jit(solution)/shard_map/ppermute | solution.py:27
  40.0 2.1 collective-permute-start.3
  42.2 2.1 collective-permute-done.2
  44.3 2.6 collective-permute-done.3
  50.1 2.6 gather_fusion.2
  53.7 2.8 copy.27
  57.7 12.9 %all-gather.5.cloned.1.call-done = bf16[4,1536,128]{2,1,0:T(8,128)(2,1)} async-done(((bf16[4,96,128]{2,1,0:T(8,128)(2,1)}), bf16[4,1536,128]{2,1,0:T(8,128)(2,1)}) %all-gather.5.cloned.1.call-update) | async-done | bytes 1572880 | tf_op jit(solution)/shard_map/all_gather | solution.py:46
  70.6 5.1 reshape_reshape.3
  75.7 4.3 copy.17
  80.0 34.8 %all-gather.3.cloned.1.call-done = bf16[4,48,64,128]{3,2,1,0:T(8,128)(2,1)} async-done(((bf16[4,3,64,128]{3,2,1,0:T(8,128)(2,1)}), bf16[4,48,64,128]{3,2,1,0:T(8,128)(2,1)}) %all-gather.3.cloned.1.call-update) | async-done | bytes 3145744 | tf_op jit(solution)/shard_map/all_gather | solution.py:38
  114.8 388.6 %while.16 = (s32[]{:T(128)}, bf16[16,6144]{1,0:T(8,128)(2,1)S(1)}, bf16[8,16,6144]{2,1,0:T(8,128)(2,1)}, s32[]{:T(128)}, pred[]{:T(512)}, /*index=5*/bf16[8,16,6...) while((s32[]{:T(128)}, bf16[16,6144]{1,0:T(8,128)(2,1)S(1)}, ...), condition=%wide.region_7.8_spmd, body=%wide.region_3.7_spmd.sunk | while | flops 78450392 | bytes 21276344 | solution.py:116
  117.8 5.9 %collective-permute-done = bf16[16,6144]{1,0:T(8,128)(2,1)S(1)} collective-permute-done((bf16[16,6144]{1,0:T(8,128)(2,1)S(1)}, bf16[16,6144]{1,0:T(8,128)(2,1)S(1)}, u32[]{:S(2)}, u32[]{:S(2)}) %collective-permute-start) | collective-permute-done | bytes 196640 | tf_op jit(solution)/shard_map/while/body/eval_jaxpr/ppermute | solution.py:19
  126.8 5.1 collective-permute-done
  134.9 4.6 collective-permute-done
  142.5 4.6 collective-permute-done
  150.1 4.7 collective-permute-done
  157.8 6.7 %collective-permute-done = bf16[16,6144]{1,0:T(8,128)(2,1)S(1)} collective-permute-done((bf16[16,6144]{1,0:T(8,128)(2,1)S(1)}, bf16[16,6144]{1,0:T(8,128)(2,1)S(1)}, u32[]{:S(2)}, u32[]{:S(2)}) %collective-permute-start) | collective-permute-done | bytes 196640 | tf_op jit(solution)/shard_map/while/body/eval_jaxpr/ppermute | solution.py:19
  167.5 119.1 %collective-permute-done = bf16[16,6144]{1,0:T(8,128)(2,1)S(1)} collective-permute-done((bf16[16,6144]{1,0:T(8,128)(2,1)S(1)}, bf16[16,6144]{1,0:T(8,128)(2,1)S(1)}, u32[]{:S(2)}, u32[]{:S(2)}) %collective-permute-start) | collective-permute-done | bytes 196640 | tf_op jit(solution)/shard_map/while/body/eval_jaxpr/ppermute | solution.py:19
  286.6 17.7 %conditional.2 = (bf16[16,6144]{1,0:T(8,128)(2,1)S(1)}) conditional(s32[]{:T(128)} %convert_element_type.52, () %tuple.47, (pred[]{:T(512)}, s32[]{:T(128)}, bf16[8,16,6144]{2,1,0:T(8,128)(2,1)}, bf16[16,6144]{1,0:T(8,128)(2,1)S(1)}, f32[6144]{0:T(1024)}, /*index=5*/s32[384]{0:T(512)S(1)}, bf16[192,64,128]{2,1,0:T(8,128)(2,1)}, s32[192]{0:T(256)S(1)}, ...), branch_computations={%region_4.4_spmd, %region_5.6_spmd} | conditional | flops 78352080 | bytes 19506548 | solution.py:102
  289.8 2.6 gather_fusion
  295.7 3.9 fusion.7
  300.9 2.3 convolution_bitcast_fusion
  307.3 6.7 %collective-permute-done = bf16[16,6144]{1,0:T(8,128)(2,1)S(1)} collective-permute-done((bf16[16,6144]{1,0:T(8,128)(2,1)S(1)}, bf16[16,6144]{1,0:T(8,128)(2,1)S(1)}, u32[]{:S(2)}, u32[]{:S(2)}) %collective-permute-start) | collective-permute-done | bytes 196640 | tf_op jit(solution)/shard_map/while/body/eval_jaxpr/ppermute | solution.py:19
  313.9 17.7 %conditional.2 = (bf16[16,6144]{1,0:T(8,128)(2,1)S(1)}) conditional(s32[]{:T(128)} %convert_element_type.52, () %tuple.47, (pred[]{:T(512)}, s32[]{:T(128)}, bf16[8,16,6144]{2,1,0:T(8,128)(2,1)}, bf16[16,6144]{1,0:T(8,128)(2,1)S(1)}, f32[6144]{0:T(1024)}, /*index=5*/s32[384]{0:T(512)S(1)}, bf16[192,64,128]{2,1,0:T(8,128)(2,1)}, s32[192]{0:T(256)S(1)}, ...), branch_computations={%region_4.4_spmd, %region_5.6_spmd} | conditional | flops 78352080 | bytes 19506548 | solution.py:102
  317.2 2.6 gather_fusion
  323.0 3.9 fusion.7
  328.3 2.3 convolution_bitcast_fusion
  334.7 6.7 %collective-permute-done = bf16[16,6144]{1,0:T(8,128)(2,1)S(1)} collective-permute-done((bf16[16,6144]{1,0:T(8,128)(2,1)S(1)}, bf16[16,6144]{1,0:T(8,128)(2,1)S(1)}, u32[]{:S(2)}, u32[]{:S(2)}) %collective-permute-start) | collective-permute-done | bytes 196640 | tf_op jit(solution)/shard_map/while/body/eval_jaxpr/ppermute | solution.py:19
  341.3 17.7 %conditional.2 = (bf16[16,6144]{1,0:T(8,128)(2,1)S(1)}) conditional(s32[]{:T(128)} %convert_element_type.52, () %tuple.47, (pred[]{:T(512)}, s32[]{:T(128)}, bf16[8,16,6144]{2,1,0:T(8,128)(2,1)}, bf16[16,6144]{1,0:T(8,128)(2,1)S(1)}, f32[6144]{0:T(1024)}, /*index=5*/s32[384]{0:T(512)S(1)}, bf16[192,64,128]{2,1,0:T(8,128)(2,1)}, s32[192]{0:T(256)S(1)}, ...), branch_computations={%region_4.4_spmd, %region_5.6_spmd} | conditional | flops 78352080 | bytes 19506548 | solution.py:102
  344.5 2.6 gather_fusion
  350.4 3.9 fusion.7
  355.7 2.3 convolution_bitcast_fusion
  362.0 6.7 %collective-permute-done = bf16[16,6144]{1,0:T(8,128)(2,1)S(1)} collective-permute-done((bf16[16,6144]{1,0:T(8,128)(2,1)S(1)}, bf16[16,6144]{1,0:T(8,128)(2,1)S(1)}, u32[]{:S(2)}, u32[]{:S(2)}) %collective-permute-start) | collective-permute-done | bytes 196640 | tf_op jit(solution)/shard_map/while/body/eval_jaxpr/ppermute | solution.py:19
  368.7 17.7 %conditional.2 = (bf16[16,6144]{1,0:T(8,128)(2,1)S(1)}) conditional(s32[]{:T(128)} %convert_element_type.52, () %tuple.47, (pred[]{:T(512)}, s32[]{:T(128)}, bf16[8,16,6144]{2,1,0:T(8,128)(2,1)}, bf16[16,6144]{1,0:T(8,128)(2,1)S(1)}, f32[6144]{0:T(1024)}, /*index=5*/s32[384]{0:T(512)S(1)}, bf16[192,64,128]{2,1,0:T(8,128)(2,1)}, s32[192]{0:T(256)S(1)}, ...), branch_computations={%region_4.4_spmd, %region_5.6_spmd} | conditional | flops 78352080 | bytes 19506548 | solution.py:102
  371.9 2.6 gather_fusion
  377.8 3.9 fusion.7
  383.1 2.3 convolution_bitcast_fusion
  389.4 6.7 %collective-permute-done = bf16[16,6144]{1,0:T(8,128)(2,1)S(1)} collective-permute-done((bf16[16,6144]{1,0:T(8,128)(2,1)S(1)}, bf16[16,6144]{1,0:T(8,128)(2,1)S(1)}, u32[]{:S(2)}, u32[]{:S(2)}) %collective-permute-start) | collective-permute-done | bytes 196640 | tf_op jit(solution)/shard_map/while/body/eval_jaxpr/ppermute | solution.py:19
  396.1 17.7 %conditional.2 = (bf16[16,6144]{1,0:T(8,128)(2,1)S(1)}) conditional(s32[]{:T(128)} %convert_element_type.52, () %tuple.47, (pred[]{:T(512)}, s32[]{:T(128)}, bf16[8,16,6144]{2,1,0:T(8,128)(2,1)}, bf16[16,6144]{1,0:T(8,128)(2,1)S(1)}, f32[6144]{0:T(1024)}, /*index=5*/s32[384]{0:T(512)S(1)}, bf16[192,64,128]{2,1,0:T(8,128)(2,1)}, s32[192]{0:T(256)S(1)}, ...), branch_computations={%region_4.4_spmd, %region_5.6_spmd} | conditional | flops 78352080 | bytes 19506548 | solution.py:102
  399.3 2.6 gather_fusion
  405.2 3.9 fusion.7
  410.4 2.3 convolution_bitcast_fusion
  416.8 6.7 %collective-permute-done = bf16[16,6144]{1,0:T(8,128)(2,1)S(1)} collective-permute-done((bf16[16,6144]{1,0:T(8,128)(2,1)S(1)}, bf16[16,6144]{1,0:T(8,128)(2,1)S(1)}, u32[]{:S(2)}, u32[]{:S(2)}) %collective-permute-start) | collective-permute-done | bytes 196640 | tf_op jit(solution)/shard_map/while/body/eval_jaxpr/ppermute | solution.py:19
  423.4 17.7 %conditional.2 = (bf16[16,6144]{1,0:T(8,128)(2,1)S(1)}) conditional(s32[]{:T(128)} %convert_element_type.52, () %tuple.47, (pred[]{:T(512)}, s32[]{:T(128)}, bf16[8,16,6144]{2,1,0:T(8,128)(2,1)}, bf16[16,6144]{1,0:T(8,128)(2,1)S(1)}, f32[6144]{0:T(1024)}, /*index=5*/s32[384]{0:T(512)S(1)}, bf16[192,64,128]{2,1,0:T(8,128)(2,1)}, s32[192]{0:T(256)S(1)}, ...), branch_computations={%region_4.4_spmd, %region_5.6_spmd} | conditional | flops 78352080 | bytes 19506548 | solution.py:102
  426.7 2.6 gather_fusion
  432.5 3.9 fusion.7
  437.8 2.3 convolution_bitcast_fusion
  444.1 6.7 %collective-permute-done = bf16[16,6144]{1,0:T(8,128)(2,1)S(1)} collective-permute-done((bf16[16,6144]{1,0:T(8,128)(2,1)S(1)}, bf16[16,6144]{1,0:T(8,128)(2,1)S(1)}, u32[]{:S(2)}, u32[]{:S(2)}) %collective-permute-start) | collective-permute-done | bytes 196640 | tf_op jit(solution)/shard_map/while/body/eval_jaxpr/ppermute | solution.py:19
  450.8 17.7 %conditional.2 = (bf16[16,6144]{1,0:T(8,128)(2,1)S(1)}) conditional(s32[]{:T(128)} %convert_element_type.52, () %tuple.47, (pred[]{:T(512)}, s32[]{:T(128)}, bf16[8,16,6144]{2,1,0:T(8,128)(2,1)}, bf16[16,6144]{1,0:T(8,128)(2,1)S(1)}, f32[6144]{0:T(1024)}, /*index=5*/s32[384]{0:T(512)S(1)}, bf16[192,64,128]{2,1,0:T(8,128)(2,1)}, s32[192]{0:T(256)S(1)}, ...), branch_computations={%region_4.4_spmd, %region_5.6_spmd} | conditional | flops 78352080 | bytes 19506548 | solution.py:102
  454.0 2.6 gather_fusion
  459.9 3.9 fusion.7
  465.2 2.3 convolution_bitcast_fusion
  471.5 6.7 %collective-permute-done = bf16[16,6144]{1,0:T(8,128)(2,1)S(1)} collective-permute-done((bf16[16,6144]{1,0:T(8,128)(2,1)S(1)}, bf16[16,6144]{1,0:T(8,128)(2,1)S(1)}, u32[]{:S(2)}, u32[]{:S(2)}) %collective-permute-start) | collective-permute-done | bytes 196640 | tf_op jit(solution)/shard_map/while/body/eval_jaxpr/ppermute | solution.py:19
  478.2 17.7 %conditional.2 = (bf16[16,6144]{1,0:T(8,128)(2,1)S(1)}) conditional(s32[]{:T(128)} %convert_element_type.52, () %tuple.47, (pred[]{:T(512)}, s32[]{:T(128)}, bf16[8,16,6144]{2,1,0:T(8,128)(2,1)}, bf16[16,6144]{1,0:T(8,128)(2,1)S(1)}, f32[6144]{0:T(1024)}, /*index=5*/s32[384]{0:T(512)S(1)}, bf16[192,64,128]{2,1,0:T(8,128)(2,1)}, s32[192]{0:T(256)S(1)}, ...), branch_computations={%region_4.4_spmd, %region_5.6_spmd} | conditional | flops 78352080 | bytes 19506548 | solution.py:102
  481.4 2.6 gather_fusion
  487.3 3.9 fusion.7
  492.6 2.3 convolution_bitcast_fusion
  498.9 4.6 collective-permute-done
  503.4 4.7 scatter_fusion
  (281 shorter events, 125.4 us)
Async XLA Ops:
  6.5 24.0 %copy-start.4 = (bf16[1,6,4096]{2,1,0:T(8,128)(2,1)S(1)}, bf16[1,6,4096]{2,1,0:T(8,128)(2,1)}, u32[]{:S(2)}) copy-start(bf16[1,6,4096]{2,1,0:T(8,128)(2,1)} %param.15) | copy-start | bytes 147460
  6.5 1.6 copy-start.3
  6.5 64.1 %all-gather.5.cloned.1.call-start = ((), (), s32[]{:S(2)}) async-start(), calls=%async_computation.1 | async-start | bytes 1671168 | tf_op jit(solution)/shard_map/all_gather | solution.py:46
  8.1 40.2 %copy-start.6 = (s32[160]{0:T(256)S(1)}, s32[160]{0:T(256)}, u32[]{:S(2)}) copy-start(s32[160]{0:T(256)} %param.12) | copy-start | bytes 1924
  8.2 18.1 %collective-permute-start.4 = (bf16[96,128]{1,0:T(8,128)(2,1)S(1)}, bf16[96,128]{1,0:T(8,128)(2,1)S(1)}, u32[]{:S(2)}, u32[]{:S(2)}) collective-permute-start(bf16[96,128]{1,0:T(8,128)(2,1)S(1)} %reshape.126), channel_id=1, source_target_pairs={{0,16},{16,32},{32,48},{48,0},{1,17},{17,33},{33,49},{49,1},{2,18}... | collective-permute-start | bytes 73736 | tf_op jit(solution)/shard_map/ppermute | solution.py:27
  14.3 12.0 %collective-permute-start.5 = (bf16[96,128]{1,0:T(8,128)(2,1)S(1)}, bf16[96,128]{1,0:T(8,128)(2,1)S(1)}, u32[]{:S(2)}, u32[]{:S(2)}) collective-permute-start(bf16[96,128]{1,0:T(8,128)(2,1)S(1)} %reshape.126), channel_id=1, source_target_pairs={{0,32},{16,48},{32,0},{48,16},{1,33},{17,49},{33,1},{49,17},{2,34}... | collective-permute-start | bytes 73736 | tf_op jit(solution)/shard_map/ppermute | solution.py:27
  22.5 6.6 %collective-permute-start.6 = (bf16[96,128]{1,0:T(8,128)(2,1)S(1)}, bf16[96,128]{1,0:T(8,128)(2,1)S(1)}, u32[]{:S(2)}, u32[]{:S(2)}) collective-permute-start(bf16[96,128]{1,0:T(8,128)(2,1)S(1)} %reshape.126), channel_id=1, source_target_pairs={{0,48},{16,0},{32,16},{48,32},{1,49},{17,1},{33,17},{49,33},{2,50}... | collective-permute-start | bytes 73736 | tf_op jit(solution)/shard_map/ppermute | solution.py:27
  30.5 84.3 %all-gather.3.cloned.1.call-start = ((), (), s32[]{:S(2)}) async-start(), calls=%async_computation | async-start | bytes 3342336 | tf_op jit(solution)/shard_map/all_gather | solution.py:38
  30.9 11.3 %collective-permute-start.1 = (bf16[3,64,128]{2,1,0:T(8,128)(2,1)S(1)}, bf16[3,64,128]{2,1,0:T(8,128)(2,1)S(1)}, u32[]{:S(2)}, u32[]{:S(2)}) collective-permute-start(bf16[3,64,128]{2,1,0:T(8,128)(2,1)S(1)} %reshape.124), channel_id=1, source_target_pairs={{0,16},{16,32},{32,48},{48,0},{1,17},{17,33},{33,49},{49,1},{2,18}... | collective-permute-start | bytes 147464 | tf_op jit(solution)/shard_map/ppermute | solution.py:27
  34.0 10.3 %collective-permute-start.2 = (bf16[3,64,128]{2,1,0:T(8,128)(2,1)S(1)}, bf16[3,64,128]{2,1,0:T(8,128)(2,1)S(1)}, u32[]{:S(2)}, u32[]{:S(2)}) collective-permute-start(bf16[3,64,128]{2,1,0:T(8,128)(2,1)S(1)} %reshape.124), channel_id=1, source_target_pairs={{0,32},{16,48},{32,0},{48,16},{1,33},{17,49},{33,1},{49,17},{2,34}... | collective-permute-start | bytes 147464 | tf_op jit(solution)/shard_map/ppermute | solution.py:27
  40.0 6.9 %collective-permute-start.3 = (bf16[3,64,128]{2,1,0:T(8,128)(2,1)S(1)}, bf16[3,64,128]{2,1,0:T(8,128)(2,1)S(1)}, u32[]{:S(2)}, u32[]{:S(2)}) collective-permute-start(bf16[3,64,128]{2,1,0:T(8,128)(2,1)S(1)} %reshape.124), channel_id=1, source_target_pairs={{0,48},{16,0},{32,16},{48,32},{1,49},{17,1},{33,17},{49,33},{2,50}... | collective-permute-start | bytes 147464 | tf_op jit(solution)/shard_map/ppermute | solution.py:27
  53.7 2.8 copy-start.7
  53.7 3.1 copy-start.8
  53.7 3.3 copy-start.5
  114.9 8.9 %collective-permute-start = (bf16[16,6144]{1,0:T(8,128)(2,1)S(1)}, bf16[16,6144]{1,0:T(8,128)(2,1)S(1)}, u32[]{:S(2)}, u32[]{:S(2)}) collective-permute-start(bf16[16,6144]{1,0:T(8,128)(2,1)S(1)} %get-tuple-element.467), channel_id=1, source_target_pairs={{0,64},{64,128},{128,192},{192,256},{256,320},{320,384},{384,448},... | collective-permute-start | bytes 589832 | tf_op jit(solution)/shard_map/while/body/eval_jaxpr/ppermute | solution.py:19
  123.8 8.1 %collective-permute-start = (bf16[16,6144]{1,0:T(8,128)(2,1)S(1)}, bf16[16,6144]{1,0:T(8,128)(2,1)S(1)}, u32[]{:S(2)}, u32[]{:S(2)}) collective-permute-start(bf16[16,6144]{1,0:T(8,128)(2,1)S(1)} %get-tuple-element.467), channel_id=1, source_target_pairs={{0,64},{64,128},{128,192},{192,256},{256,320},{320,384},{384,448},... | collective-permute-start | bytes 589832 | tf_op jit(solution)/shard_map/while/body/eval_jaxpr/ppermute | solution.py:19
  131.9 7.6 %collective-permute-start = (bf16[16,6144]{1,0:T(8,128)(2,1)S(1)}, bf16[16,6144]{1,0:T(8,128)(2,1)S(1)}, u32[]{:S(2)}, u32[]{:S(2)}) collective-permute-start(bf16[16,6144]{1,0:T(8,128)(2,1)S(1)} %get-tuple-element.467), channel_id=1, source_target_pairs={{0,64},{64,128},{128,192},{192,256},{256,320},{320,384},{384,448},... | collective-permute-start | bytes 589832 | tf_op jit(solution)/shard_map/while/body/eval_jaxpr/ppermute | solution.py:19
  139.5 7.6 %collective-permute-start = (bf16[16,6144]{1,0:T(8,128)(2,1)S(1)}, bf16[16,6144]{1,0:T(8,128)(2,1)S(1)}, u32[]{:S(2)}, u32[]{:S(2)}) collective-permute-start(bf16[16,6144]{1,0:T(8,128)(2,1)S(1)} %get-tuple-element.467), channel_id=1, source_target_pairs={{0,64},{64,128},{128,192},{192,256},{256,320},{320,384},{384,448},... | collective-permute-start | bytes 589832 | tf_op jit(solution)/shard_map/while/body/eval_jaxpr/ppermute | solution.py:19
  147.1 7.7 %collective-permute-start = (bf16[16,6144]{1,0:T(8,128)(2,1)S(1)}, bf16[16,6144]{1,0:T(8,128)(2,1)S(1)}, u32[]{:S(2)}, u32[]{:S(2)}) collective-permute-start(bf16[16,6144]{1,0:T(8,128)(2,1)S(1)} %get-tuple-element.467), channel_id=1, source_target_pairs={{0,64},{64,128},{128,192},{192,256},{256,320},{320,384},{384,448},... | collective-permute-start | bytes 589832 | tf_op jit(solution)/shard_map/while/body/eval_jaxpr/ppermute | solution.py:19
  154.8 9.7 %collective-permute-start = (bf16[16,6144]{1,0:T(8,128)(2,1)S(1)}, bf16[16,6144]{1,0:T(8,128)(2,1)S(1)}, u32[]{:S(2)}, u32[]{:S(2)}) collective-permute-start(bf16[16,6144]{1,0:T(8,128)(2,1)S(1)} %get-tuple-element.467), channel_id=1, source_target_pairs={{0,64},{64,128},{128,192},{192,256},{256,320},{320,384},{384,448},... | collective-permute-start | bytes 589832 | tf_op jit(solution)/shard_map/while/body/eval_jaxpr/ppermute | solution.py:19
  164.5 122.0 %collective-permute-start = (bf16[16,6144]{1,0:T(8,128)(2,1)S(1)}, bf16[16,6144]{1,0:T(8,128)(2,1)S(1)}, u32[]{:S(2)}, u32[]{:S(2)}) collective-permute-start(bf16[16,6144]{1,0:T(8,128)(2,1)S(1)} %get-tuple-element.467), channel_id=1, source_target_pairs={{0,64},{64,128},{128,192},{192,256},{256,320},{320,384},{384,448},... | collective-permute-start | bytes 589832 | tf_op jit(solution)/shard_map/while/body/eval_jaxpr/ppermute | solution.py:19
  287.7 0.7 copy-start.1
  303.3 0.9 copy-start.2
  304.3 9.7 %collective-permute-start = (bf16[16,6144]{1,0:T(8,128)(2,1)S(1)}, bf16[16,6144]{1,0:T(8,128)(2,1)S(1)}, u32[]{:S(2)}, u32[]{:S(2)}) collective-permute-start(bf16[16,6144]{1,0:T(8,128)(2,1)S(1)} %get-tuple-element.467), channel_id=1, source_target_pairs={{0,64},{64,128},{128,192},{192,256},{256,320},{320,384},{384,448},... | collective-permute-start | bytes 589832 | tf_op jit(solution)/shard_map/while/body/eval_jaxpr/ppermute | solution.py:19
  315.0 0.7 copy-start.1
  330.6 0.9 copy-start.2
  331.6 9.7 %collective-permute-start = (bf16[16,6144]{1,0:T(8,128)(2,1)S(1)}, bf16[16,6144]{1,0:T(8,128)(2,1)S(1)}, u32[]{:S(2)}, u32[]{:S(2)}) collective-permute-start(bf16[16,6144]{1,0:T(8,128)(2,1)S(1)} %get-tuple-element.467), channel_id=1, source_target_pairs={{0,64},{64,128},{128,192},{192,256},{256,320},{320,384},{384,448},... | collective-permute-start | bytes 589832 | tf_op jit(solution)/shard_map/while/body/eval_jaxpr/ppermute | solution.py:19
  342.4 0.7 copy-start.1
  358.0 0.9 copy-start.2
  359.0 9.7 %collective-permute-start = (bf16[16,6144]{1,0:T(8,128)(2,1)S(1)}, bf16[16,6144]{1,0:T(8,128)(2,1)S(1)}, u32[]{:S(2)}, u32[]{:S(2)}) collective-permute-start(bf16[16,6144]{1,0:T(8,128)(2,1)S(1)} %get-tuple-element.467), channel_id=1, source_target_pairs={{0,64},{64,128},{128,192},{192,256},{256,320},{320,384},{384,448},... | collective-permute-start | bytes 589832 | tf_op jit(solution)/shard_map/while/body/eval_jaxpr/ppermute | solution.py:19
  369.8 0.7 copy-start.1
  385.4 0.9 copy-start.2
  386.4 9.7 %collective-permute-start = (bf16[16,6144]{1,0:T(8,128)(2,1)S(1)}, bf16[16,6144]{1,0:T(8,128)(2,1)S(1)}, u32[]{:S(2)}, u32[]{:S(2)}) collective-permute-start(bf16[16,6144]{1,0:T(8,128)(2,1)S(1)} %get-tuple-element.467), channel_id=1, source_target_pairs={{0,64},{64,128},{128,192},{192,256},{256,320},{320,384},{384,448},... | collective-permute-start | bytes 589832 | tf_op jit(solution)/shard_map/while/body/eval_jaxpr/ppermute | solution.py:19
  397.2 0.7 copy-start.1
  412.8 0.9 copy-start.2
  413.7 9.7 %collective-permute-start = (bf16[16,6144]{1,0:T(8,128)(2,1)S(1)}, bf16[16,6144]{1,0:T(8,128)(2,1)S(1)}, u32[]{:S(2)}, u32[]{:S(2)}) collective-permute-start(bf16[16,6144]{1,0:T(8,128)(2,1)S(1)} %get-tuple-element.467), channel_id=1, source_target_pairs={{0,64},{64,128},{128,192},{192,256},{256,320},{320,384},{384,448},... | collective-permute-start | bytes 589832 | tf_op jit(solution)/shard_map/while/body/eval_jaxpr/ppermute | solution.py:19
  424.5 0.7 copy-start.1
  440.1 0.9 copy-start.2
  441.1 9.7 %collective-permute-start = (bf16[16,6144]{1,0:T(8,128)(2,1)S(1)}, bf16[16,6144]{1,0:T(8,128)(2,1)S(1)}, u32[]{:S(2)}, u32[]{:S(2)}) collective-permute-start(bf16[16,6144]{1,0:T(8,128)(2,1)S(1)} %get-tuple-element.467), channel_id=1, source_target_pairs={{0,64},{64,128},{128,192},{192,256},{256,320},{320,384},{384,448},... | collective-permute-start | bytes 589832 | tf_op jit(solution)/shard_map/while/body/eval_jaxpr/ppermute | solution.py:19
  451.9 0.7 copy-start.1
  467.5 0.9 copy-start.2
  468.5 9.7 %collective-permute-start = (bf16[16,6144]{1,0:T(8,128)(2,1)S(1)}, bf16[16,6144]{1,0:T(8,128)(2,1)S(1)}, u32[]{:S(2)}, u32[]{:S(2)}) collective-permute-start(bf16[16,6144]{1,0:T(8,128)(2,1)S(1)} %get-tuple-element.467), channel_id=1, source_target_pairs={{0,64},{64,128},{128,192},{192,256},{256,320},{320,384},{384,448},... | collective-permute-start | bytes 589832 | tf_op jit(solution)/shard_map/while/body/eval_jaxpr/ppermute | solution.py:19
  479.3 0.7 copy-start.1
  494.9 0.9 copy-start.2
  495.9 7.6 %collective-permute-start = (bf16[16,6144]{1,0:T(8,128)(2,1)S(1)}, bf16[16,6144]{1,0:T(8,128)(2,1)S(1)}, u32[]{:S(2)}, u32[]{:S(2)}) collective-permute-start(bf16[16,6144]{1,0:T(8,128)(2,1)S(1)} %get-tuple-element.467), channel_id=1, source_target_pairs={{0,64},{64,128},{128,192},{192,256},{256,320},{320,384},{384,448},... | collective-permute-start | bytes 589832 | tf_op jit(solution)/shard_map/while/body/eval_jaxpr/ppermute | solution.py:19
  508.1 1.3 copy-start
Sparse Core Ops, SparseCore 0:
  30.6 39.9 all-gather.4
  72.7 42.0 all-gather.2

commit v3 on v2

--- a/solution.py
+++ b/solution.py
@@ -1,6 +1,8 @@
 import jax
 import jax.numpy as jnp
 from jax import lax
+from jax.experimental import pallas as pl
+from jax.experimental.pallas import tpu as pltpu
 from jax.sharding import Mesh
 from jax.sharding import PartitionSpec as P
 
@@ -47,36 +49,121 @@
     return full.reshape(-1, 4096)
 
 
-def make_layer(gain, up_index, up_values, down_index, down_values):
-    width = gain.shape[0]
-    hidden_width = up_values.shape[0] * BLK
-    blocks_in = width // BLK
-    blocks_hid = hidden_width // BLK
-    weights_up = up_values
-    weights_down = down_values.reshape(blocks_in, DOWN_DEPTH * BLK, BLK)
-    gain_wide = gain.astype(jnp.float32)
-
-    def layer(block):
-        count = block.shape[0]
-        wide = block.astype(jnp.float32)
-        meansq = jnp.mean(wide * wide, axis=-1, keepdims=True)
-        normed = (wide * lax.rsqrt(meansq + 1e-05) * gain_wide).astype(jnp.bfloat16)
-        picked = normed.reshape(count, blocks_in, BLK)[:, up_index, :]
-        picked = picked.reshape(count, blocks_hid, UP_DEPTH * BLK)
-        up_sums = jnp.einsum("ncr,cjr->ncj", picked, weights_up, preferred_element_type=jnp.float32)
-        hidden = jax.nn.gelu(up_sums, approximate=True).astype(jnp.bfloat16)
-        second = hidden[:, down_index, :].reshape(count, blocks_in, DOWN_DEPTH * BLK)
-        down_sums = jnp.einsum(
-            "ncr,crj->ncj", second, weights_down, preferred_element_type=jnp.float32
-        )
-        return (wide + down_sums.reshape(count, width)).astype(jnp.bfloat16)
-
-    return layer
+LANE = 128
+NT = (((1,), (1,)), ((), ()))
+
+
+def _gelu(v):
+    return 0.5 * v * (1.0 + jnp.tanh(0.7978845608028654 * (v + 0.044715 * (v * v * v))))
+
+
+def _pick(s_ref, a, b, lane):
+    left = s_ref[a % 2, (a + 1) // 2]
+    right = s_ref[1 - b % 2, b // 2]
+    return jnp.where(lane < BLK, left, right)
+
+
+def _shifted(prev, cur):
+    lane = lax.broadcasted_iota(jnp.int32, cur.shape, 1)
+    return jnp.where(lane < BLK, pltpu.roll(prev, BLK, 1), pltpu.roll(cur, BLK, 1))
+
+
+def _layer_kernel(up_idx, dn_idx, x_ref, g_ref, wu_ref, wd_ref, o_ref, sx_ref, sh_ref):
+    count, width = x_ref.shape
+    pairs_in = width // LANE
+    pairs_hid = wu_ref.shape[0]
+    x = x_ref[...].astype(jnp.float32)
+    scale = lax.rsqrt(jnp.mean(x * x, axis=1, keepdims=True) + 1e-05)
+    zero = jnp.zeros((count, LANE), jnp.bfloat16)
+    prev = zero
+    for p in range(pairs_in):
+        cur = (x[:, p * LANE:(p + 1) * LANE] * scale * g_ref[:, p * LANE:(p + 1) * LANE]).astype(jnp.bfloat16)
+        sx_ref[0, p] = cur
+        sx_ref[1, p] = _shifted(prev, cur)
+        prev = cur
+    sx_ref[0, pairs_in] = zero
+    sx_ref[1, pairs_in] = _shifted(prev, zero)
+    lane = lax.broadcasted_iota(jnp.int32, (count, LANE), 1)
+
+    def up(cp, prev):
+        c0 = 2 * cp
+        l0 = _pick(sx_ref, up_idx[2 * c0], up_idx[2 * c0 + 1], lane)
+        l1 = _pick(sx_ref, up_idx[2 * c0 + 2], up_idx[2 * c0 + 3], lane)
+        s = lax.dot_general(l0, wu_ref[cp, 0], NT, preferred_element_type=jnp.float32)
+        s = s + lax.dot_general(l1, wu_ref[cp, 1], NT, preferred_element_type=jnp.float32)
+        cur = _gelu(s).astype(jnp.bfloat16)
+        sh_ref[0, cp] = cur
+        sh_ref[1, cp] = _shifted(prev, cur)
+        return cur
+
+    last = lax.fori_loop(0, pairs_hid, up, zero, unroll=8)
+    sh_ref[0, pairs_hid] = zero
+    sh_ref[1, pairs_hid] = _shifted(last, zero)
+
+    for cp in range(pairs_in):
+        c0 = 2 * cp
+        l0 = _pick(sh_ref, dn_idx[2 * c0], dn_idx[2 * c0 + 1], lane)
+        l1 = _pick(sh_ref, dn_idx[2 * c0 + 2], dn_idx[2 * c0 + 3], lane)
+        s = lax.dot_general(l0, wd_ref[cp, 0], NT, preferred_element_type=jnp.float32)
+        s = s + lax.dot_general(l1, wd_ref[cp, 1], NT, preferred_element_type=jnp.float32)
+        o_ref[:, cp * LANE:(cp + 1) * LANE] = (x[:, cp * LANE:(cp + 1) * LANE] + s).astype(jnp.bfloat16)
+
+
+def pad_pairs(wt):
+    cols = wt.shape[0]
+    w = wt.reshape(cols // 2, 2, BLK, LANE)
+    z = jnp.zeros_like(w[:, :1])
+    first = jnp.concatenate([w[:, :1], z], axis=2)
+    second = jnp.concatenate([z, w[:, 1:]], axis=2)
+    return jnp.concatenate([first, second], axis=1)
+
+
+def layer(x, gain_row, up_idx, wu_p, dn_idx, wd_p):
+    count, width = x.shape
+    pairs_in = width // LANE
+    pairs_hid = wu_p.shape[0]
+    return pl.pallas_call(
+        _layer_kernel,
+        out_shape=jax.ShapeDtypeStruct((count, width), jnp.bfloat16),
+        grid_spec=pltpu.PrefetchScalarGridSpec(
+            num_scalar_prefetch=2,
+            grid=(1,),
+            in_specs=[
+                pl.BlockSpec((count, width), lambda i, u, d: (0, 0)),
+                pl.BlockSpec((1, width), lambda i, u, d: (0, 0)),
+                pl.BlockSpec(wu_p.shape, lambda i, u, d: (0, 0, 0, 0)),
+                pl.BlockSpec(wd_p.shape, lambda i, u, d: (0, 0, 0, 0)),
+            ],
+            out_specs=pl.BlockSpec((count, width), lambda i, u, d: (0, 0)),
+            scratch_shapes=[
+                pltpu.VMEM((2, pairs_in + 1, count, LANE), jnp.bfloat16),
+                pltpu.VMEM((2, pairs_hid + 1, count, LANE), jnp.bfloat16),
+            ],
+        ),
+        compiler_params=pltpu.CompilerParams(vmem_limit_bytes=40 * 1024 * 1024),
+    )(up_idx, dn_idx, x, gain_row, wu_p, wd_p)
+
+
+def column_major_down(rows):
+    cols = rows.shape[0] // DOWN_DEPTH
+    w = rows.reshape(cols, DOWN_DEPTH, BLK, BLK).transpose(0, 3, 1, 2)
+    return w.reshape(cols, BLK, DOWN_DEPTH * BLK)
+
+
+def make_layer(gain, up_index, up_cols, down_index, down_cols):
+    gain_row = gain.astype(jnp.float32)[None, :]
+    up_pairs = pad_pairs(up_cols)
+    down_pairs = pad_pairs(down_cols)
+
+    def apply(block):
+        return layer(block, gain_row, up_index, up_pairs, down_index, down_pairs)
+
+    return apply
 
 
 def per_device(activations, keep, gains, up_rows, up_blocks, down_rows, down_blocks):
     up_all = gather_up(up_blocks)
-    down_all = gather_rows(down_blocks)
+    down_all = column_major_down(gather_rows(down_blocks))
     apply = make_layer(
         gains[0], up_rows[0].reshape(-1), up_all, down_rows[0].reshape(-1), down_all
     )

time: 519 us -> 453 us (0.87)
  Pallas kernels: 0 us -> 96.1 us
  local copies, waits for them, and re-layouts: 116 us -> 47.3 us
  matrix products: 49.8 us -> 0 us
  waiting for transfers between devices: 257 us -> 218 us
    pallas_call x0 -> x8, Pallas kernels: none -> 96.1 us  [layer(): pl.pallas_call(_layer_kernel, out_shape=jax.ShapeDtypeStruct((count, widt...]
    dot_general x16 -> x0, matrix products: 49.8 us -> none  [the longest x8 31.2 us: layer(): jnp.einsum('ncr,cjr->ncj', picked, weights_up, preferred_element_type=jnp...]
    gather x32 -> x0, local copies, waits for them, and re-layouts: 42.9 us -> none  [the longest x16 35 us: layer(): picked = normed.reshape(count, blocks_in, BLK)[:, up_index, :]]
    ppermute x15, waiting for transfers between devices: 202 us -> 169 us  [from_behind(): lax.ppermute(value, axis, [(source, source + steps) for source in range(i...]
    reshape x41 -> x1, local copies, waits for them, and re-layouts: 21.2 us -> 0.01 us  [the longest x8 12 us: layer(): picked = picked.reshape(count, blocks_hid, UP_DEPTH * BLK)]
    reduce_sum x8 -> x0, other arithmetic: 8.86 us -> none  [layer(): meansq = jnp.mean(wide * wide, axis=-1, keepdims=True)]
    cond x32 -> x0, local copies, waits for them, and re-layouts: 8.59 us -> none
    convert_element_type x17 -> x1, other arithmetic: 7.72 us -> 0.03 us  [make_layer(): gain_row = gain.astype(jnp.float32)[None, :]]
  transfers between devices with their start and end apart: 23 -> 23, of which waited for: 20 -> 20; matrix products, arithmetic and copies ran while one was open for 9% -> 12% of each run, Pallas kernels for 0% -> 0%
where the time goes in v3:
time: 453 us; the launch traced here: 451 us
  waiting for transfers between devices  218 us (48%)
  Pallas kernels  96.1 us (21%)
  starting transfers between devices  48.7 us (11%)
  local copies, waits for them, and re-layouts  47.3 us (10%)
  other arithmetic  27.5 us (6%)
  between operations  13.7 us (3%)
    ppermute x15, waiting for transfers between devices, from_behind(): lax.ppermute(value, axis, [(source, source + steps) for source in range(i...  169 us
    pallas_call x8, Pallas kernels, layer(): pl.pallas_call(_layer_kernel, out_shape=jax.ShapeDtypeStruct((count, widt...  96.1 us
    ppermute x6, starting transfers between devices, exchange_zh(): lax.ppermute(part, 'zh', [(i, (i + shift) % count) for i in range(count)])  29.2 us
    all_gather x1, waiting for transfers between devices, gather_up(): full = lax.all_gather(full, ('y', 'c'), axis=1, tiled=True)  27.6 us
    ppermute x15, starting transfers between devices, from_behind(): lax.ppermute(value, axis, [(source, source + steps) for source in range(i...  19.5 us
    dynamic_slice x15, local copies, waits for them, and re-layouts, advance(): current = lax.dynamic_index_in_dim(record, slot, 0, keepdims=False)  14.2 us
    all_gather x1, waiting for transfers between devices, gather_rows(): full = lax.all_gather(full, ('y', 'c'), axis=1, tiled=True)  13.6 us
    dynamic_update_slice x15, other arithmetic, advance(): record = lax.dynamic_update_index_in_dim(record, updated, slot, 0)  11 us
  transfers between devices with their start and end apart: 23, of which 20 were waited for; matrix products, arithmetic and copies ran while one was open for 12% of the time, Pallas kernels for 0%

profile of v3, /device:TPU:70, one launch (start us, length us, event | category | flops | bytes accessed | tf_op | source)
XLA Modules:
  0.0 451.4 jit_solution(10218299964740800565)
XLA Ops:
  6.5 1.6 copy.29
  8.2 6.1 %collective-permute-start.4 = (bf16[96,128]{1,0:T(8,128)(2,1)S(1)}, bf16[96,128]{1,0:T(8,128)(2,1)S(1)}, u32[]{:S(2)}, u32[]{:S(2)}) collective-permute-start(bf16[96,128]{1,0:T(8,128)(2,1)S(1)} %reshape.90), channel_id=1, source_target_pairs={{0,16},{16,32},{32,48},{48,0},{1,17},{17,33},{33,49},{49,1},{2,18}... | collective-permute-start | bytes 73736 | tf_op jit(solution)/shard_map/ppermute | solution.py:29
  14.3 8.2 %collective-permute-start.5 = (bf16[96,128]{1,0:T(8,128)(2,1)S(1)}, bf16[96,128]{1,0:T(8,128)(2,1)S(1)}, u32[]{:S(2)}, u32[]{:S(2)}) collective-permute-start(bf16[96,128]{1,0:T(8,128)(2,1)S(1)} %reshape.90), channel_id=1, source_target_pairs={{0,32},{16,48},{32,0},{48,16},{1,33},{17,49},{33,1},{49,17},{2,34}... | collective-permute-start | bytes 73736 | tf_op jit(solution)/shard_map/ppermute | solution.py:29
  22.5 3.7 collective-permute-start.6
  26.3 2.8 collective-permute-done.6
  30.9 3.1 collective-permute-start.1
  34.0 6.0 %collective-permute-start.2 = (bf16[3,64,128]{2,1,0:T(8,128)(2,1)S(1)}, bf16[3,64,128]{2,1,0:T(8,128)(2,1)S(1)}, u32[]{:S(2)}, u32[]{:S(2)}) collective-permute-start(bf16[3,64,128]{2,1,0:T(8,128)(2,1)S(1)} %reshape.89), channel_id=1, source_target_pairs={{0,32},{16,48},{32,0},{48,16},{1,33},{17,49},{33,1},{49,17},{2,34}... | collective-permute-start | bytes 147464 | tf_op jit(solution)/shard_map/ppermute | solution.py:29
  40.1 2.1 collective-permute-start.3
  42.3 2.1 collective-permute-done.2
  44.4 2.6 collective-permute-done.3
  50.1 2.6 gather_fusion
  53.7 2.7 copy.20
  57.0 13.6 %all-gather.5.cloned.1.call-done = bf16[4,1536,128]{2,1,0:T(8,128)(2,1)} async-done(((bf16[4,96,128]{2,1,0:T(8,128)(2,1)}), bf16[4,1536,128]{2,1,0:T(8,128)(2,1)}) %all-gather.5.cloned.1.call-update) | async-done | bytes 1572880 | tf_op jit(solution)/shard_map/all_gather | solution.py:48
  70.6 5.1 %reshape_reshape.10 = bf16[96,2,64,64]{3,2,1,0:T(8,128)(2,1)} reshape(bf16[4,1536,128]{2,1,0:T(8,128)(2,1)} %all-gather.5.cloned.1.call-done) | data formatting | bytes 3145728 | tf_op jit(solution)/shard_map/reshape;reshape | solution.py:149
  75.7 4.0 fusion.11
  79.7 1.7 copy.13
  81.5 2.4 copy.14
  83.9 3.4 fusion.5
  87.3 27.6 %all-gather.3.cloned.1.call-done = bf16[4,48,64,128]{3,2,1,0:T(8,128)(2,1)} async-done(((bf16[4,3,64,128]{3,2,1,0:T(8,128)(2,1)}), bf16[4,48,64,128]{3,2,1,0:T(8,128)(2,1)}) %all-gather.3.cloned.1.call-update) | async-done | bytes 3145744 | tf_op jit(solution)/shard_map/all_gather | solution.py:40
  115.0 2.6 fusion.12
  117.6 3.4 fusion.2
  120.9 317.8 %while.16 = (s32[]{:T(128)}, bf16[16,6144]{1,0:T(8,128)(2,1)S(1)}, bf16[8,16,6144]{2,1,0:T(8,128)(2,1)}, s32[]{:T(128)}, pred[]{:T(512)}, /*index=5*/bf16[8,16,6...) while((s32[]{:T(128)}, bf16[16,6144]{1,0:T(8,128)(2,1)S(1)}, ...), condition=%wide.region_6.7_spmd, body=%wide.region_3.6_spmd.sunk | while | flops 196621 | bytes 2359679 | solution.py:203
  124.0 5.9 %collective-permute-done = bf16[16,6144]{1,0:T(8,128)(2,1)S(1)} collective-permute-done((bf16[16,6144]{1,0:T(8,128)(2,1)S(1)}, bf16[16,6144]{1,0:T(8,128)(2,1)S(1)}, u32[]{:S(2)}, u32[]{:S(2)}) %collective-permute-start) | collective-permute-done | bytes 196640 | tf_op jit(solution)/shard_map/while/body/eval_jaxpr/ppermute | solution.py:21
  132.9 5.1 %collective-permute-done = bf16[16,6144]{1,0:T(8,128)(2,1)S(1)} collective-permute-done((bf16[16,6144]{1,0:T(8,128)(2,1)S(1)}, bf16[16,6144]{1,0:T(8,128)(2,1)S(1)}, u32[]{:S(2)}, u32[]{:S(2)}) %collective-permute-start) | collective-permute-done | bytes 196640 | tf_op jit(solution)/shard_map/while/body/eval_jaxpr/ppermute | solution.py:21
  141.0 4.6 %collective-permute-done = bf16[16,6144]{1,0:T(8,128)(2,1)S(1)} collective-permute-done((bf16[16,6144]{1,0:T(8,128)(2,1)S(1)}, bf16[16,6144]{1,0:T(8,128)(2,1)S(1)}, u32[]{:S(2)}, u32[]{:S(2)}) %collective-permute-start) | collective-permute-done | bytes 196640 | tf_op jit(solution)/shard_map/while/body/eval_jaxpr/ppermute | solution.py:21
  145.6 1.3 collective-permute-start
  148.6 4.6 %collective-permute-done = bf16[16,6144]{1,0:T(8,128)(2,1)S(1)} collective-permute-done((bf16[16,6144]{1,0:T(8,128)(2,1)S(1)}, bf16[16,6144]{1,0:T(8,128)(2,1)S(1)}, u32[]{:S(2)}, u32[]{:S(2)}) %collective-permute-start) | collective-permute-done | bytes 196640 | tf_op jit(solution)/shard_map/while/body/eval_jaxpr/ppermute | solution.py:21
  156.2 4.7 %collective-permute-done = bf16[16,6144]{1,0:T(8,128)(2,1)S(1)} collective-permute-done((bf16[16,6144]{1,0:T(8,128)(2,1)S(1)}, bf16[16,6144]{1,0:T(8,128)(2,1)S(1)}, u32[]{:S(2)}, u32[]{:S(2)}) %collective-permute-start) | collective-permute-done | bytes 196640 | tf_op jit(solution)/shard_map/while/body/eval_jaxpr/ppermute | solution.py:21
  163.9 6.7 %collective-permute-done = bf16[16,6144]{1,0:T(8,128)(2,1)S(1)} collective-permute-done((bf16[16,6144]{1,0:T(8,128)(2,1)S(1)}, bf16[16,6144]{1,0:T(8,128)(2,1)S(1)}, u32[]{:S(2)}, u32[]{:S(2)}) %collective-permute-start) | collective-permute-done | bytes 196640 | tf_op jit(solution)/shard_map/while/body/eval_jaxpr/ppermute | solution.py:21
  170.6 1.3 collective-permute-start
  173.6 86.0 %collective-permute-done = bf16[16,6144]{1,0:T(8,128)(2,1)S(1)} collective-permute-done((bf16[16,6144]{1,0:T(8,128)(2,1)S(1)}, bf16[16,6144]{1,0:T(8,128)(2,1)S(1)}, u32[]{:S(2)}, u32[]{:S(2)}) %collective-permute-start) | collective-permute-done | bytes 196640 | tf_op jit(solution)/shard_map/while/body/eval_jaxpr/ppermute | solution.py:21
  259.6 13.0 %conditional.2 = (bf16[16,6144]{1,0:T(8,128)(2,1)S(1)}) conditional(s32[]{:T(128)} %convert_element_type.14, () %tuple.47, (pred[]{:T(512)}, s32[]{:T(128)}, bf16[8,16,6144]{2,1,0:T(8,128)(2,1)}, bf16[16,6144]{1,0:T(8,128)(2,1)S(1)}, s32[384]{0:T(512)S(1)}, /*index=5*/s32[192]{0:T(256)S(1)}, f32[1,6144]{1,0:T(1,128)S(1)}, ...), branch_computations={%region_4.4_spmd, %region_5.5_spmd} | conditional | flops 98308 | bytes 589883 | solution.py:189
  260.6 12.0 %branch_1_fun.3 = bf16[16,6144]{1,0:T(8,128)(2,1)S(1)} custom-call(s32[384]{0:T(512)S(1)} %get-tuple-element.287.up_idx, s32[192]{0:T(256)S(1)} %get-tuple-element.288.dn_idx, bf16[16,6144]{1,0:T(8,128)(2,1)S(1)} %bitcast_select_fusion.x_ref, f32[1,6144]{1,0:T(1,128)S(1)} %get-tuple-element.293.g_ref, bf16[96,2,128,128]{3,2,1,0:T(8,128)(2,1)} %get-tuple-element.294.wu_ref, ...), custom_call_target="tpu_custom_call" | custom-call | tf_op jit(solution)/shard_map/while/body/eval_jaxpr/cond/branch_1_fun/pallas_call | solution.py:125
  272.6 1.3 collective-permute-start
  275.6 6.7 %collective-permute-done = bf16[16,6144]{1,0:T(8,128)(2,1)S(1)} collective-permute-done((bf16[16,6144]{1,0:T(8,128)(2,1)S(1)}, bf16[16,6144]{1,0:T(8,128)(2,1)S(1)}, u32[]{:S(2)}, u32[]{:S(2)}) %collective-permute-start) | collective-permute-done | bytes 196640 | tf_op jit(solution)/shard_map/while/body/eval_jaxpr/ppermute | solution.py:21
  282.3 13.0 %conditional.2 = (bf16[16,6144]{1,0:T(8,128)(2,1)S(1)}) conditional(s32[]{:T(128)} %convert_element_type.14, () %tuple.47, (pred[]{:T(512)}, s32[]{:T(128)}, bf16[8,16,6144]{2,1,0:T(8,128)(2,1)}, bf16[16,6144]{1,0:T(8,128)(2,1)S(1)}, s32[384]{0:T(512)S(1)}, /*index=5*/s32[192]{0:T(256)S(1)}, f32[1,6144]{1,0:T(1,128)S(1)}, ...), branch_computations={%region_4.4_spmd, %region_5.5_spmd} | conditional | flops 98308 | bytes 589883 | solution.py:189
  283.2 12.0 %branch_1_fun.3 = bf16[16,6144]{1,0:T(8,128)(2,1)S(1)} custom-call(s32[384]{0:T(512)S(1)} %get-tuple-element.287.up_idx, s32[192]{0:T(256)S(1)} %get-tuple-element.288.dn_idx, bf16[16,6144]{1,0:T(8,128)(2,1)S(1)} %bitcast_select_fusion.x_ref, f32[1,6144]{1,0:T(1,128)S(1)} %get-tuple-element.293.g_ref, bf16[96,2,128,128]{3,2,1,0:T(8,128)(2,1)} %get-tuple-element.294.wu_ref, ...), custom_call_target="tpu_custom_call" | custom-call | tf_op jit(solution)/shard_map/while/body/eval_jaxpr/cond/branch_1_fun/pallas_call | solution.py:125
  295.2 1.3 collective-permute-start
  298.2 6.7 %collective-permute-done = bf16[16,6144]{1,0:T(8,128)(2,1)S(1)} collective-permute-done((bf16[16,6144]{1,0:T(8,128)(2,1)S(1)}, bf16[16,6144]{1,0:T(8,128)(2,1)S(1)}, u32[]{:S(2)}, u32[]{:S(2)}) %collective-permute-start) | collective-permute-done | bytes 196640 | tf_op jit(solution)/shard_map/while/body/eval_jaxpr/ppermute | solution.py:21
  304.9 13.0 %conditional.2 = (bf16[16,6144]{1,0:T(8,128)(2,1)S(1)}) conditional(s32[]{:T(128)} %convert_element_type.14, () %tuple.47, (pred[]{:T(512)}, s32[]{:T(128)}, bf16[8,16,6144]{2,1,0:T(8,128)(2,1)}, bf16[16,6144]{1,0:T(8,128)(2,1)S(1)}, s32[384]{0:T(512)S(1)}, /*index=5*/s32[192]{0:T(256)S(1)}, f32[1,6144]{1,0:T(1,128)S(1)}, ...), branch_computations={%region_4.4_spmd, %region_5.5_spmd} | conditional | flops 98308 | bytes 589883 | solution.py:189
  305.9 12.0 %branch_1_fun.3 = bf16[16,6144]{1,0:T(8,128)(2,1)S(1)} custom-call(s32[384]{0:T(512)S(1)} %get-tuple-element.287.up_idx, s32[192]{0:T(256)S(1)} %get-tuple-element.288.dn_idx, bf16[16,6144]{1,0:T(8,128)(2,1)S(1)} %bitcast_select_fusion.x_ref, f32[1,6144]{1,0:T(1,128)S(1)} %get-tuple-element.293.g_ref, bf16[96,2,128,128]{3,2,1,0:T(8,128)(2,1)} %get-tuple-element.294.wu_ref, ...), custom_call_target="tpu_custom_call" | custom-call | tf_op jit(solution)/shard_map/while/body/eval_jaxpr/cond/branch_1_fun/pallas_call | solution.py:125
  317.9 1.3 collective-permute-start
  320.9 6.7 %collective-permute-done = bf16[16,6144]{1,0:T(8,128)(2,1)S(1)} collective-permute-done((bf16[16,6144]{1,0:T(8,128)(2,1)S(1)}, bf16[16,6144]{1,0:T(8,128)(2,1)S(1)}, u32[]{:S(2)}, u32[]{:S(2)}) %collective-permute-start) | collective-permute-done | bytes 196640 | tf_op jit(solution)/shard_map/while/body/eval_jaxpr/ppermute | solution.py:21
  327.6 13.0 %conditional.2 = (bf16[16,6144]{1,0:T(8,128)(2,1)S(1)}) conditional(s32[]{:T(128)} %convert_element_type.14, () %tuple.47, (pred[]{:T(512)}, s32[]{:T(128)}, bf16[8,16,6144]{2,1,0:T(8,128)(2,1)}, bf16[16,6144]{1,0:T(8,128)(2,1)S(1)}, s32[384]{0:T(512)S(1)}, /*index=5*/s32[192]{0:T(256)S(1)}, f32[1,6144]{1,0:T(1,128)S(1)}, ...), branch_computations={%region_4.4_spmd, %region_5.5_spmd} | conditional | flops 98308 | bytes 589883 | solution.py:189
  328.5 12.0 %branch_1_fun.3 = bf16[16,6144]{1,0:T(8,128)(2,1)S(1)} custom-call(s32[384]{0:T(512)S(1)} %get-tuple-element.287.up_idx, s32[192]{0:T(256)S(1)} %get-tuple-element.288.dn_idx, bf16[16,6144]{1,0:T(8,128)(2,1)S(1)} %bitcast_select_fusion.x_ref, f32[1,6144]{1,0:T(1,128)S(1)} %get-tuple-element.293.g_ref, bf16[96,2,128,128]{3,2,1,0:T(8,128)(2,1)} %get-tuple-element.294.wu_ref, ...), custom_call_target="tpu_custom_call" | custom-call | tf_op jit(solution)/shard_map/while/body/eval_jaxpr/cond/branch_1_fun/pallas_call | solution.py:125
  340.5 1.3 collective-permute-start
  343.5 6.7 %collective-permute-done = bf16[16,6144]{1,0:T(8,128)(2,1)S(1)} collective-permute-done((bf16[16,6144]{1,0:T(8,128)(2,1)S(1)}, bf16[16,6144]{1,0:T(8,128)(2,1)S(1)}, u32[]{:S(2)}, u32[]{:S(2)}) %collective-permute-start) | collective-permute-done | bytes 196640 | tf_op jit(solution)/shard_map/while/body/eval_jaxpr/ppermute | solution.py:21
  350.2 13.0 %conditional.2 = (bf16[16,6144]{1,0:T(8,128)(2,1)S(1)}) conditional(s32[]{:T(128)} %convert_element_type.14, () %tuple.47, (pred[]{:T(512)}, s32[]{:T(128)}, bf16[8,16,6144]{2,1,0:T(8,128)(2,1)}, bf16[16,6144]{1,0:T(8,128)(2,1)S(1)}, s32[384]{0:T(512)S(1)}, /*index=5*/s32[192]{0:T(256)S(1)}, f32[1,6144]{1,0:T(1,128)S(1)}, ...), branch_computations={%region_4.4_spmd, %region_5.5_spmd} | conditional | flops 98308 | bytes 589883 | solution.py:189
  351.2 12.0 %branch_1_fun.3 = bf16[16,6144]{1,0:T(8,128)(2,1)S(1)} custom-call(s32[384]{0:T(512)S(1)} %get-tuple-element.287.up_idx, s32[192]{0:T(256)S(1)} %get-tuple-element.288.dn_idx, bf16[16,6144]{1,0:T(8,128)(2,1)S(1)} %bitcast_select_fusion.x_ref, f32[1,6144]{1,0:T(1,128)S(1)} %get-tuple-element.293.g_ref, bf16[96,2,128,128]{3,2,1,0:T(8,128)(2,1)} %get-tuple-element.294.wu_ref, ...), custom_call_target="tpu_custom_call" | custom-call | tf_op jit(solution)/shard_map/while/body/eval_jaxpr/cond/branch_1_fun/pallas_call | solution.py:125
  363.2 1.3 collective-permute-start
  366.2 6.7 %collective-permute-done = bf16[16,6144]{1,0:T(8,128)(2,1)S(1)} collective-permute-done((bf16[16,6144]{1,0:T(8,128)(2,1)S(1)}, bf16[16,6144]{1,0:T(8,128)(2,1)S(1)}, u32[]{:S(2)}, u32[]{:S(2)}) %collective-permute-start) | collective-permute-done | bytes 196640 | tf_op jit(solution)/shard_map/while/body/eval_jaxpr/ppermute | solution.py:21
  372.9 13.0 %conditional.2 = (bf16[16,6144]{1,0:T(8,128)(2,1)S(1)}) conditional(s32[]{:T(128)} %convert_element_type.14, () %tuple.47, (pred[]{:T(512)}, s32[]{:T(128)}, bf16[8,16,6144]{2,1,0:T(8,128)(2,1)}, bf16[16,6144]{1,0:T(8,128)(2,1)S(1)}, s32[384]{0:T(512)S(1)}, /*index=5*/s32[192]{0:T(256)S(1)}, f32[1,6144]{1,0:T(1,128)S(1)}, ...), branch_computations={%region_4.4_spmd, %region_5.5_spmd} | conditional | flops 98308 | bytes 589883 | solution.py:189
  373.8 12.0 %branch_1_fun.3 = bf16[16,6144]{1,0:T(8,128)(2,1)S(1)} custom-call(s32[384]{0:T(512)S(1)} %get-tuple-element.287.up_idx, s32[192]{0:T(256)S(1)} %get-tuple-element.288.dn_idx, bf16[16,6144]{1,0:T(8,128)(2,1)S(1)} %bitcast_select_fusion.x_ref, f32[1,6144]{1,0:T(1,128)S(1)} %get-tuple-element.293.g_ref, bf16[96,2,128,128]{3,2,1,0:T(8,128)(2,1)} %get-tuple-element.294.wu_ref, ...), custom_call_target="tpu_custom_call" | custom-call | tf_op jit(solution)/shard_map/while/body/eval_jaxpr/cond/branch_1_fun/pallas_call | solution.py:125
  385.8 1.3 collective-permute-start
  388.8 6.7 %collective-permute-done = bf16[16,6144]{1,0:T(8,128)(2,1)S(1)} collective-permute-done((bf16[16,6144]{1,0:T(8,128)(2,1)S(1)}, bf16[16,6144]{1,0:T(8,128)(2,1)S(1)}, u32[]{:S(2)}, u32[]{:S(2)}) %collective-permute-start) | collective-permute-done | bytes 196640 | tf_op jit(solution)/shard_map/while/body/eval_jaxpr/ppermute | solution.py:21
  395.5 13.0 %conditional.2 = (bf16[16,6144]{1,0:T(8,128)(2,1)S(1)}) conditional(s32[]{:T(128)} %convert_element_type.14, () %tuple.47, (pred[]{:T(512)}, s32[]{:T(128)}, bf16[8,16,6144]{2,1,0:T(8,128)(2,1)}, bf16[16,6144]{1,0:T(8,128)(2,1)S(1)}, s32[384]{0:T(512)S(1)}, /*index=5*/s32[192]{0:T(256)S(1)}, f32[1,6144]{1,0:T(1,128)S(1)}, ...), branch_computations={%region_4.4_spmd, %region_5.5_spmd} | conditional | flops 98308 | bytes 589883 | solution.py:189
  396.5 12.0 %branch_1_fun.3 = bf16[16,6144]{1,0:T(8,128)(2,1)S(1)} custom-call(s32[384]{0:T(512)S(1)} %get-tuple-element.287.up_idx, s32[192]{0:T(256)S(1)} %get-tuple-element.288.dn_idx, bf16[16,6144]{1,0:T(8,128)(2,1)S(1)} %bitcast_select_fusion.x_ref, f32[1,6144]{1,0:T(1,128)S(1)} %get-tuple-element.293.g_ref, bf16[96,2,128,128]{3,2,1,0:T(8,128)(2,1)} %get-tuple-element.294.wu_ref, ...), custom_call_target="tpu_custom_call" | custom-call | tf_op jit(solution)/shard_map/while/body/eval_jaxpr/cond/branch_1_fun/pallas_call | solution.py:125
  408.5 1.3 collective-permute-start
  411.5 6.7 %collective-permute-done = bf16[16,6144]{1,0:T(8,128)(2,1)S(1)} collective-permute-done((bf16[16,6144]{1,0:T(8,128)(2,1)S(1)}, bf16[16,6144]{1,0:T(8,128)(2,1)S(1)}, u32[]{:S(2)}, u32[]{:S(2)}) %collective-permute-start) | collective-permute-done | bytes 196640 | tf_op jit(solution)/shard_map/while/body/eval_jaxpr/ppermute | solution.py:21
  418.2 13.0 %conditional.2 = (bf16[16,6144]{1,0:T(8,128)(2,1)S(1)}) conditional(s32[]{:T(128)} %convert_element_type.14, () %tuple.47, (pred[]{:T(512)}, s32[]{:T(128)}, bf16[8,16,6144]{2,1,0:T(8,128)(2,1)}, bf16[16,6144]{1,0:T(8,128)(2,1)S(1)}, s32[384]{0:T(512)S(1)}, /*index=5*/s32[192]{0:T(256)S(1)}, f32[1,6144]{1,0:T(1,128)S(1)}, ...), branch_computations={%region_4.4_spmd, %region_5.5_spmd} | conditional | flops 98308 | bytes 589883 | solution.py:189
  419.1 12.0 %branch_1_fun.3 = bf16[16,6144]{1,0:T(8,128)(2,1)S(1)} custom-call(s32[384]{0:T(512)S(1)} %get-tuple-element.287.up_idx, s32[192]{0:T(256)S(1)} %get-tuple-element.288.dn_idx, bf16[16,6144]{1,0:T(8,128)(2,1)S(1)} %bitcast_select_fusion.x_ref, f32[1,6144]{1,0:T(1,128)S(1)} %get-tuple-element.293.g_ref, bf16[96,2,128,128]{3,2,1,0:T(8,128)(2,1)} %get-tuple-element.294.wu_ref, ...), custom_call_target="tpu_custom_call" | custom-call | tf_op jit(solution)/shard_map/while/body/eval_jaxpr/cond/branch_1_fun/pallas_call | solution.py:125
  431.1 1.3 collective-permute-start
  434.2 4.6 %collective-permute-done = bf16[16,6144]{1,0:T(8,128)(2,1)S(1)} collective-permute-done((bf16[16,6144]{1,0:T(8,128)(2,1)S(1)}, bf16[16,6144]{1,0:T(8,128)(2,1)S(1)}, u32[]{:S(2)}, u32[]{:S(2)}) %collective-permute-start) | collective-permute-done | bytes 196640 | tf_op jit(solution)/shard_map/while/body/eval_jaxpr/ppermute | solution.py:21
  438.7 4.5 %scatter_fusion = bf16[160,6144]{1,0:T(8,128)(2,1)S(1)} fusion(bf16[160,6144]{1,0:T(8,128)(2,1)S(1)} %copy.29, s32[128]{0:T(128)S(1)} %compare_select_fusion.3, bf16[128,6144]{1,0:T(8,128)(2,1)} %bitcast.33), kind=kCustom, calls=%fused_computation.4 | custom fusion | bytes 4719104 | tf_op jit(solution)/shard_map/scatter | solution.py:205
  (110 shorter events, 47.4 us)
Async XLA Ops:
  6.5 24.0 %copy-start.2 = (bf16[1,6,4096]{2,1,0:T(8,128)(2,1)S(1)}, bf16[1,6,4096]{2,1,0:T(8,128)(2,1)}, u32[]{:S(2)}) copy-start(bf16[1,6,4096]{2,1,0:T(8,128)(2,1)} %param.15) | copy-start | bytes 147460
  6.5 1.6 copy-start.1
  6.5 64.1 %all-gather.5.cloned.1.call-start = ((), (), s32[]{:S(2)}) async-start(), calls=%async_computation.1 | async-start | bytes 1671168 | tf_op jit(solution)/shard_map/all_gather | solution.py:48
  8.1 40.2 %copy-start.4 = (s32[160]{0:T(256)S(1)}, s32[160]{0:T(256)}, u32[]{:S(2)}) copy-start(s32[160]{0:T(256)} %param.12) | copy-start | bytes 1924
  8.2 18.1 %collective-permute-start.4 = (bf16[96,128]{1,0:T(8,128)(2,1)S(1)}, bf16[96,128]{1,0:T(8,128)(2,1)S(1)}, u32[]{:S(2)}, u32[]{:S(2)}) collective-permute-start(bf16[96,128]{1,0:T(8,128)(2,1)S(1)} %reshape.90), channel_id=1, source_target_pairs={{0,16},{16,32},{32,48},{48,0},{1,17},{17,33},{33,49},{49,1},{2,18}... | collective-permute-start | bytes 73736 | tf_op jit(solution)/shard_map/ppermute | solution.py:29
  14.3 12.0 %collective-permute-start.5 = (bf16[96,128]{1,0:T(8,128)(2,1)S(1)}, bf16[96,128]{1,0:T(8,128)(2,1)S(1)}, u32[]{:S(2)}, u32[]{:S(2)}) collective-permute-start(bf16[96,128]{1,0:T(8,128)(2,1)S(1)} %reshape.90), channel_id=1, source_target_pairs={{0,32},{16,48},{32,0},{48,16},{1,33},{17,49},{33,1},{49,17},{2,34}... | collective-permute-start | bytes 73736 | tf_op jit(solution)/shard_map/ppermute | solution.py:29
  22.5 6.6 %collective-permute-start.6 = (bf16[96,128]{1,0:T(8,128)(2,1)S(1)}, bf16[96,128]{1,0:T(8,128)(2,1)S(1)}, u32[]{:S(2)}, u32[]{:S(2)}) collective-permute-start(bf16[96,128]{1,0:T(8,128)(2,1)S(1)} %reshape.90), channel_id=1, source_target_pairs={{0,48},{16,0},{32,16},{48,32},{1,49},{17,1},{33,17},{49,33},{2,50}... | collective-permute-start | bytes 73736 | tf_op jit(solution)/shard_map/ppermute | solution.py:29
  30.5 84.5 %all-gather.3.cloned.1.call-start = ((), (), s32[]{:S(2)}) async-start(), calls=%async_computation | async-start | bytes 3342336 | tf_op jit(solution)/shard_map/all_gather | solution.py:40
  30.9 11.3 %collective-permute-start.1 = (bf16[3,64,128]{2,1,0:T(8,128)(2,1)S(1)}, bf16[3,64,128]{2,1,0:T(8,128)(2,1)S(1)}, u32[]{:S(2)}, u32[]{:S(2)}) collective-permute-start(bf16[3,64,128]{2,1,0:T(8,128)(2,1)S(1)} %reshape.89), channel_id=1, source_target_pairs={{0,16},{16,32},{32,48},{48,0},{1,17},{17,33},{33,49},{49,1},{2,18}... | collective-permute-start | bytes 147464 | tf_op jit(solution)/shard_map/ppermute | solution.py:29
  34.0 10.3 %collective-permute-start.2 = (bf16[3,64,128]{2,1,0:T(8,128)(2,1)S(1)}, bf16[3,64,128]{2,1,0:T(8,128)(2,1)S(1)}, u32[]{:S(2)}, u32[]{:S(2)}) collective-permute-start(bf16[3,64,128]{2,1,0:T(8,128)(2,1)S(1)} %reshape.89), channel_id=1, source_target_pairs={{0,32},{16,48},{32,0},{48,16},{1,33},{17,49},{33,1},{49,17},{2,34}... | collective-permute-start | bytes 147464 | tf_op jit(solution)/shard_map/ppermute | solution.py:29
  40.1 6.9 %collective-permute-start.3 = (bf16[3,64,128]{2,1,0:T(8,128)(2,1)S(1)}, bf16[3,64,128]{2,1,0:T(8,128)(2,1)S(1)}, u32[]{:S(2)}, u32[]{:S(2)}) collective-permute-start(bf16[3,64,128]{2,1,0:T(8,128)(2,1)S(1)} %reshape.89), channel_id=1, source_target_pairs={{0,48},{16,0},{32,16},{48,32},{1,49},{17,1},{33,17},{49,33},{2,50}... | collective-permute-start | bytes 147464 | tf_op jit(solution)/shard_map/ppermute | solution.py:29
  52.7 3.7 copy-start.5
  52.7 4.0 copy-start.6
  52.7 4.2 copy-start.3
  121.0 8.9 %collective-permute-start = (bf16[16,6144]{1,0:T(8,128)(2,1)S(1)}, bf16[16,6144]{1,0:T(8,128)(2,1)S(1)}, u32[]{:S(2)}, u32[]{:S(2)}) collective-permute-start(bf16[16,6144]{1,0:T(8,128)(2,1)S(1)} %get-tuple-element.448), channel_id=1, source_target_pairs={{0,64},{64,128},{128,192},{192,256},{256,320},{320,384},{384,448},... | collective-permute-start | bytes 589832 | tf_op jit(solution)/shard_map/while/body/eval_jaxpr/ppermute | solution.py:21
  129.9 8.1 %collective-permute-start = (bf16[16,6144]{1,0:T(8,128)(2,1)S(1)}, bf16[16,6144]{1,0:T(8,128)(2,1)S(1)}, u32[]{:S(2)}, u32[]{:S(2)}) collective-permute-start(bf16[16,6144]{1,0:T(8,128)(2,1)S(1)} %get-tuple-element.448), channel_id=1, source_target_pairs={{0,64},{64,128},{128,192},{192,256},{256,320},{320,384},{384,448},... | collective-permute-start | bytes 589832 | tf_op jit(solution)/shard_map/while/body/eval_jaxpr/ppermute | solution.py:21
  138.0 7.6 %collective-permute-start = (bf16[16,6144]{1,0:T(8,128)(2,1)S(1)}, bf16[16,6144]{1,0:T(8,128)(2,1)S(1)}, u32[]{:S(2)}, u32[]{:S(2)}) collective-permute-start(bf16[16,6144]{1,0:T(8,128)(2,1)S(1)} %get-tuple-element.448), channel_id=1, source_target_pairs={{0,64},{64,128},{128,192},{192,256},{256,320},{320,384},{384,448},... | collective-permute-start | bytes 589832 | tf_op jit(solution)/shard_map/while/body/eval_jaxpr/ppermute | solution.py:21
  145.6 7.6 %collective-permute-start = (bf16[16,6144]{1,0:T(8,128)(2,1)S(1)}, bf16[16,6144]{1,0:T(8,128)(2,1)S(1)}, u32[]{:S(2)}, u32[]{:S(2)}) collective-permute-start(bf16[16,6144]{1,0:T(8,128)(2,1)S(1)} %get-tuple-element.448), channel_id=1, source_target_pairs={{0,64},{64,128},{128,192},{192,256},{256,320},{320,384},{384,448},... | collective-permute-start | bytes 589832 | tf_op jit(solution)/shard_map/while/body/eval_jaxpr/ppermute | solution.py:21
  153.2 7.7 %collective-permute-start = (bf16[16,6144]{1,0:T(8,128)(2,1)S(1)}, bf16[16,6144]{1,0:T(8,128)(2,1)S(1)}, u32[]{:S(2)}, u32[]{:S(2)}) collective-permute-start(bf16[16,6144]{1,0:T(8,128)(2,1)S(1)} %get-tuple-element.448), channel_id=1, source_target_pairs={{0,64},{64,128},{128,192},{192,256},{256,320},{320,384},{384,448},... | collective-permute-start | bytes 589832 | tf_op jit(solution)/shard_map/while/body/eval_jaxpr/ppermute | solution.py:21
  160.9 9.7 %collective-permute-start = (bf16[16,6144]{1,0:T(8,128)(2,1)S(1)}, bf16[16,6144]{1,0:T(8,128)(2,1)S(1)}, u32[]{:S(2)}, u32[]{:S(2)}) collective-permute-start(bf16[16,6144]{1,0:T(8,128)(2,1)S(1)} %get-tuple-element.448), channel_id=1, source_target_pairs={{0,64},{64,128},{128,192},{192,256},{256,320},{320,384},{384,448},... | collective-permute-start | bytes 589832 | tf_op jit(solution)/shard_map/while/body/eval_jaxpr/ppermute | solution.py:21
  170.6 89.0 %collective-permute-start = (bf16[16,6144]{1,0:T(8,128)(2,1)S(1)}, bf16[16,6144]{1,0:T(8,128)(2,1)S(1)}, u32[]{:S(2)}, u32[]{:S(2)}) collective-permute-start(bf16[16,6144]{1,0:T(8,128)(2,1)S(1)} %get-tuple-element.448), channel_id=1, source_target_pairs={{0,64},{64,128},{128,192},{192,256},{256,320},{320,384},{384,448},... | collective-permute-start | bytes 589832 | tf_op jit(solution)/shard_map/while/body/eval_jaxpr/ppermute | solution.py:21
  272.6 9.7 %collective-permute-start = (bf16[16,6144]{1,0:T(8,128)(2,1)S(1)}, bf16[16,6144]{1,0:T(8,128)(2,1)S(1)}, u32[]{:S(2)}, u32[]{:S(2)}) collective-permute-start(bf16[16,6144]{1,0:T(8,128)(2,1)S(1)} %get-tuple-element.448), channel_id=1, source_target_pairs={{0,64},{64,128},{128,192},{192,256},{256,320},{320,384},{384,448},... | collective-permute-start | bytes 589832 | tf_op jit(solution)/shard_map/while/body/eval_jaxpr/ppermute | solution.py:21
  295.2 9.7 %collective-permute-start = (bf16[16,6144]{1,0:T(8,128)(2,1)S(1)}, bf16[16,6144]{1,0:T(8,128)(2,1)S(1)}, u32[]{:S(2)}, u32[]{:S(2)}) collective-permute-start(bf16[16,6144]{1,0:T(8,128)(2,1)S(1)} %get-tuple-element.448), channel_id=1, source_target_pairs={{0,64},{64,128},{128,192},{192,256},{256,320},{320,384},{384,448},... | collective-permute-start | bytes 589832 | tf_op jit(solution)/shard_map/while/body/eval_jaxpr/ppermute | solution.py:21
  317.9 9.7 %collective-permute-start = (bf16[16,6144]{1,0:T(8,128)(2,1)S(1)}, bf16[16,6144]{1,0:T(8,128)(2,1)S(1)}, u32[]{:S(2)}, u32[]{:S(2)}) collective-permute-start(bf16[16,6144]{1,0:T(8,128)(2,1)S(1)} %get-tuple-element.448), channel_id=1, source_target_pairs={{0,64},{64,128},{128,192},{192,256},{256,320},{320,384},{384,448},... | collective-permute-start | bytes 589832 | tf_op jit(solution)/shard_map/while/body/eval_jaxpr/ppermute | solution.py:21
  340.5 9.7 %collective-permute-start = (bf16[16,6144]{1,0:T(8,128)(2,1)S(1)}, bf16[16,6144]{1,0:T(8,128)(2,1)S(1)}, u32[]{:S(2)}, u32[]{:S(2)}) collective-permute-start(bf16[16,6144]{1,0:T(8,128)(2,1)S(1)} %get-tuple-element.448), channel_id=1, source_target_pairs={{0,64},{64,128},{128,192},{192,256},{256,320},{320,384},{384,448},... | collective-permute-start | bytes 589832 | tf_op jit(solution)/shard_map/while/body/eval_jaxpr/ppermute | solution.py:21
  363.2 9.7 %collective-permute-start = (bf16[16,6144]{1,0:T(8,128)(2,1)S(1)}, bf16[16,6144]{1,0:T(8,128)(2,1)S(1)}, u32[]{:S(2)}, u32[]{:S(2)}) collective-permute-start(bf16[16,6144]{1,0:T(8,128)(2,1)S(1)} %get-tuple-element.448), channel_id=1, source_target_pairs={{0,64},{64,128},{128,192},{192,256},{256,320},{320,384},{384,448},... | collective-permute-start | bytes 589832 | tf_op jit(solution)/shard_map/while/body/eval_jaxpr/ppermute | solution.py:21
  385.8 9.7 %collective-permute-start = (bf16[16,6144]{1,0:T(8,128)(2,1)S(1)}, bf16[16,6144]{1,0:T(8,128)(2,1)S(1)}, u32[]{:S(2)}, u32[]{:S(2)}) collective-permute-start(bf16[16,6144]{1,0:T(8,128)(2,1)S(1)} %get-tuple-element.448), channel_id=1, source_target_pairs={{0,64},{64,128},{128,192},{192,256},{256,320},{320,384},{384,448},... | collective-permute-start | bytes 589832 | tf_op jit(solution)/shard_map/while/body/eval_jaxpr/ppermute | solution.py:21
  408.5 9.7 %collective-permute-start = (bf16[16,6144]{1,0:T(8,128)(2,1)S(1)}, bf16[16,6144]{1,0:T(8,128)(2,1)S(1)}, u32[]{:S(2)}, u32[]{:S(2)}) collective-permute-start(bf16[16,6144]{1,0:T(8,128)(2,1)S(1)} %get-tuple-element.448), channel_id=1, source_target_pairs={{0,64},{64,128},{128,192},{192,256},{256,320},{320,384},{384,448},... | collective-permute-start | bytes 589832 | tf_op jit(solution)/shard_map/while/body/eval_jaxpr/ppermute | solution.py:21
  431.1 7.6 %collective-permute-start = (bf16[16,6144]{1,0:T(8,128)(2,1)S(1)}, bf16[16,6144]{1,0:T(8,128)(2,1)S(1)}, u32[]{:S(2)}, u32[]{:S(2)}) collective-permute-start(bf16[16,6144]{1,0:T(8,128)(2,1)S(1)} %get-tuple-element.448), channel_id=1, source_target_pairs={{0,64},{64,128},{128,192},{192,256},{256,320},{320,384},{384,448},... | collective-permute-start | bytes 589832 | tf_op jit(solution)/shard_map/while/body/eval_jaxpr/ppermute | solution.py:21
  443.3 1.3 copy-start
Sparse Core Ops, SparseCore 0:
  30.6 39.9 all-gather.4
  72.8 42.1 all-gather.2

commit v4 on v3

--- a/solution.py
+++ b/solution.py
@@ -32,21 +32,16 @@
     return jnp.take(stacked, order, axis=0)
 
 
-def gather_up(shard):
-    cols = shard.shape[1] // UP_DEPTH
-    part = shard.reshape(cols, UP_DEPTH, BLK, BLK).transpose(0, 3, 1, 2)
-    part = part.reshape(cols, BLK, UP_DEPTH * BLK)
-    full = exchange_zh(part)
-    full = lax.all_gather(full, ("y", "c"), axis=1, tiled=True)
-    return full.reshape(-1, BLK, UP_DEPTH * BLK)
-
-
-def gather_rows(shard):
-    n = shard.shape[1]
-    part = shard.reshape(n * 32, 128)
-    full = exchange_zh(part)
-    full = lax.all_gather(full, ("y", "c"), axis=1, tiled=True)
-    return full.reshape(-1, 4096)
+def gather_weights(up_shard, down_shard):
+    cols = up_shard.shape[1] // UP_DEPTH
+    up_part = up_shard.reshape(cols, UP_DEPTH, BLK, BLK).transpose(0, 3, 1, 2)
+    up_part = up_part.reshape(cols * BLK, UP_DEPTH * BLK)
+    down_part = down_shard.reshape(down_shard.shape[1] * 32, 128)
+    split = up_part.shape[0]
+    full = exchange_zh(jnp.concatenate([up_part, down_part], axis=0))
+    up_full = lax.all_gather(full[:, :split], ("y", "c"), axis=1, tiled=True)
+    down_full = lax.all_gather(full[:, split:], ("y", "c"), axis=1, tiled=True)
+    return up_full.reshape(-1, BLK, UP_DEPTH * BLK), down_full.reshape(-1, 4096)
 
 
 LANE = 128
@@ -68,10 +63,25 @@
     return jnp.where(lane < BLK, pltpu.roll(prev, BLK, 1), pltpu.roll(cur, BLK, 1))
 
 
-def _layer_kernel(up_idx, dn_idx, x_ref, g_ref, wu_ref, wd_ref, o_ref, sx_ref, sh_ref):
+UP_CHUNKS = 4
+DOWN_CHUNKS = 2
+
+
+def _layer_kernel(up_idx, dn_idx, x_ref, g_ref, wu_hbm, wd_hbm, o_ref, sx_ref, sh_ref, wu_ref, wd_ref, sems):
     count, width = x_ref.shape
     pairs_in = width // LANE
     pairs_hid = wu_ref.shape[0]
+    up_step = pairs_hid // UP_CHUNKS
+    down_step = pairs_in // DOWN_CHUNKS
+    copies = []
+    for k in range(UP_CHUNKS):
+        part = pl.ds(k * up_step, up_step)
+        copies.append(pltpu.make_async_copy(wu_hbm.at[part], wu_ref.at[part], sems.at[k]))
+    for k in range(DOWN_CHUNKS):
+        part = pl.ds(k * down_step, down_step)
+        copies.append(pltpu.make_async_copy(wd_hbm.at[part], wd_ref.at[part], sems.at[UP_CHUNKS + k]))
+    for copy in copies:
+        copy.start()
     x = x_ref[...].astype(jnp.float32)
     scale = lax.rsqrt(jnp.mean(x * x, axis=1, keepdims=True) + 1e-05)
     zero = jnp.zeros((count, LANE), jnp.bfloat16)
@@ -96,11 +106,16 @@
         sh_ref[1, cp] = _shifted(prev, cur)
         return cur
 
-    last = lax.fori_loop(0, pairs_hid, up, zero, unroll=8)
+    last = zero
+    for k in range(UP_CHUNKS):
+        copies[k].wait()
+        last = lax.fori_loop(k * up_step, (k + 1) * up_step, up, last, unroll=8)
     sh_ref[0, pairs_hid] = zero
     sh_ref[1, pairs_hid] = _shifted(last, zero)
 
     for cp in range(pairs_in):
+        if cp % down_step == 0:
+            copies[UP_CHUNKS + cp // down_step].wait()
         c0 = 2 * cp
         l0 = _pick(sh_ref, dn_idx[2 * c0], dn_idx[2 * c0 + 1], lane)
         l1 = _pick(sh_ref, dn_idx[2 * c0 + 2], dn_idx[2 * c0 + 3], lane)
@@ -131,13 +146,16 @@
             in_specs=[
                 pl.BlockSpec((count, width), lambda i, u, d: (0, 0)),
                 pl.BlockSpec((1, width), lambda i, u, d: (0, 0)),
-                pl.BlockSpec(wu_p.shape, lambda i, u, d: (0, 0, 0, 0)),
-                pl.BlockSpec(wd_p.shape, lambda i, u, d: (0, 0, 0, 0)),
+                pl.BlockSpec(memory_space=pl.ANY),
+                pl.BlockSpec(memory_space=pl.ANY),
             ],
             out_specs=pl.BlockSpec((count, width), lambda i, u, d: (0, 0)),
             scratch_shapes=[
                 pltpu.VMEM((2, pairs_in + 1, count, LANE), jnp.bfloat16),
                 pltpu.VMEM((2, pairs_hid + 1, count, LANE), jnp.bfloat16),
+                pltpu.VMEM(wu_p.shape, wu_p.dtype),
+                pltpu.VMEM(wd_p.shape, wd_p.dtype),
+                pltpu.SemaphoreType.DMA((UP_CHUNKS + DOWN_CHUNKS,)),
             ],
         ),
         compiler_params=pltpu.CompilerParams(vmem_limit_bytes=40 * 1024 * 1024),
@@ -162,8 +180,8 @@
 
 
 def per_device(activations, keep, gains, up_rows, up_blocks, down_rows, down_blocks):
-    up_all = gather_up(up_blocks)
-    down_all = column_major_down(gather_rows(down_blocks))
+    up_all, down_rows_all = gather_weights(up_blocks, down_blocks)
+    down_all = column_major_down(down_rows_all)
     apply = make_layer(
         gains[0], up_rows[0].reshape(-1), up_all, down_rows[0].reshape(-1), down_all
     )

time: 453 us -> 424 us (0.936)
  Pallas kernels: 96.1 us -> 78.7 us
  starting transfers between devices: 48.7 us -> 36.2 us
    all_gather x2, waiting for transfers between devices: 41.3 us -> 59.4 us  [the longest x1 31.8 us: gather_weights(): down_full = lax.all_gather(full[:, split:], ('y', 'c'), axis=1, tiled=True)]
    pallas_call x8, Pallas kernels: 96.1 us -> 78.7 us  [layer(): pl.pallas_call(_layer_kernel, out_shape=jax.ShapeDtypeStruct((count, widt...]
    ppermute x15, waiting for transfers between devices: 169 us -> 154 us  [from_behind(): lax.ppermute(value, axis, [(source, source + steps) for source in range(i...]
    ppermute x6 -> x3, starting transfers between devices: 29.2 us -> 16.8 us  [exchange_zh(): lax.ppermute(part, 'zh', [(i, (i + shift) % count) for i in range(count)])]
    unnamed x20 -> x21, local copies, waits for them, and re-layouts: 9.98 us -> 9.95 us
  transfers between devices with their start and end apart: 23 -> 20, of which waited for: 20 -> 19; matrix products, arithmetic and copies ran while one was open for 12% -> 12% of each run, Pallas kernels for 0% -> 0%
where the time goes in v4:
time: 424 us; the launch traced here: 422 us
  waiting for transfers between devices  220 us (52%)
  Pallas kernels  78.7 us (19%)
  local copies, waits for them, and re-layouts  47.9 us (11%)
  starting transfers between devices  36.2 us (9%)
  other arithmetic  26 us (6%)
  between operations  13.6 us (3%)
    ppermute x15, waiting for transfers between devices, from_behind(): lax.ppermute(value, axis, [(source, source + steps) for source in range(i...  154 us
    pallas_call x8, Pallas kernels, layer(): pl.pallas_call(_layer_kernel, out_shape=jax.ShapeDtypeStruct((count, widt...  78.7 us
    all_gather x1, waiting for transfers between devices, gather_weights(): down_full = lax.all_gather(full[:, split:], ('y', 'c'), axis=1, tiled=True)  31.8 us
    all_gather x1, waiting for transfers between devices, gather_weights(): up_full = lax.all_gather(full[:, :split], ('y', 'c'), axis=1, tiled=True)  27.7 us
    ppermute x15, starting transfers between devices, from_behind(): lax.ppermute(value, axis, [(source, source + steps) for source in range(i...  19.4 us
    ppermute x3, starting transfers between devices, exchange_zh(): lax.ppermute(part, 'zh', [(i, (i + shift) % count) for i in range(count)])  16.8 us
    dynamic_slice x15, local copies, waits for them, and re-layouts, advance(): current = lax.dynamic_index_in_dim(record, slot, 0, keepdims=False)  14.2 us
    dynamic_update_slice x15, other arithmetic, advance(): record = lax.dynamic_update_index_in_dim(record, updated, slot, 0)  10.9 us
  transfers between devices with their start and end apart: 20, of which 19 were waited for; matrix products, arithmetic and copies ran while one was open for 12% of the time, Pallas kernels for 0%

profile of v4, /device:TPU:70, one launch (start us, length us, event | category | flops | bytes accessed | tf_op | source)
XLA Modules:
  0.0 422.4 jit_solution(18369628305838600269)
XLA Ops:
  6.5 1.6 copy.30
  8.6 10.0 %collective-permute-start.3 = (bf16[288,128]{1,0:T(8,128)(2,1)S(1)}, bf16[288,128]{1,0:T(8,128)(2,1)S(1)}, u32[]{:S(2)}, u32[]{:S(2)}) collective-permute-start(bf16[288,128]{1,0:T(8,128)(2,1)S(1)} %constant_dynamic-update-slice_fusion), channel_id=1, source_target_pairs={{0,48},{16,0},{32,16},{48,32},{1,49},{17,1},{33,17},{49,33},{2,50}... | collective-permute-start | bytes 221192 | tf_op jit(solution)/shard_map/ppermute | solution.py:29
  18.6 1.9 collective-permute-start.1
  20.5 4.8 %collective-permute-start.2 = (bf16[288,128]{1,0:T(8,128)(2,1)S(1)}, bf16[288,128]{1,0:T(8,128)(2,1)S(1)}, u32[]{:S(2)}, u32[]{:S(2)}) collective-permute-start(bf16[288,128]{1,0:T(8,128)(2,1)S(1)} %constant_dynamic-update-slice_fusion), channel_id=1, source_target_pairs={{0,32},{16,48},{32,0},{48,16},{1,33},{17,49},{33,1},{49,17},{2,34}... | collective-permute-start | bytes 221192 | tf_op jit(solution)/shard_map/ppermute | solution.py:29
  25.4 5.7 %collective-permute-done.1 = bf16[288,128]{1,0:T(8,128)(2,1)S(1)} collective-permute-done((bf16[288,128]{1,0:T(8,128)(2,1)S(1)}, bf16[288,128]{1,0:T(8,128)(2,1)S(1)}, u32[]{:S(2)}, u32[]{:S(2)}) %collective-permute-start.1) | collective-permute-done | bytes 73760 | tf_op jit(solution)/shard_map/ppermute | solution.py:29
  35.7 2.6 gather_fusion
  39.3 2.7 copy.21
  42.5 31.8 %all-gather.5.cloned.1.call-done = bf16[4,1536,128]{2,1,0:T(8,128)(2,1)} async-done(((bf16[4,96,128]{2,1,0:T(8,128)(2,1)}), bf16[4,1536,128]{2,1,0:T(8,128)(2,1)}) %all-gather.5.cloned.1.call-update) | async-done | bytes 1572880 | tf_op jit(solution)/shard_map/all_gather | solution.py:43
  74.3 5.1 %reshape_reshape.10 = bf16[96,2,64,64]{3,2,1,0:T(8,128)(2,1)} reshape(bf16[4,1536,128]{2,1,0:T(8,128)(2,1)} %all-gather.5.cloned.1.call-done) | data formatting | bytes 3145728 | tf_op jit(solution)/shard_map/reshape;reshape | solution.py:167
  79.4 4.0 fusion.11
  83.4 1.7 copy.13
  85.1 2.4 copy.14
  87.5 3.4 fusion.5
  91.0 27.7 %all-gather.3.cloned.1.call-done = bf16[4,3072,128]{2,1,0:T(8,128)(2,1)} async-done(((bf16[4,192,128]{2,1,0:T(8,128)(2,1)}), bf16[4,3072,128]{2,1,0:T(8,128)(2,1)}) %all-gather.3.cloned.1.call-update) | async-done | bytes 3145744 | tf_op jit(solution)/shard_map/all_gather | solution.py:42
  118.7 2.6 fusion.12
  121.2 3.4 fusion.2
  124.6 285.1 %while.16 = (s32[]{:T(128)}, bf16[16,6144]{1,0:T(8,128)(2,1)S(1)}, bf16[8,16,6144]{2,1,0:T(8,128)(2,1)}, s32[]{:T(128)}, pred[]{:T(512)}, /*index=5*/bf16[8,16,6...) while((s32[]{:T(128)}, bf16[16,6144]{1,0:T(8,128)(2,1)S(1)}, ...), condition=%wide.region_6.7_spmd, body=%wide.region_3.6_spmd.sunk | while | flops 196621 | bytes 2359679 | solution.py:221
  124.7 1.3 collective-permute-start
  127.6 5.9 %collective-permute-done = bf16[16,6144]{1,0:T(8,128)(2,1)S(1)} collective-permute-done((bf16[16,6144]{1,0:T(8,128)(2,1)S(1)}, bf16[16,6144]{1,0:T(8,128)(2,1)S(1)}, u32[]{:S(2)}, u32[]{:S(2)}) %collective-permute-start) | collective-permute-done | bytes 196640 | tf_op jit(solution)/shard_map/while/body/eval_jaxpr/ppermute | solution.py:21
  133.6 1.3 collective-permute-start
  136.6 5.1 %collective-permute-done = bf16[16,6144]{1,0:T(8,128)(2,1)S(1)} collective-permute-done((bf16[16,6144]{1,0:T(8,128)(2,1)S(1)}, bf16[16,6144]{1,0:T(8,128)(2,1)S(1)}, u32[]{:S(2)}, u32[]{:S(2)}) %collective-permute-start) | collective-permute-done | bytes 196640 | tf_op jit(solution)/shard_map/while/body/eval_jaxpr/ppermute | solution.py:21
  141.7 1.3 collective-permute-start
  144.7 4.6 %collective-permute-done = bf16[16,6144]{1,0:T(8,128)(2,1)S(1)} collective-permute-done((bf16[16,6144]{1,0:T(8,128)(2,1)S(1)}, bf16[16,6144]{1,0:T(8,128)(2,1)S(1)}, u32[]{:S(2)}, u32[]{:S(2)}) %collective-permute-start) | collective-permute-done | bytes 196640 | tf_op jit(solution)/shard_map/while/body/eval_jaxpr/ppermute | solution.py:21
  149.3 1.3 collective-permute-start
  152.3 4.6 %collective-permute-done = bf16[16,6144]{1,0:T(8,128)(2,1)S(1)} collective-permute-done((bf16[16,6144]{1,0:T(8,128)(2,1)S(1)}, bf16[16,6144]{1,0:T(8,128)(2,1)S(1)}, u32[]{:S(2)}, u32[]{:S(2)}) %collective-permute-start) | collective-permute-done | bytes 196640 | tf_op jit(solution)/shard_map/while/body/eval_jaxpr/ppermute | solution.py:21
  156.9 1.3 collective-permute-start
  159.9 4.7 %collective-permute-done = bf16[16,6144]{1,0:T(8,128)(2,1)S(1)} collective-permute-done((bf16[16,6144]{1,0:T(8,128)(2,1)S(1)}, bf16[16,6144]{1,0:T(8,128)(2,1)S(1)}, u32[]{:S(2)}, u32[]{:S(2)}) %collective-permute-start) | collective-permute-done | bytes 196640 | tf_op jit(solution)/shard_map/while/body/eval_jaxpr/ppermute | solution.py:21
  164.6 1.3 collective-permute-start
  167.6 6.7 %collective-permute-done = bf16[16,6144]{1,0:T(8,128)(2,1)S(1)} collective-permute-done((bf16[16,6144]{1,0:T(8,128)(2,1)S(1)}, bf16[16,6144]{1,0:T(8,128)(2,1)S(1)}, u32[]{:S(2)}, u32[]{:S(2)}) %collective-permute-start) | collective-permute-done | bytes 196640 | tf_op jit(solution)/shard_map/while/body/eval_jaxpr/ppermute | solution.py:21
  174.3 1.3 collective-permute-start
  177.3 70.8 %collective-permute-done = bf16[16,6144]{1,0:T(8,128)(2,1)S(1)} collective-permute-done((bf16[16,6144]{1,0:T(8,128)(2,1)S(1)}, bf16[16,6144]{1,0:T(8,128)(2,1)S(1)}, u32[]{:S(2)}, u32[]{:S(2)}) %collective-permute-start) | collective-permute-done | bytes 196640 | tf_op jit(solution)/shard_map/while/body/eval_jaxpr/ppermute | solution.py:21
  248.1 10.8 %conditional.2 = (bf16[16,6144]{1,0:T(8,128)(2,1)S(1)}) conditional(s32[]{:T(128)} %convert_element_type.14, () %tuple.47, (pred[]{:T(512)}, s32[]{:T(128)}, bf16[8,16,6144]{2,1,0:T(8,128)(2,1)}, bf16[16,6144]{1,0:T(8,128)(2,1)S(1)}, s32[384]{0:T(512)S(1)}, /*index=5*/s32[192]{0:T(256)S(1)}, f32[1,6144]{1,0:T(1,128)S(1)}, ...), branch_computations={%region_4.4_spmd, %region_5.5_spmd} | conditional | flops 98308 | bytes 589883 | solution.py:207
  249.0 9.8 %branch_1_fun.3 = bf16[16,6144]{1,0:T(8,128)(2,1)S(1)} custom-call(s32[384]{0:T(512)S(1)} %get-tuple-element.287.up_idx, s32[192]{0:T(256)S(1)} %get-tuple-element.288.dn_idx, bf16[16,6144]{1,0:T(8,128)(2,1)S(1)} %bitcast_select_fusion.x_ref, f32[1,6144]{1,0:T(1,128)S(1)} %get-tuple-element.293.g_ref, bf16[96,2,128,128]{3,2,1,0:T(8,128)(2,1)} %get-tuple-element.294.wu_hbm, ...), custom_call_target="tpu_custom_call" | custom-call | tf_op jit(solution)/shard_map/while/body/eval_jaxpr/cond/branch_1_fun/pallas_call | solution.py:140
  258.9 1.3 collective-permute-start
  261.8 6.7 %collective-permute-done = bf16[16,6144]{1,0:T(8,128)(2,1)S(1)} collective-permute-done((bf16[16,6144]{1,0:T(8,128)(2,1)S(1)}, bf16[16,6144]{1,0:T(8,128)(2,1)S(1)}, u32[]{:S(2)}, u32[]{:S(2)}) %collective-permute-start) | collective-permute-done | bytes 196640 | tf_op jit(solution)/shard_map/while/body/eval_jaxpr/ppermute | solution.py:21
  268.5 10.8 %conditional.2 = (bf16[16,6144]{1,0:T(8,128)(2,1)S(1)}) conditional(s32[]{:T(128)} %convert_element_type.14, () %tuple.47, (pred[]{:T(512)}, s32[]{:T(128)}, bf16[8,16,6144]{2,1,0:T(8,128)(2,1)}, bf16[16,6144]{1,0:T(8,128)(2,1)S(1)}, s32[384]{0:T(512)S(1)}, /*index=5*/s32[192]{0:T(256)S(1)}, f32[1,6144]{1,0:T(1,128)S(1)}, ...), branch_computations={%region_4.4_spmd, %region_5.5_spmd} | conditional | flops 98308 | bytes 589883 | solution.py:207
  269.5 9.8 %branch_1_fun.3 = bf16[16,6144]{1,0:T(8,128)(2,1)S(1)} custom-call(s32[384]{0:T(512)S(1)} %get-tuple-element.287.up_idx, s32[192]{0:T(256)S(1)} %get-tuple-element.288.dn_idx, bf16[16,6144]{1,0:T(8,128)(2,1)S(1)} %bitcast_select_fusion.x_ref, f32[1,6144]{1,0:T(1,128)S(1)} %get-tuple-element.293.g_ref, bf16[96,2,128,128]{3,2,1,0:T(8,128)(2,1)} %get-tuple-element.294.wu_hbm, ...), custom_call_target="tpu_custom_call" | custom-call | tf_op jit(solution)/shard_map/while/body/eval_jaxpr/cond/branch_1_fun/pallas_call | solution.py:140
  279.3 1.3 collective-permute-start
  282.3 6.7 %collective-permute-done = bf16[16,6144]{1,0:T(8,128)(2,1)S(1)} collective-permute-done((bf16[16,6144]{1,0:T(8,128)(2,1)S(1)}, bf16[16,6144]{1,0:T(8,128)(2,1)S(1)}, u32[]{:S(2)}, u32[]{:S(2)}) %collective-permute-start) | collective-permute-done | bytes 196640 | tf_op jit(solution)/shard_map/while/body/eval_jaxpr/ppermute | solution.py:21
  289.0 10.8 %conditional.2 = (bf16[16,6144]{1,0:T(8,128)(2,1)S(1)}) conditional(s32[]{:T(128)} %convert_element_type.14, () %tuple.47, (pred[]{:T(512)}, s32[]{:T(128)}, bf16[8,16,6144]{2,1,0:T(8,128)(2,1)}, bf16[16,6144]{1,0:T(8,128)(2,1)S(1)}, s32[384]{0:T(512)S(1)}, /*index=5*/s32[192]{0:T(256)S(1)}, f32[1,6144]{1,0:T(1,128)S(1)}, ...), branch_computations={%region_4.4_spmd, %region_5.5_spmd} | conditional | flops 98308 | bytes 589883 | solution.py:207
  290.0 9.8 %branch_1_fun.3 = bf16[16,6144]{1,0:T(8,128)(2,1)S(1)} custom-call(s32[384]{0:T(512)S(1)} %get-tuple-element.287.up_idx, s32[192]{0:T(256)S(1)} %get-tuple-element.288.dn_idx, bf16[16,6144]{1,0:T(8,128)(2,1)S(1)} %bitcast_select_fusion.x_ref, f32[1,6144]{1,0:T(1,128)S(1)} %get-tuple-element.293.g_ref, bf16[96,2,128,128]{3,2,1,0:T(8,128)(2,1)} %get-tuple-element.294.wu_hbm, ...), custom_call_target="tpu_custom_call" | custom-call | tf_op jit(solution)/shard_map/while/body/eval_jaxpr/cond/branch_1_fun/pallas_call | solution.py:140
  299.8 1.3 collective-permute-start
  302.8 6.7 %collective-permute-done = bf16[16,6144]{1,0:T(8,128)(2,1)S(1)} collective-permute-done((bf16[16,6144]{1,0:T(8,128)(2,1)S(1)}, bf16[16,6144]{1,0:T(8,128)(2,1)S(1)}, u32[]{:S(2)}, u32[]{:S(2)}) %collective-permute-start) | collective-permute-done | bytes 196640 | tf_op jit(solution)/shard_map/while/body/eval_jaxpr/ppermute | solution.py:21
  309.5 10.8 %conditional.2 = (bf16[16,6144]{1,0:T(8,128)(2,1)S(1)}) conditional(s32[]{:T(128)} %convert_element_type.14, () %tuple.47, (pred[]{:T(512)}, s32[]{:T(128)}, bf16[8,16,6144]{2,1,0:T(8,128)(2,1)}, bf16[16,6144]{1,0:T(8,128)(2,1)S(1)}, s32[384]{0:T(512)S(1)}, /*index=5*/s32[192]{0:T(256)S(1)}, f32[1,6144]{1,0:T(1,128)S(1)}, ...), branch_computations={%region_4.4_spmd, %region_5.5_spmd} | conditional | flops 98308 | bytes 589883 | solution.py:207
  310.4 9.8 %branch_1_fun.3 = bf16[16,6144]{1,0:T(8,128)(2,1)S(1)} custom-call(s32[384]{0:T(512)S(1)} %get-tuple-element.287.up_idx, s32[192]{0:T(256)S(1)} %get-tuple-element.288.dn_idx, bf16[16,6144]{1,0:T(8,128)(2,1)S(1)} %bitcast_select_fusion.x_ref, f32[1,6144]{1,0:T(1,128)S(1)} %get-tuple-element.293.g_ref, bf16[96,2,128,128]{3,2,1,0:T(8,128)(2,1)} %get-tuple-element.294.wu_hbm, ...), custom_call_target="tpu_custom_call" | custom-call | tf_op jit(solution)/shard_map/while/body/eval_jaxpr/cond/branch_1_fun/pallas_call | solution.py:140
  320.3 1.3 collective-permute-start
  323.3 6.7 %collective-permute-done = bf16[16,6144]{1,0:T(8,128)(2,1)S(1)} collective-permute-done((bf16[16,6144]{1,0:T(8,128)(2,1)S(1)}, bf16[16,6144]{1,0:T(8,128)(2,1)S(1)}, u32[]{:S(2)}, u32[]{:S(2)}) %collective-permute-start) | collective-permute-done | bytes 196640 | tf_op jit(solution)/shard_map/while/body/eval_jaxpr/ppermute | solution.py:21
  330.0 10.8 %conditional.2 = (bf16[16,6144]{1,0:T(8,128)(2,1)S(1)}) conditional(s32[]{:T(128)} %convert_element_type.14, () %tuple.47, (pred[]{:T(512)}, s32[]{:T(128)}, bf16[8,16,6144]{2,1,0:T(8,128)(2,1)}, bf16[16,6144]{1,0:T(8,128)(2,1)S(1)}, s32[384]{0:T(512)S(1)}, /*index=5*/s32[192]{0:T(256)S(1)}, f32[1,6144]{1,0:T(1,128)S(1)}, ...), branch_computations={%region_4.4_spmd, %region_5.5_spmd} | conditional | flops 98308 | bytes 589883 | solution.py:207
  330.9 9.8 %branch_1_fun.3 = bf16[16,6144]{1,0:T(8,128)(2,1)S(1)} custom-call(s32[384]{0:T(512)S(1)} %get-tuple-element.287.up_idx, s32[192]{0:T(256)S(1)} %get-tuple-element.288.dn_idx, bf16[16,6144]{1,0:T(8,128)(2,1)S(1)} %bitcast_select_fusion.x_ref, f32[1,6144]{1,0:T(1,128)S(1)} %get-tuple-element.293.g_ref, bf16[96,2,128,128]{3,2,1,0:T(8,128)(2,1)} %get-tuple-element.294.wu_hbm, ...), custom_call_target="tpu_custom_call" | custom-call | tf_op jit(solution)/shard_map/while/body/eval_jaxpr/cond/branch_1_fun/pallas_call | solution.py:140
  340.8 1.3 collective-permute-start
  343.7 6.7 %collective-permute-done = bf16[16,6144]{1,0:T(8,128)(2,1)S(1)} collective-permute-done((bf16[16,6144]{1,0:T(8,128)(2,1)S(1)}, bf16[16,6144]{1,0:T(8,128)(2,1)S(1)}, u32[]{:S(2)}, u32[]{:S(2)}) %collective-permute-start) | collective-permute-done | bytes 196640 | tf_op jit(solution)/shard_map/while/body/eval_jaxpr/ppermute | solution.py:21
  350.4 10.8 %conditional.2 = (bf16[16,6144]{1,0:T(8,128)(2,1)S(1)}) conditional(s32[]{:T(128)} %convert_element_type.14, () %tuple.47, (pred[]{:T(512)}, s32[]{:T(128)}, bf16[8,16,6144]{2,1,0:T(8,128)(2,1)}, bf16[16,6144]{1,0:T(8,128)(2,1)S(1)}, s32[384]{0:T(512)S(1)}, /*index=5*/s32[192]{0:T(256)S(1)}, f32[1,6144]{1,0:T(1,128)S(1)}, ...), branch_computations={%region_4.4_spmd, %region_5.5_spmd} | conditional | flops 98308 | bytes 589883 | solution.py:207
  351.4 9.8 %branch_1_fun.3 = bf16[16,6144]{1,0:T(8,128)(2,1)S(1)} custom-call(s32[384]{0:T(512)S(1)} %get-tuple-element.287.up_idx, s32[192]{0:T(256)S(1)} %get-tuple-element.288.dn_idx, bf16[16,6144]{1,0:T(8,128)(2,1)S(1)} %bitcast_select_fusion.x_ref, f32[1,6144]{1,0:T(1,128)S(1)} %get-tuple-element.293.g_ref, bf16[96,2,128,128]{3,2,1,0:T(8,128)(2,1)} %get-tuple-element.294.wu_hbm, ...), custom_call_target="tpu_custom_call" | custom-call | tf_op jit(solution)/shard_map/while/body/eval_jaxpr/cond/branch_1_fun/pallas_call | solution.py:140
  361.2 1.3 collective-permute-start
  364.2 6.7 %collective-permute-done = bf16[16,6144]{1,0:T(8,128)(2,1)S(1)} collective-permute-done((bf16[16,6144]{1,0:T(8,128)(2,1)S(1)}, bf16[16,6144]{1,0:T(8,128)(2,1)S(1)}, u32[]{:S(2)}, u32[]{:S(2)}) %collective-permute-start) | collective-permute-done | bytes 196640 | tf_op jit(solution)/shard_map/while/body/eval_jaxpr/ppermute | solution.py:21
  370.9 10.8 %conditional.2 = (bf16[16,6144]{1,0:T(8,128)(2,1)S(1)}) conditional(s32[]{:T(128)} %convert_element_type.14, () %tuple.47, (pred[]{:T(512)}, s32[]{:T(128)}, bf16[8,16,6144]{2,1,0:T(8,128)(2,1)}, bf16[16,6144]{1,0:T(8,128)(2,1)S(1)}, s32[384]{0:T(512)S(1)}, /*index=5*/s32[192]{0:T(256)S(1)}, f32[1,6144]{1,0:T(1,128)S(1)}, ...), branch_computations={%region_4.4_spmd, %region_5.5_spmd} | conditional | flops 98308 | bytes 589883 | solution.py:207
  371.9 9.8 %branch_1_fun.3 = bf16[16,6144]{1,0:T(8,128)(2,1)S(1)} custom-call(s32[384]{0:T(512)S(1)} %get-tuple-element.287.up_idx, s32[192]{0:T(256)S(1)} %get-tuple-element.288.dn_idx, bf16[16,6144]{1,0:T(8,128)(2,1)S(1)} %bitcast_select_fusion.x_ref, f32[1,6144]{1,0:T(1,128)S(1)} %get-tuple-element.293.g_ref, bf16[96,2,128,128]{3,2,1,0:T(8,128)(2,1)} %get-tuple-element.294.wu_hbm, ...), custom_call_target="tpu_custom_call" | custom-call | tf_op jit(solution)/shard_map/while/body/eval_jaxpr/cond/branch_1_fun/pallas_call | solution.py:140
  381.7 1.3 collective-permute-start
  384.7 6.7 %collective-permute-done = bf16[16,6144]{1,0:T(8,128)(2,1)S(1)} collective-permute-done((bf16[16,6144]{1,0:T(8,128)(2,1)S(1)}, bf16[16,6144]{1,0:T(8,128)(2,1)S(1)}, u32[]{:S(2)}, u32[]{:S(2)}) %collective-permute-start) | collective-permute-done | bytes 196640 | tf_op jit(solution)/shard_map/while/body/eval_jaxpr/ppermute | solution.py:21
  391.4 10.8 %conditional.2 = (bf16[16,6144]{1,0:T(8,128)(2,1)S(1)}) conditional(s32[]{:T(128)} %convert_element_type.14, () %tuple.47, (pred[]{:T(512)}, s32[]{:T(128)}, bf16[8,16,6144]{2,1,0:T(8,128)(2,1)}, bf16[16,6144]{1,0:T(8,128)(2,1)S(1)}, s32[384]{0:T(512)S(1)}, /*index=5*/s32[192]{0:T(256)S(1)}, f32[1,6144]{1,0:T(1,128)S(1)}, ...), branch_computations={%region_4.4_spmd, %region_5.5_spmd} | conditional | flops 98308 | bytes 589883 | solution.py:207
  392.4 9.8 %branch_1_fun.3 = bf16[16,6144]{1,0:T(8,128)(2,1)S(1)} custom-call(s32[384]{0:T(512)S(1)} %get-tuple-element.287.up_idx, s32[192]{0:T(256)S(1)} %get-tuple-element.288.dn_idx, bf16[16,6144]{1,0:T(8,128)(2,1)S(1)} %bitcast_select_fusion.x_ref, f32[1,6144]{1,0:T(1,128)S(1)} %get-tuple-element.293.g_ref, bf16[96,2,128,128]{3,2,1,0:T(8,128)(2,1)} %get-tuple-element.294.wu_hbm, ...), custom_call_target="tpu_custom_call" | custom-call | tf_op jit(solution)/shard_map/while/body/eval_jaxpr/cond/branch_1_fun/pallas_call | solution.py:140
  402.2 1.3 collective-permute-start
  405.2 4.6 %collective-permute-done = bf16[16,6144]{1,0:T(8,128)(2,1)S(1)} collective-permute-done((bf16[16,6144]{1,0:T(8,128)(2,1)S(1)}, bf16[16,6144]{1,0:T(8,128)(2,1)S(1)}, u32[]{:S(2)}, u32[]{:S(2)}) %collective-permute-start) | collective-permute-done | bytes 196640 | tf_op jit(solution)/shard_map/while/body/eval_jaxpr/ppermute | solution.py:21
  409.8 4.5 %scatter_fusion = bf16[160,6144]{1,0:T(8,128)(2,1)S(1)} fusion(bf16[160,6144]{1,0:T(8,128)(2,1)S(1)} %copy.30, s32[128]{0:T(128)S(1)} %compare_select_fusion.3, bf16[128,6144]{1,0:T(8,128)(2,1)} %bitcast.31), kind=kCustom, calls=%fused_computation.3 | custom fusion | bytes 4719104 | tf_op jit(solution)/shard_map/scatter | solution.py:223
  (103 shorter events, 40.7 us)
Async XLA Ops:
  6.5 1.6 copy-start.1
  6.5 2.0 copy-start.2
  6.5 67.8 %all-gather.5.cloned.1.call-start = ((), (), s32[]{:S(2)}) async-start(), calls=%async_computation.1 | async-start | bytes 1671168 | tf_op jit(solution)/shard_map/all_gather | solution.py:43
  8.1 25.8 %copy-start.4 = (s32[160]{0:T(256)S(1)}, s32[160]{0:T(256)}, u32[]{:S(2)}) copy-start(s32[160]{0:T(256)} %param.12) | copy-start | bytes 1924
  8.6 16.8 %collective-permute-start.3 = (bf16[288,128]{1,0:T(8,128)(2,1)S(1)}, bf16[288,128]{1,0:T(8,128)(2,1)S(1)}, u32[]{:S(2)}, u32[]{:S(2)}) collective-permute-start(bf16[288,128]{1,0:T(8,128)(2,1)S(1)} %constant_dynamic-update-slice_fusion), channel_id=1, source_target_pairs={{0,48},{16,0},{32,16},{48,32},{1,49},{17,1},{33,17},{49,33},{2,50}... | collective-permute-start | bytes 221192 | tf_op jit(solution)/shard_map/ppermute | solution.py:29
  18.6 12.5 %collective-permute-start.1 = (bf16[288,128]{1,0:T(8,128)(2,1)S(1)}, bf16[288,128]{1,0:T(8,128)(2,1)S(1)}, u32[]{:S(2)}, u32[]{:S(2)}) collective-permute-start(bf16[288,128]{1,0:T(8,128)(2,1)S(1)} %constant_dynamic-update-slice_fusion), channel_id=1, source_target_pairs={{0,16},{16,32},{32,48},{48,0},{1,17},{17,33},{33,49},{49,1},{2,18}... | collective-permute-start | bytes 221192 | tf_op jit(solution)/shard_map/ppermute | solution.py:29
  20.5 11.2 %collective-permute-start.2 = (bf16[288,128]{1,0:T(8,128)(2,1)S(1)}, bf16[288,128]{1,0:T(8,128)(2,1)S(1)}, u32[]{:S(2)}, u32[]{:S(2)}) collective-permute-start(bf16[288,128]{1,0:T(8,128)(2,1)S(1)} %constant_dynamic-update-slice_fusion), channel_id=1, source_target_pairs={{0,32},{16,48},{32,0},{48,16},{1,33},{17,49},{33,1},{49,17},{2,34}... | collective-permute-start | bytes 221192 | tf_op jit(solution)/shard_map/ppermute | solution.py:29
  33.1 85.5 %all-gather.3.cloned.1.call-start = ((), (), s32[]{:S(2)}) async-start(), calls=%async_computation | async-start | bytes 3342336 | tf_op jit(solution)/shard_map/all_gather | solution.py:42
  38.3 3.7 copy-start.5
  38.3 4.0 copy-start.6
  38.3 4.2 copy-start.3
  124.7 8.9 %collective-permute-start = (bf16[16,6144]{1,0:T(8,128)(2,1)S(1)}, bf16[16,6144]{1,0:T(8,128)(2,1)S(1)}, u32[]{:S(2)}, u32[]{:S(2)}) collective-permute-start(bf16[16,6144]{1,0:T(8,128)(2,1)S(1)} %get-tuple-element.448), channel_id=1, source_target_pairs={{0,64},{64,128},{128,192},{192,256},{256,320},{320,384},{384,448},... | collective-permute-start | bytes 589832 | tf_op jit(solution)/shard_map/while/body/eval_jaxpr/ppermute | solution.py:21
  133.6 8.1 %collective-permute-start = (bf16[16,6144]{1,0:T(8,128)(2,1)S(1)}, bf16[16,6144]{1,0:T(8,128)(2,1)S(1)}, u32[]{:S(2)}, u32[]{:S(2)}) collective-permute-start(bf16[16,6144]{1,0:T(8,128)(2,1)S(1)} %get-tuple-element.448), channel_id=1, source_target_pairs={{0,64},{64,128},{128,192},{192,256},{256,320},{320,384},{384,448},... | collective-permute-start | bytes 589832 | tf_op jit(solution)/shard_map/while/body/eval_jaxpr/ppermute | solution.py:21
  141.7 7.6 %collective-permute-start = (bf16[16,6144]{1,0:T(8,128)(2,1)S(1)}, bf16[16,6144]{1,0:T(8,128)(2,1)S(1)}, u32[]{:S(2)}, u32[]{:S(2)}) collective-permute-start(bf16[16,6144]{1,0:T(8,128)(2,1)S(1)} %get-tuple-element.448), channel_id=1, source_target_pairs={{0,64},{64,128},{128,192},{192,256},{256,320},{320,384},{384,448},... | collective-permute-start | bytes 589832 | tf_op jit(solution)/shard_map/while/body/eval_jaxpr/ppermute | solution.py:21
  149.3 7.6 %collective-permute-start = (bf16[16,6144]{1,0:T(8,128)(2,1)S(1)}, bf16[16,6144]{1,0:T(8,128)(2,1)S(1)}, u32[]{:S(2)}, u32[]{:S(2)}) collective-permute-start(bf16[16,6144]{1,0:T(8,128)(2,1)S(1)} %get-tuple-element.448), channel_id=1, source_target_pairs={{0,64},{64,128},{128,192},{192,256},{256,320},{320,384},{384,448},... | collective-permute-start | bytes 589832 | tf_op jit(solution)/shard_map/while/body/eval_jaxpr/ppermute | solution.py:21
  156.9 7.7 %collective-permute-start = (bf16[16,6144]{1,0:T(8,128)(2,1)S(1)}, bf16[16,6144]{1,0:T(8,128)(2,1)S(1)}, u32[]{:S(2)}, u32[]{:S(2)}) collective-permute-start(bf16[16,6144]{1,0:T(8,128)(2,1)S(1)} %get-tuple-element.448), channel_id=1, source_target_pairs={{0,64},{64,128},{128,192},{192,256},{256,320},{320,384},{384,448},... | collective-permute-start | bytes 589832 | tf_op jit(solution)/shard_map/while/body/eval_jaxpr/ppermute | solution.py:21
  164.6 9.7 %collective-permute-start = (bf16[16,6144]{1,0:T(8,128)(2,1)S(1)}, bf16[16,6144]{1,0:T(8,128)(2,1)S(1)}, u32[]{:S(2)}, u32[]{:S(2)}) collective-permute-start(bf16[16,6144]{1,0:T(8,128)(2,1)S(1)} %get-tuple-element.448), channel_id=1, source_target_pairs={{0,64},{64,128},{128,192},{192,256},{256,320},{320,384},{384,448},... | collective-permute-start | bytes 589832 | tf_op jit(solution)/shard_map/while/body/eval_jaxpr/ppermute | solution.py:21
  174.3 73.7 %collective-permute-start = (bf16[16,6144]{1,0:T(8,128)(2,1)S(1)}, bf16[16,6144]{1,0:T(8,128)(2,1)S(1)}, u32[]{:S(2)}, u32[]{:S(2)}) collective-permute-start(bf16[16,6144]{1,0:T(8,128)(2,1)S(1)} %get-tuple-element.448), channel_id=1, source_target_pairs={{0,64},{64,128},{128,192},{192,256},{256,320},{320,384},{384,448},... | collective-permute-start | bytes 589832 | tf_op jit(solution)/shard_map/while/body/eval_jaxpr/ppermute | solution.py:21
  258.9 9.7 %collective-permute-start = (bf16[16,6144]{1,0:T(8,128)(2,1)S(1)}, bf16[16,6144]{1,0:T(8,128)(2,1)S(1)}, u32[]{:S(2)}, u32[]{:S(2)}) collective-permute-start(bf16[16,6144]{1,0:T(8,128)(2,1)S(1)} %get-tuple-element.448), channel_id=1, source_target_pairs={{0,64},{64,128},{128,192},{192,256},{256,320},{320,384},{384,448},... | collective-permute-start | bytes 589832 | tf_op jit(solution)/shard_map/while/body/eval_jaxpr/ppermute | solution.py:21
  279.3 9.7 %collective-permute-start = (bf16[16,6144]{1,0:T(8,128)(2,1)S(1)}, bf16[16,6144]{1,0:T(8,128)(2,1)S(1)}, u32[]{:S(2)}, u32[]{:S(2)}) collective-permute-start(bf16[16,6144]{1,0:T(8,128)(2,1)S(1)} %get-tuple-element.448), channel_id=1, source_target_pairs={{0,64},{64,128},{128,192},{192,256},{256,320},{320,384},{384,448},... | collective-permute-start | bytes 589832 | tf_op jit(solution)/shard_map/while/body/eval_jaxpr/ppermute | solution.py:21
  299.8 9.7 %collective-permute-start = (bf16[16,6144]{1,0:T(8,128)(2,1)S(1)}, bf16[16,6144]{1,0:T(8,128)(2,1)S(1)}, u32[]{:S(2)}, u32[]{:S(2)}) collective-permute-start(bf16[16,6144]{1,0:T(8,128)(2,1)S(1)} %get-tuple-element.448), channel_id=1, source_target_pairs={{0,64},{64,128},{128,192},{192,256},{256,320},{320,384},{384,448},... | collective-permute-start | bytes 589832 | tf_op jit(solution)/shard_map/while/body/eval_jaxpr/ppermute | solution.py:21
  320.3 9.7 %collective-permute-start = (bf16[16,6144]{1,0:T(8,128)(2,1)S(1)}, bf16[16,6144]{1,0:T(8,128)(2,1)S(1)}, u32[]{:S(2)}, u32[]{:S(2)}) collective-permute-start(bf16[16,6144]{1,0:T(8,128)(2,1)S(1)} %get-tuple-element.448), channel_id=1, source_target_pairs={{0,64},{64,128},{128,192},{192,256},{256,320},{320,384},{384,448},... | collective-permute-start | bytes 589832 | tf_op jit(solution)/shard_map/while/body/eval_jaxpr/ppermute | solution.py:21
  340.8 9.7 %collective-permute-start = (bf16[16,6144]{1,0:T(8,128)(2,1)S(1)}, bf16[16,6144]{1,0:T(8,128)(2,1)S(1)}, u32[]{:S(2)}, u32[]{:S(2)}) collective-permute-start(bf16[16,6144]{1,0:T(8,128)(2,1)S(1)} %get-tuple-element.448), channel_id=1, source_target_pairs={{0,64},{64,128},{128,192},{192,256},{256,320},{320,384},{384,448},... | collective-permute-start | bytes 589832 | tf_op jit(solution)/shard_map/while/body/eval_jaxpr/ppermute | solution.py:21
  361.2 9.7 %collective-permute-start = (bf16[16,6144]{1,0:T(8,128)(2,1)S(1)}, bf16[16,6144]{1,0:T(8,128)(2,1)S(1)}, u32[]{:S(2)}, u32[]{:S(2)}) collective-permute-start(bf16[16,6144]{1,0:T(8,128)(2,1)S(1)} %get-tuple-element.448), channel_id=1, source_target_pairs={{0,64},{64,128},{128,192},{192,256},{256,320},{320,384},{384,448},... | collective-permute-start | bytes 589832 | tf_op jit(solution)/shard_map/while/body/eval_jaxpr/ppermute | solution.py:21
  381.7 9.7 %collective-permute-start = (bf16[16,6144]{1,0:T(8,128)(2,1)S(1)}, bf16[16,6144]{1,0:T(8,128)(2,1)S(1)}, u32[]{:S(2)}, u32[]{:S(2)}) collective-permute-start(bf16[16,6144]{1,0:T(8,128)(2,1)S(1)} %get-tuple-element.448), channel_id=1, source_target_pairs={{0,64},{64,128},{128,192},{192,256},{256,320},{320,384},{384,448},... | collective-permute-start | bytes 589832 | tf_op jit(solution)/shard_map/while/body/eval_jaxpr/ppermute | solution.py:21
  402.2 7.6 %collective-permute-start = (bf16[16,6144]{1,0:T(8,128)(2,1)S(1)}, bf16[16,6144]{1,0:T(8,128)(2,1)S(1)}, u32[]{:S(2)}, u32[]{:S(2)}) collective-permute-start(bf16[16,6144]{1,0:T(8,128)(2,1)S(1)} %get-tuple-element.448), channel_id=1, source_target_pairs={{0,64},{64,128},{128,192},{192,256},{256,320},{320,384},{384,448},... | collective-permute-start | bytes 589832 | tf_op jit(solution)/shard_map/while/body/eval_jaxpr/ppermute | solution.py:21
  414.3 1.3 copy-start
Sparse Core Ops, SparseCore 0:
  33.2 41.0 all-gather.4
  76.4 42.1 all-gather.2

commit v5 on v4

--- a/solution.py
+++ b/solution.py
@@ -99,9 +99,10 @@
         c0 = 2 * cp
         l0 = _pick(sx_ref, up_idx[2 * c0], up_idx[2 * c0 + 1], lane)
         l1 = _pick(sx_ref, up_idx[2 * c0 + 2], up_idx[2 * c0 + 3], lane)
-        s = lax.dot_general(l0, wu_ref[cp, 0], NT, preferred_element_type=jnp.float32)
-        s = s + lax.dot_general(l1, wu_ref[cp, 1], NT, preferred_element_type=jnp.float32)
-        cur = _gelu(s).astype(jnp.bfloat16)
+        w = wu_ref[cp]
+        s0 = lax.dot_general(l0, w, NT, preferred_element_type=jnp.float32)
+        s1 = lax.dot_general(l1, w, NT, preferred_element_type=jnp.float32)
+        cur = _gelu(jnp.where(lane < BLK, s0, s1)).astype(jnp.bfloat16)
         sh_ref[0, cp] = cur
         sh_ref[1, cp] = _shifted(prev, cur)
         return cur
@@ -119,18 +120,15 @@
         c0 = 2 * cp
         l0 = _pick(sh_ref, dn_idx[2 * c0], dn_idx[2 * c0 + 1], lane)
         l1 = _pick(sh_ref, dn_idx[2 * c0 + 2], dn_idx[2 * c0 + 3], lane)
-        s = lax.dot_general(l0, wd_ref[cp, 0], NT, preferred_element_type=jnp.float32)
-        s = s + lax.dot_general(l1, wd_ref[cp, 1], NT, preferred_element_type=jnp.float32)
+        w = wd_ref[cp]
+        s0 = lax.dot_general(l0, w, NT, preferred_element_type=jnp.float32)
+        s1 = lax.dot_general(l1, w, NT, preferred_element_type=jnp.float32)
+        s = jnp.where(lane < BLK, s0, s1)
         o_ref[:, cp * LANE:(cp + 1) * LANE] = (x[:, cp * LANE:(cp + 1) * LANE] + s).astype(jnp.bfloat16)
 
 
-def pad_pairs(wt):
-    cols = wt.shape[0]
-    w = wt.reshape(cols // 2, 2, BLK, LANE)
-    z = jnp.zeros_like(w[:, :1])
-    first = jnp.concatenate([w[:, :1], z], axis=2)
-    second = jnp.concatenate([z, w[:, 1:]], axis=2)
-    return jnp.concatenate([first, second], axis=1)
+def as_pairs(wt):
+    return wt.reshape(wt.shape[0] // 2, 2 * BLK, LANE)
 
 
 def layer(x, gain_row, up_idx, wu_p, dn_idx, wd_p):
@@ -170,8 +168,8 @@
 
 def make_layer(gain, up_index, up_cols, down_index, down_cols):
     gain_row = gain.astype(jnp.float32)[None, :]
-    up_pairs = pad_pairs(up_cols)
-    down_pairs = pad_pairs(down_cols)
+    up_pairs = as_pairs(up_cols)
+    down_pairs = as_pairs(down_cols)
 
     def apply(block):
         return layer(block, gain_row, up_index, up_pairs, down_index, down_pairs)
@@ -196,7 +194,7 @@
     width = selected.shape[1]
     section = lax.axis_index(SEC)
     sections = lax.axis_size(SEC)
-    pieces = 8
+    pieces = 4
     group_rows = selected.shape[0] // pieces
     split = selected.reshape(pieces, group_rows, width)
 

time: 424 us -> 387 us (0.913)
  Pallas kernels: 78.7 us -> 43.8 us
  other arithmetic: 26 us -> 20 us
  waiting for transfers between devices: 220 us -> 226 us
  starting transfers between devices: 36.2 us -> 30.9 us
    pallas_call x8 -> x4, Pallas kernels: 78.7 us -> 43.8 us  [layer(): pl.pallas_call(_layer_kernel, out_shape=jax.ShapeDtypeStruct((count, widt...]
    while x0 -> x2, local copies, waits for them, and re-layouts: none -> 13.6 us  [per_device(): held, record = lax.fori_loop(0, turns, turn_step, (split[0], split))]
    ppermute x15 -> x11, waiting for transfers between devices: 154 us -> 161 us  [from_behind(): lax.ppermute(value, axis, [(source, source + steps) for source in range(i...]
    concatenate x2 -> x0, other arithmetic: 6.82 us -> none  [pad_pairs(): return jnp.concatenate([first, second], axis=1)]
    slice x3 -> x1, local copies, waits for them, and re-layouts: 6.62 us -> 0.07 us  [the longest x2 6.55 us: pad_pairs(): first = jnp.concatenate([w[:, :1], z], axis=2)]
    unnamed x21 -> x19, local copies, waits for them, and re-layouts: 9.95 us -> 4.24 us
    another operation x8, local copies, waits for them, and re-layouts: 0.23 us -> 5.55 us
    ppermute x15 -> x11, starting transfers between devices: 19.4 us -> 14.1 us  [from_behind(): lax.ppermute(value, axis, [(source, source + steps) for source in range(i...]
  transfers between devices with their start and end apart: 20 -> 16, of which waited for: 19 -> 15; matrix products, arithmetic and copies ran while one was open for 12% -> 13% of each run, Pallas kernels for 0% -> 0%
where the time goes in v5:
time: 387 us; the launch traced here: 385 us
  waiting for transfers between devices  226 us (58%)
  local copies, waits for them, and re-layouts  50.4 us (13%)
  Pallas kernels  43.8 us (11%)
  starting transfers between devices  30.9 us (8%)
  other arithmetic  20 us (5%)
  between operations  13.6 us (4%)
    ppermute x11, waiting for transfers between devices, from_behind(): lax.ppermute(value, axis, [(source, source + steps) for source in range(i...  161 us
    pallas_call x4, Pallas kernels, layer(): pl.pallas_call(_layer_kernel, out_shape=jax.ShapeDtypeStruct((count, widt...  43.8 us
    all_gather x1, waiting for transfers between devices, gather_weights(): down_full = lax.all_gather(full[:, split:], ('y', 'c'), axis=1, tiled=True)  33.3 us
    all_gather x1, waiting for transfers between devices, gather_weights(): up_full = lax.all_gather(full[:, :split], ('y', 'c'), axis=1, tiled=True)  25.6 us
    ppermute x3, starting transfers between devices, exchange_zh(): lax.ppermute(part, 'zh', [(i, (i + shift) % count) for i in range(count)])  16.8 us
    ppermute x11, starting transfers between devices, from_behind(): lax.ppermute(value, axis, [(source, source + steps) for source in range(i...  14.1 us
    while x2, local copies, waits for them, and re-layouts, per_device(): held, record = lax.fori_loop(0, turns, turn_step, (split[0], split))  13.6 us
    dynamic_update_slice x11, other arithmetic, advance(): record = lax.dynamic_update_index_in_dim(record, updated, slot, 0)  13.4 us
  transfers between devices with their start and end apart: 16, of which 15 were waited for; matrix products, arithmetic and copies ran while one was open for 13% of the time, Pallas kernels for 0%

profile of v5, /device:TPU:70, one launch (start us, length us, event | category | flops | bytes accessed | tf_op | source)
XLA Modules:
  0.0 385.3 jit_solution(3758402772816229133)
XLA Ops:
  6.5 1.6 copy.30
  8.6 10.0 %collective-permute-start.3 = (bf16[288,128]{1,0:T(8,128)(2,1)S(1)}, bf16[288,128]{1,0:T(8,128)(2,1)S(1)}, u32[]{:S(2)}, u32[]{:S(2)}) collective-permute-start(bf16[288,128]{1,0:T(8,128)(2,1)S(1)} %constant_dynamic-update-slice_fusion), channel_id=1, source_target_pairs={{0,48},{16,0},{32,16},{48,32},{1,49},{17,1},{33,17},{49,33},{2,50}... | collective-permute-start | bytes 221192 | tf_op jit(solution)/shard_map/ppermute | solution.py:29
  18.6 1.9 collective-permute-start.1
  20.5 4.8 %collective-permute-start.2 = (bf16[288,128]{1,0:T(8,128)(2,1)S(1)}, bf16[288,128]{1,0:T(8,128)(2,1)S(1)}, u32[]{:S(2)}, u32[]{:S(2)}) collective-permute-start(bf16[288,128]{1,0:T(8,128)(2,1)S(1)} %constant_dynamic-update-slice_fusion), channel_id=1, source_target_pairs={{0,32},{16,48},{32,0},{48,16},{1,33},{17,49},{33,1},{49,17},{2,34}... | collective-permute-start | bytes 221192 | tf_op jit(solution)/shard_map/ppermute | solution.py:29
  25.4 5.7 %collective-permute-done.1 = bf16[288,128]{1,0:T(8,128)(2,1)S(1)} collective-permute-done((bf16[288,128]{1,0:T(8,128)(2,1)S(1)}, bf16[288,128]{1,0:T(8,128)(2,1)S(1)}, u32[]{:S(2)}, u32[]{:S(2)}) %collective-permute-start.1) | collective-permute-done | bytes 73760 | tf_op jit(solution)/shard_map/ppermute | solution.py:29
  34.5 1.1 scatter_custom_fusion
  35.7 1.5 gather_fusion
  38.0 1.1 copy.21
  39.7 1.4 convert_element_type.12
  41.0 33.3 %all-gather.5.cloned.1.call-done = bf16[4,1536,128]{2,1,0:T(8,128)(2,1)} async-done(((bf16[4,96,128]{2,1,0:T(8,128)(2,1)}), bf16[4,1536,128]{2,1,0:T(8,128)(2,1)}) %all-gather.5.cloned.1.call-update) | async-done | bytes 1572880 | tf_op jit(solution)/shard_map/all_gather | solution.py:43
  74.3 5.1 %reshape_reshape.10 = bf16[96,2,64,64]{3,2,1,0:T(8,128)(2,1)} reshape(bf16[4,1536,128]{2,1,0:T(8,128)(2,1)} %all-gather.5.cloned.1.call-done) | data formatting | bytes 3145728 | tf_op jit(solution)/shard_map/reshape;reshape | solution.py:165
  79.4 8.3 %copy.13 = bf16[96,64,2,64]{3,2,1,0:T(2,128)(2,1)} copy(bf16[96,64,2,64]{1,3,2,0:T(8,128)(2,1)} %bitcast.32) | data formatting | bytes 3145728 | tf_op jit(solution)/shard_map/while | solution.py:219
  87.7 5.3 %reshape.127 = bf16[48,128,128]{2,1,0:T(8,128)(2,1)S(1)} reshape(bf16[96,64,2,64]{3,2,1,0:T(2,128)(2,1)} %copy.13) | data formatting | bytes 3145728 | tf_op jit(solution)/shard_map/while | solution.py:219
  93.0 25.6 %all-gather.3.cloned.1.call-done = bf16[4,3072,128]{2,1,0:T(8,128)(2,1)} async-done(((bf16[4,192,128]{2,1,0:T(8,128)(2,1)}), bf16[4,3072,128]{2,1,0:T(8,128)(2,1)}) %all-gather.3.cloned.1.call-update) | async-done | bytes 3145744 | tf_op jit(solution)/shard_map/all_gather | solution.py:42
  118.7 254.0 %while.16 = (s32[]{:T(128)}, bf16[32,6144]{1,0:T(8,128)(2,1)}, bf16[4,32,6144]{2,1,0:T(8,128)(2,1)}, s32[]{:T(128)}, pred[]{:T(512)}, /*index=5*/bf16[4,32,6144]...) while((s32[]{:T(128)}, bf16[32,6144]{1,0:T(8,128)(2,1)}, ...), condition=%wide.region_6.7_spmd, body=%wide.region_3.6_spmd.sunk | while | flops 393229 | bytes 4718975 | solution.py:219
  119.4 1.3 collective-permute-start
  120.7 1.0 constant_dynamic-slice_fusion.2
  122.6 10.3 %collective-permute-done = bf16[32,6144]{1,0:T(8,128)(2,1)} collective-permute-done((bf16[32,6144]{1,0:T(8,128)(2,1)}, bf16[32,6144]{1,0:T(8,128)(2,1)}, u32[]{:S(2)}, u32[]{:S(2)}) %collective-permute-start) | collective-permute-done | bytes 393248 | tf_op jit(solution)/shard_map/while/body/eval_jaxpr/ppermute | solution.py:21
  133.7 1.3 collective-permute-start
  134.9 1.0 constant_dynamic-slice_fusion.2
  136.8 9.4 %collective-permute-done = bf16[32,6144]{1,0:T(8,128)(2,1)} collective-permute-done((bf16[32,6144]{1,0:T(8,128)(2,1)}, bf16[32,6144]{1,0:T(8,128)(2,1)}, u32[]{:S(2)}, u32[]{:S(2)}) %collective-permute-start) | collective-permute-done | bytes 393248 | tf_op jit(solution)/shard_map/while/body/eval_jaxpr/ppermute | solution.py:21
  147.0 1.3 collective-permute-start
  148.3 1.0 constant_dynamic-slice_fusion.2
  150.2 8.5 %collective-permute-done = bf16[32,6144]{1,0:T(8,128)(2,1)} collective-permute-done((bf16[32,6144]{1,0:T(8,128)(2,1)}, bf16[32,6144]{1,0:T(8,128)(2,1)}, u32[]{:S(2)}, u32[]{:S(2)}) %collective-permute-start) | collective-permute-done | bytes 393248 | tf_op jit(solution)/shard_map/while/body/eval_jaxpr/ppermute | solution.py:21
  159.5 1.3 collective-permute-start
  160.8 1.0 constant_dynamic-slice_fusion.2
  162.7 7.7 %collective-permute-done = bf16[32,6144]{1,0:T(8,128)(2,1)} collective-permute-done((bf16[32,6144]{1,0:T(8,128)(2,1)}, bf16[32,6144]{1,0:T(8,128)(2,1)}, u32[]{:S(2)}, u32[]{:S(2)}) %collective-permute-start) | collective-permute-done | bytes 393248 | tf_op jit(solution)/shard_map/while/body/eval_jaxpr/ppermute | solution.py:21
  171.2 1.3 collective-permute-start
  172.5 1.0 constant_dynamic-slice_fusion.2
  174.3 8.7 %collective-permute-done = bf16[32,6144]{1,0:T(8,128)(2,1)} collective-permute-done((bf16[32,6144]{1,0:T(8,128)(2,1)}, bf16[32,6144]{1,0:T(8,128)(2,1)}, u32[]{:S(2)}, u32[]{:S(2)}) %collective-permute-start) | collective-permute-done | bytes 393248 | tf_op jit(solution)/shard_map/while/body/eval_jaxpr/ppermute | solution.py:21
  183.8 1.3 collective-permute-start
  185.1 1.0 constant_dynamic-slice_fusion.2
  187.0 8.1 %collective-permute-done = bf16[32,6144]{1,0:T(8,128)(2,1)} collective-permute-done((bf16[32,6144]{1,0:T(8,128)(2,1)}, bf16[32,6144]{1,0:T(8,128)(2,1)}, u32[]{:S(2)}, u32[]{:S(2)}) %collective-permute-start) | collective-permute-done | bytes 393248 | tf_op jit(solution)/shard_map/while/body/eval_jaxpr/ppermute | solution.py:21
  195.8 1.3 collective-permute-start
  199.0 80.0 %collective-permute-done = bf16[32,6144]{1,0:T(8,128)(2,1)} collective-permute-done((bf16[32,6144]{1,0:T(8,128)(2,1)}, bf16[32,6144]{1,0:T(8,128)(2,1)}, u32[]{:S(2)}, u32[]{:S(2)}) %collective-permute-start) | collective-permute-done | bytes 393248 | tf_op jit(solution)/shard_map/while/body/eval_jaxpr/ppermute | solution.py:21
  279.0 12.1 %conditional.2 = (bf16[32,6144]{1,0:T(8,128)(2,1)}) conditional(s32[]{:T(128)} %convert_element_type.14, () %tuple.46, (pred[]{:T(512)}, s32[]{:T(128)}, bf16[4,32,6144]{2,1,0:T(8,128)(2,1)}, bf16[32,6144]{1,0:T(8,128)(2,1)}, s32[384]{0:T(512)S(1)}, /*index=5*/s32[192]{0:T(256)S(1)}, f32[1,6144]{1,0:T(1,128)}, bf16[96,128,128]{2,1,0:T(8,128)(2,1)}, ...), branch_computations={%region_4.4_spmd, %region_5.5_spmd} | conditional | flops 196612 | bytes 1179707 | solution.py:205
  279.0 1.2 bitcast_select_fusion.x_ref
  280.2 10.9 %branch_1_fun.3 = bf16[32,6144]{1,0:T(8,128)(2,1)} custom-call(s32[384]{0:T(512)S(1)} %get-tuple-element.287.up_idx, s32[192]{0:T(256)S(1)} %get-tuple-element.288.dn_idx, bf16[32,6144]{1,0:T(8,128)(2,1)S(1)} %bitcast_select_fusion.x_ref, f32[1,6144]{1,0:T(1,128)} %get-tuple-element.293.g_ref, bf16[96,128,128]{2,1,0:T(8,128)(2,1)} %get-tuple-element.294.wu_hbm, ...), custom_call_target="tpu_custom_call" | custom-call | tf_op jit(solution)/shard_map/while/body/eval_jaxpr/cond/branch_1_fun/pallas_call | solution.py:138
  291.1 1.3 collective-permute-start
  293.5 1.8 bitcast_dynamic-update-slice_fusion.2
  295.3 7.1 %collective-permute-done = bf16[32,6144]{1,0:T(8,128)(2,1)} collective-permute-done((bf16[32,6144]{1,0:T(8,128)(2,1)}, bf16[32,6144]{1,0:T(8,128)(2,1)}, u32[]{:S(2)}, u32[]{:S(2)}) %collective-permute-start) | collective-permute-done | bytes 393248 | tf_op jit(solution)/shard_map/while/body/eval_jaxpr/ppermute | solution.py:21
  302.4 12.1 %conditional.2 = (bf16[32,6144]{1,0:T(8,128)(2,1)}) conditional(s32[]{:T(128)} %convert_element_type.14, () %tuple.46, (pred[]{:T(512)}, s32[]{:T(128)}, bf16[4,32,6144]{2,1,0:T(8,128)(2,1)}, bf16[32,6144]{1,0:T(8,128)(2,1)}, s32[384]{0:T(512)S(1)}, /*index=5*/s32[192]{0:T(256)S(1)}, f32[1,6144]{1,0:T(1,128)}, bf16[96,128,128]{2,1,0:T(8,128)(2,1)}, ...), branch_computations={%region_4.4_spmd, %region_5.5_spmd} | conditional | flops 196612 | bytes 1179707 | solution.py:205
  302.4 1.2 bitcast_select_fusion.x_ref
  303.6 10.9 %branch_1_fun.3 = bf16[32,6144]{1,0:T(8,128)(2,1)} custom-call(s32[384]{0:T(512)S(1)} %get-tuple-element.287.up_idx, s32[192]{0:T(256)S(1)} %get-tuple-element.288.dn_idx, bf16[32,6144]{1,0:T(8,128)(2,1)S(1)} %bitcast_select_fusion.x_ref, f32[1,6144]{1,0:T(1,128)} %get-tuple-element.293.g_ref, bf16[96,128,128]{2,1,0:T(8,128)(2,1)} %get-tuple-element.294.wu_hbm, ...), custom_call_target="tpu_custom_call" | custom-call | tf_op jit(solution)/shard_map/while/body/eval_jaxpr/cond/branch_1_fun/pallas_call | solution.py:138
  314.5 1.3 collective-permute-start
  315.8 1.0 constant_dynamic-slice_fusion.2
  316.9 1.8 bitcast_dynamic-update-slice_fusion.2
  318.7 7.6 %collective-permute-done = bf16[32,6144]{1,0:T(8,128)(2,1)} collective-permute-done((bf16[32,6144]{1,0:T(8,128)(2,1)}, bf16[32,6144]{1,0:T(8,128)(2,1)}, u32[]{:S(2)}, u32[]{:S(2)}) %collective-permute-start) | collective-permute-done | bytes 393248 | tf_op jit(solution)/shard_map/while/body/eval_jaxpr/ppermute | solution.py:21
  326.3 12.1 %conditional.2 = (bf16[32,6144]{1,0:T(8,128)(2,1)}) conditional(s32[]{:T(128)} %convert_element_type.14, () %tuple.46, (pred[]{:T(512)}, s32[]{:T(128)}, bf16[4,32,6144]{2,1,0:T(8,128)(2,1)}, bf16[32,6144]{1,0:T(8,128)(2,1)}, s32[384]{0:T(512)S(1)}, /*index=5*/s32[192]{0:T(256)S(1)}, f32[1,6144]{1,0:T(1,128)}, bf16[96,128,128]{2,1,0:T(8,128)(2,1)}, ...), branch_computations={%region_4.4_spmd, %region_5.5_spmd} | conditional | flops 196612 | bytes 1179707 | solution.py:205
  326.3 1.2 bitcast_select_fusion.x_ref
  327.5 10.9 %branch_1_fun.3 = bf16[32,6144]{1,0:T(8,128)(2,1)} custom-call(s32[384]{0:T(512)S(1)} %get-tuple-element.287.up_idx, s32[192]{0:T(256)S(1)} %get-tuple-element.288.dn_idx, bf16[32,6144]{1,0:T(8,128)(2,1)S(1)} %bitcast_select_fusion.x_ref, f32[1,6144]{1,0:T(1,128)} %get-tuple-element.293.g_ref, bf16[96,128,128]{2,1,0:T(8,128)(2,1)} %get-tuple-element.294.wu_hbm, ...), custom_call_target="tpu_custom_call" | custom-call | tf_op jit(solution)/shard_map/while/body/eval_jaxpr/cond/branch_1_fun/pallas_call | solution.py:138
  338.5 1.3 collective-permute-start
  339.8 1.0 constant_dynamic-slice_fusion.2
  340.8 1.8 bitcast_dynamic-update-slice_fusion.2
  342.6 7.9 %collective-permute-done = bf16[32,6144]{1,0:T(8,128)(2,1)} collective-permute-done((bf16[32,6144]{1,0:T(8,128)(2,1)}, bf16[32,6144]{1,0:T(8,128)(2,1)}, u32[]{:S(2)}, u32[]{:S(2)}) %collective-permute-start) | collective-permute-done | bytes 393248 | tf_op jit(solution)/shard_map/while/body/eval_jaxpr/ppermute | solution.py:21
  350.5 12.1 %conditional.2 = (bf16[32,6144]{1,0:T(8,128)(2,1)}) conditional(s32[]{:T(128)} %convert_element_type.14, () %tuple.46, (pred[]{:T(512)}, s32[]{:T(128)}, bf16[4,32,6144]{2,1,0:T(8,128)(2,1)}, bf16[32,6144]{1,0:T(8,128)(2,1)}, s32[384]{0:T(512)S(1)}, /*index=5*/s32[192]{0:T(256)S(1)}, f32[1,6144]{1,0:T(1,128)}, bf16[96,128,128]{2,1,0:T(8,128)(2,1)}, ...), branch_computations={%region_4.4_spmd, %region_5.5_spmd} | conditional | flops 196612 | bytes 1179707 | solution.py:205
  350.6 1.2 bitcast_select_fusion.x_ref
  351.7 10.9 %branch_1_fun.3 = bf16[32,6144]{1,0:T(8,128)(2,1)} custom-call(s32[384]{0:T(512)S(1)} %get-tuple-element.287.up_idx, s32[192]{0:T(256)S(1)} %get-tuple-element.288.dn_idx, bf16[32,6144]{1,0:T(8,128)(2,1)S(1)} %bitcast_select_fusion.x_ref, f32[1,6144]{1,0:T(1,128)} %get-tuple-element.293.g_ref, bf16[96,128,128]{2,1,0:T(8,128)(2,1)} %get-tuple-element.294.wu_hbm, ...), custom_call_target="tpu_custom_call" | custom-call | tf_op jit(solution)/shard_map/while/body/eval_jaxpr/cond/branch_1_fun/pallas_call | solution.py:138
  362.7 1.3 collective-permute-start
  364.0 1.0 constant_dynamic-slice_fusion.2
  365.0 1.8 bitcast_dynamic-update-slice_fusion.2
  366.8 5.8 %collective-permute-done = bf16[32,6144]{1,0:T(8,128)(2,1)} collective-permute-done((bf16[32,6144]{1,0:T(8,128)(2,1)}, bf16[32,6144]{1,0:T(8,128)(2,1)}, u32[]{:S(2)}, u32[]{:S(2)}) %collective-permute-start) | collective-permute-done | bytes 393248 | tf_op jit(solution)/shard_map/while/body/eval_jaxpr/ppermute | solution.py:21
  372.7 4.5 %scatter_fusion = bf16[160,6144]{1,0:T(8,128)(2,1)S(1)} fusion(bf16[160,6144]{1,0:T(8,128)(2,1)S(1)} %copy.30, s32[128]{0:T(128)S(1)} %compare_select_fusion.3, bf16[128,6144]{1,0:T(8,128)(2,1)} %bitcast.31), kind=kCustom, calls=%fused_computation.3 | custom fusion | bytes 4719104 | tf_op jit(solution)/shard_map/scatter | solution.py:221
  377.2 1.3 copy-done
  (71 shorter events, 24.1 us)
Async XLA Ops:
  6.5 1.6 copy-start.2
  6.5 2.0 copy-start.3
  6.5 67.8 %all-gather.5.cloned.1.call-start = ((), (), s32[]{:S(2)}) async-start(), calls=%async_computation.1 | async-start | bytes 1671168 | tf_op jit(solution)/shard_map/all_gather | solution.py:43
  8.2 25.7 %copy-start.4 = (s32[160]{0:T(256)S(1)}, s32[160]{0:T(256)}, u32[]{:S(2)}) copy-start(s32[160]{0:T(256)} %param.12) | copy-start | bytes 1924
  8.6 16.8 %collective-permute-start.3 = (bf16[288,128]{1,0:T(8,128)(2,1)S(1)}, bf16[288,128]{1,0:T(8,128)(2,1)S(1)}, u32[]{:S(2)}, u32[]{:S(2)}) collective-permute-start(bf16[288,128]{1,0:T(8,128)(2,1)S(1)} %constant_dynamic-update-slice_fusion), channel_id=1, source_target_pairs={{0,48},{16,0},{32,16},{48,32},{1,49},{17,1},{33,17},{49,33},{2,50}... | collective-permute-start | bytes 221192 | tf_op jit(solution)/shard_map/ppermute | solution.py:29
  18.6 12.5 %collective-permute-start.1 = (bf16[288,128]{1,0:T(8,128)(2,1)S(1)}, bf16[288,128]{1,0:T(8,128)(2,1)S(1)}, u32[]{:S(2)}, u32[]{:S(2)}) collective-permute-start(bf16[288,128]{1,0:T(8,128)(2,1)S(1)} %constant_dynamic-update-slice_fusion), channel_id=1, source_target_pairs={{0,16},{16,32},{32,48},{48,0},{1,17},{17,33},{33,49},{49,1},{2,18}... | collective-permute-start | bytes 221192 | tf_op jit(solution)/shard_map/ppermute | solution.py:29
  20.5 11.2 %collective-permute-start.2 = (bf16[288,128]{1,0:T(8,128)(2,1)S(1)}, bf16[288,128]{1,0:T(8,128)(2,1)S(1)}, u32[]{:S(2)}, u32[]{:S(2)}) collective-permute-start(bf16[288,128]{1,0:T(8,128)(2,1)S(1)} %constant_dynamic-update-slice_fusion), channel_id=1, source_target_pairs={{0,32},{16,48},{32,0},{48,16},{1,33},{17,49},{33,1},{49,17},{2,34}... | collective-permute-start | bytes 221192 | tf_op jit(solution)/shard_map/ppermute | solution.py:29
  33.1 85.5 %all-gather.3.cloned.1.call-start = ((), (), s32[]{:S(2)}) async-start(), calls=%async_computation | async-start | bytes 3342336 | tf_op jit(solution)/shard_map/all_gather | solution.py:42
  37.2 2.0 copy-start.1
  38.0 1.2 copy-start.5
  38.0 1.4 copy-start.6
  119.4 13.4 %collective-permute-start = (bf16[32,6144]{1,0:T(8,128)(2,1)}, bf16[32,6144]{1,0:T(8,128)(2,1)}, u32[]{:S(2)}, u32[]{:S(2)}) collective-permute-start(bf16[32,6144]{1,0:T(8,128)(2,1)} %get-tuple-element.455), channel_id=1, source_target_pairs={{0,64},{64,128},{128,192},{192,256},{256,320},{320,384},{384,448},... | collective-permute-start | bytes 1179656 | tf_op jit(solution)/shard_map/while/body/eval_jaxpr/ppermute | solution.py:21
  133.7 12.6 %collective-permute-start = (bf16[32,6144]{1,0:T(8,128)(2,1)}, bf16[32,6144]{1,0:T(8,128)(2,1)}, u32[]{:S(2)}, u32[]{:S(2)}) collective-permute-start(bf16[32,6144]{1,0:T(8,128)(2,1)} %get-tuple-element.455), channel_id=1, source_target_pairs={{0,64},{64,128},{128,192},{192,256},{256,320},{320,384},{384,448},... | collective-permute-start | bytes 1179656 | tf_op jit(solution)/shard_map/while/body/eval_jaxpr/ppermute | solution.py:21
  147.0 11.7 %collective-permute-start = (bf16[32,6144]{1,0:T(8,128)(2,1)}, bf16[32,6144]{1,0:T(8,128)(2,1)}, u32[]{:S(2)}, u32[]{:S(2)}) collective-permute-start(bf16[32,6144]{1,0:T(8,128)(2,1)} %get-tuple-element.455), channel_id=1, source_target_pairs={{0,64},{64,128},{128,192},{192,256},{256,320},{320,384},{384,448},... | collective-permute-start | bytes 1179656 | tf_op jit(solution)/shard_map/while/body/eval_jaxpr/ppermute | solution.py:21
  159.5 10.9 %collective-permute-start = (bf16[32,6144]{1,0:T(8,128)(2,1)}, bf16[32,6144]{1,0:T(8,128)(2,1)}, u32[]{:S(2)}, u32[]{:S(2)}) collective-permute-start(bf16[32,6144]{1,0:T(8,128)(2,1)} %get-tuple-element.455), channel_id=1, source_target_pairs={{0,64},{64,128},{128,192},{192,256},{256,320},{320,384},{384,448},... | collective-permute-start | bytes 1179656 | tf_op jit(solution)/shard_map/while/body/eval_jaxpr/ppermute | solution.py:21
  171.2 11.8 %collective-permute-start = (bf16[32,6144]{1,0:T(8,128)(2,1)}, bf16[32,6144]{1,0:T(8,128)(2,1)}, u32[]{:S(2)}, u32[]{:S(2)}) collective-permute-start(bf16[32,6144]{1,0:T(8,128)(2,1)} %get-tuple-element.455), channel_id=1, source_target_pairs={{0,64},{64,128},{128,192},{192,256},{256,320},{320,384},{384,448},... | collective-permute-start | bytes 1179656 | tf_op jit(solution)/shard_map/while/body/eval_jaxpr/ppermute | solution.py:21
  183.8 11.3 %collective-permute-start = (bf16[32,6144]{1,0:T(8,128)(2,1)}, bf16[32,6144]{1,0:T(8,128)(2,1)}, u32[]{:S(2)}, u32[]{:S(2)}) collective-permute-start(bf16[32,6144]{1,0:T(8,128)(2,1)} %get-tuple-element.455), channel_id=1, source_target_pairs={{0,64},{64,128},{128,192},{192,256},{256,320},{320,384},{384,448},... | collective-permute-start | bytes 1179656 | tf_op jit(solution)/shard_map/while/body/eval_jaxpr/ppermute | solution.py:21
  195.8 83.2 %collective-permute-start = (bf16[32,6144]{1,0:T(8,128)(2,1)}, bf16[32,6144]{1,0:T(8,128)(2,1)}, u32[]{:S(2)}, u32[]{:S(2)}) collective-permute-start(bf16[32,6144]{1,0:T(8,128)(2,1)} %get-tuple-element.455), channel_id=1, source_target_pairs={{0,64},{64,128},{128,192},{192,256},{256,320},{320,384},{384,448},... | collective-permute-start | bytes 1179656 | tf_op jit(solution)/shard_map/while/body/eval_jaxpr/ppermute | solution.py:21
  291.1 11.3 %collective-permute-start = (bf16[32,6144]{1,0:T(8,128)(2,1)}, bf16[32,6144]{1,0:T(8,128)(2,1)}, u32[]{:S(2)}, u32[]{:S(2)}) collective-permute-start(bf16[32,6144]{1,0:T(8,128)(2,1)} %get-tuple-element.455), channel_id=1, source_target_pairs={{0,64},{64,128},{128,192},{192,256},{256,320},{320,384},{384,448},... | collective-permute-start | bytes 1179656 | tf_op jit(solution)/shard_map/while/body/eval_jaxpr/ppermute | solution.py:21
  314.5 11.8 %collective-permute-start = (bf16[32,6144]{1,0:T(8,128)(2,1)}, bf16[32,6144]{1,0:T(8,128)(2,1)}, u32[]{:S(2)}, u32[]{:S(2)}) collective-permute-start(bf16[32,6144]{1,0:T(8,128)(2,1)} %get-tuple-element.455), channel_id=1, source_target_pairs={{0,64},{64,128},{128,192},{192,256},{256,320},{320,384},{384,448},... | collective-permute-start | bytes 1179656 | tf_op jit(solution)/shard_map/while/body/eval_jaxpr/ppermute | solution.py:21
  338.5 12.1 %collective-permute-start = (bf16[32,6144]{1,0:T(8,128)(2,1)}, bf16[32,6144]{1,0:T(8,128)(2,1)}, u32[]{:S(2)}, u32[]{:S(2)}) collective-permute-start(bf16[32,6144]{1,0:T(8,128)(2,1)} %get-tuple-element.455), channel_id=1, source_target_pairs={{0,64},{64,128},{128,192},{192,256},{256,320},{320,384},{384,448},... | collective-permute-start | bytes 1179656 | tf_op jit(solution)/shard_map/while/body/eval_jaxpr/ppermute | solution.py:21
  362.7 10.0 %collective-permute-start = (bf16[32,6144]{1,0:T(8,128)(2,1)}, bf16[32,6144]{1,0:T(8,128)(2,1)}, u32[]{:S(2)}, u32[]{:S(2)}) collective-permute-start(bf16[32,6144]{1,0:T(8,128)(2,1)} %get-tuple-element.455), channel_id=1, source_target_pairs={{0,64},{64,128},{128,192},{192,256},{256,320},{320,384},{384,448},... | collective-permute-start | bytes 1179656 | tf_op jit(solution)/shard_map/while/body/eval_jaxpr/ppermute | solution.py:21
  377.2 1.3 copy-start
Sparse Core Ops, SparseCore 0:
  33.2 41.0 all-gather.4
  76.4 42.1 all-gather.2

commit v6 on v5

--- a/solution.py
+++ b/solution.py
@@ -39,8 +39,9 @@
     down_part = down_shard.reshape(down_shard.shape[1] * 32, 128)
     split = up_part.shape[0]
     full = exchange_zh(jnp.concatenate([up_part, down_part], axis=0))
-    up_full = lax.all_gather(full[:, :split], ("y", "c"), axis=1, tiled=True)
-    down_full = lax.all_gather(full[:, split:], ("y", "c"), axis=1, tiled=True)
+    full = lax.all_gather(full[:, None], ("y", "c"), axis=1, tiled=True)
+    up_full = full[:, :, :split]
+    down_full = full[:, :, split:]
     return up_full.reshape(-1, BLK, UP_DEPTH * BLK), down_full.reshape(-1, 4096)
 
 

time: 387 us -> 368 us (0.951)
  waiting for transfers between devices: 226 us -> 205 us
    all_gather x2 -> x1, waiting for transfers between devices: 58.9 us -> 37.1 us  [gather_weights(): full = lax.all_gather(full[:, None], ('y', 'c'), axis=1, tiled=True)]
  transfers between devices with their start and end apart: 16 -> 15, of which waited for: 15 -> 14; matrix products, arithmetic and copies ran while one was open for 13% -> 9% of each run, Pallas kernels for 0% -> 0%
where the time goes in v6:
time: 368 us; the launch traced here: 366 us
  waiting for transfers between devices  205 us (56%)
  local copies, waits for them, and re-layouts  52.2 us (14%)
  Pallas kernels  43.8 us (12%)
  starting transfers between devices  30.9 us (8%)
  other arithmetic  20.7 us (6%)
  between operations  13.6 us (4%)
    ppermute x11, waiting for transfers between devices, from_behind(): lax.ppermute(value, axis, [(source, source + steps) for source in range(i...  161 us
    pallas_call x4, Pallas kernels, layer(): pl.pallas_call(_layer_kernel, out_shape=jax.ShapeDtypeStruct((count, widt...  43.8 us
    all_gather x1, waiting for transfers between devices, gather_weights(): full = lax.all_gather(full[:, None], ('y', 'c'), axis=1, tiled=True)  37.1 us
    ppermute x3, starting transfers between devices, exchange_zh(): lax.ppermute(part, 'zh', [(i, (i + shift) % count) for i in range(count)])  16.8 us
    ppermute x11, starting transfers between devices, from_behind(): lax.ppermute(value, axis, [(source, source + steps) for source in range(i...  14.1 us
    while x2, local copies, waits for them, and re-layouts, per_device(): held, record = lax.fori_loop(0, turns, turn_step, (split[0], split))  13.6 us
    dynamic_update_slice x11, other arithmetic, advance(): record = lax.dynamic_update_index_in_dim(record, updated, slot, 0)  13.4 us
    dynamic_slice x11, local copies, waits for them, and re-layouts, advance(): current = lax.dynamic_index_in_dim(record, slot, 0, keepdims=False)  11.3 us
  transfers between devices with their start and end apart: 15, of which 14 were waited for; matrix products, arithmetic and copies ran while one was open for 9% of the time, Pallas kernels for 0%

profile of v6, /device:TPU:70, one launch (start us, length us, event | category | flops | bytes accessed | tf_op | source)
XLA Modules:
  0.0 366.0 jit_solution(5892172990397208184)
XLA Ops:
  6.5 1.6 copy.46
  8.6 10.0 %collective-permute-start.3 = (bf16[288,128]{1,0:T(8,128)(2,1)S(1)}, bf16[288,128]{1,0:T(8,128)(2,1)S(1)}, u32[]{:S(2)}, u32[]{:S(2)}) collective-permute-start(bf16[288,128]{1,0:T(8,128)(2,1)S(1)} %constant_dynamic-update-slice_fusion), channel_id=1, source_target_pairs={{0,48},{16,0},{32,16},{48,32},{1,49},{17,1},{33,17},{49,33},{2,50}... | collective-permute-start | bytes 221192 | tf_op jit(solution)/shard_map/ppermute | solution.py:29
  18.6 1.9 collective-permute-start.1
  20.5 4.8 %collective-permute-start.2 = (bf16[288,128]{1,0:T(8,128)(2,1)S(1)}, bf16[288,128]{1,0:T(8,128)(2,1)S(1)}, u32[]{:S(2)}, u32[]{:S(2)}) collective-permute-start(bf16[288,128]{1,0:T(8,128)(2,1)S(1)} %constant_dynamic-update-slice_fusion), channel_id=1, source_target_pairs={{0,32},{16,48},{32,0},{48,16},{1,33},{17,49},{33,1},{49,17},{2,34}... | collective-permute-start | bytes 221192 | tf_op jit(solution)/shard_map/ppermute | solution.py:29
  25.4 5.7 %collective-permute-done.1 = bf16[288,128]{1,0:T(8,128)(2,1)S(1)} collective-permute-done((bf16[288,128]{1,0:T(8,128)(2,1)S(1)}, bf16[288,128]{1,0:T(8,128)(2,1)S(1)}, u32[]{:S(2)}, u32[]{:S(2)}) %collective-permute-start.1) | collective-permute-done | bytes 73760 | tf_op jit(solution)/shard_map/ppermute | solution.py:29
  33.8 1.1 scatter_custom_fusion
  35.0 1.5 gather_fusion
  37.3 1.1 copy.37
  39.0 1.4 convert_element_type.12
  40.4 37.1 %all-gather.2.cloned.1.call-done = bf16[4,16,288,128]{3,2,0,1:T(8,128)(2,1)} async-done(((bf16[4,1,288,128]{3,2,0,1:T(8,128)(2,1)}), bf16[4,16,288,128]{3,2,0,1:T(8,128)(2,1)}) %all-gather.2.cloned.1.call-update) | async-done | bytes 4718608 | tf_op jit(solution)/shard_map/all_gather | solution.py:42
  77.5 1.4 slice-done
  79.0 2.9 reshape_reshape.10
  81.9 8.3 %copy.28 = bf16[96,64,2,64]{3,2,1,0:T(2,128)(2,1)} copy(bf16[96,64,2,64]{1,3,2,0:T(8,128)(2,1)} %bitcast.36) | data formatting | bytes 3145728 | tf_op jit(solution)/shard_map/while | solution.py:220
  90.2 5.3 %reshape.134 = bf16[48,128,128]{2,1,0:T(8,128)(2,1)S(1)} reshape(bf16[96,64,2,64]{3,2,1,0:T(2,128)(2,1)} %copy.28) | data formatting | bytes 3145728 | tf_op jit(solution)/shard_map/while | solution.py:220
  95.5 1.9 slice-done.1
  97.4 1.9 copy.30
  99.3 254.1 %while.16 = (s32[]{:T(128)}, bf16[32,6144]{1,0:T(8,128)(2,1)}, bf16[4,32,6144]{2,1,0:T(8,128)(2,1)}, s32[]{:T(128)}, pred[]{:T(512)}, /*index=5*/bf16[4,32,6144]...) while((s32[]{:T(128)}, bf16[32,6144]{1,0:T(8,128)(2,1)}, ...), condition=%wide.region_6.7_spmd, body=%wide.region_3.6_spmd.sunk | while | flops 393229 | bytes 4718975 | solution.py:220
  100.1 1.3 collective-permute-start
  101.4 1.0 constant_dynamic-slice_fusion.2
  103.3 10.3 %collective-permute-done = bf16[32,6144]{1,0:T(8,128)(2,1)} collective-permute-done((bf16[32,6144]{1,0:T(8,128)(2,1)}, bf16[32,6144]{1,0:T(8,128)(2,1)}, u32[]{:S(2)}, u32[]{:S(2)}) %collective-permute-start) | collective-permute-done | bytes 393248 | tf_op jit(solution)/shard_map/while/body/eval_jaxpr/ppermute | solution.py:21
  114.3 1.3 collective-permute-start
  115.6 1.0 constant_dynamic-slice_fusion.2
  117.5 9.4 %collective-permute-done = bf16[32,6144]{1,0:T(8,128)(2,1)} collective-permute-done((bf16[32,6144]{1,0:T(8,128)(2,1)}, bf16[32,6144]{1,0:T(8,128)(2,1)}, u32[]{:S(2)}, u32[]{:S(2)}) %collective-permute-start) | collective-permute-done | bytes 393248 | tf_op jit(solution)/shard_map/while/body/eval_jaxpr/ppermute | solution.py:21
  127.7 1.3 collective-permute-start
  129.0 1.0 constant_dynamic-slice_fusion.2
  130.9 8.6 %collective-permute-done = bf16[32,6144]{1,0:T(8,128)(2,1)} collective-permute-done((bf16[32,6144]{1,0:T(8,128)(2,1)}, bf16[32,6144]{1,0:T(8,128)(2,1)}, u32[]{:S(2)}, u32[]{:S(2)}) %collective-permute-start) | collective-permute-done | bytes 393248 | tf_op jit(solution)/shard_map/while/body/eval_jaxpr/ppermute | solution.py:21
  140.2 1.3 collective-permute-start
  141.5 1.0 constant_dynamic-slice_fusion.2
  143.4 7.7 %collective-permute-done = bf16[32,6144]{1,0:T(8,128)(2,1)} collective-permute-done((bf16[32,6144]{1,0:T(8,128)(2,1)}, bf16[32,6144]{1,0:T(8,128)(2,1)}, u32[]{:S(2)}, u32[]{:S(2)}) %collective-permute-start) | collective-permute-done | bytes 393248 | tf_op jit(solution)/shard_map/while/body/eval_jaxpr/ppermute | solution.py:21
  151.9 1.3 collective-permute-start
  153.2 1.0 constant_dynamic-slice_fusion.2
  155.0 8.7 %collective-permute-done = bf16[32,6144]{1,0:T(8,128)(2,1)} collective-permute-done((bf16[32,6144]{1,0:T(8,128)(2,1)}, bf16[32,6144]{1,0:T(8,128)(2,1)}, u32[]{:S(2)}, u32[]{:S(2)}) %collective-permute-start) | collective-permute-done | bytes 393248 | tf_op jit(solution)/shard_map/while/body/eval_jaxpr/ppermute | solution.py:21
  164.5 1.3 collective-permute-start
  165.8 1.0 constant_dynamic-slice_fusion.2
  167.7 8.1 %collective-permute-done = bf16[32,6144]{1,0:T(8,128)(2,1)} collective-permute-done((bf16[32,6144]{1,0:T(8,128)(2,1)}, bf16[32,6144]{1,0:T(8,128)(2,1)}, u32[]{:S(2)}, u32[]{:S(2)}) %collective-permute-start) | collective-permute-done | bytes 393248 | tf_op jit(solution)/shard_map/while/body/eval_jaxpr/ppermute | solution.py:21
  176.5 1.3 collective-permute-start
  179.7 80.1 %collective-permute-done = bf16[32,6144]{1,0:T(8,128)(2,1)} collective-permute-done((bf16[32,6144]{1,0:T(8,128)(2,1)}, bf16[32,6144]{1,0:T(8,128)(2,1)}, u32[]{:S(2)}, u32[]{:S(2)}) %collective-permute-start) | collective-permute-done | bytes 393248 | tf_op jit(solution)/shard_map/while/body/eval_jaxpr/ppermute | solution.py:21
  259.8 12.1 %conditional.2 = (bf16[32,6144]{1,0:T(8,128)(2,1)}) conditional(s32[]{:T(128)} %convert_element_type.14, () %tuple.48, (pred[]{:T(512)}, s32[]{:T(128)}, bf16[4,32,6144]{2,1,0:T(8,128)(2,1)}, bf16[32,6144]{1,0:T(8,128)(2,1)}, s32[384]{0:T(512)S(1)}, /*index=5*/s32[192]{0:T(256)S(1)}, f32[1,6144]{1,0:T(1,128)}, bf16[96,128,128]{2,1,0:T(8,128)(2,1)}, ...), branch_computations={%region_4.4_spmd, %region_5.5_spmd} | conditional | flops 196612 | bytes 1179707 | solution.py:206
  259.8 1.2 bitcast_select_fusion.x_ref
  261.0 10.9 %branch_1_fun.3 = bf16[32,6144]{1,0:T(8,128)(2,1)} custom-call(s32[384]{0:T(512)S(1)} %get-tuple-element.287.up_idx, s32[192]{0:T(256)S(1)} %get-tuple-element.288.dn_idx, bf16[32,6144]{1,0:T(8,128)(2,1)S(1)} %bitcast_select_fusion.x_ref, f32[1,6144]{1,0:T(1,128)} %get-tuple-element.293.g_ref, bf16[96,128,128]{2,1,0:T(8,128)(2,1)} %get-tuple-element.294.wu_hbm, ...), custom_call_target="tpu_custom_call" | custom-call | tf_op jit(solution)/shard_map/while/body/eval_jaxpr/cond/branch_1_fun/pallas_call | solution.py:139
  271.9 1.3 collective-permute-start
  273.2 1.0 constant_dynamic-slice_fusion.2
  274.2 1.8 bitcast_dynamic-update-slice_fusion.2
  276.1 7.1 %collective-permute-done = bf16[32,6144]{1,0:T(8,128)(2,1)} collective-permute-done((bf16[32,6144]{1,0:T(8,128)(2,1)}, bf16[32,6144]{1,0:T(8,128)(2,1)}, u32[]{:S(2)}, u32[]{:S(2)}) %collective-permute-start) | collective-permute-done | bytes 393248 | tf_op jit(solution)/shard_map/while/body/eval_jaxpr/ppermute | solution.py:21
  283.2 12.1 %conditional.2 = (bf16[32,6144]{1,0:T(8,128)(2,1)}) conditional(s32[]{:T(128)} %convert_element_type.14, () %tuple.48, (pred[]{:T(512)}, s32[]{:T(128)}, bf16[4,32,6144]{2,1,0:T(8,128)(2,1)}, bf16[32,6144]{1,0:T(8,128)(2,1)}, s32[384]{0:T(512)S(1)}, /*index=5*/s32[192]{0:T(256)S(1)}, f32[1,6144]{1,0:T(1,128)}, bf16[96,128,128]{2,1,0:T(8,128)(2,1)}, ...), branch_computations={%region_4.4_spmd, %region_5.5_spmd} | conditional | flops 196612 | bytes 1179707 | solution.py:206
  283.2 1.2 bitcast_select_fusion.x_ref
  284.3 10.9 %branch_1_fun.3 = bf16[32,6144]{1,0:T(8,128)(2,1)} custom-call(s32[384]{0:T(512)S(1)} %get-tuple-element.287.up_idx, s32[192]{0:T(256)S(1)} %get-tuple-element.288.dn_idx, bf16[32,6144]{1,0:T(8,128)(2,1)S(1)} %bitcast_select_fusion.x_ref, f32[1,6144]{1,0:T(1,128)} %get-tuple-element.293.g_ref, bf16[96,128,128]{2,1,0:T(8,128)(2,1)} %get-tuple-element.294.wu_hbm, ...), custom_call_target="tpu_custom_call" | custom-call | tf_op jit(solution)/shard_map/while/body/eval_jaxpr/cond/branch_1_fun/pallas_call | solution.py:139
  295.3 1.3 collective-permute-start
  297.6 1.8 bitcast_dynamic-update-slice_fusion.2
  299.5 7.6 %collective-permute-done = bf16[32,6144]{1,0:T(8,128)(2,1)} collective-permute-done((bf16[32,6144]{1,0:T(8,128)(2,1)}, bf16[32,6144]{1,0:T(8,128)(2,1)}, u32[]{:S(2)}, u32[]{:S(2)}) %collective-permute-start) | collective-permute-done | bytes 393248 | tf_op jit(solution)/shard_map/while/body/eval_jaxpr/ppermute | solution.py:21
  307.1 12.1 %conditional.2 = (bf16[32,6144]{1,0:T(8,128)(2,1)}) conditional(s32[]{:T(128)} %convert_element_type.14, () %tuple.48, (pred[]{:T(512)}, s32[]{:T(128)}, bf16[4,32,6144]{2,1,0:T(8,128)(2,1)}, bf16[32,6144]{1,0:T(8,128)(2,1)}, s32[384]{0:T(512)S(1)}, /*index=5*/s32[192]{0:T(256)S(1)}, f32[1,6144]{1,0:T(1,128)}, bf16[96,128,128]{2,1,0:T(8,128)(2,1)}, ...), branch_computations={%region_4.4_spmd, %region_5.5_spmd} | conditional | flops 196612 | bytes 1179707 | solution.py:206
  307.1 1.2 bitcast_select_fusion.x_ref
  308.2 10.9 %branch_1_fun.3 = bf16[32,6144]{1,0:T(8,128)(2,1)} custom-call(s32[384]{0:T(512)S(1)} %get-tuple-element.287.up_idx, s32[192]{0:T(256)S(1)} %get-tuple-element.288.dn_idx, bf16[32,6144]{1,0:T(8,128)(2,1)S(1)} %bitcast_select_fusion.x_ref, f32[1,6144]{1,0:T(1,128)} %get-tuple-element.293.g_ref, bf16[96,128,128]{2,1,0:T(8,128)(2,1)} %get-tuple-element.294.wu_hbm, ...), custom_call_target="tpu_custom_call" | custom-call | tf_op jit(solution)/shard_map/while/body/eval_jaxpr/cond/branch_1_fun/pallas_call | solution.py:139
  319.2 1.3 collective-permute-start
  321.5 1.8 bitcast_dynamic-update-slice_fusion.2
  323.4 7.9 %collective-permute-done = bf16[32,6144]{1,0:T(8,128)(2,1)} collective-permute-done((bf16[32,6144]{1,0:T(8,128)(2,1)}, bf16[32,6144]{1,0:T(8,128)(2,1)}, u32[]{:S(2)}, u32[]{:S(2)}) %collective-permute-start) | collective-permute-done | bytes 393248 | tf_op jit(solution)/shard_map/while/body/eval_jaxpr/ppermute | solution.py:21
  331.3 12.1 %conditional.2 = (bf16[32,6144]{1,0:T(8,128)(2,1)}) conditional(s32[]{:T(128)} %convert_element_type.14, () %tuple.48, (pred[]{:T(512)}, s32[]{:T(128)}, bf16[4,32,6144]{2,1,0:T(8,128)(2,1)}, bf16[32,6144]{1,0:T(8,128)(2,1)}, s32[384]{0:T(512)S(1)}, /*index=5*/s32[192]{0:T(256)S(1)}, f32[1,6144]{1,0:T(1,128)}, bf16[96,128,128]{2,1,0:T(8,128)(2,1)}, ...), branch_computations={%region_4.4_spmd, %region_5.5_spmd} | conditional | flops 196612 | bytes 1179707 | solution.py:206
  331.3 1.2 bitcast_select_fusion.x_ref
  332.5 10.9 %branch_1_fun.3 = bf16[32,6144]{1,0:T(8,128)(2,1)} custom-call(s32[384]{0:T(512)S(1)} %get-tuple-element.287.up_idx, s32[192]{0:T(256)S(1)} %get-tuple-element.288.dn_idx, bf16[32,6144]{1,0:T(8,128)(2,1)S(1)} %bitcast_select_fusion.x_ref, f32[1,6144]{1,0:T(1,128)} %get-tuple-element.293.g_ref, bf16[96,128,128]{2,1,0:T(8,128)(2,1)} %get-tuple-element.294.wu_hbm, ...), custom_call_target="tpu_custom_call" | custom-call | tf_op jit(solution)/shard_map/while/body/eval_jaxpr/cond/branch_1_fun/pallas_call | solution.py:139
  343.4 1.3 collective-permute-start
  345.7 1.8 bitcast_dynamic-update-slice_fusion.2
  347.6 5.8 %collective-permute-done = bf16[32,6144]{1,0:T(8,128)(2,1)} collective-permute-done((bf16[32,6144]{1,0:T(8,128)(2,1)}, bf16[32,6144]{1,0:T(8,128)(2,1)}, u32[]{:S(2)}, u32[]{:S(2)}) %collective-permute-start) | collective-permute-done | bytes 393248 | tf_op jit(solution)/shard_map/while/body/eval_jaxpr/ppermute | solution.py:21
  353.4 4.5 %scatter_fusion = bf16[160,6144]{1,0:T(8,128)(2,1)S(1)} fusion(bf16[160,6144]{1,0:T(8,128)(2,1)S(1)} %copy.46, s32[128]{0:T(128)S(1)} %compare_select_fusion.3, bf16[128,6144]{1,0:T(8,128)(2,1)} %bitcast.35), kind=kCustom, calls=%fused_computation.3 | custom fusion | bytes 4719104 | tf_op jit(solution)/shard_map/scatter | solution.py:222
  357.9 1.3 copy-done
  (72 shorter events, 25.6 us)
Async XLA Ops:
  6.5 1.6 copy-start.2
  6.5 2.0 copy-start.3
  6.5 71.0 %all-gather.2.cloned.1.call-start = ((), (), s32[]{:S(2)}) async-start(), calls=%async_computation | async-start | bytes 5013504 | tf_op jit(solution)/shard_map/all_gather | solution.py:42
  8.1 25.1 %copy-start.4 = (s32[160]{0:T(256)S(1)}, s32[160]{0:T(256)}, u32[]{:S(2)}) copy-start(s32[160]{0:T(256)} %param.12) | copy-start | bytes 1924
  8.6 16.8 %collective-permute-start.3 = (bf16[288,128]{1,0:T(8,128)(2,1)S(1)}, bf16[288,128]{1,0:T(8,128)(2,1)S(1)}, u32[]{:S(2)}, u32[]{:S(2)}) collective-permute-start(bf16[288,128]{1,0:T(8,128)(2,1)S(1)} %constant_dynamic-update-slice_fusion), channel_id=1, source_target_pairs={{0,48},{16,0},{32,16},{48,32},{1,49},{17,1},{33,17},{49,33},{2,50}... | collective-permute-start | bytes 221192 | tf_op jit(solution)/shard_map/ppermute | solution.py:29
  18.6 12.5 %collective-permute-start.1 = (bf16[288,128]{1,0:T(8,128)(2,1)S(1)}, bf16[288,128]{1,0:T(8,128)(2,1)S(1)}, u32[]{:S(2)}, u32[]{:S(2)}) collective-permute-start(bf16[288,128]{1,0:T(8,128)(2,1)S(1)} %constant_dynamic-update-slice_fusion), channel_id=1, source_target_pairs={{0,16},{16,32},{32,48},{48,0},{1,17},{17,33},{33,49},{49,1},{2,18}... | collective-permute-start | bytes 221192 | tf_op jit(solution)/shard_map/ppermute | solution.py:29
  20.5 11.2 %collective-permute-start.2 = (bf16[288,128]{1,0:T(8,128)(2,1)S(1)}, bf16[288,128]{1,0:T(8,128)(2,1)S(1)}, u32[]{:S(2)}, u32[]{:S(2)}) collective-permute-start(bf16[288,128]{1,0:T(8,128)(2,1)S(1)} %constant_dynamic-update-slice_fusion), channel_id=1, source_target_pairs={{0,32},{16,48},{32,0},{48,16},{1,33},{17,49},{33,1},{49,17},{2,34}... | collective-permute-start | bytes 221192 | tf_op jit(solution)/shard_map/ppermute | solution.py:29
  36.5 2.0 copy-start.1
  37.3 1.2 copy-start.5
  37.3 1.4 copy-start.6
  77.5 1.4 slice-start
  95.5 1.9 slice-start.1
  100.1 13.4 %collective-permute-start = (bf16[32,6144]{1,0:T(8,128)(2,1)}, bf16[32,6144]{1,0:T(8,128)(2,1)}, u32[]{:S(2)}, u32[]{:S(2)}) collective-permute-start(bf16[32,6144]{1,0:T(8,128)(2,1)} %get-tuple-element.477), channel_id=1, source_target_pairs={{0,64},{64,128},{128,192},{192,256},{256,320},{320,384},{384,448},... | collective-permute-start | bytes 1179656 | tf_op jit(solution)/shard_map/while/body/eval_jaxpr/ppermute | solution.py:21
  114.3 12.6 %collective-permute-start = (bf16[32,6144]{1,0:T(8,128)(2,1)}, bf16[32,6144]{1,0:T(8,128)(2,1)}, u32[]{:S(2)}, u32[]{:S(2)}) collective-permute-start(bf16[32,6144]{1,0:T(8,128)(2,1)} %get-tuple-element.477), channel_id=1, source_target_pairs={{0,64},{64,128},{128,192},{192,256},{256,320},{320,384},{384,448},... | collective-permute-start | bytes 1179656 | tf_op jit(solution)/shard_map/while/body/eval_jaxpr/ppermute | solution.py:21
  127.7 11.7 %collective-permute-start = (bf16[32,6144]{1,0:T(8,128)(2,1)}, bf16[32,6144]{1,0:T(8,128)(2,1)}, u32[]{:S(2)}, u32[]{:S(2)}) collective-permute-start(bf16[32,6144]{1,0:T(8,128)(2,1)} %get-tuple-element.477), channel_id=1, source_target_pairs={{0,64},{64,128},{128,192},{192,256},{256,320},{320,384},{384,448},... | collective-permute-start | bytes 1179656 | tf_op jit(solution)/shard_map/while/body/eval_jaxpr/ppermute | solution.py:21
  140.2 10.9 %collective-permute-start = (bf16[32,6144]{1,0:T(8,128)(2,1)}, bf16[32,6144]{1,0:T(8,128)(2,1)}, u32[]{:S(2)}, u32[]{:S(2)}) collective-permute-start(bf16[32,6144]{1,0:T(8,128)(2,1)} %get-tuple-element.477), channel_id=1, source_target_pairs={{0,64},{64,128},{128,192},{192,256},{256,320},{320,384},{384,448},... | collective-permute-start | bytes 1179656 | tf_op jit(solution)/shard_map/while/body/eval_jaxpr/ppermute | solution.py:21
  151.9 11.8 %collective-permute-start = (bf16[32,6144]{1,0:T(8,128)(2,1)}, bf16[32,6144]{1,0:T(8,128)(2,1)}, u32[]{:S(2)}, u32[]{:S(2)}) collective-permute-start(bf16[32,6144]{1,0:T(8,128)(2,1)} %get-tuple-element.477), channel_id=1, source_target_pairs={{0,64},{64,128},{128,192},{192,256},{256,320},{320,384},{384,448},... | collective-permute-start | bytes 1179656 | tf_op jit(solution)/shard_map/while/body/eval_jaxpr/ppermute | solution.py:21
  164.5 11.3 %collective-permute-start = (bf16[32,6144]{1,0:T(8,128)(2,1)}, bf16[32,6144]{1,0:T(8,128)(2,1)}, u32[]{:S(2)}, u32[]{:S(2)}) collective-permute-start(bf16[32,6144]{1,0:T(8,128)(2,1)} %get-tuple-element.477), channel_id=1, source_target_pairs={{0,64},{64,128},{128,192},{192,256},{256,320},{320,384},{384,448},... | collective-permute-start | bytes 1179656 | tf_op jit(solution)/shard_map/while/body/eval_jaxpr/ppermute | solution.py:21
  176.5 83.3 %collective-permute-start = (bf16[32,6144]{1,0:T(8,128)(2,1)}, bf16[32,6144]{1,0:T(8,128)(2,1)}, u32[]{:S(2)}, u32[]{:S(2)}) collective-permute-start(bf16[32,6144]{1,0:T(8,128)(2,1)} %get-tuple-element.477), channel_id=1, source_target_pairs={{0,64},{64,128},{128,192},{192,256},{256,320},{320,384},{384,448},... | collective-permute-start | bytes 1179656 | tf_op jit(solution)/shard_map/while/body/eval_jaxpr/ppermute | solution.py:21
  271.9 11.3 %collective-permute-start = (bf16[32,6144]{1,0:T(8,128)(2,1)}, bf16[32,6144]{1,0:T(8,128)(2,1)}, u32[]{:S(2)}, u32[]{:S(2)}) collective-permute-start(bf16[32,6144]{1,0:T(8,128)(2,1)} %get-tuple-element.477), channel_id=1, source_target_pairs={{0,64},{64,128},{128,192},{192,256},{256,320},{320,384},{384,448},... | collective-permute-start | bytes 1179656 | tf_op jit(solution)/shard_map/while/body/eval_jaxpr/ppermute | solution.py:21
  295.3 11.8 %collective-permute-start = (bf16[32,6144]{1,0:T(8,128)(2,1)}, bf16[32,6144]{1,0:T(8,128)(2,1)}, u32[]{:S(2)}, u32[]{:S(2)}) collective-permute-start(bf16[32,6144]{1,0:T(8,128)(2,1)} %get-tuple-element.477), channel_id=1, source_target_pairs={{0,64},{64,128},{128,192},{192,256},{256,320},{320,384},{384,448},... | collective-permute-start | bytes 1179656 | tf_op jit(solution)/shard_map/while/body/eval_jaxpr/ppermute | solution.py:21
  319.2 12.1 %collective-permute-start = (bf16[32,6144]{1,0:T(8,128)(2,1)}, bf16[32,6144]{1,0:T(8,128)(2,1)}, u32[]{:S(2)}, u32[]{:S(2)}) collective-permute-start(bf16[32,6144]{1,0:T(8,128)(2,1)} %get-tuple-element.477), channel_id=1, source_target_pairs={{0,64},{64,128},{128,192},{192,256},{256,320},{320,384},{384,448},... | collective-permute-start | bytes 1179656 | tf_op jit(solution)/shard_map/while/body/eval_jaxpr/ppermute | solution.py:21
  343.4 10.0 %collective-permute-start = (bf16[32,6144]{1,0:T(8,128)(2,1)}, bf16[32,6144]{1,0:T(8,128)(2,1)}, u32[]{:S(2)}, u32[]{:S(2)}) collective-permute-start(bf16[32,6144]{1,0:T(8,128)(2,1)} %get-tuple-element.477), channel_id=1, source_target_pairs={{0,64},{64,128},{128,192},{192,256},{256,320},{320,384},{384,448},... | collective-permute-start | bytes 1179656 | tf_op jit(solution)/shard_map/while/body/eval_jaxpr/ppermute | solution.py:21
  357.9 1.3 copy-start
Sparse Core Ops, SparseCore 0:
  33.3 44.1 all-gather.1

commit v7 on v6

--- a/solution.py
+++ b/solution.py
@@ -68,8 +68,10 @@
 DOWN_CHUNKS = 2
 
 
-def _layer_kernel(up_idx, dn_idx, x_ref, g_ref, wu_hbm, wd_hbm, o_ref, sx_ref, sh_ref, wu_ref, wd_ref, sems):
-    count, width = x_ref.shape
+def _layer_kernel(up_idx, dn_idx, flags, xs_ref, xh_ref, g_ref, wu_hbm, wd_hbm, rec_hbm, o_ref, r_ref,
+                  sx_ref, sh_ref, wu_ref, wd_ref, sems):
+    del rec_hbm
+    count, width = xh_ref.shape
     pairs_in = width // LANE
     pairs_hid = wu_ref.shape[0]
     up_step = pairs_hid // UP_CHUNKS
@@ -83,7 +85,8 @@
         copies.append(pltpu.make_async_copy(wd_hbm.at[part], wd_ref.at[part], sems.at[UP_CHUNKS + k]))
     for copy in copies:
         copy.start()
-    x = x_ref[...].astype(jnp.float32)
+    first = jnp.full((count, width), flags[0], jnp.int32) == 1
+    x = jnp.where(first, xs_ref[...], xh_ref[...]).astype(jnp.float32)
     scale = lax.rsqrt(jnp.mean(x * x, axis=1, keepdims=True) + 1e-05)
     zero = jnp.zeros((count, LANE), jnp.bfloat16)
     prev = zero
@@ -125,30 +128,40 @@
         s0 = lax.dot_general(l0, w, NT, preferred_element_type=jnp.float32)
         s1 = lax.dot_general(l1, w, NT, preferred_element_type=jnp.float32)
         s = jnp.where(lane < BLK, s0, s1)
-        o_ref[:, cp * LANE:(cp + 1) * LANE] = (x[:, cp * LANE:(cp + 1) * LANE] + s).astype(jnp.bfloat16)
+        out = (x[:, cp * LANE:(cp + 1) * LANE] + s).astype(jnp.bfloat16)
+        o_ref[:, cp * LANE:(cp + 1) * LANE] = out
+        r_ref[:, cp * LANE:(cp + 1) * LANE] = out
 
 
 def as_pairs(wt):
     return wt.reshape(wt.shape[0] // 2, 2 * BLK, LANE)
 
 
-def layer(x, gain_row, up_idx, wu_p, dn_idx, wd_p):
-    count, width = x.shape
+def layer(flags, split, held, record, gain_row, up_idx, wu_p, dn_idx, wd_p):
+    count, width = held.shape
     pairs_in = width // LANE
     pairs_hid = wu_p.shape[0]
     return pl.pallas_call(
         _layer_kernel,
-        out_shape=jax.ShapeDtypeStruct((count, width), jnp.bfloat16),
+        out_shape=(
+            jax.ShapeDtypeStruct((count, width), jnp.bfloat16),
+            jax.ShapeDtypeStruct(record.shape, record.dtype),
+        ),
         grid_spec=pltpu.PrefetchScalarGridSpec(
-            num_scalar_prefetch=2,
+            num_scalar_prefetch=3,
             grid=(1,),
             in_specs=[
-                pl.BlockSpec((count, width), lambda i, u, d: (0, 0)),
-                pl.BlockSpec((1, width), lambda i, u, d: (0, 0)),
+                pl.BlockSpec((None, count, width), lambda i, u, d, f: (f[1], 0, 0)),
+                pl.BlockSpec((count, width), lambda i, u, d, f: (0, 0)),
+                pl.BlockSpec((1, width), lambda i, u, d, f: (0, 0)),
+                pl.BlockSpec(memory_space=pl.ANY),
                 pl.BlockSpec(memory_space=pl.ANY),
                 pl.BlockSpec(memory_space=pl.ANY),
             ],
-            out_specs=pl.BlockSpec((count, width), lambda i, u, d: (0, 0)),
+            out_specs=[
+                pl.BlockSpec((count, width), lambda i, u, d, f: (0, 0)),
+                pl.BlockSpec((None, count, width), lambda i, u, d, f: (f[2], 0, 0)),
+            ],
             scratch_shapes=[
                 pltpu.VMEM((2, pairs_in + 1, count, LANE), jnp.bfloat16),
                 pltpu.VMEM((2, pairs_hid + 1, count, LANE), jnp.bfloat16),
@@ -157,8 +170,9 @@
                 pltpu.SemaphoreType.DMA((UP_CHUNKS + DOWN_CHUNKS,)),
             ],
         ),
+        input_output_aliases={8: 1},
         compiler_params=pltpu.CompilerParams(vmem_limit_bytes=40 * 1024 * 1024),
-    )(up_idx, dn_idx, x, gain_row, wu_p, wd_p)
+    )(up_idx, dn_idx, flags, split, held, gain_row, wu_p, wd_p, record)
 
 
 def column_major_down(rows):
@@ -172,8 +186,8 @@
     up_pairs = as_pairs(up_cols)
     down_pairs = as_pairs(down_cols)
 
-    def apply(block):
-        return layer(block, gain_row, up_index, up_pairs, down_index, down_pairs)
+    def apply(flags, split, held, record):
+        return layer(flags, split, held, record, gain_row, up_index, up_pairs, down_index, down_pairs)
 
     return apply
 
@@ -201,14 +215,18 @@
 
     def advance(turn, held, record):
         offset = turn - section
-        entry = jnp.where(section == 0, split[jnp.minimum(turn, pieces - 1)], held)
         active = (offset >= 0) & (offset < pieces)
-        result = lax.cond(active, apply, jnp.zeros_like, entry)
-        slot = jnp.clip(offset, 0, pieces - 1)
-        current = lax.dynamic_index_in_dim(record, slot, 0, keepdims=False)
-        updated = jnp.where(active, result, current)
-        record = lax.dynamic_update_index_in_dim(record, updated, slot, 0)
-        return (result, record)
+        flags = jnp.stack(
+            [(section == 0).astype(jnp.int32), jnp.minimum(turn, pieces - 1), jnp.clip(offset, 0, pieces - 1)]
+        ).astype(jnp.int32)
+
+        def run(held, record):
+            return apply(flags, split, held, record)
+
+        def skip(held, record):
+            return held, record
+
+        return lax.cond(active, run, skip, held, record)
 
     def turn_step(turn, carry):
         held, record = carry

time: 368 us -> 392 us (1.065)
  waiting for transfers between devices: 205 us -> 236 us
  other arithmetic: 20.7 us -> 2.8 us
  local copies, waits for them, and re-layouts: 52.2 us -> 63.2 us
    ppermute x11, waiting for transfers between devices: 161 us -> 191 us  [from_behind(): lax.ppermute(value, axis, [(source, source + steps) for source in range(i...]
    while x0 -> x11, local copies, waits for them, and re-layouts: none -> 19.5 us
    dynamic_update_slice x11 -> x0, other arithmetic: 13.4 us -> none  [advance(): record = lax.dynamic_update_index_in_dim(record, updated, slot, 0)]
    dynamic_slice x11 -> x0, local copies, waits for them, and re-layouts: 11.3 us -> none  [advance(): current = lax.dynamic_index_in_dim(record, slot, 0, keepdims=False)]
    another operation x8 -> x1, local copies, waits for them, and re-layouts: 5.52 us -> 0.11 us
    select_n x4 -> x0, other arithmetic: 4.63 us -> none  [advance(): entry = jnp.where(section == 0, split[jnp.minimum(turn, pieces - 1)], held)]
    cond x0 -> x4, local copies, waits for them, and re-layouts: none -> 3.99 us
  transfers between devices with their start and end apart: 15 -> 15, of which waited for: 14 -> 14; matrix products, arithmetic and copies ran while one was open for 9% -> 2% of each run, Pallas kernels for 0% -> 0%
where the time goes in v7:
time: 392 us; the launch traced here: 391 us
  waiting for transfers between devices  236 us (60%)
  local copies, waits for them, and re-layouts  63.2 us (16%)
  Pallas kernels  44.3 us (11%)
  starting transfers between devices  30.9 us (8%)
  between operations  13.6 us (3%)
    ppermute x11, waiting for transfers between devices, from_behind(): lax.ppermute(value, axis, [(source, source + steps) for source in range(i...  191 us
    pallas_call x4, Pallas kernels, layer(): pl.pallas_call(_layer_kernel, out_shape=(jax.ShapeDtypeStruct((count, wid...  44.3 us
    all_gather x1, waiting for transfers between devices, gather_weights(): full = lax.all_gather(full[:, None], ('y', 'c'), axis=1, tiled=True)  38.3 us
    while x11, local copies, waits for them, and re-layouts  19.5 us
    ppermute x3, starting transfers between devices, exchange_zh(): lax.ppermute(part, 'zh', [(i, (i + shift) % count) for i in range(count)])  16.8 us
    while x2, local copies, waits for them, and re-layouts, per_device(): held, record = lax.fori_loop(0, turns, turn_step, (split[0], split))  14.5 us
    ppermute x11, starting transfers between devices, from_behind(): lax.ppermute(value, axis, [(source, source + steps) for source in range(i...  14.1 us
  transfers between devices with their start and end apart: 15, of which 14 were waited for; matrix products, arithmetic and copies ran while one was open for 2% of the time, Pallas kernels for 0%

profile of v7, /device:TPU:70, one launch (start us, length us, event | category | flops | bytes accessed | tf_op | source)
XLA Modules:
  0.0 390.5 jit_solution(8582321362455384071)
XLA Ops:
  6.5 1.6 copy.50
  8.6 10.0 %collective-permute-start.3 = (bf16[288,128]{1,0:T(8,128)(2,1)S(1)}, bf16[288,128]{1,0:T(8,128)(2,1)S(1)}, u32[]{:S(2)}, u32[]{:S(2)}) collective-permute-start(bf16[288,128]{1,0:T(8,128)(2,1)S(1)} %constant_dynamic-update-slice_fusion), channel_id=1, source_target_pairs={{0,48},{16,0},{32,16},{48,32},{1,49},{17,1},{33,17},{49,33},{2,50}... | collective-permute-start | bytes 221192 | tf_op jit(solution)/shard_map/ppermute | solution.py:29
  18.6 1.9 collective-permute-start.2
  20.6 4.8 %collective-permute-start.1 = (bf16[288,128]{1,0:T(8,128)(2,1)S(1)}, bf16[288,128]{1,0:T(8,128)(2,1)S(1)}, u32[]{:S(2)}, u32[]{:S(2)}) collective-permute-start(bf16[288,128]{1,0:T(8,128)(2,1)S(1)} %constant_dynamic-update-slice_fusion), channel_id=1, source_target_pairs={{0,16},{16,32},{32,48},{48,0},{1,17},{17,33},{33,49},{49,1},{2,18}... | collective-permute-start | bytes 221192 | tf_op jit(solution)/shard_map/ppermute | solution.py:29
  25.4 3.4 collective-permute-done.2
  28.8 2.5 collective-permute-done.1
  34.7 1.1 scatter_custom_fusion
  35.8 1.5 gather_fusion
  38.1 1.1 copy.40
  39.2 38.3 %all-gather.2.cloned.1.call-done = bf16[4,16,288,128]{3,2,0,1:T(8,128)(2,1)} async-done(((bf16[4,1,288,128]{3,2,0,1:T(8,128)(2,1)}), bf16[4,16,288,128]{3,2,0,1:T(8,128)(2,1)}) %all-gather.2.cloned.1.call-update) | async-done | bytes 4718608 | tf_op jit(solution)/shard_map/all_gather | solution.py:42
  77.5 1.9 slice-done
  79.4 1.9 copy.31
  81.3 1.4 slice-done.1
  82.7 1.3 copy.26
  84.0 5.1 %reshape_reshape.10 = bf16[96,2,64,64]{3,2,1,0:T(8,128)(2,1)} reshape(bf16[4,16,96,128]{3,2,1,0:T(8,128)(2,1)} %copy.26) | data formatting | bytes 3145728 | tf_op jit(solution)/shard_map/reshape;reshape | solution.py:180
  89.1 8.3 %copy.29 = bf16[96,64,2,64]{3,2,1,0:T(2,128)(2,1)} copy(bf16[96,64,2,64]{1,3,2,0:T(8,128)(2,1)} %bitcast.35) | data formatting | bytes 3145728 | tf_op jit(solution)/shard_map/while | solution.py:238
  97.4 6.3 %reshape.135 = bf16[48,128,128]{2,1,0:T(8,128)(2,1)} reshape(bf16[96,64,2,64]{3,2,1,0:T(2,128)(2,1)} %copy.29) | data formatting | bytes 3145728 | tf_op jit(solution)/shard_map/while | solution.py:238
  103.6 274.3 %while.16 = (s32[]{:T(128)}, bf16[32,6144]{1,0:T(8,128)(2,1)}, bf16[4,32,6144]{2,1,0:T(8,128)(2,1)}, s32[]{:T(128)}, pred[]{:T(512)}, /*index=5*/s32[384]{0:T(51...) while((s32[]{:T(128)}, bf16[32,6144]{1,0:T(8,128)(2,1)}, ...), condition=%wide.region_6.7_spmd, body=%wide.region_3.6_spmd.sunk | while | flops 17 | bytes 3146108 | solution.py:238
  103.7 1.3 collective-permute-start
  105.0 12.2 %collective-permute-done = bf16[32,6144]{1,0:T(8,128)(2,1)} collective-permute-done((bf16[32,6144]{1,0:T(8,128)(2,1)}, bf16[32,6144]{1,0:T(8,128)(2,1)}, u32[]{:S(2)}, u32[]{:S(2)}) %collective-permute-start) | collective-permute-done | bytes 393248 | tf_op jit(solution)/shard_map/while/body/eval_jaxpr/ppermute | solution.py:21
  117.2 1.8 copy.45
  119.0 1.3 collective-permute-start
  120.3 11.3 %collective-permute-done = bf16[32,6144]{1,0:T(8,128)(2,1)} collective-permute-done((bf16[32,6144]{1,0:T(8,128)(2,1)}, bf16[32,6144]{1,0:T(8,128)(2,1)}, u32[]{:S(2)}, u32[]{:S(2)}) %collective-permute-start) | collective-permute-done | bytes 393248 | tf_op jit(solution)/shard_map/while/body/eval_jaxpr/ppermute | solution.py:21
  131.6 1.8 copy.45
  133.4 1.3 collective-permute-start
  134.7 10.4 %collective-permute-done = bf16[32,6144]{1,0:T(8,128)(2,1)} collective-permute-done((bf16[32,6144]{1,0:T(8,128)(2,1)}, bf16[32,6144]{1,0:T(8,128)(2,1)}, u32[]{:S(2)}, u32[]{:S(2)}) %collective-permute-start) | collective-permute-done | bytes 393248 | tf_op jit(solution)/shard_map/while/body/eval_jaxpr/ppermute | solution.py:21
  145.2 1.8 copy.45
  147.0 1.3 collective-permute-start
  148.3 9.6 %collective-permute-done = bf16[32,6144]{1,0:T(8,128)(2,1)} collective-permute-done((bf16[32,6144]{1,0:T(8,128)(2,1)}, bf16[32,6144]{1,0:T(8,128)(2,1)}, u32[]{:S(2)}, u32[]{:S(2)}) %collective-permute-start) | collective-permute-done | bytes 393248 | tf_op jit(solution)/shard_map/while/body/eval_jaxpr/ppermute | solution.py:21
  157.9 1.8 copy.45
  159.8 1.3 collective-permute-start
  161.0 10.6 %collective-permute-done = bf16[32,6144]{1,0:T(8,128)(2,1)} collective-permute-done((bf16[32,6144]{1,0:T(8,128)(2,1)}, bf16[32,6144]{1,0:T(8,128)(2,1)}, u32[]{:S(2)}, u32[]{:S(2)}) %collective-permute-start) | collective-permute-done | bytes 393248 | tf_op jit(solution)/shard_map/while/body/eval_jaxpr/ppermute | solution.py:21
  171.6 1.8 copy.45
  173.5 1.3 collective-permute-start
  174.7 10.0 %collective-permute-done = bf16[32,6144]{1,0:T(8,128)(2,1)} collective-permute-done((bf16[32,6144]{1,0:T(8,128)(2,1)}, bf16[32,6144]{1,0:T(8,128)(2,1)}, u32[]{:S(2)}, u32[]{:S(2)}) %collective-permute-start) | collective-permute-done | bytes 393248 | tf_op jit(solution)/shard_map/while/body/eval_jaxpr/ppermute | solution.py:21
  184.7 1.8 copy.45
  186.6 1.3 collective-permute-start
  187.9 87.3 %collective-permute-done = bf16[32,6144]{1,0:T(8,128)(2,1)} collective-permute-done((bf16[32,6144]{1,0:T(8,128)(2,1)}, bf16[32,6144]{1,0:T(8,128)(2,1)}, u32[]{:S(2)}, u32[]{:S(2)}) %collective-permute-start) | collective-permute-done | bytes 393248 | tf_op jit(solution)/shard_map/while/body/eval_jaxpr/ppermute | solution.py:21
  275.2 1.8 copy.45
  277.1 12.1 %conditional.2 = ((bf16[32,6144]{1,0:T(8,128)(2,1)}, bf16[4,32,6144]{2,1,0:T(8,128)(2,1)})) conditional(s32[]{:T(128)} %convert_element_type.20, (bf16[32,6144]{1,0:T(8,128)(2,1)}, bf16[4,32,6144]{2,1,0:T(8,128)(2,1)}) %tuple.43, (s32[384]{0:T(512)S(1)}, s32[192]{0:T(256)S(1)}, s32[3]{0:T(128)S(1)}, bf16[4,32,6144]{2,1,0:T(8,128)(2,1)S(1)}, ...), branch_computations={%region_4.4_spmd, %region_5.5_spmd} | conditional | bytes 786440 | solution.py:229
  277.1 1.0 copy.48.xh_ref
  278.1 11.1 %branch_1_fun.1 = (bf16[32,6144]{1,0:T(8,128)(2,1)}, bf16[4,32,6144]{2,1,0:T(8,128)(2,1)}) custom-call(s32[384]{0:T(512)S(1)} %get-tuple-element.231.up_idx, s32[192]{0:T(256)S(1)} %get-tuple-element.232.dn_idx, s32[3]{0:T(128)S(1)} %get-tuple-element.233.flags, bf16[4,32,6144]{2,1,0:T(8,128)(2,1)S(1)} %get-tuple-element.234.xs_ref, ...), custom_call_target="tpu_custom_call", output_to_operand_aliasing={{1}: (8, {})} | custom-call | tf_op jit(solution)/shard_map/while/body/eval_jaxpr/cond/branch_1_fun/pallas_call | solution.py:144
  289.2 1.3 collective-permute-start
  290.5 10.0 %collective-permute-done = bf16[32,6144]{1,0:T(8,128)(2,1)} collective-permute-done((bf16[32,6144]{1,0:T(8,128)(2,1)}, bf16[32,6144]{1,0:T(8,128)(2,1)}, u32[]{:S(2)}, u32[]{:S(2)}) %collective-permute-start) | collective-permute-done | bytes 393248 | tf_op jit(solution)/shard_map/while/body/eval_jaxpr/ppermute | solution.py:21
  300.4 1.8 copy.45
  302.3 12.1 %conditional.2 = ((bf16[32,6144]{1,0:T(8,128)(2,1)}, bf16[4,32,6144]{2,1,0:T(8,128)(2,1)})) conditional(s32[]{:T(128)} %convert_element_type.20, (bf16[32,6144]{1,0:T(8,128)(2,1)}, bf16[4,32,6144]{2,1,0:T(8,128)(2,1)}) %tuple.43, (s32[384]{0:T(512)S(1)}, s32[192]{0:T(256)S(1)}, s32[3]{0:T(128)S(1)}, bf16[4,32,6144]{2,1,0:T(8,128)(2,1)S(1)}, ...), branch_computations={%region_4.4_spmd, %region_5.5_spmd} | conditional | bytes 786440 | solution.py:229
  302.3 1.0 copy.48.xh_ref
  303.3 11.1 %branch_1_fun.1 = (bf16[32,6144]{1,0:T(8,128)(2,1)}, bf16[4,32,6144]{2,1,0:T(8,128)(2,1)}) custom-call(s32[384]{0:T(512)S(1)} %get-tuple-element.231.up_idx, s32[192]{0:T(256)S(1)} %get-tuple-element.232.dn_idx, s32[3]{0:T(128)S(1)} %get-tuple-element.233.flags, bf16[4,32,6144]{2,1,0:T(8,128)(2,1)S(1)} %get-tuple-element.234.xs_ref, ...), custom_call_target="tpu_custom_call", output_to_operand_aliasing={{1}: (8, {})} | custom-call | tf_op jit(solution)/shard_map/while/body/eval_jaxpr/cond/branch_1_fun/pallas_call | solution.py:144
  314.4 1.3 collective-permute-start
  315.7 10.5 %collective-permute-done = bf16[32,6144]{1,0:T(8,128)(2,1)} collective-permute-done((bf16[32,6144]{1,0:T(8,128)(2,1)}, bf16[32,6144]{1,0:T(8,128)(2,1)}, u32[]{:S(2)}, u32[]{:S(2)}) %collective-permute-start) | collective-permute-done | bytes 393248 | tf_op jit(solution)/shard_map/while/body/eval_jaxpr/ppermute | solution.py:21
  326.2 1.8 copy.45
  328.0 12.1 %conditional.2 = ((bf16[32,6144]{1,0:T(8,128)(2,1)}, bf16[4,32,6144]{2,1,0:T(8,128)(2,1)})) conditional(s32[]{:T(128)} %convert_element_type.20, (bf16[32,6144]{1,0:T(8,128)(2,1)}, bf16[4,32,6144]{2,1,0:T(8,128)(2,1)}) %tuple.43, (s32[384]{0:T(512)S(1)}, s32[192]{0:T(256)S(1)}, s32[3]{0:T(128)S(1)}, bf16[4,32,6144]{2,1,0:T(8,128)(2,1)S(1)}, ...), branch_computations={%region_4.4_spmd, %region_5.5_spmd} | conditional | bytes 786440 | solution.py:229
  328.0 1.0 copy.48.xh_ref
  329.0 11.1 %branch_1_fun.1 = (bf16[32,6144]{1,0:T(8,128)(2,1)}, bf16[4,32,6144]{2,1,0:T(8,128)(2,1)}) custom-call(s32[384]{0:T(512)S(1)} %get-tuple-element.231.up_idx, s32[192]{0:T(256)S(1)} %get-tuple-element.232.dn_idx, s32[3]{0:T(128)S(1)} %get-tuple-element.233.flags, bf16[4,32,6144]{2,1,0:T(8,128)(2,1)S(1)} %get-tuple-element.234.xs_ref, ...), custom_call_target="tpu_custom_call", output_to_operand_aliasing={{1}: (8, {})} | custom-call | tf_op jit(solution)/shard_map/while/body/eval_jaxpr/cond/branch_1_fun/pallas_call | solution.py:144
  340.1 1.3 collective-permute-start
  341.4 10.8 %collective-permute-done = bf16[32,6144]{1,0:T(8,128)(2,1)} collective-permute-done((bf16[32,6144]{1,0:T(8,128)(2,1)}, bf16[32,6144]{1,0:T(8,128)(2,1)}, u32[]{:S(2)}, u32[]{:S(2)}) %collective-permute-start) | collective-permute-done | bytes 393248 | tf_op jit(solution)/shard_map/while/body/eval_jaxpr/ppermute | solution.py:21
  352.2 1.8 copy.45
  354.0 12.1 %conditional.2 = ((bf16[32,6144]{1,0:T(8,128)(2,1)}, bf16[4,32,6144]{2,1,0:T(8,128)(2,1)})) conditional(s32[]{:T(128)} %convert_element_type.20, (bf16[32,6144]{1,0:T(8,128)(2,1)}, bf16[4,32,6144]{2,1,0:T(8,128)(2,1)}) %tuple.43, (s32[384]{0:T(512)S(1)}, s32[192]{0:T(256)S(1)}, s32[3]{0:T(128)S(1)}, bf16[4,32,6144]{2,1,0:T(8,128)(2,1)S(1)}, ...), branch_computations={%region_4.4_spmd, %region_5.5_spmd} | conditional | bytes 786440 | solution.py:229
  355.0 11.1 %branch_1_fun.1 = (bf16[32,6144]{1,0:T(8,128)(2,1)}, bf16[4,32,6144]{2,1,0:T(8,128)(2,1)}) custom-call(s32[384]{0:T(512)S(1)} %get-tuple-element.231.up_idx, s32[192]{0:T(256)S(1)} %get-tuple-element.232.dn_idx, s32[3]{0:T(128)S(1)} %get-tuple-element.233.flags, bf16[4,32,6144]{2,1,0:T(8,128)(2,1)S(1)} %get-tuple-element.234.xs_ref, ...), custom_call_target="tpu_custom_call", output_to_operand_aliasing={{1}: (8, {})} | custom-call | tf_op jit(solution)/shard_map/while/body/eval_jaxpr/cond/branch_1_fun/pallas_call | solution.py:144
  366.1 1.3 collective-permute-start
  367.4 8.7 %collective-permute-done = bf16[32,6144]{1,0:T(8,128)(2,1)} collective-permute-done((bf16[32,6144]{1,0:T(8,128)(2,1)}, bf16[32,6144]{1,0:T(8,128)(2,1)}, u32[]{:S(2)}, u32[]{:S(2)}) %collective-permute-start) | collective-permute-done | bytes 393248 | tf_op jit(solution)/shard_map/while/body/eval_jaxpr/ppermute | solution.py:21
  376.1 1.8 copy.45
  377.9 4.5 %scatter_fusion = bf16[160,6144]{1,0:T(8,128)(2,1)S(1)} fusion(bf16[160,6144]{1,0:T(8,128)(2,1)S(1)} %copy.50, s32[128]{0:T(128)S(1)} %compare_select_fusion.3, bf16[128,6144]{1,0:T(8,128)(2,1)} %bitcast.34), kind=kCustom, calls=%fused_computation.3 | custom fusion | bytes 4719104 | tf_op jit(solution)/shard_map/scatter | solution.py:240
  382.4 1.3 copy-done
  (65 shorter events, 6.3 us)
Async XLA Ops:
  6.5 1.6 copy-start.2
  6.5 1.7 copy-start.1
  6.5 70.9 %all-gather.2.cloned.1.call-start = ((), (), s32[]{:S(2)}) async-start(), calls=%async_computation | async-start | bytes 5013504 | tf_op jit(solution)/shard_map/all_gather | solution.py:42
  8.1 24.7 %copy-start.4 = (s32[160]{0:T(256)S(1)}, s32[160]{0:T(256)}, u32[]{:S(2)}) copy-start(s32[160]{0:T(256)} %param.12) | copy-start | bytes 1924
  8.1 25.2 %copy-start.3 = (bf16[1,6144]{1,0:T(2,128)(2,1)S(1)}, bf16[1,6144]{1,0:T(2,128)(2,1)}, u32[]{:S(2)}) copy-start(bf16[1,6144]{1,0:T(2,128)(2,1)} %param.13) | copy-start | bytes 36868
  8.1 25.8 %copy-start.6 = (s32[1,96,2]{1,2,0:T(2,128)S(1)}, s32[1,96,2]{1,2,0:T(2,128)}, u32[]{:S(2)}) copy-start(s32[1,96,2]{1,2,0:T(2,128)} %param.16) | copy-start | bytes 2308
  8.1 26.0 %copy-start.5 = (s32[1,192,2]{1,2,0:T(2,128)S(1)}, s32[1,192,2]{1,2,0:T(2,128)}, u32[]{:S(2)}) copy-start(s32[1,192,2]{1,2,0:T(2,128)} %param.14) | copy-start | bytes 4612
  8.6 16.8 %collective-permute-start.3 = (bf16[288,128]{1,0:T(8,128)(2,1)S(1)}, bf16[288,128]{1,0:T(8,128)(2,1)S(1)}, u32[]{:S(2)}, u32[]{:S(2)}) collective-permute-start(bf16[288,128]{1,0:T(8,128)(2,1)S(1)} %constant_dynamic-update-slice_fusion), channel_id=1, source_target_pairs={{0,48},{16,0},{32,16},{48,32},{1,49},{17,1},{33,17},{49,33},{2,50}... | collective-permute-start | bytes 221192 | tf_op jit(solution)/shard_map/ppermute | solution.py:29
  18.6 10.2 %collective-permute-start.2 = (bf16[288,128]{1,0:T(8,128)(2,1)S(1)}, bf16[288,128]{1,0:T(8,128)(2,1)S(1)}, u32[]{:S(2)}, u32[]{:S(2)}) collective-permute-start(bf16[288,128]{1,0:T(8,128)(2,1)S(1)} %constant_dynamic-update-slice_fusion), channel_id=1, source_target_pairs={{0,32},{16,48},{32,0},{48,16},{1,33},{17,49},{33,1},{49,17},{2,34}... | collective-permute-start | bytes 221192 | tf_op jit(solution)/shard_map/ppermute | solution.py:29
  20.6 10.8 %collective-permute-start.1 = (bf16[288,128]{1,0:T(8,128)(2,1)S(1)}, bf16[288,128]{1,0:T(8,128)(2,1)S(1)}, u32[]{:S(2)}, u32[]{:S(2)}) collective-permute-start(bf16[288,128]{1,0:T(8,128)(2,1)S(1)} %constant_dynamic-update-slice_fusion), channel_id=1, source_target_pairs={{0,16},{16,32},{32,48},{48,0},{1,17},{17,33},{33,49},{49,1},{2,18}... | collective-permute-start | bytes 221192 | tf_op jit(solution)/shard_map/ppermute | solution.py:29
  77.5 1.9 slice-start
  81.3 1.4 slice-start.1
  103.7 13.5 %collective-permute-start = (bf16[32,6144]{1,0:T(8,128)(2,1)}, bf16[32,6144]{1,0:T(8,128)(2,1)}, u32[]{:S(2)}, u32[]{:S(2)}) collective-permute-start(bf16[32,6144]{1,0:T(8,128)(2,1)} %get-tuple-element.380), channel_id=1, source_target_pairs={{0,64},{64,128},{128,192},{192,256},{256,320},{320,384},{384,448},... | collective-permute-start | bytes 1179656 | tf_op jit(solution)/shard_map/while/body/eval_jaxpr/ppermute | solution.py:21
  119.0 12.6 %collective-permute-start = (bf16[32,6144]{1,0:T(8,128)(2,1)}, bf16[32,6144]{1,0:T(8,128)(2,1)}, u32[]{:S(2)}, u32[]{:S(2)}) collective-permute-start(bf16[32,6144]{1,0:T(8,128)(2,1)} %get-tuple-element.380), channel_id=1, source_target_pairs={{0,64},{64,128},{128,192},{192,256},{256,320},{320,384},{384,448},... | collective-permute-start | bytes 1179656 | tf_op jit(solution)/shard_map/while/body/eval_jaxpr/ppermute | solution.py:21
  133.4 11.7 %collective-permute-start = (bf16[32,6144]{1,0:T(8,128)(2,1)}, bf16[32,6144]{1,0:T(8,128)(2,1)}, u32[]{:S(2)}, u32[]{:S(2)}) collective-permute-start(bf16[32,6144]{1,0:T(8,128)(2,1)} %get-tuple-element.380), channel_id=1, source_target_pairs={{0,64},{64,128},{128,192},{192,256},{256,320},{320,384},{384,448},... | collective-permute-start | bytes 1179656 | tf_op jit(solution)/shard_map/while/body/eval_jaxpr/ppermute | solution.py:21
  147.0 10.9 %collective-permute-start = (bf16[32,6144]{1,0:T(8,128)(2,1)}, bf16[32,6144]{1,0:T(8,128)(2,1)}, u32[]{:S(2)}, u32[]{:S(2)}) collective-permute-start(bf16[32,6144]{1,0:T(8,128)(2,1)} %get-tuple-element.380), channel_id=1, source_target_pairs={{0,64},{64,128},{128,192},{192,256},{256,320},{320,384},{384,448},... | collective-permute-start | bytes 1179656 | tf_op jit(solution)/shard_map/while/body/eval_jaxpr/ppermute | solution.py:21
  159.8 11.8 %collective-permute-start = (bf16[32,6144]{1,0:T(8,128)(2,1)}, bf16[32,6144]{1,0:T(8,128)(2,1)}, u32[]{:S(2)}, u32[]{:S(2)}) collective-permute-start(bf16[32,6144]{1,0:T(8,128)(2,1)} %get-tuple-element.380), channel_id=1, source_target_pairs={{0,64},{64,128},{128,192},{192,256},{256,320},{320,384},{384,448},... | collective-permute-start | bytes 1179656 | tf_op jit(solution)/shard_map/while/body/eval_jaxpr/ppermute | solution.py:21
  173.5 11.3 %collective-permute-start = (bf16[32,6144]{1,0:T(8,128)(2,1)}, bf16[32,6144]{1,0:T(8,128)(2,1)}, u32[]{:S(2)}, u32[]{:S(2)}) collective-permute-start(bf16[32,6144]{1,0:T(8,128)(2,1)} %get-tuple-element.380), channel_id=1, source_target_pairs={{0,64},{64,128},{128,192},{192,256},{256,320},{320,384},{384,448},... | collective-permute-start | bytes 1179656 | tf_op jit(solution)/shard_map/while/body/eval_jaxpr/ppermute | solution.py:21
  186.6 88.6 %collective-permute-start = (bf16[32,6144]{1,0:T(8,128)(2,1)}, bf16[32,6144]{1,0:T(8,128)(2,1)}, u32[]{:S(2)}, u32[]{:S(2)}) collective-permute-start(bf16[32,6144]{1,0:T(8,128)(2,1)} %get-tuple-element.380), channel_id=1, source_target_pairs={{0,64},{64,128},{128,192},{192,256},{256,320},{320,384},{384,448},... | collective-permute-start | bytes 1179656 | tf_op jit(solution)/shard_map/while/body/eval_jaxpr/ppermute | solution.py:21
  289.2 11.3 %collective-permute-start = (bf16[32,6144]{1,0:T(8,128)(2,1)}, bf16[32,6144]{1,0:T(8,128)(2,1)}, u32[]{:S(2)}, u32[]{:S(2)}) collective-permute-start(bf16[32,6144]{1,0:T(8,128)(2,1)} %get-tuple-element.380), channel_id=1, source_target_pairs={{0,64},{64,128},{128,192},{192,256},{256,320},{320,384},{384,448},... | collective-permute-start | bytes 1179656 | tf_op jit(solution)/shard_map/while/body/eval_jaxpr/ppermute | solution.py:21
  314.4 11.8 %collective-permute-start = (bf16[32,6144]{1,0:T(8,128)(2,1)}, bf16[32,6144]{1,0:T(8,128)(2,1)}, u32[]{:S(2)}, u32[]{:S(2)}) collective-permute-start(bf16[32,6144]{1,0:T(8,128)(2,1)} %get-tuple-element.380), channel_id=1, source_target_pairs={{0,64},{64,128},{128,192},{192,256},{256,320},{320,384},{384,448},... | collective-permute-start | bytes 1179656 | tf_op jit(solution)/shard_map/while/body/eval_jaxpr/ppermute | solution.py:21
  340.1 12.1 %collective-permute-start = (bf16[32,6144]{1,0:T(8,128)(2,1)}, bf16[32,6144]{1,0:T(8,128)(2,1)}, u32[]{:S(2)}, u32[]{:S(2)}) collective-permute-start(bf16[32,6144]{1,0:T(8,128)(2,1)} %get-tuple-element.380), channel_id=1, source_target_pairs={{0,64},{64,128},{128,192},{192,256},{256,320},{320,384},{384,448},... | collective-permute-start | bytes 1179656 | tf_op jit(solution)/shard_map/while/body/eval_jaxpr/ppermute | solution.py:21
  366.1 10.0 %collective-permute-start = (bf16[32,6144]{1,0:T(8,128)(2,1)}, bf16[32,6144]{1,0:T(8,128)(2,1)}, u32[]{:S(2)}, u32[]{:S(2)}) collective-permute-start(bf16[32,6144]{1,0:T(8,128)(2,1)} %get-tuple-element.380), channel_id=1, source_target_pairs={{0,64},{64,128},{128,192},{192,256},{256,320},{320,384},{384,448},... | collective-permute-start | bytes 1179656 | tf_op jit(solution)/shard_map/while/body/eval_jaxpr/ppermute | solution.py:21
  382.4 1.3 copy-start
Sparse Core Ops, SparseCore 0:
  33.0 44.4 all-gather.1

commit v8 on v6

--- a/solution.py
+++ b/solution.py
@@ -36,13 +36,19 @@
     cols = up_shard.shape[1] // UP_DEPTH
     up_part = up_shard.reshape(cols, UP_DEPTH, BLK, BLK).transpose(0, 3, 1, 2)
     up_part = up_part.reshape(cols * BLK, UP_DEPTH * BLK)
-    down_part = down_shard.reshape(down_shard.shape[1] * 32, 128)
+    count = down_shard.shape[1]
+    blocks = down_shard.reshape(count, BLK, BLK).transpose(0, 2, 1)
+    zeros = jnp.zeros_like(blocks)
+    first = lax.axis_index(FS) * count + jnp.arange(count, dtype=jnp.int32)
+    odd = (first % DOWN_DEPTH == 1)[:, None, None]
+    placed = jnp.where(odd, jnp.concatenate([zeros, blocks], axis=2), jnp.concatenate([blocks, zeros], axis=2))
+    down_part = placed.reshape(count * BLK, DOWN_DEPTH * BLK)
     split = up_part.shape[0]
     full = exchange_zh(jnp.concatenate([up_part, down_part], axis=0))
     full = lax.all_gather(full[:, None], ("y", "c"), axis=1, tiled=True)
-    up_full = full[:, :, :split]
-    down_full = full[:, :, split:]
-    return up_full.reshape(-1, BLK, UP_DEPTH * BLK), down_full.reshape(-1, 4096)
+    up_full = full[:, :, :split].reshape(-1, BLK, UP_DEPTH * BLK)
+    down_full = full[:, :, split:].reshape(-1, DOWN_DEPTH, BLK, DOWN_DEPTH * BLK)
+    return up_full, down_full[:, 0] + down_full[:, 1]
 
 
 LANE = 128
@@ -161,12 +167,6 @@
     )(up_idx, dn_idx, x, gain_row, wu_p, wd_p)
 
 
-def column_major_down(rows):
-    cols = rows.shape[0] // DOWN_DEPTH
-    w = rows.reshape(cols, DOWN_DEPTH, BLK, BLK).transpose(0, 3, 1, 2)
-    return w.reshape(cols, BLK, DOWN_DEPTH * BLK)
-
-
 def make_layer(gain, up_index, up_cols, down_index, down_cols):
     gain_row = gain.astype(jnp.float32)[None, :]
     up_pairs = as_pairs(up_cols)
@@ -179,8 +179,7 @@
 
 
 def per_device(activations, keep, gains, up_rows, up_blocks, down_rows, down_blocks):
-    up_all, down_rows_all = gather_weights(up_blocks, down_blocks)
-    down_all = column_major_down(down_rows_all)
+    up_all, down_all = gather_weights(up_blocks, down_blocks)
     apply = make_layer(
         gains[0], up_rows[0].reshape(-1), up_all, down_rows[0].reshape(-1), down_all
     )

time: 368 us -> 357 us (0.970)
  local copies, waits for them, and re-layouts: 52.2 us -> 37.6 us
    while x2 -> x0, local copies, waits for them, and re-layouts: 13.6 us -> none  [per_device(): held, record = lax.fori_loop(0, turns, turn_step, (split[0], split))]
    all_gather x1, waiting for transfers between devices: 37.1 us -> 40.9 us  [gather_weights(): full = lax.all_gather(full[:, None], ('y', 'c'), axis=1, tiled=True)]
    another operation x9 -> x8, local copies, waits for them, and re-layouts: 8.4 us -> 5.46 us
where the time goes in v8:
time: 357 us; the launch traced here: 355 us
  waiting for transfers between devices  207 us (58%)
  Pallas kernels  43.7 us (12%)
  local copies, waits for them, and re-layouts  37.6 us (11%)
  starting transfers between devices  32.1 us (9%)
  other arithmetic  21 us (6%)
  between operations  13.6 us (4%)
    ppermute x11, waiting for transfers between devices, from_behind(): lax.ppermute(value, axis, [(source, source + steps) for source in range(i...  161 us
    pallas_call x4, Pallas kernels, layer(): pl.pallas_call(_layer_kernel, out_shape=jax.ShapeDtypeStruct((count, widt...  43.7 us
    all_gather x1, waiting for transfers between devices, gather_weights(): full = lax.all_gather(full[:, None], ('y', 'c'), axis=1, tiled=True)  40.9 us
    ppermute x3, starting transfers between devices, exchange_zh(): lax.ppermute(part, 'zh', [(i, (i + shift) % count) for i in range(count)])  18 us
    ppermute x11, starting transfers between devices, from_behind(): lax.ppermute(value, axis, [(source, source + steps) for source in range(i...  14.1 us
    dynamic_update_slice x11, other arithmetic, advance(): record = lax.dynamic_update_index_in_dim(record, updated, slot, 0)  13.4 us
    dynamic_slice x11, local copies, waits for them, and re-layouts, advance(): current = lax.dynamic_index_in_dim(record, slot, 0, keepdims=False)  11.3 us
  transfers between devices with their start and end apart: 15, of which 14 were waited for; matrix products, arithmetic and copies ran while one was open for 9% of the time, Pallas kernels for 0%

profile of v8, /device:TPU:70, one launch (start us, length us, event | category | flops | bytes accessed | tf_op | source)
XLA Modules:
  0.0 355.1 jit_solution(12462969608201238465)
XLA Ops:
  6.5 1.6 copy.40
  8.9 6.1 %collective-permute-start.1 = (bf16[384,128]{1,0:T(8,128)(2,1)S(1)}, bf16[384,128]{1,0:T(8,128)(2,1)S(1)}, u32[]{:S(2)}, u32[]{:S(2)}) collective-permute-start(bf16[384,128]{1,0:T(8,128)(2,1)S(1)} %get-tuple-element.335), channel_id=1, source_target_pairs={{0,16},{16,32},{32,48},{48,0},{1,17},{17,33},{33,49},{49,1},{2,18}... | collective-permute-start | bytes 294920 | tf_op jit(solution)/shard_map/ppermute | solution.py:29
  15.0 8.2 %collective-permute-start.2 = (bf16[384,128]{1,0:T(8,128)(2,1)S(1)}, bf16[384,128]{1,0:T(8,128)(2,1)S(1)}, u32[]{:S(2)}, u32[]{:S(2)}) collective-permute-start(bf16[384,128]{1,0:T(8,128)(2,1)S(1)} %get-tuple-element.335), channel_id=1, source_target_pairs={{0,32},{16,48},{32,0},{48,16},{1,33},{17,49},{33,1},{49,17},{2,34}... | collective-permute-start | bytes 294920 | tf_op jit(solution)/shard_map/ppermute | solution.py:29
  23.2 3.7 %collective-permute-start.3 = (bf16[384,128]{1,0:T(8,128)(2,1)S(1)}, bf16[384,128]{1,0:T(8,128)(2,1)S(1)}, u32[]{:S(2)}, u32[]{:S(2)}) collective-permute-start(bf16[384,128]{1,0:T(8,128)(2,1)S(1)} %get-tuple-element.335), channel_id=1, source_target_pairs={{0,48},{16,0},{32,16},{48,32},{1,49},{17,1},{33,17},{49,33},{2,50}... | collective-permute-start | bytes 294920 | tf_op jit(solution)/shard_map/ppermute | solution.py:29
  26.9 1.1 collective-permute-done.2
  28.0 3.5 collective-permute-done.3
  33.8 1.1 scatter_custom_fusion
  34.9 1.5 gather_fusion
  37.3 1.1 copy.31
  40.5 1.4 convert_element_type.12
  41.9 40.9 %all-gather.2.cloned.1.call-done = bf16[4,16,384,128]{3,2,0,1:T(8,128)(2,1)} async-done(((bf16[4,1,384,128]{3,2,0,1:T(8,128)(2,1)}), bf16[4,16,384,128]{3,2,0,1:T(8,128)(2,1)}) %all-gather.2.cloned.1.call-update) | async-done | bytes 6291472 | tf_op jit(solution)/shard_map/all_gather | solution.py:48
  82.8 3.4 fusion.8
  86.6 1.9 copy.24
  88.6 253.9 %while.16 = (s32[]{:T(128)}, bf16[32,6144]{1,0:T(8,128)(2,1)}, bf16[4,32,6144]{2,1,0:T(8,128)(2,1)}, s32[]{:T(128)}, pred[]{:T(512)}, /*index=5*/bf16[4,32,6144]...) while((s32[]{:T(128)}, bf16[32,6144]{1,0:T(8,128)(2,1)}, ...), condition=%wide.region_6.7_spmd, body=%wide.region_3.6_spmd.sunk | while | flops 393229 | bytes 4718975 | solution.py:219
  89.3 1.3 collective-permute-start
  90.6 1.0 constant_dynamic-slice_fusion.2
  92.5 10.3 %collective-permute-done = bf16[32,6144]{1,0:T(8,128)(2,1)} collective-permute-done((bf16[32,6144]{1,0:T(8,128)(2,1)}, bf16[32,6144]{1,0:T(8,128)(2,1)}, u32[]{:S(2)}, u32[]{:S(2)}) %collective-permute-start) | collective-permute-done | bytes 393248 | tf_op jit(solution)/shard_map/while/body/eval_jaxpr/ppermute | solution.py:21
  103.5 1.3 collective-permute-start
  104.8 1.0 constant_dynamic-slice_fusion.2
  106.7 9.4 %collective-permute-done = bf16[32,6144]{1,0:T(8,128)(2,1)} collective-permute-done((bf16[32,6144]{1,0:T(8,128)(2,1)}, bf16[32,6144]{1,0:T(8,128)(2,1)}, u32[]{:S(2)}, u32[]{:S(2)}) %collective-permute-start) | collective-permute-done | bytes 393248 | tf_op jit(solution)/shard_map/while/body/eval_jaxpr/ppermute | solution.py:21
  116.9 1.3 collective-permute-start
  118.2 1.0 constant_dynamic-slice_fusion.2
  120.1 8.6 %collective-permute-done = bf16[32,6144]{1,0:T(8,128)(2,1)} collective-permute-done((bf16[32,6144]{1,0:T(8,128)(2,1)}, bf16[32,6144]{1,0:T(8,128)(2,1)}, u32[]{:S(2)}, u32[]{:S(2)}) %collective-permute-start) | collective-permute-done | bytes 393248 | tf_op jit(solution)/shard_map/while/body/eval_jaxpr/ppermute | solution.py:21
  129.4 1.3 collective-permute-start
  132.6 7.7 %collective-permute-done = bf16[32,6144]{1,0:T(8,128)(2,1)} collective-permute-done((bf16[32,6144]{1,0:T(8,128)(2,1)}, bf16[32,6144]{1,0:T(8,128)(2,1)}, u32[]{:S(2)}, u32[]{:S(2)}) %collective-permute-start) | collective-permute-done | bytes 393248 | tf_op jit(solution)/shard_map/while/body/eval_jaxpr/ppermute | solution.py:21
  141.1 1.3 collective-permute-start
  142.3 1.0 constant_dynamic-slice_fusion.2
  144.2 8.7 %collective-permute-done = bf16[32,6144]{1,0:T(8,128)(2,1)} collective-permute-done((bf16[32,6144]{1,0:T(8,128)(2,1)}, bf16[32,6144]{1,0:T(8,128)(2,1)}, u32[]{:S(2)}, u32[]{:S(2)}) %collective-permute-start) | collective-permute-done | bytes 393248 | tf_op jit(solution)/shard_map/while/body/eval_jaxpr/ppermute | solution.py:21
  153.7 1.3 collective-permute-start
  155.0 1.0 constant_dynamic-slice_fusion.2
  156.8 8.1 %collective-permute-done = bf16[32,6144]{1,0:T(8,128)(2,1)} collective-permute-done((bf16[32,6144]{1,0:T(8,128)(2,1)}, bf16[32,6144]{1,0:T(8,128)(2,1)}, u32[]{:S(2)}, u32[]{:S(2)}) %collective-permute-start) | collective-permute-done | bytes 393248 | tf_op jit(solution)/shard_map/while/body/eval_jaxpr/ppermute | solution.py:21
  165.7 1.3 collective-permute-start
  167.0 1.0 constant_dynamic-slice_fusion.2
  168.9 80.0 %collective-permute-done = bf16[32,6144]{1,0:T(8,128)(2,1)} collective-permute-done((bf16[32,6144]{1,0:T(8,128)(2,1)}, bf16[32,6144]{1,0:T(8,128)(2,1)}, u32[]{:S(2)}, u32[]{:S(2)}) %collective-permute-start) | collective-permute-done | bytes 393248 | tf_op jit(solution)/shard_map/while/body/eval_jaxpr/ppermute | solution.py:21
  248.9 12.1 %conditional.2 = (bf16[32,6144]{1,0:T(8,128)(2,1)}) conditional(s32[]{:T(128)} %convert_element_type.14, () %tuple.47, (pred[]{:T(512)}, s32[]{:T(128)}, bf16[4,32,6144]{2,1,0:T(8,128)(2,1)}, bf16[32,6144]{1,0:T(8,128)(2,1)}, s32[384]{0:T(512)S(1)}, /*index=5*/s32[192]{0:T(256)S(1)}, f32[1,6144]{1,0:T(1,128)}, bf16[96,128,128]{2,1,0:T(8,128)(2,1)}, ...), branch_computations={%region_4.4_spmd, %region_5.5_spmd} | conditional | flops 196612 | bytes 1179707 | solution.py:205
  248.9 1.2 bitcast_select_fusion.x_ref
  250.1 10.9 %branch_1_fun.3 = bf16[32,6144]{1,0:T(8,128)(2,1)} custom-call(s32[384]{0:T(512)S(1)} %get-tuple-element.287.up_idx, s32[192]{0:T(256)S(1)} %get-tuple-element.288.dn_idx, bf16[32,6144]{1,0:T(8,128)(2,1)S(1)} %bitcast_select_fusion.x_ref, f32[1,6144]{1,0:T(1,128)} %get-tuple-element.293.g_ref, bf16[96,128,128]{2,1,0:T(8,128)(2,1)} %get-tuple-element.294.wu_hbm, ...), custom_call_target="tpu_custom_call" | custom-call | tf_op jit(solution)/shard_map/while/body/eval_jaxpr/cond/branch_1_fun/pallas_call | solution.py:145
  261.0 1.3 collective-permute-start
  262.3 1.0 constant_dynamic-slice_fusion.2
  263.4 1.8 bitcast_dynamic-update-slice_fusion.2
  265.2 7.1 %collective-permute-done = bf16[32,6144]{1,0:T(8,128)(2,1)} collective-permute-done((bf16[32,6144]{1,0:T(8,128)(2,1)}, bf16[32,6144]{1,0:T(8,128)(2,1)}, u32[]{:S(2)}, u32[]{:S(2)}) %collective-permute-start) | collective-permute-done | bytes 393248 | tf_op jit(solution)/shard_map/while/body/eval_jaxpr/ppermute | solution.py:21
  272.3 12.1 %conditional.2 = (bf16[32,6144]{1,0:T(8,128)(2,1)}) conditional(s32[]{:T(128)} %convert_element_type.14, () %tuple.47, (pred[]{:T(512)}, s32[]{:T(128)}, bf16[4,32,6144]{2,1,0:T(8,128)(2,1)}, bf16[32,6144]{1,0:T(8,128)(2,1)}, s32[384]{0:T(512)S(1)}, /*index=5*/s32[192]{0:T(256)S(1)}, f32[1,6144]{1,0:T(1,128)}, bf16[96,128,128]{2,1,0:T(8,128)(2,1)}, ...), branch_computations={%region_4.4_spmd, %region_5.5_spmd} | conditional | flops 196612 | bytes 1179707 | solution.py:205
  272.3 1.2 bitcast_select_fusion.x_ref
  273.5 10.9 %branch_1_fun.3 = bf16[32,6144]{1,0:T(8,128)(2,1)} custom-call(s32[384]{0:T(512)S(1)} %get-tuple-element.287.up_idx, s32[192]{0:T(256)S(1)} %get-tuple-element.288.dn_idx, bf16[32,6144]{1,0:T(8,128)(2,1)S(1)} %bitcast_select_fusion.x_ref, f32[1,6144]{1,0:T(1,128)} %get-tuple-element.293.g_ref, bf16[96,128,128]{2,1,0:T(8,128)(2,1)} %get-tuple-element.294.wu_hbm, ...), custom_call_target="tpu_custom_call" | custom-call | tf_op jit(solution)/shard_map/while/body/eval_jaxpr/cond/branch_1_fun/pallas_call | solution.py:145
  284.4 1.3 collective-permute-start
  285.7 1.0 constant_dynamic-slice_fusion.2
  286.7 1.8 bitcast_dynamic-update-slice_fusion.2
  288.6 7.6 %collective-permute-done = bf16[32,6144]{1,0:T(8,128)(2,1)} collective-permute-done((bf16[32,6144]{1,0:T(8,128)(2,1)}, bf16[32,6144]{1,0:T(8,128)(2,1)}, u32[]{:S(2)}, u32[]{:S(2)}) %collective-permute-start) | collective-permute-done | bytes 393248 | tf_op jit(solution)/shard_map/while/body/eval_jaxpr/ppermute | solution.py:21
  296.2 12.1 %conditional.2 = (bf16[32,6144]{1,0:T(8,128)(2,1)}) conditional(s32[]{:T(128)} %convert_element_type.14, () %tuple.47, (pred[]{:T(512)}, s32[]{:T(128)}, bf16[4,32,6144]{2,1,0:T(8,128)(2,1)}, bf16[32,6144]{1,0:T(8,128)(2,1)}, s32[384]{0:T(512)S(1)}, /*index=5*/s32[192]{0:T(256)S(1)}, f32[1,6144]{1,0:T(1,128)}, bf16[96,128,128]{2,1,0:T(8,128)(2,1)}, ...), branch_computations={%region_4.4_spmd, %region_5.5_spmd} | conditional | flops 196612 | bytes 1179707 | solution.py:205
  296.2 1.2 bitcast_select_fusion.x_ref
  297.4 10.9 %branch_1_fun.3 = bf16[32,6144]{1,0:T(8,128)(2,1)} custom-call(s32[384]{0:T(512)S(1)} %get-tuple-element.287.up_idx, s32[192]{0:T(256)S(1)} %get-tuple-element.288.dn_idx, bf16[32,6144]{1,0:T(8,128)(2,1)S(1)} %bitcast_select_fusion.x_ref, f32[1,6144]{1,0:T(1,128)} %get-tuple-element.293.g_ref, bf16[96,128,128]{2,1,0:T(8,128)(2,1)} %get-tuple-element.294.wu_hbm, ...), custom_call_target="tpu_custom_call" | custom-call | tf_op jit(solution)/shard_map/while/body/eval_jaxpr/cond/branch_1_fun/pallas_call | solution.py:145
  308.3 1.3 collective-permute-start
  309.6 1.0 constant_dynamic-slice_fusion.2
  310.6 1.8 bitcast_dynamic-update-slice_fusion.2
  312.5 7.9 %collective-permute-done = bf16[32,6144]{1,0:T(8,128)(2,1)} collective-permute-done((bf16[32,6144]{1,0:T(8,128)(2,1)}, bf16[32,6144]{1,0:T(8,128)(2,1)}, u32[]{:S(2)}, u32[]{:S(2)}) %collective-permute-start) | collective-permute-done | bytes 393248 | tf_op jit(solution)/shard_map/while/body/eval_jaxpr/ppermute | solution.py:21
  320.4 12.1 %conditional.2 = (bf16[32,6144]{1,0:T(8,128)(2,1)}) conditional(s32[]{:T(128)} %convert_element_type.14, () %tuple.47, (pred[]{:T(512)}, s32[]{:T(128)}, bf16[4,32,6144]{2,1,0:T(8,128)(2,1)}, bf16[32,6144]{1,0:T(8,128)(2,1)}, s32[384]{0:T(512)S(1)}, /*index=5*/s32[192]{0:T(256)S(1)}, f32[1,6144]{1,0:T(1,128)}, bf16[96,128,128]{2,1,0:T(8,128)(2,1)}, ...), branch_computations={%region_4.4_spmd, %region_5.5_spmd} | conditional | flops 196612 | bytes 1179707 | solution.py:205
  320.4 1.2 bitcast_select_fusion.x_ref
  321.6 10.9 %branch_1_fun.3 = bf16[32,6144]{1,0:T(8,128)(2,1)} custom-call(s32[384]{0:T(512)S(1)} %get-tuple-element.287.up_idx, s32[192]{0:T(256)S(1)} %get-tuple-element.288.dn_idx, bf16[32,6144]{1,0:T(8,128)(2,1)S(1)} %bitcast_select_fusion.x_ref, f32[1,6144]{1,0:T(1,128)} %get-tuple-element.293.g_ref, bf16[96,128,128]{2,1,0:T(8,128)(2,1)} %get-tuple-element.294.wu_hbm, ...), custom_call_target="tpu_custom_call" | custom-call | tf_op jit(solution)/shard_map/while/body/eval_jaxpr/cond/branch_1_fun/pallas_call | solution.py:145
  332.5 1.3 collective-permute-start
  333.8 1.0 constant_dynamic-slice_fusion.2
  334.8 1.8 bitcast_dynamic-update-slice_fusion.2
  336.7 5.8 %collective-permute-done = bf16[32,6144]{1,0:T(8,128)(2,1)} collective-permute-done((bf16[32,6144]{1,0:T(8,128)(2,1)}, bf16[32,6144]{1,0:T(8,128)(2,1)}, u32[]{:S(2)}, u32[]{:S(2)}) %collective-permute-start) | collective-permute-done | bytes 393248 | tf_op jit(solution)/shard_map/while/body/eval_jaxpr/ppermute | solution.py:21
  342.5 4.5 %scatter_fusion = bf16[160,6144]{1,0:T(8,128)(2,1)S(1)} fusion(bf16[160,6144]{1,0:T(8,128)(2,1)S(1)} %copy.40, s32[128]{0:T(128)S(1)} %compare_select_fusion.3, bf16[128,6144]{1,0:T(8,128)(2,1)} %bitcast.38), kind=kCustom, calls=%fused_computation.3 | custom fusion | bytes 4719104 | tf_op jit(solution)/shard_map/scatter | solution.py:221
  347.0 1.3 copy-done
  (69 shorter events, 23.9 us)
Async XLA Ops:
  6.5 1.9 copy-start.2
  6.5 1.6 copy-start.3
  6.5 76.2 %all-gather.2.cloned.1.call-start = ((), (), s32[]{:S(2)}) async-start(), calls=%async_computation | async-start | bytes 6684672 | tf_op jit(solution)/shard_map/all_gather | solution.py:48
  8.8 24.3 %copy-start.4 = (s32[160]{0:T(256)S(1)}, s32[160]{0:T(256)}, u32[]{:S(2)}) copy-start(s32[160]{0:T(256)} %param.12) | copy-start | bytes 1924
  8.9 18.0 %collective-permute-start.1 = (bf16[384,128]{1,0:T(8,128)(2,1)S(1)}, bf16[384,128]{1,0:T(8,128)(2,1)S(1)}, u32[]{:S(2)}, u32[]{:S(2)}) collective-permute-start(bf16[384,128]{1,0:T(8,128)(2,1)S(1)} %get-tuple-element.335), channel_id=1, source_target_pairs={{0,16},{16,32},{32,48},{48,0},{1,17},{17,33},{33,49},{49,1},{2,18}... | collective-permute-start | bytes 294920 | tf_op jit(solution)/shard_map/ppermute | solution.py:29
  15.0 13.0 %collective-permute-start.2 = (bf16[384,128]{1,0:T(8,128)(2,1)S(1)}, bf16[384,128]{1,0:T(8,128)(2,1)S(1)}, u32[]{:S(2)}, u32[]{:S(2)}) collective-permute-start(bf16[384,128]{1,0:T(8,128)(2,1)S(1)} %get-tuple-element.335), channel_id=1, source_target_pairs={{0,32},{16,48},{32,0},{48,16},{1,33},{17,49},{33,1},{49,17},{2,34}... | collective-permute-start | bytes 294920 | tf_op jit(solution)/shard_map/ppermute | solution.py:29
  23.2 8.4 %collective-permute-start.3 = (bf16[384,128]{1,0:T(8,128)(2,1)S(1)}, bf16[384,128]{1,0:T(8,128)(2,1)S(1)}, u32[]{:S(2)}, u32[]{:S(2)}) collective-permute-start(bf16[384,128]{1,0:T(8,128)(2,1)S(1)} %get-tuple-element.335), channel_id=1, source_target_pairs={{0,48},{16,0},{32,16},{48,32},{1,49},{17,1},{33,17},{49,33},{2,50}... | collective-permute-start | bytes 294920 | tf_op jit(solution)/shard_map/ppermute | solution.py:29
  36.4 2.0 copy-start.1
  37.3 1.2 copy-start.5
  37.3 3.0 copy-start.6
  89.3 13.5 %collective-permute-start = (bf16[32,6144]{1,0:T(8,128)(2,1)}, bf16[32,6144]{1,0:T(8,128)(2,1)}, u32[]{:S(2)}, u32[]{:S(2)}) collective-permute-start(bf16[32,6144]{1,0:T(8,128)(2,1)} %get-tuple-element.448), channel_id=1, source_target_pairs={{0,64},{64,128},{128,192},{192,256},{256,320},{320,384},{384,448},... | collective-permute-start | bytes 1179656 | tf_op jit(solution)/shard_map/while/body/eval_jaxpr/ppermute | solution.py:21
  103.5 12.6 %collective-permute-start = (bf16[32,6144]{1,0:T(8,128)(2,1)}, bf16[32,6144]{1,0:T(8,128)(2,1)}, u32[]{:S(2)}, u32[]{:S(2)}) collective-permute-start(bf16[32,6144]{1,0:T(8,128)(2,1)} %get-tuple-element.448), channel_id=1, source_target_pairs={{0,64},{64,128},{128,192},{192,256},{256,320},{320,384},{384,448},... | collective-permute-start | bytes 1179656 | tf_op jit(solution)/shard_map/while/body/eval_jaxpr/ppermute | solution.py:21
  116.9 11.7 %collective-permute-start = (bf16[32,6144]{1,0:T(8,128)(2,1)}, bf16[32,6144]{1,0:T(8,128)(2,1)}, u32[]{:S(2)}, u32[]{:S(2)}) collective-permute-start(bf16[32,6144]{1,0:T(8,128)(2,1)} %get-tuple-element.448), channel_id=1, source_target_pairs={{0,64},{64,128},{128,192},{192,256},{256,320},{320,384},{384,448},... | collective-permute-start | bytes 1179656 | tf_op jit(solution)/shard_map/while/body/eval_jaxpr/ppermute | solution.py:21
  129.4 10.9 %collective-permute-start = (bf16[32,6144]{1,0:T(8,128)(2,1)}, bf16[32,6144]{1,0:T(8,128)(2,1)}, u32[]{:S(2)}, u32[]{:S(2)}) collective-permute-start(bf16[32,6144]{1,0:T(8,128)(2,1)} %get-tuple-element.448), channel_id=1, source_target_pairs={{0,64},{64,128},{128,192},{192,256},{256,320},{320,384},{384,448},... | collective-permute-start | bytes 1179656 | tf_op jit(solution)/shard_map/while/body/eval_jaxpr/ppermute | solution.py:21
  141.1 11.8 %collective-permute-start = (bf16[32,6144]{1,0:T(8,128)(2,1)}, bf16[32,6144]{1,0:T(8,128)(2,1)}, u32[]{:S(2)}, u32[]{:S(2)}) collective-permute-start(bf16[32,6144]{1,0:T(8,128)(2,1)} %get-tuple-element.448), channel_id=1, source_target_pairs={{0,64},{64,128},{128,192},{192,256},{256,320},{320,384},{384,448},... | collective-permute-start | bytes 1179656 | tf_op jit(solution)/shard_map/while/body/eval_jaxpr/ppermute | solution.py:21
  153.7 11.3 %collective-permute-start = (bf16[32,6144]{1,0:T(8,128)(2,1)}, bf16[32,6144]{1,0:T(8,128)(2,1)}, u32[]{:S(2)}, u32[]{:S(2)}) collective-permute-start(bf16[32,6144]{1,0:T(8,128)(2,1)} %get-tuple-element.448), channel_id=1, source_target_pairs={{0,64},{64,128},{128,192},{192,256},{256,320},{320,384},{384,448},... | collective-permute-start | bytes 1179656 | tf_op jit(solution)/shard_map/while/body/eval_jaxpr/ppermute | solution.py:21
  165.7 83.2 %collective-permute-start = (bf16[32,6144]{1,0:T(8,128)(2,1)}, bf16[32,6144]{1,0:T(8,128)(2,1)}, u32[]{:S(2)}, u32[]{:S(2)}) collective-permute-start(bf16[32,6144]{1,0:T(8,128)(2,1)} %get-tuple-element.448), channel_id=1, source_target_pairs={{0,64},{64,128},{128,192},{192,256},{256,320},{320,384},{384,448},... | collective-permute-start | bytes 1179656 | tf_op jit(solution)/shard_map/while/body/eval_jaxpr/ppermute | solution.py:21
  261.0 11.3 %collective-permute-start = (bf16[32,6144]{1,0:T(8,128)(2,1)}, bf16[32,6144]{1,0:T(8,128)(2,1)}, u32[]{:S(2)}, u32[]{:S(2)}) collective-permute-start(bf16[32,6144]{1,0:T(8,128)(2,1)} %get-tuple-element.448), channel_id=1, source_target_pairs={{0,64},{64,128},{128,192},{192,256},{256,320},{320,384},{384,448},... | collective-permute-start | bytes 1179656 | tf_op jit(solution)/shard_map/while/body/eval_jaxpr/ppermute | solution.py:21
  284.4 11.8 %collective-permute-start = (bf16[32,6144]{1,0:T(8,128)(2,1)}, bf16[32,6144]{1,0:T(8,128)(2,1)}, u32[]{:S(2)}, u32[]{:S(2)}) collective-permute-start(bf16[32,6144]{1,0:T(8,128)(2,1)} %get-tuple-element.448), channel_id=1, source_target_pairs={{0,64},{64,128},{128,192},{192,256},{256,320},{320,384},{384,448},... | collective-permute-start | bytes 1179656 | tf_op jit(solution)/shard_map/while/body/eval_jaxpr/ppermute | solution.py:21
  308.3 12.1 %collective-permute-start = (bf16[32,6144]{1,0:T(8,128)(2,1)}, bf16[32,6144]{1,0:T(8,128)(2,1)}, u32[]{:S(2)}, u32[]{:S(2)}) collective-permute-start(bf16[32,6144]{1,0:T(8,128)(2,1)} %get-tuple-element.448), channel_id=1, source_target_pairs={{0,64},{64,128},{128,192},{192,256},{256,320},{320,384},{384,448},... | collective-permute-start | bytes 1179656 | tf_op jit(solution)/shard_map/while/body/eval_jaxpr/ppermute | solution.py:21
  332.5 10.0 %collective-permute-start = (bf16[32,6144]{1,0:T(8,128)(2,1)}, bf16[32,6144]{1,0:T(8,128)(2,1)}, u32[]{:S(2)}, u32[]{:S(2)}) collective-permute-start(bf16[32,6144]{1,0:T(8,128)(2,1)} %get-tuple-element.448), channel_id=1, source_target_pairs={{0,64},{64,128},{128,192},{192,256},{256,320},{320,384},{384,448},... | collective-permute-start | bytes 1179656 | tf_op jit(solution)/shard_map/while/body/eval_jaxpr/ppermute | solution.py:21
  347.0 1.3 copy-start
Sparse Core Ops, SparseCore 0:
  33.3 49.4 all-gather.1

commit v9 on v8

--- a/solution.py
+++ b/solution.py
@@ -106,10 +106,8 @@
         c0 = 2 * cp
         l0 = _pick(sx_ref, up_idx[2 * c0], up_idx[2 * c0 + 1], lane)
         l1 = _pick(sx_ref, up_idx[2 * c0 + 2], up_idx[2 * c0 + 3], lane)
-        w = wu_ref[cp]
-        s0 = lax.dot_general(l0, w, NT, preferred_element_type=jnp.float32)
-        s1 = lax.dot_general(l1, w, NT, preferred_element_type=jnp.float32)
-        cur = _gelu(jnp.where(lane < BLK, s0, s1)).astype(jnp.bfloat16)
+        s = lax.dot_general(jnp.concatenate([l0, l1], axis=0), wu_ref[cp], NT, preferred_element_type=jnp.float32)
+        cur = _gelu(jnp.where(lane < BLK, s[:count], s[count:])).astype(jnp.bfloat16)
         sh_ref[0, cp] = cur
         sh_ref[1, cp] = _shifted(prev, cur)
         return cur
@@ -117,7 +115,7 @@
     last = zero
     for k in range(UP_CHUNKS):
         copies[k].wait()
-        last = lax.fori_loop(k * up_step, (k + 1) * up_step, up, last, unroll=8)
+        last = lax.fori_loop(k * up_step, (k + 1) * up_step, up, last, unroll=24)
     sh_ref[0, pairs_hid] = zero
     sh_ref[1, pairs_hid] = _shifted(last, zero)
 
@@ -127,10 +125,8 @@
         c0 = 2 * cp
         l0 = _pick(sh_ref, dn_idx[2 * c0], dn_idx[2 * c0 + 1], lane)
         l1 = _pick(sh_ref, dn_idx[2 * c0 + 2], dn_idx[2 * c0 + 3], lane)
-        w = wd_ref[cp]
-        s0 = lax.dot_general(l0, w, NT, preferred_element_type=jnp.float32)
-        s1 = lax.dot_general(l1, w, NT, preferred_element_type=jnp.float32)
-        s = jnp.where(lane < BLK, s0, s1)
+        s = lax.dot_general(jnp.concatenate([l0, l1], axis=0), wd_ref[cp], NT, preferred_element_type=jnp.float32)
+        s = jnp.where(lane < BLK, s[:count], s[count:])
         o_ref[:, cp * LANE:(cp + 1) * LANE] = (x[:, cp * LANE:(cp + 1) * LANE] + s).astype(jnp.bfloat16)
 
 

time: 357 us -> 333 us (0.933)
  waiting for transfers between devices: 207 us -> 192 us
  Pallas kernels: 43.7 us -> 35.1 us
    ppermute x11, waiting for transfers between devices: 161 us -> 146 us  [from_behind(): lax.ppermute(value, axis, [(source, source + steps) for source in range(i...]
    pallas_call x4, Pallas kernels: 43.7 us -> 35.1 us  [layer(): pl.pallas_call(_layer_kernel, out_shape=jax.ShapeDtypeStruct((count, widt...]
  transfers between devices with their start and end apart: 15 -> 15, of which waited for: 14 -> 14; matrix products, arithmetic and copies ran while one was open for 9% -> 10% of each run, Pallas kernels for 0% -> 0%
where the time goes in v9:
time: 333 us; the launch traced here: 332 us
  waiting for transfers between devices  192 us (58%)
  local copies, waits for them, and re-layouts  37.8 us (11%)
  Pallas kernels  35.1 us (11%)
  starting transfers between devices  32.1 us (10%)
  other arithmetic  21 us (6%)
  between operations  13.6 us (4%)
    ppermute x11, waiting for transfers between devices, from_behind(): lax.ppermute(value, axis, [(source, source + steps) for source in range(i...  146 us
    all_gather x1, waiting for transfers between devices, gather_weights(): full = lax.all_gather(full[:, None], ('y', 'c'), axis=1, tiled=True)  40.9 us
    pallas_call x4, Pallas kernels, layer(): pl.pallas_call(_layer_kernel, out_shape=jax.ShapeDtypeStruct((count, widt...  35.1 us
    ppermute x3, starting transfers between devices, exchange_zh(): lax.ppermute(part, 'zh', [(i, (i + shift) % count) for i in range(count)])  18 us
    ppermute x11, starting transfers between devices, from_behind(): lax.ppermute(value, axis, [(source, source + steps) for source in range(i...  14.1 us
    dynamic_update_slice x11, other arithmetic, advance(): record = lax.dynamic_update_index_in_dim(record, updated, slot, 0)  13.4 us
    dynamic_slice x11, local copies, waits for them, and re-layouts, advance(): current = lax.dynamic_index_in_dim(record, slot, 0, keepdims=False)  11.3 us
    unnamed x20, local copies, waits for them, and re-layouts  7.08 us
  transfers between devices with their start and end apart: 15, of which 14 were waited for; matrix products, arithmetic and copies ran while one was open for 10% of the time, Pallas kernels for 0%

profile of v9, /device:TPU:70, one launch (start us, length us, event | category | flops | bytes accessed | tf_op | source)
XLA Modules:
  0.0 331.7 jit_solution(859370768122436224)
XLA Ops:
  6.5 1.6 copy.40
  8.9 6.1 %collective-permute-start.1 = (bf16[384,128]{1,0:T(8,128)(2,1)S(1)}, bf16[384,128]{1,0:T(8,128)(2,1)S(1)}, u32[]{:S(2)}, u32[]{:S(2)}) collective-permute-start(bf16[384,128]{1,0:T(8,128)(2,1)S(1)} %get-tuple-element.335), channel_id=1, source_target_pairs={{0,16},{16,32},{32,48},{48,0},{1,17},{17,33},{33,49},{49,1},{2,18}... | collective-permute-start | bytes 294920 | tf_op jit(solution)/shard_map/ppermute | solution.py:29
  15.0 8.2 %collective-permute-start.2 = (bf16[384,128]{1,0:T(8,128)(2,1)S(1)}, bf16[384,128]{1,0:T(8,128)(2,1)S(1)}, u32[]{:S(2)}, u32[]{:S(2)}) collective-permute-start(bf16[384,128]{1,0:T(8,128)(2,1)S(1)} %get-tuple-element.335), channel_id=1, source_target_pairs={{0,32},{16,48},{32,0},{48,16},{1,33},{17,49},{33,1},{49,17},{2,34}... | collective-permute-start | bytes 294920 | tf_op jit(solution)/shard_map/ppermute | solution.py:29
  23.2 3.7 %collective-permute-start.3 = (bf16[384,128]{1,0:T(8,128)(2,1)S(1)}, bf16[384,128]{1,0:T(8,128)(2,1)S(1)}, u32[]{:S(2)}, u32[]{:S(2)}) collective-permute-start(bf16[384,128]{1,0:T(8,128)(2,1)S(1)} %get-tuple-element.335), channel_id=1, source_target_pairs={{0,48},{16,0},{32,16},{48,32},{1,49},{17,1},{33,17},{49,33},{2,50}... | collective-permute-start | bytes 294920 | tf_op jit(solution)/shard_map/ppermute | solution.py:29
  26.9 1.1 collective-permute-done.2
  28.0 3.5 %collective-permute-done.3 = bf16[384,128]{1,0:T(8,128)(2,1)S(1)} collective-permute-done((bf16[384,128]{1,0:T(8,128)(2,1)S(1)}, bf16[384,128]{1,0:T(8,128)(2,1)S(1)}, u32[]{:S(2)}, u32[]{:S(2)}) %collective-permute-start.3) | collective-permute-done | bytes 98336 | tf_op jit(solution)/shard_map/ppermute | solution.py:29
  33.8 1.1 scatter_custom_fusion
  34.9 1.5 gather_fusion
  37.3 1.1 copy.31
  39.2 1.0 reshape_squeeze.6
  40.5 1.4 convert_element_type.12
  41.9 40.9 %all-gather.2.cloned.1.call-done = bf16[4,16,384,128]{3,2,0,1:T(8,128)(2,1)} async-done(((bf16[4,1,384,128]{3,2,0,1:T(8,128)(2,1)}), bf16[4,16,384,128]{3,2,0,1:T(8,128)(2,1)}) %all-gather.2.cloned.1.call-update) | async-done | bytes 6291472 | tf_op jit(solution)/shard_map/all_gather | solution.py:48
  82.8 3.4 %fusion.8 = (bf16[4,16,192,128]{3,2,0,1:T(8,128)(2,1)S(1)}, bf16[4,16,192,128]{3,2,0,1:T(8,128)(2,1)S(1)}) fusion(bf16[4,16,384,128]{3,2,0,1:T(8,128)(2,1)} %all-gather.2.cloned.1.call-done), kind=kLoop, calls=%fused_computation.41 | loop fusion | bytes 12582912 | tf_op jit(solution)/shard_map/slice | solution.py:50
  86.6 1.9 copy.24
  88.6 230.3 %while.16 = (s32[]{:T(128)}, bf16[32,6144]{1,0:T(8,128)(2,1)}, bf16[4,32,6144]{2,1,0:T(8,128)(2,1)}, s32[]{:T(128)}, pred[]{:T(512)}, /*index=5*/bf16[4,32,6144]...) while((s32[]{:T(128)}, bf16[32,6144]{1,0:T(8,128)(2,1)}, ...), condition=%wide.region_6.7_spmd, body=%wide.region_3.6_spmd.sunk | while | flops 393229 | bytes 4718975 | solution.py:215
  89.3 1.3 collective-permute-start
  90.6 1.0 constant_dynamic-slice_fusion.2
  92.5 10.3 %collective-permute-done = bf16[32,6144]{1,0:T(8,128)(2,1)} collective-permute-done((bf16[32,6144]{1,0:T(8,128)(2,1)}, bf16[32,6144]{1,0:T(8,128)(2,1)}, u32[]{:S(2)}, u32[]{:S(2)}) %collective-permute-start) | collective-permute-done | bytes 393248 | tf_op jit(solution)/shard_map/while/body/eval_jaxpr/ppermute | solution.py:21
  103.5 1.3 collective-permute-start
  104.8 1.0 constant_dynamic-slice_fusion.2
  106.7 9.4 %collective-permute-done = bf16[32,6144]{1,0:T(8,128)(2,1)} collective-permute-done((bf16[32,6144]{1,0:T(8,128)(2,1)}, bf16[32,6144]{1,0:T(8,128)(2,1)}, u32[]{:S(2)}, u32[]{:S(2)}) %collective-permute-start) | collective-permute-done | bytes 393248 | tf_op jit(solution)/shard_map/while/body/eval_jaxpr/ppermute | solution.py:21
  116.9 1.3 collective-permute-start
  118.2 1.0 constant_dynamic-slice_fusion.2
  120.1 8.6 %collective-permute-done = bf16[32,6144]{1,0:T(8,128)(2,1)} collective-permute-done((bf16[32,6144]{1,0:T(8,128)(2,1)}, bf16[32,6144]{1,0:T(8,128)(2,1)}, u32[]{:S(2)}, u32[]{:S(2)}) %collective-permute-start) | collective-permute-done | bytes 393248 | tf_op jit(solution)/shard_map/while/body/eval_jaxpr/ppermute | solution.py:21
  129.4 1.3 collective-permute-start
  130.7 1.0 constant_dynamic-slice_fusion.2
  132.6 7.7 %collective-permute-done = bf16[32,6144]{1,0:T(8,128)(2,1)} collective-permute-done((bf16[32,6144]{1,0:T(8,128)(2,1)}, bf16[32,6144]{1,0:T(8,128)(2,1)}, u32[]{:S(2)}, u32[]{:S(2)}) %collective-permute-start) | collective-permute-done | bytes 393248 | tf_op jit(solution)/shard_map/while/body/eval_jaxpr/ppermute | solution.py:21
  141.1 1.3 collective-permute-start
  142.3 1.0 constant_dynamic-slice_fusion.2
  144.2 8.7 %collective-permute-done = bf16[32,6144]{1,0:T(8,128)(2,1)} collective-permute-done((bf16[32,6144]{1,0:T(8,128)(2,1)}, bf16[32,6144]{1,0:T(8,128)(2,1)}, u32[]{:S(2)}, u32[]{:S(2)}) %collective-permute-start) | collective-permute-done | bytes 393248 | tf_op jit(solution)/shard_map/while/body/eval_jaxpr/ppermute | solution.py:21
  153.7 1.3 collective-permute-start
  155.0 1.0 constant_dynamic-slice_fusion.2
  156.8 8.1 %collective-permute-done = bf16[32,6144]{1,0:T(8,128)(2,1)} collective-permute-done((bf16[32,6144]{1,0:T(8,128)(2,1)}, bf16[32,6144]{1,0:T(8,128)(2,1)}, u32[]{:S(2)}, u32[]{:S(2)}) %collective-permute-start) | collective-permute-done | bytes 393248 | tf_op jit(solution)/shard_map/while/body/eval_jaxpr/ppermute | solution.py:21
  165.7 1.3 collective-permute-start
  167.0 1.0 constant_dynamic-slice_fusion.2
  168.9 65.0 %collective-permute-done = bf16[32,6144]{1,0:T(8,128)(2,1)} collective-permute-done((bf16[32,6144]{1,0:T(8,128)(2,1)}, bf16[32,6144]{1,0:T(8,128)(2,1)}, u32[]{:S(2)}, u32[]{:S(2)}) %collective-permute-start) | collective-permute-done | bytes 393248 | tf_op jit(solution)/shard_map/while/body/eval_jaxpr/ppermute | solution.py:21
  233.9 9.9 %conditional.2 = (bf16[32,6144]{1,0:T(8,128)(2,1)}) conditional(s32[]{:T(128)} %convert_element_type.14, () %tuple.47, (pred[]{:T(512)}, s32[]{:T(128)}, bf16[4,32,6144]{2,1,0:T(8,128)(2,1)}, bf16[32,6144]{1,0:T(8,128)(2,1)}, s32[384]{0:T(512)S(1)}, /*index=5*/s32[192]{0:T(256)S(1)}, f32[1,6144]{1,0:T(1,128)}, bf16[96,128,128]{2,1,0:T(8,128)(2,1)}, ...), branch_computations={%region_4.4_spmd, %region_5.5_spmd} | conditional | flops 196612 | bytes 1179707 | solution.py:201
  233.9 1.2 bitcast_select_fusion.x_ref
  235.1 8.8 %branch_1_fun.3 = bf16[32,6144]{1,0:T(8,128)(2,1)} custom-call(s32[384]{0:T(512)S(1)} %get-tuple-element.287.up_idx, s32[192]{0:T(256)S(1)} %get-tuple-element.288.dn_idx, bf16[32,6144]{1,0:T(8,128)(2,1)S(1)} %bitcast_select_fusion.x_ref, f32[1,6144]{1,0:T(1,128)} %get-tuple-element.293.g_ref, bf16[96,128,128]{2,1,0:T(8,128)(2,1)} %get-tuple-element.294.wu_hbm, ...), custom_call_target="tpu_custom_call" | custom-call | tf_op jit(solution)/shard_map/while/body/eval_jaxpr/cond/branch_1_fun/pallas_call | solution.py:141
  243.9 1.3 collective-permute-start
  245.2 1.0 constant_dynamic-slice_fusion.2
  246.2 1.8 bitcast_dynamic-update-slice_fusion.2
  248.1 7.1 %collective-permute-done = bf16[32,6144]{1,0:T(8,128)(2,1)} collective-permute-done((bf16[32,6144]{1,0:T(8,128)(2,1)}, bf16[32,6144]{1,0:T(8,128)(2,1)}, u32[]{:S(2)}, u32[]{:S(2)}) %collective-permute-start) | collective-permute-done | bytes 393248 | tf_op jit(solution)/shard_map/while/body/eval_jaxpr/ppermute | solution.py:21
  255.1 9.9 %conditional.2 = (bf16[32,6144]{1,0:T(8,128)(2,1)}) conditional(s32[]{:T(128)} %convert_element_type.14, () %tuple.47, (pred[]{:T(512)}, s32[]{:T(128)}, bf16[4,32,6144]{2,1,0:T(8,128)(2,1)}, bf16[32,6144]{1,0:T(8,128)(2,1)}, s32[384]{0:T(512)S(1)}, /*index=5*/s32[192]{0:T(256)S(1)}, f32[1,6144]{1,0:T(1,128)}, bf16[96,128,128]{2,1,0:T(8,128)(2,1)}, ...), branch_computations={%region_4.4_spmd, %region_5.5_spmd} | conditional | flops 196612 | bytes 1179707 | solution.py:201
  255.1 1.2 bitcast_select_fusion.x_ref
  256.3 8.8 %branch_1_fun.3 = bf16[32,6144]{1,0:T(8,128)(2,1)} custom-call(s32[384]{0:T(512)S(1)} %get-tuple-element.287.up_idx, s32[192]{0:T(256)S(1)} %get-tuple-element.288.dn_idx, bf16[32,6144]{1,0:T(8,128)(2,1)S(1)} %bitcast_select_fusion.x_ref, f32[1,6144]{1,0:T(1,128)} %get-tuple-element.293.g_ref, bf16[96,128,128]{2,1,0:T(8,128)(2,1)} %get-tuple-element.294.wu_hbm, ...), custom_call_target="tpu_custom_call" | custom-call | tf_op jit(solution)/shard_map/while/body/eval_jaxpr/cond/branch_1_fun/pallas_call | solution.py:141
  265.1 1.3 collective-permute-start
  267.4 1.8 bitcast_dynamic-update-slice_fusion.2
  269.3 7.6 %collective-permute-done = bf16[32,6144]{1,0:T(8,128)(2,1)} collective-permute-done((bf16[32,6144]{1,0:T(8,128)(2,1)}, bf16[32,6144]{1,0:T(8,128)(2,1)}, u32[]{:S(2)}, u32[]{:S(2)}) %collective-permute-start) | collective-permute-done | bytes 393248 | tf_op jit(solution)/shard_map/while/body/eval_jaxpr/ppermute | solution.py:21
  276.9 9.9 %conditional.2 = (bf16[32,6144]{1,0:T(8,128)(2,1)}) conditional(s32[]{:T(128)} %convert_element_type.14, () %tuple.47, (pred[]{:T(512)}, s32[]{:T(128)}, bf16[4,32,6144]{2,1,0:T(8,128)(2,1)}, bf16[32,6144]{1,0:T(8,128)(2,1)}, s32[384]{0:T(512)S(1)}, /*index=5*/s32[192]{0:T(256)S(1)}, f32[1,6144]{1,0:T(1,128)}, bf16[96,128,128]{2,1,0:T(8,128)(2,1)}, ...), branch_computations={%region_4.4_spmd, %region_5.5_spmd} | conditional | flops 196612 | bytes 1179707 | solution.py:201
  276.9 1.2 bitcast_select_fusion.x_ref
  278.0 8.8 %branch_1_fun.3 = bf16[32,6144]{1,0:T(8,128)(2,1)} custom-call(s32[384]{0:T(512)S(1)} %get-tuple-element.287.up_idx, s32[192]{0:T(256)S(1)} %get-tuple-element.288.dn_idx, bf16[32,6144]{1,0:T(8,128)(2,1)S(1)} %bitcast_select_fusion.x_ref, f32[1,6144]{1,0:T(1,128)} %get-tuple-element.293.g_ref, bf16[96,128,128]{2,1,0:T(8,128)(2,1)} %get-tuple-element.294.wu_hbm, ...), custom_call_target="tpu_custom_call" | custom-call | tf_op jit(solution)/shard_map/while/body/eval_jaxpr/cond/branch_1_fun/pallas_call | solution.py:141
  286.8 1.3 collective-permute-start
  289.2 1.8 bitcast_dynamic-update-slice_fusion.2
  291.0 7.9 %collective-permute-done = bf16[32,6144]{1,0:T(8,128)(2,1)} collective-permute-done((bf16[32,6144]{1,0:T(8,128)(2,1)}, bf16[32,6144]{1,0:T(8,128)(2,1)}, u32[]{:S(2)}, u32[]{:S(2)}) %collective-permute-start) | collective-permute-done | bytes 393248 | tf_op jit(solution)/shard_map/while/body/eval_jaxpr/ppermute | solution.py:21
  298.9 9.9 %conditional.2 = (bf16[32,6144]{1,0:T(8,128)(2,1)}) conditional(s32[]{:T(128)} %convert_element_type.14, () %tuple.47, (pred[]{:T(512)}, s32[]{:T(128)}, bf16[4,32,6144]{2,1,0:T(8,128)(2,1)}, bf16[32,6144]{1,0:T(8,128)(2,1)}, s32[384]{0:T(512)S(1)}, /*index=5*/s32[192]{0:T(256)S(1)}, f32[1,6144]{1,0:T(1,128)}, bf16[96,128,128]{2,1,0:T(8,128)(2,1)}, ...), branch_computations={%region_4.4_spmd, %region_5.5_spmd} | conditional | flops 196612 | bytes 1179707 | solution.py:201
  298.9 1.2 bitcast_select_fusion.x_ref
  300.1 8.8 %branch_1_fun.3 = bf16[32,6144]{1,0:T(8,128)(2,1)} custom-call(s32[384]{0:T(512)S(1)} %get-tuple-element.287.up_idx, s32[192]{0:T(256)S(1)} %get-tuple-element.288.dn_idx, bf16[32,6144]{1,0:T(8,128)(2,1)S(1)} %bitcast_select_fusion.x_ref, f32[1,6144]{1,0:T(1,128)} %get-tuple-element.293.g_ref, bf16[96,128,128]{2,1,0:T(8,128)(2,1)} %get-tuple-element.294.wu_hbm, ...), custom_call_target="tpu_custom_call" | custom-call | tf_op jit(solution)/shard_map/while/body/eval_jaxpr/cond/branch_1_fun/pallas_call | solution.py:141
  308.9 1.3 collective-permute-start
  310.2 1.0 constant_dynamic-slice_fusion.2
  311.2 1.8 bitcast_dynamic-update-slice_fusion.2
  313.1 5.8 %collective-permute-done = bf16[32,6144]{1,0:T(8,128)(2,1)} collective-permute-done((bf16[32,6144]{1,0:T(8,128)(2,1)}, bf16[32,6144]{1,0:T(8,128)(2,1)}, u32[]{:S(2)}, u32[]{:S(2)}) %collective-permute-start) | collective-permute-done | bytes 393248 | tf_op jit(solution)/shard_map/while/body/eval_jaxpr/ppermute | solution.py:21
  318.9 4.7 %scatter_fusion = bf16[160,6144]{1,0:T(8,128)(2,1)S(1)} fusion(bf16[160,6144]{1,0:T(8,128)(2,1)S(1)} %copy.40, s32[128]{0:T(128)S(1)} %compare_select_fusion.3, bf16[128,6144]{1,0:T(8,128)(2,1)} %bitcast.38), kind=kCustom, calls=%fused_computation.3 | custom fusion | bytes 4719104 | tf_op jit(solution)/shard_map/scatter | solution.py:217
  323.6 1.3 copy-done
  (69 shorter events, 23.9 us)
Async XLA Ops:
  6.5 1.9 copy-start.2
  6.5 1.6 copy-start.3
  6.5 76.2 %all-gather.2.cloned.1.call-start = ((), (), s32[]{:S(2)}) async-start(), calls=%async_computation | async-start | bytes 6684672 | tf_op jit(solution)/shard_map/all_gather | solution.py:48
  8.8 24.3 %copy-start.4 = (s32[160]{0:T(256)S(1)}, s32[160]{0:T(256)}, u32[]{:S(2)}) copy-start(s32[160]{0:T(256)} %param.12) | copy-start | bytes 1924
  8.9 18.0 %collective-permute-start.1 = (bf16[384,128]{1,0:T(8,128)(2,1)S(1)}, bf16[384,128]{1,0:T(8,128)(2,1)S(1)}, u32[]{:S(2)}, u32[]{:S(2)}) collective-permute-start(bf16[384,128]{1,0:T(8,128)(2,1)S(1)} %get-tuple-element.335), channel_id=1, source_target_pairs={{0,16},{16,32},{32,48},{48,0},{1,17},{17,33},{33,49},{49,1},{2,18}... | collective-permute-start | bytes 294920 | tf_op jit(solution)/shard_map/ppermute | solution.py:29
  15.0 13.0 %collective-permute-start.2 = (bf16[384,128]{1,0:T(8,128)(2,1)S(1)}, bf16[384,128]{1,0:T(8,128)(2,1)S(1)}, u32[]{:S(2)}, u32[]{:S(2)}) collective-permute-start(bf16[384,128]{1,0:T(8,128)(2,1)S(1)} %get-tuple-element.335), channel_id=1, source_target_pairs={{0,32},{16,48},{32,0},{48,16},{1,33},{17,49},{33,1},{49,17},{2,34}... | collective-permute-start | bytes 294920 | tf_op jit(solution)/shard_map/ppermute | solution.py:29
  23.2 8.4 %collective-permute-start.3 = (bf16[384,128]{1,0:T(8,128)(2,1)S(1)}, bf16[384,128]{1,0:T(8,128)(2,1)S(1)}, u32[]{:S(2)}, u32[]{:S(2)}) collective-permute-start(bf16[384,128]{1,0:T(8,128)(2,1)S(1)} %get-tuple-element.335), channel_id=1, source_target_pairs={{0,48},{16,0},{32,16},{48,32},{1,49},{17,1},{33,17},{49,33},{2,50}... | collective-permute-start | bytes 294920 | tf_op jit(solution)/shard_map/ppermute | solution.py:29
  36.4 2.0 copy-start.1
  37.3 1.2 copy-start.5
  37.3 3.0 copy-start.6
  89.3 13.5 %collective-permute-start = (bf16[32,6144]{1,0:T(8,128)(2,1)}, bf16[32,6144]{1,0:T(8,128)(2,1)}, u32[]{:S(2)}, u32[]{:S(2)}) collective-permute-start(bf16[32,6144]{1,0:T(8,128)(2,1)} %get-tuple-element.448), channel_id=1, source_target_pairs={{0,64},{64,128},{128,192},{192,256},{256,320},{320,384},{384,448},... | collective-permute-start | bytes 1179656 | tf_op jit(solution)/shard_map/while/body/eval_jaxpr/ppermute | solution.py:21
  103.5 12.6 %collective-permute-start = (bf16[32,6144]{1,0:T(8,128)(2,1)}, bf16[32,6144]{1,0:T(8,128)(2,1)}, u32[]{:S(2)}, u32[]{:S(2)}) collective-permute-start(bf16[32,6144]{1,0:T(8,128)(2,1)} %get-tuple-element.448), channel_id=1, source_target_pairs={{0,64},{64,128},{128,192},{192,256},{256,320},{320,384},{384,448},... | collective-permute-start | bytes 1179656 | tf_op jit(solution)/shard_map/while/body/eval_jaxpr/ppermute | solution.py:21
  116.9 11.7 %collective-permute-start = (bf16[32,6144]{1,0:T(8,128)(2,1)}, bf16[32,6144]{1,0:T(8,128)(2,1)}, u32[]{:S(2)}, u32[]{:S(2)}) collective-permute-start(bf16[32,6144]{1,0:T(8,128)(2,1)} %get-tuple-element.448), channel_id=1, source_target_pairs={{0,64},{64,128},{128,192},{192,256},{256,320},{320,384},{384,448},... | collective-permute-start | bytes 1179656 | tf_op jit(solution)/shard_map/while/body/eval_jaxpr/ppermute | solution.py:21
  129.4 10.9 %collective-permute-start = (bf16[32,6144]{1,0:T(8,128)(2,1)}, bf16[32,6144]{1,0:T(8,128)(2,1)}, u32[]{:S(2)}, u32[]{:S(2)}) collective-permute-start(bf16[32,6144]{1,0:T(8,128)(2,1)} %get-tuple-element.448), channel_id=1, source_target_pairs={{0,64},{64,128},{128,192},{192,256},{256,320},{320,384},{384,448},... | collective-permute-start | bytes 1179656 | tf_op jit(solution)/shard_map/while/body/eval_jaxpr/ppermute | solution.py:21
  141.1 11.8 %collective-permute-start = (bf16[32,6144]{1,0:T(8,128)(2,1)}, bf16[32,6144]{1,0:T(8,128)(2,1)}, u32[]{:S(2)}, u32[]{:S(2)}) collective-permute-start(bf16[32,6144]{1,0:T(8,128)(2,1)} %get-tuple-element.448), channel_id=1, source_target_pairs={{0,64},{64,128},{128,192},{192,256},{256,320},{320,384},{384,448},... | collective-permute-start | bytes 1179656 | tf_op jit(solution)/shard_map/while/body/eval_jaxpr/ppermute | solution.py:21
  153.7 11.3 %collective-permute-start = (bf16[32,6144]{1,0:T(8,128)(2,1)}, bf16[32,6144]{1,0:T(8,128)(2,1)}, u32[]{:S(2)}, u32[]{:S(2)}) collective-permute-start(bf16[32,6144]{1,0:T(8,128)(2,1)} %get-tuple-element.448), channel_id=1, source_target_pairs={{0,64},{64,128},{128,192},{192,256},{256,320},{320,384},{384,448},... | collective-permute-start | bytes 1179656 | tf_op jit(solution)/shard_map/while/body/eval_jaxpr/ppermute | solution.py:21
  165.7 68.2 %collective-permute-start = (bf16[32,6144]{1,0:T(8,128)(2,1)}, bf16[32,6144]{1,0:T(8,128)(2,1)}, u32[]{:S(2)}, u32[]{:S(2)}) collective-permute-start(bf16[32,6144]{1,0:T(8,128)(2,1)} %get-tuple-element.448), channel_id=1, source_target_pairs={{0,64},{64,128},{128,192},{192,256},{256,320},{320,384},{384,448},... | collective-permute-start | bytes 1179656 | tf_op jit(solution)/shard_map/while/body/eval_jaxpr/ppermute | solution.py:21
  243.9 11.3 %collective-permute-start = (bf16[32,6144]{1,0:T(8,128)(2,1)}, bf16[32,6144]{1,0:T(8,128)(2,1)}, u32[]{:S(2)}, u32[]{:S(2)}) collective-permute-start(bf16[32,6144]{1,0:T(8,128)(2,1)} %get-tuple-element.448), channel_id=1, source_target_pairs={{0,64},{64,128},{128,192},{192,256},{256,320},{320,384},{384,448},... | collective-permute-start | bytes 1179656 | tf_op jit(solution)/shard_map/while/body/eval_jaxpr/ppermute | solution.py:21
  265.1 11.8 %collective-permute-start = (bf16[32,6144]{1,0:T(8,128)(2,1)}, bf16[32,6144]{1,0:T(8,128)(2,1)}, u32[]{:S(2)}, u32[]{:S(2)}) collective-permute-start(bf16[32,6144]{1,0:T(8,128)(2,1)} %get-tuple-element.448), channel_id=1, source_target_pairs={{0,64},{64,128},{128,192},{192,256},{256,320},{320,384},{384,448},... | collective-permute-start | bytes 1179656 | tf_op jit(solution)/shard_map/while/body/eval_jaxpr/ppermute | solution.py:21
  286.8 12.1 %collective-permute-start = (bf16[32,6144]{1,0:T(8,128)(2,1)}, bf16[32,6144]{1,0:T(8,128)(2,1)}, u32[]{:S(2)}, u32[]{:S(2)}) collective-permute-start(bf16[32,6144]{1,0:T(8,128)(2,1)} %get-tuple-element.448), channel_id=1, source_target_pairs={{0,64},{64,128},{128,192},{192,256},{256,320},{320,384},{384,448},... | collective-permute-start | bytes 1179656 | tf_op jit(solution)/shard_map/while/body/eval_jaxpr/ppermute | solution.py:21
  308.9 10.0 %collective-permute-start = (bf16[32,6144]{1,0:T(8,128)(2,1)}, bf16[32,6144]{1,0:T(8,128)(2,1)}, u32[]{:S(2)}, u32[]{:S(2)}) collective-permute-start(bf16[32,6144]{1,0:T(8,128)(2,1)} %get-tuple-element.448), channel_id=1, source_target_pairs={{0,64},{64,128},{128,192},{192,256},{256,320},{320,384},{384,448},... | collective-permute-start | bytes 1179656 | tf_op jit(solution)/shard_map/while/body/eval_jaxpr/ppermute | solution.py:21
  323.6 1.3 copy-start
Sparse Core Ops, SparseCore 0:
  33.3 49.4 all-gather.1

commit v10 on v9

--- a/solution.py
+++ b/solution.py
@@ -214,7 +214,8 @@
     turns = sections + pieces - 1
     held, record = lax.fori_loop(0, turns, turn_step, (split[0], split))
     final = record.reshape(selected.shape[0], width)
-    merged = activations.at[chosen].set(final)
+    rows = final[jnp.clip(places, 0, KEEP_DEV - 1)]
+    merged = jnp.where((keep == 1)[:, None], rows, activations)
     return merged[None]
 
 

time: 333 us -> 336 us (level)
  waiting for transfers between devices: 192 us -> 209 us
  local copies, waits for them, and re-layouts: 37.8 us -> 26.4 us
  other arithmetic: 21 us -> 17.6 us
    ppermute x11, waiting for transfers between devices: 146 us -> 166 us  [from_behind(): lax.ppermute(value, axis, [(source, source + steps) for source in range(i...]
    dynamic_slice x11, local copies, waits for them, and re-layouts: 11.3 us -> 0.39 us  [advance(): current = lax.dynamic_index_in_dim(record, slot, 0, keepdims=False)]
    dynamic_update_slice x11, other arithmetic: 13.4 us -> 5.18 us  [advance(): record = lax.dynamic_update_index_in_dim(record, updated, slot, 0)]
    scatter x1 -> x0, local copies, waits for them, and re-layouts: 4.7 us -> none  [per_device(): merged = activations.at[chosen].set(final)]
    unnamed x20 -> x17, local copies, waits for them, and re-layouts: 7.08 us -> 5.56 us
  transfers between devices with their start and end apart: 15 -> 15, of which waited for: 14 -> 14; matrix products, arithmetic and copies ran while one was open for 10% -> 5% of each run, Pallas kernels for 0% -> 0%
where the time goes in v10:
time: 336 us; the launch traced here: 335 us
  waiting for transfers between devices  209 us (62%)
  Pallas kernels  35.7 us (11%)
  starting transfers between devices  32.1 us (10%)
  local copies, waits for them, and re-layouts  26.4 us (8%)
  other arithmetic  17.6 us (5%)
  between operations  13.6 us (4%)
    ppermute x11, waiting for transfers between devices, from_behind(): lax.ppermute(value, axis, [(source, source + steps) for source in range(i...  166 us
    all_gather x1, waiting for transfers between devices, gather_weights(): full = lax.all_gather(full[:, None], ('y', 'c'), axis=1, tiled=True)  38.3 us
    pallas_call x4, Pallas kernels, layer(): pl.pallas_call(_layer_kernel, out_shape=jax.ShapeDtypeStruct((count, widt...  35.7 us
    ppermute x3, starting transfers between devices, exchange_zh(): lax.ppermute(part, 'zh', [(i, (i + shift) % count) for i in range(count)])  18 us
    ppermute x11, starting transfers between devices, from_behind(): lax.ppermute(value, axis, [(source, source + steps) for source in range(i...  14.1 us
  transfers between devices with their start and end apart: 15, of which 14 were waited for; matrix products, arithmetic and copies ran while one was open for 5% of the time, Pallas kernels for 0%

profile of v10, /device:TPU:70, one launch (start us, length us, event | category | flops | bytes accessed | tf_op | source)
XLA Modules:
  0.0 334.5 jit_solution(15605041324851269439)
XLA Ops:
  6.6 0.9 reshape.124
  7.6 1.1 reshape.122
  9.0 6.1 %collective-permute-start.1 = (bf16[384,128]{1,0:T(8,128)(2,1)S(1)}, bf16[384,128]{1,0:T(8,128)(2,1)S(1)}, u32[]{:S(2)}, u32[]{:S(2)}) collective-permute-start(bf16[384,128]{1,0:T(8,128)(2,1)S(1)} %get-tuple-element.337), channel_id=1, source_target_pairs={{0,16},{16,32},{32,48},{48,0},{1,17},{17,33},{33,49},{49,1},{2,18}... | collective-permute-start | bytes 294920 | tf_op jit(solution)/shard_map/ppermute | solution.py:29
  15.1 8.2 %collective-permute-start.2 = (bf16[384,128]{1,0:T(8,128)(2,1)S(1)}, bf16[384,128]{1,0:T(8,128)(2,1)S(1)}, u32[]{:S(2)}, u32[]{:S(2)}) collective-permute-start(bf16[384,128]{1,0:T(8,128)(2,1)S(1)} %get-tuple-element.337), channel_id=1, source_target_pairs={{0,32},{16,48},{32,0},{48,16},{1,33},{17,49},{33,1},{49,17},{2,34}... | collective-permute-start | bytes 294920 | tf_op jit(solution)/shard_map/ppermute | solution.py:29
  23.3 3.7 %collective-permute-start.3 = (bf16[384,128]{1,0:T(8,128)(2,1)S(1)}, bf16[384,128]{1,0:T(8,128)(2,1)S(1)}, u32[]{:S(2)}, u32[]{:S(2)}) collective-permute-start(bf16[384,128]{1,0:T(8,128)(2,1)S(1)} %get-tuple-element.337), channel_id=1, source_target_pairs={{0,48},{16,0},{32,16},{48,32},{1,49},{17,1},{33,17},{49,33},{2,50}... | collective-permute-start | bytes 294920 | tf_op jit(solution)/shard_map/ppermute | solution.py:29
  27.1 1.1 collective-permute-done.2
  28.1 3.5 %collective-permute-done.3 = bf16[384,128]{1,0:T(8,128)(2,1)S(1)} collective-permute-done((bf16[384,128]{1,0:T(8,128)(2,1)S(1)}, bf16[384,128]{1,0:T(8,128)(2,1)S(1)}, u32[]{:S(2)}, u32[]{:S(2)}) %collective-permute-start.3) | collective-permute-done | bytes 98336 | tf_op jit(solution)/shard_map/ppermute | solution.py:29
  32.4 0.9 bitcast_select_fusion.2
  34.4 1.1 scatter_custom_fusion
  35.5 1.5 gather_fusion
  38.3 1.4 copy.31
  40.5 1.0 reshape_squeeze.6
  42.2 0.9 reshape_squeeze.7
  43.2 1.4 convert_element_type.12
  44.5 38.3 %all-gather.2.cloned.1.call-done = bf16[4,16,384,128]{3,2,0,1:T(8,128)(2,1)} async-done(((bf16[4,1,384,128]{3,2,0,1:T(8,128)(2,1)}), bf16[4,16,384,128]{3,2,0,1:T(8,128)(2,1)}) %all-gather.2.cloned.1.call-update) | async-done | bytes 6291472 | tf_op jit(solution)/shard_map/all_gather | solution.py:48
  82.9 3.4 %fusion.8 = (bf16[4,16,192,128]{3,2,0,1:T(8,128)(2,1)S(1)}, bf16[4,16,192,128]{3,2,0,1:T(8,128)(2,1)S(1)}) fusion(bf16[4,16,384,128]{3,2,0,1:T(8,128)(2,1)} %all-gather.2.cloned.1.call-done), kind=kLoop, calls=%fused_computation.45 | loop fusion | bytes 12582912 | tf_op jit(solution)/shard_map/slice | solution.py:50
  86.6 1.3 slice_add_fusion
  87.9 1.9 copy.24
  89.8 231.8 %while.16 = (s32[]{:T(128)}, bf16[32,6144]{1,0:T(8,128)(2,1)}, bf16[4,32,6144]{2,1,0:T(8,128)(2,1)S(1)}, s32[]{:T(128)}, pred[]{:T(512)}, /*index=5*/bf16[4,32,6...) while((s32[]{:T(128)}, bf16[32,6144]{1,0:T(8,128)(2,1)}, ...), condition=%wide.region_6.7_spmd, body=%wide.region_3.6_spmd.sunk | while | flops 393229 | bytes 4718975 | solution.py:215
  90.6 1.3 collective-permute-start
  92.1 12.0 %collective-permute-done = bf16[32,6144]{1,0:T(8,128)(2,1)} collective-permute-done((bf16[32,6144]{1,0:T(8,128)(2,1)}, bf16[32,6144]{1,0:T(8,128)(2,1)}, u32[]{:S(2)}, u32[]{:S(2)}) %collective-permute-start) | collective-permute-done | bytes 393248 | tf_op jit(solution)/shard_map/while/body/eval_jaxpr/ppermute | solution.py:21
  104.1 0.8 conditional.2
  104.9 1.3 collective-permute-start
  106.3 11.1 %collective-permute-done = bf16[32,6144]{1,0:T(8,128)(2,1)} collective-permute-done((bf16[32,6144]{1,0:T(8,128)(2,1)}, bf16[32,6144]{1,0:T(8,128)(2,1)}, u32[]{:S(2)}, u32[]{:S(2)}) %collective-permute-start) | collective-permute-done | bytes 393248 | tf_op jit(solution)/shard_map/while/body/eval_jaxpr/ppermute | solution.py:21
  117.5 0.8 conditional.2
  118.3 1.3 collective-permute-start
  119.7 10.3 %collective-permute-done = bf16[32,6144]{1,0:T(8,128)(2,1)} collective-permute-done((bf16[32,6144]{1,0:T(8,128)(2,1)}, bf16[32,6144]{1,0:T(8,128)(2,1)}, u32[]{:S(2)}, u32[]{:S(2)}) %collective-permute-start) | collective-permute-done | bytes 393248 | tf_op jit(solution)/shard_map/while/body/eval_jaxpr/ppermute | solution.py:21
  130.0 0.8 conditional.2
  130.8 1.3 collective-permute-start
  132.3 9.4 %collective-permute-done = bf16[32,6144]{1,0:T(8,128)(2,1)} collective-permute-done((bf16[32,6144]{1,0:T(8,128)(2,1)}, bf16[32,6144]{1,0:T(8,128)(2,1)}, u32[]{:S(2)}, u32[]{:S(2)}) %collective-permute-start) | collective-permute-done | bytes 393248 | tf_op jit(solution)/shard_map/while/body/eval_jaxpr/ppermute | solution.py:21
  141.7 0.8 conditional.2
  142.5 1.3 collective-permute-start
  144.0 10.4 %collective-permute-done = bf16[32,6144]{1,0:T(8,128)(2,1)} collective-permute-done((bf16[32,6144]{1,0:T(8,128)(2,1)}, bf16[32,6144]{1,0:T(8,128)(2,1)}, u32[]{:S(2)}, u32[]{:S(2)}) %collective-permute-start) | collective-permute-done | bytes 393248 | tf_op jit(solution)/shard_map/while/body/eval_jaxpr/ppermute | solution.py:21
  155.2 1.3 collective-permute-start
  156.6 9.8 %collective-permute-done = bf16[32,6144]{1,0:T(8,128)(2,1)} collective-permute-done((bf16[32,6144]{1,0:T(8,128)(2,1)}, bf16[32,6144]{1,0:T(8,128)(2,1)}, u32[]{:S(2)}, u32[]{:S(2)}) %collective-permute-start) | collective-permute-done | bytes 393248 | tf_op jit(solution)/shard_map/while/body/eval_jaxpr/ppermute | solution.py:21
  166.5 0.8 conditional.2
  167.3 1.3 collective-permute-start
  168.7 67.4 %collective-permute-done = bf16[32,6144]{1,0:T(8,128)(2,1)} collective-permute-done((bf16[32,6144]{1,0:T(8,128)(2,1)}, bf16[32,6144]{1,0:T(8,128)(2,1)}, u32[]{:S(2)}, u32[]{:S(2)}) %collective-permute-start) | collective-permute-done | bytes 393248 | tf_op jit(solution)/shard_map/while/body/eval_jaxpr/ppermute | solution.py:21
  236.1 10.1 %conditional.2 = (bf16[32,6144]{1,0:T(8,128)(2,1)}) conditional(s32[]{:T(128)} %convert_element_type.14, () %tuple.49, (pred[]{:T(512)}, s32[]{:T(128)}, bf16[4,32,6144]{2,1,0:T(8,128)(2,1)}, bf16[32,6144]{1,0:T(8,128)(2,1)}, s32[384]{0:T(512)S(1)}, /*index=5*/s32[192]{0:T(256)S(1)}, f32[1,6144]{1,0:T(1,128)}, bf16[96,128,128]{2,1,0:T(8,128)(2,1)}, ...), branch_computations={%region_4.4_spmd, %region_5.5_spmd} | conditional | flops 196612 | bytes 1179707 | solution.py:201
  236.1 1.2 bitcast_select_fusion.x_ref
  237.3 8.9 %branch_1_fun.3 = bf16[32,6144]{1,0:T(8,128)(2,1)} custom-call(s32[384]{0:T(512)S(1)} %get-tuple-element.287.up_idx, s32[192]{0:T(256)S(1)} %get-tuple-element.288.dn_idx, bf16[32,6144]{1,0:T(8,128)(2,1)S(1)} %bitcast_select_fusion.x_ref, f32[1,6144]{1,0:T(1,128)} %get-tuple-element.293.g_ref, bf16[96,128,128]{2,1,0:T(8,128)(2,1)} %get-tuple-element.294.wu_hbm, ...), custom_call_target="tpu_custom_call" | custom-call | tf_op jit(solution)/shard_map/while/body/eval_jaxpr/cond/branch_1_fun/pallas_call | solution.py:141
  246.2 1.3 collective-permute-start
  247.6 1.1 bitcast_dynamic-update-slice_fusion.2
  248.7 8.8 %collective-permute-done = bf16[32,6144]{1,0:T(8,128)(2,1)} collective-permute-done((bf16[32,6144]{1,0:T(8,128)(2,1)}, bf16[32,6144]{1,0:T(8,128)(2,1)}, u32[]{:S(2)}, u32[]{:S(2)}) %collective-permute-start) | collective-permute-done | bytes 393248 | tf_op jit(solution)/shard_map/while/body/eval_jaxpr/ppermute | solution.py:21
  257.5 10.1 %conditional.2 = (bf16[32,6144]{1,0:T(8,128)(2,1)}) conditional(s32[]{:T(128)} %convert_element_type.14, () %tuple.49, (pred[]{:T(512)}, s32[]{:T(128)}, bf16[4,32,6144]{2,1,0:T(8,128)(2,1)}, bf16[32,6144]{1,0:T(8,128)(2,1)}, s32[384]{0:T(512)S(1)}, /*index=5*/s32[192]{0:T(256)S(1)}, f32[1,6144]{1,0:T(1,128)}, bf16[96,128,128]{2,1,0:T(8,128)(2,1)}, ...), branch_computations={%region_4.4_spmd, %region_5.5_spmd} | conditional | flops 196612 | bytes 1179707 | solution.py:201
  257.5 1.2 bitcast_select_fusion.x_ref
  258.6 8.9 %branch_1_fun.3 = bf16[32,6144]{1,0:T(8,128)(2,1)} custom-call(s32[384]{0:T(512)S(1)} %get-tuple-element.287.up_idx, s32[192]{0:T(256)S(1)} %get-tuple-element.288.dn_idx, bf16[32,6144]{1,0:T(8,128)(2,1)S(1)} %bitcast_select_fusion.x_ref, f32[1,6144]{1,0:T(1,128)} %get-tuple-element.293.g_ref, bf16[96,128,128]{2,1,0:T(8,128)(2,1)} %get-tuple-element.294.wu_hbm, ...), custom_call_target="tpu_custom_call" | custom-call | tf_op jit(solution)/shard_map/while/body/eval_jaxpr/cond/branch_1_fun/pallas_call | solution.py:141
  267.5 1.3 collective-permute-start
  268.9 1.1 bitcast_dynamic-update-slice_fusion.2
  270.0 9.3 %collective-permute-done = bf16[32,6144]{1,0:T(8,128)(2,1)} collective-permute-done((bf16[32,6144]{1,0:T(8,128)(2,1)}, bf16[32,6144]{1,0:T(8,128)(2,1)}, u32[]{:S(2)}, u32[]{:S(2)}) %collective-permute-start) | collective-permute-done | bytes 393248 | tf_op jit(solution)/shard_map/while/body/eval_jaxpr/ppermute | solution.py:21
  279.3 10.1 %conditional.2 = (bf16[32,6144]{1,0:T(8,128)(2,1)}) conditional(s32[]{:T(128)} %convert_element_type.14, () %tuple.49, (pred[]{:T(512)}, s32[]{:T(128)}, bf16[4,32,6144]{2,1,0:T(8,128)(2,1)}, bf16[32,6144]{1,0:T(8,128)(2,1)}, s32[384]{0:T(512)S(1)}, /*index=5*/s32[192]{0:T(256)S(1)}, f32[1,6144]{1,0:T(1,128)}, bf16[96,128,128]{2,1,0:T(8,128)(2,1)}, ...), branch_computations={%region_4.4_spmd, %region_5.5_spmd} | conditional | flops 196612 | bytes 1179707 | solution.py:201
  279.3 1.2 bitcast_select_fusion.x_ref
  280.5 8.9 %branch_1_fun.3 = bf16[32,6144]{1,0:T(8,128)(2,1)} custom-call(s32[384]{0:T(512)S(1)} %get-tuple-element.287.up_idx, s32[192]{0:T(256)S(1)} %get-tuple-element.288.dn_idx, bf16[32,6144]{1,0:T(8,128)(2,1)S(1)} %bitcast_select_fusion.x_ref, f32[1,6144]{1,0:T(1,128)} %get-tuple-element.293.g_ref, bf16[96,128,128]{2,1,0:T(8,128)(2,1)} %get-tuple-element.294.wu_hbm, ...), custom_call_target="tpu_custom_call" | custom-call | tf_op jit(solution)/shard_map/while/body/eval_jaxpr/cond/branch_1_fun/pallas_call | solution.py:141
  289.4 1.3 collective-permute-start
  290.8 1.1 bitcast_dynamic-update-slice_fusion.2
  291.9 9.6 %collective-permute-done = bf16[32,6144]{1,0:T(8,128)(2,1)} collective-permute-done((bf16[32,6144]{1,0:T(8,128)(2,1)}, bf16[32,6144]{1,0:T(8,128)(2,1)}, u32[]{:S(2)}, u32[]{:S(2)}) %collective-permute-start) | collective-permute-done | bytes 393248 | tf_op jit(solution)/shard_map/while/body/eval_jaxpr/ppermute | solution.py:21
  301.5 10.1 %conditional.2 = (bf16[32,6144]{1,0:T(8,128)(2,1)}) conditional(s32[]{:T(128)} %convert_element_type.14, () %tuple.49, (pred[]{:T(512)}, s32[]{:T(128)}, bf16[4,32,6144]{2,1,0:T(8,128)(2,1)}, bf16[32,6144]{1,0:T(8,128)(2,1)}, s32[384]{0:T(512)S(1)}, /*index=5*/s32[192]{0:T(256)S(1)}, f32[1,6144]{1,0:T(1,128)}, bf16[96,128,128]{2,1,0:T(8,128)(2,1)}, ...), branch_computations={%region_4.4_spmd, %region_5.5_spmd} | conditional | flops 196612 | bytes 1179707 | solution.py:201
  301.5 1.2 bitcast_select_fusion.x_ref
  302.7 8.9 %branch_1_fun.3 = bf16[32,6144]{1,0:T(8,128)(2,1)} custom-call(s32[384]{0:T(512)S(1)} %get-tuple-element.287.up_idx, s32[192]{0:T(256)S(1)} %get-tuple-element.288.dn_idx, bf16[32,6144]{1,0:T(8,128)(2,1)S(1)} %bitcast_select_fusion.x_ref, f32[1,6144]{1,0:T(1,128)} %get-tuple-element.293.g_ref, bf16[96,128,128]{2,1,0:T(8,128)(2,1)} %get-tuple-element.294.wu_hbm, ...), custom_call_target="tpu_custom_call" | custom-call | tf_op jit(solution)/shard_map/while/body/eval_jaxpr/cond/branch_1_fun/pallas_call | solution.py:141
  311.6 1.3 collective-permute-start
  313.0 1.1 bitcast_dynamic-update-slice_fusion.2
  314.1 7.5 %collective-permute-done = bf16[32,6144]{1,0:T(8,128)(2,1)} collective-permute-done((bf16[32,6144]{1,0:T(8,128)(2,1)}, bf16[32,6144]{1,0:T(8,128)(2,1)}, u32[]{:S(2)}, u32[]{:S(2)}) %collective-permute-start) | collective-permute-done | bytes 393248 | tf_op jit(solution)/shard_map/while/body/eval_jaxpr/ppermute | solution.py:21
  321.6 3.0 gather_fusion.2
  324.6 3.1 select_bitcast_fusion
  (68 shorter events, 13.7 us)
Async XLA Ops:
  6.5 76.4 %all-gather.2.cloned.1.call-start = ((), (), s32[]{:S(2)}) async-start(), calls=%async_computation | async-start | bytes 6684672 | tf_op jit(solution)/shard_map/all_gather | solution.py:48
  7.4 25.9 %copy-start.2 = (s32[160]{0:T(256)S(1)}, s32[160]{0:T(256)}, u32[]{:S(2)}) copy-start(s32[160]{0:T(256)} %param.12) | copy-start | bytes 1924
  7.4 28.1 %copy-start = (bf16[160,6144]{1,0:T(8,128)(2,1)S(1)}, bf16[160,6144]{1,0:T(8,128)(2,1)}, u32[]{:S(2)}) copy-start(bf16[160,6144]{1,0:T(8,128)(2,1)} %param.11) | copy-start | bytes 5898244
  9.0 18.0 %collective-permute-start.1 = (bf16[384,128]{1,0:T(8,128)(2,1)S(1)}, bf16[384,128]{1,0:T(8,128)(2,1)S(1)}, u32[]{:S(2)}, u32[]{:S(2)}) collective-permute-start(bf16[384,128]{1,0:T(8,128)(2,1)S(1)} %get-tuple-element.337), channel_id=1, source_target_pairs={{0,16},{16,32},{32,48},{48,0},{1,17},{17,33},{33,49},{49,1},{2,18}... | collective-permute-start | bytes 294920 | tf_op jit(solution)/shard_map/ppermute | solution.py:29
  15.1 13.0 %collective-permute-start.2 = (bf16[384,128]{1,0:T(8,128)(2,1)S(1)}, bf16[384,128]{1,0:T(8,128)(2,1)S(1)}, u32[]{:S(2)}, u32[]{:S(2)}) collective-permute-start(bf16[384,128]{1,0:T(8,128)(2,1)S(1)} %get-tuple-element.337), channel_id=1, source_target_pairs={{0,32},{16,48},{32,0},{48,16},{1,33},{17,49},{33,1},{49,17},{2,34}... | collective-permute-start | bytes 294920 | tf_op jit(solution)/shard_map/ppermute | solution.py:29
  23.3 8.4 %collective-permute-start.3 = (bf16[384,128]{1,0:T(8,128)(2,1)S(1)}, bf16[384,128]{1,0:T(8,128)(2,1)S(1)}, u32[]{:S(2)}, u32[]{:S(2)}) collective-permute-start(bf16[384,128]{1,0:T(8,128)(2,1)S(1)} %get-tuple-element.337), channel_id=1, source_target_pairs={{0,48},{16,0},{32,16},{48,32},{1,49},{17,1},{33,17},{49,33},{2,50}... | collective-permute-start | bytes 294920 | tf_op jit(solution)/shard_map/ppermute | solution.py:29
  37.0 1.3 copy-start.1
  37.1 2.7 copy-start.4
  37.1 4.5 %copy-start.5 = (s32[1,96,2]{1,2,0:T(2,128)S(1)}, s32[1,96,2]{1,2,0:T(2,128)}, u32[]{:S(2)}) copy-start(s32[1,96,2]{1,2,0:T(2,128)} %param.16) | copy-start | bytes 2308
  90.6 13.5 %collective-permute-start = (bf16[32,6144]{1,0:T(8,128)(2,1)}, bf16[32,6144]{1,0:T(8,128)(2,1)}, u32[]{:S(2)}, u32[]{:S(2)}) collective-permute-start(bf16[32,6144]{1,0:T(8,128)(2,1)} %get-tuple-element.451), channel_id=1, source_target_pairs={{0,64},{64,128},{128,192},{192,256},{256,320},{320,384},{384,448},... | collective-permute-start | bytes 1179656 | tf_op jit(solution)/shard_map/while/body/eval_jaxpr/ppermute | solution.py:21
  104.9 12.6 %collective-permute-start = (bf16[32,6144]{1,0:T(8,128)(2,1)}, bf16[32,6144]{1,0:T(8,128)(2,1)}, u32[]{:S(2)}, u32[]{:S(2)}) collective-permute-start(bf16[32,6144]{1,0:T(8,128)(2,1)} %get-tuple-element.451), channel_id=1, source_target_pairs={{0,64},{64,128},{128,192},{192,256},{256,320},{320,384},{384,448},... | collective-permute-start | bytes 1179656 | tf_op jit(solution)/shard_map/while/body/eval_jaxpr/ppermute | solution.py:21
  118.3 11.7 %collective-permute-start = (bf16[32,6144]{1,0:T(8,128)(2,1)}, bf16[32,6144]{1,0:T(8,128)(2,1)}, u32[]{:S(2)}, u32[]{:S(2)}) collective-permute-start(bf16[32,6144]{1,0:T(8,128)(2,1)} %get-tuple-element.451), channel_id=1, source_target_pairs={{0,64},{64,128},{128,192},{192,256},{256,320},{320,384},{384,448},... | collective-permute-start | bytes 1179656 | tf_op jit(solution)/shard_map/while/body/eval_jaxpr/ppermute | solution.py:21
  130.8 10.9 %collective-permute-start = (bf16[32,6144]{1,0:T(8,128)(2,1)}, bf16[32,6144]{1,0:T(8,128)(2,1)}, u32[]{:S(2)}, u32[]{:S(2)}) collective-permute-start(bf16[32,6144]{1,0:T(8,128)(2,1)} %get-tuple-element.451), channel_id=1, source_target_pairs={{0,64},{64,128},{128,192},{192,256},{256,320},{320,384},{384,448},... | collective-permute-start | bytes 1179656 | tf_op jit(solution)/shard_map/while/body/eval_jaxpr/ppermute | solution.py:21
  142.5 11.8 %collective-permute-start = (bf16[32,6144]{1,0:T(8,128)(2,1)}, bf16[32,6144]{1,0:T(8,128)(2,1)}, u32[]{:S(2)}, u32[]{:S(2)}) collective-permute-start(bf16[32,6144]{1,0:T(8,128)(2,1)} %get-tuple-element.451), channel_id=1, source_target_pairs={{0,64},{64,128},{128,192},{192,256},{256,320},{320,384},{384,448},... | collective-permute-start | bytes 1179656 | tf_op jit(solution)/shard_map/while/body/eval_jaxpr/ppermute | solution.py:21
  155.2 11.3 %collective-permute-start = (bf16[32,6144]{1,0:T(8,128)(2,1)}, bf16[32,6144]{1,0:T(8,128)(2,1)}, u32[]{:S(2)}, u32[]{:S(2)}) collective-permute-start(bf16[32,6144]{1,0:T(8,128)(2,1)} %get-tuple-element.451), channel_id=1, source_target_pairs={{0,64},{64,128},{128,192},{192,256},{256,320},{320,384},{384,448},... | collective-permute-start | bytes 1179656 | tf_op jit(solution)/shard_map/while/body/eval_jaxpr/ppermute | solution.py:21
  167.3 68.9 %collective-permute-start = (bf16[32,6144]{1,0:T(8,128)(2,1)}, bf16[32,6144]{1,0:T(8,128)(2,1)}, u32[]{:S(2)}, u32[]{:S(2)}) collective-permute-start(bf16[32,6144]{1,0:T(8,128)(2,1)} %get-tuple-element.451), channel_id=1, source_target_pairs={{0,64},{64,128},{128,192},{192,256},{256,320},{320,384},{384,448},... | collective-permute-start | bytes 1179656 | tf_op jit(solution)/shard_map/while/body/eval_jaxpr/ppermute | solution.py:21
  246.2 11.3 %collective-permute-start = (bf16[32,6144]{1,0:T(8,128)(2,1)}, bf16[32,6144]{1,0:T(8,128)(2,1)}, u32[]{:S(2)}, u32[]{:S(2)}) collective-permute-start(bf16[32,6144]{1,0:T(8,128)(2,1)} %get-tuple-element.451), channel_id=1, source_target_pairs={{0,64},{64,128},{128,192},{192,256},{256,320},{320,384},{384,448},... | collective-permute-start | bytes 1179656 | tf_op jit(solution)/shard_map/while/body/eval_jaxpr/ppermute | solution.py:21
  267.5 11.8 %collective-permute-start = (bf16[32,6144]{1,0:T(8,128)(2,1)}, bf16[32,6144]{1,0:T(8,128)(2,1)}, u32[]{:S(2)}, u32[]{:S(2)}) collective-permute-start(bf16[32,6144]{1,0:T(8,128)(2,1)} %get-tuple-element.451), channel_id=1, source_target_pairs={{0,64},{64,128},{128,192},{192,256},{256,320},{320,384},{384,448},... | collective-permute-start | bytes 1179656 | tf_op jit(solution)/shard_map/while/body/eval_jaxpr/ppermute | solution.py:21
  289.4 12.1 %collective-permute-start = (bf16[32,6144]{1,0:T(8,128)(2,1)}, bf16[32,6144]{1,0:T(8,128)(2,1)}, u32[]{:S(2)}, u32[]{:S(2)}) collective-permute-start(bf16[32,6144]{1,0:T(8,128)(2,1)} %get-tuple-element.451), channel_id=1, source_target_pairs={{0,64},{64,128},{128,192},{192,256},{256,320},{320,384},{384,448},... | collective-permute-start | bytes 1179656 | tf_op jit(solution)/shard_map/while/body/eval_jaxpr/ppermute | solution.py:21
  311.6 10.0 %collective-permute-start = (bf16[32,6144]{1,0:T(8,128)(2,1)}, bf16[32,6144]{1,0:T(8,128)(2,1)}, u32[]{:S(2)}, u32[]{:S(2)}) collective-permute-start(bf16[32,6144]{1,0:T(8,128)(2,1)} %get-tuple-element.451), channel_id=1, source_target_pairs={{0,64},{64,128},{128,192},{192,256},{256,320},{320,384},{384,448},... | collective-permute-start | bytes 1179656 | tf_op jit(solution)/shard_map/while/body/eval_jaxpr/ppermute | solution.py:21
  321.6 3.0 copy-start.3
Sparse Core Ops, SparseCore 0:
  33.4 49.4 all-gather.1

commit v11 on v9

--- a/solution.py
+++ b/solution.py
@@ -70,7 +70,7 @@
     return jnp.where(lane < BLK, pltpu.roll(prev, BLK, 1), pltpu.roll(cur, BLK, 1))
 
 
-UP_CHUNKS = 4
+UP_CHUNKS = 2
 DOWN_CHUNKS = 2
 
 
@@ -115,7 +115,7 @@
     last = zero
     for k in range(UP_CHUNKS):
         copies[k].wait()
-        last = lax.fori_loop(k * up_step, (k + 1) * up_step, up, last, unroll=24)
+        last = lax.fori_loop(k * up_step, (k + 1) * up_step, up, last, unroll=48)
     sh_ref[0, pairs_hid] = zero
     sh_ref[1, pairs_hid] = _shifted(last, zero)
 

time: 333 us -> 331 us (level)
  no operation moved by 1% of the time
where the time goes in v11:
time: 331 us; the launch traced here: 330 us
  waiting for transfers between devices  191 us (58%)
  local copies, waits for them, and re-layouts  37.8 us (11%)
  Pallas kernels  34.5 us (10%)
  starting transfers between devices  32.1 us (10%)
  other arithmetic  21 us (6%)
  between operations  13.6 us (4%)
    ppermute x11, waiting for transfers between devices, from_behind(): lax.ppermute(value, axis, [(source, source + steps) for source in range(i...  145 us
    all_gather x1, waiting for transfers between devices, gather_weights(): full = lax.all_gather(full[:, None], ('y', 'c'), axis=1, tiled=True)  40.9 us
    pallas_call x4, Pallas kernels, layer(): pl.pallas_call(_layer_kernel, out_shape=jax.ShapeDtypeStruct((count, widt...  34.5 us
    ppermute x3, starting transfers between devices, exchange_zh(): lax.ppermute(part, 'zh', [(i, (i + shift) % count) for i in range(count)])  18 us
    ppermute x11, starting transfers between devices, from_behind(): lax.ppermute(value, axis, [(source, source + steps) for source in range(i...  14.1 us
    dynamic_update_slice x11, other arithmetic, advance(): record = lax.dynamic_update_index_in_dim(record, updated, slot, 0)  13.4 us
    dynamic_slice x11, local copies, waits for them, and re-layouts, advance(): current = lax.dynamic_index_in_dim(record, slot, 0, keepdims=False)  11.3 us
    unnamed x20, local copies, waits for them, and re-layouts  7.08 us
  transfers between devices with their start and end apart: 15, of which 14 were waited for; matrix products, arithmetic and copies ran while one was open for 10% of the time, Pallas kernels for 0%

profile of v11, /device:TPU:70, one launch (start us, length us, event | category | flops | bytes accessed | tf_op | source)
XLA Modules:
  0.0 329.8 jit_solution(4819893490356170256)
XLA Ops:
  6.5 1.6 copy.40
  8.9 6.1 %collective-permute-start.1 = (bf16[384,128]{1,0:T(8,128)(2,1)S(1)}, bf16[384,128]{1,0:T(8,128)(2,1)S(1)}, u32[]{:S(2)}, u32[]{:S(2)}) collective-permute-start(bf16[384,128]{1,0:T(8,128)(2,1)S(1)} %get-tuple-element.335), channel_id=1, source_target_pairs={{0,16},{16,32},{32,48},{48,0},{1,17},{17,33},{33,49},{49,1},{2,18}... | collective-permute-start | bytes 294920 | tf_op jit(solution)/shard_map/ppermute | solution.py:29
  15.0 8.2 %collective-permute-start.2 = (bf16[384,128]{1,0:T(8,128)(2,1)S(1)}, bf16[384,128]{1,0:T(8,128)(2,1)S(1)}, u32[]{:S(2)}, u32[]{:S(2)}) collective-permute-start(bf16[384,128]{1,0:T(8,128)(2,1)S(1)} %get-tuple-element.335), channel_id=1, source_target_pairs={{0,32},{16,48},{32,0},{48,16},{1,33},{17,49},{33,1},{49,17},{2,34}... | collective-permute-start | bytes 294920 | tf_op jit(solution)/shard_map/ppermute | solution.py:29
  23.2 3.7 %collective-permute-start.3 = (bf16[384,128]{1,0:T(8,128)(2,1)S(1)}, bf16[384,128]{1,0:T(8,128)(2,1)S(1)}, u32[]{:S(2)}, u32[]{:S(2)}) collective-permute-start(bf16[384,128]{1,0:T(8,128)(2,1)S(1)} %get-tuple-element.335), channel_id=1, source_target_pairs={{0,48},{16,0},{32,16},{48,32},{1,49},{17,1},{33,17},{49,33},{2,50}... | collective-permute-start | bytes 294920 | tf_op jit(solution)/shard_map/ppermute | solution.py:29
  26.9 1.1 collective-permute-done.2
  28.0 3.5 %collective-permute-done.3 = bf16[384,128]{1,0:T(8,128)(2,1)S(1)} collective-permute-done((bf16[384,128]{1,0:T(8,128)(2,1)S(1)}, bf16[384,128]{1,0:T(8,128)(2,1)S(1)}, u32[]{:S(2)}, u32[]{:S(2)}) %collective-permute-start.3) | collective-permute-done | bytes 98336 | tf_op jit(solution)/shard_map/ppermute | solution.py:29
  33.8 1.1 scatter_custom_fusion
  34.9 1.5 gather_fusion
  37.3 1.1 copy.31
  39.2 1.0 reshape_squeeze.6
  40.5 1.4 convert_element_type.12
  41.9 40.9 %all-gather.2.cloned.1.call-done = bf16[4,16,384,128]{3,2,0,1:T(8,128)(2,1)} async-done(((bf16[4,1,384,128]{3,2,0,1:T(8,128)(2,1)}), bf16[4,16,384,128]{3,2,0,1:T(8,128)(2,1)}) %all-gather.2.cloned.1.call-update) | async-done | bytes 6291472 | tf_op jit(solution)/shard_map/all_gather | solution.py:48
  82.8 3.4 %fusion.8 = (bf16[4,16,192,128]{3,2,0,1:T(8,128)(2,1)S(1)}, bf16[4,16,192,128]{3,2,0,1:T(8,128)(2,1)S(1)}) fusion(bf16[4,16,384,128]{3,2,0,1:T(8,128)(2,1)} %all-gather.2.cloned.1.call-done), kind=kLoop, calls=%fused_computation.41 | loop fusion | bytes 12582912 | tf_op jit(solution)/shard_map/slice | solution.py:50
  86.6 1.9 copy.24
  88.6 228.5 %while.16 = (s32[]{:T(128)}, bf16[32,6144]{1,0:T(8,128)(2,1)}, bf16[4,32,6144]{2,1,0:T(8,128)(2,1)}, s32[]{:T(128)}, pred[]{:T(512)}, /*index=5*/bf16[4,32,6144]...) while((s32[]{:T(128)}, bf16[32,6144]{1,0:T(8,128)(2,1)}, ...), condition=%wide.region_6.7_spmd, body=%wide.region_3.6_spmd.sunk | while | flops 393229 | bytes 4718975 | solution.py:215
  89.3 1.3 collective-permute-start
  90.6 1.0 constant_dynamic-slice_fusion.2
  92.5 10.3 %collective-permute-done = bf16[32,6144]{1,0:T(8,128)(2,1)} collective-permute-done((bf16[32,6144]{1,0:T(8,128)(2,1)}, bf16[32,6144]{1,0:T(8,128)(2,1)}, u32[]{:S(2)}, u32[]{:S(2)}) %collective-permute-start) | collective-permute-done | bytes 393248 | tf_op jit(solution)/shard_map/while/body/eval_jaxpr/ppermute | solution.py:21
  103.5 1.3 collective-permute-start
  104.8 1.0 constant_dynamic-slice_fusion.2
  106.7 9.4 %collective-permute-done = bf16[32,6144]{1,0:T(8,128)(2,1)} collective-permute-done((bf16[32,6144]{1,0:T(8,128)(2,1)}, bf16[32,6144]{1,0:T(8,128)(2,1)}, u32[]{:S(2)}, u32[]{:S(2)}) %collective-permute-start) | collective-permute-done | bytes 393248 | tf_op jit(solution)/shard_map/while/body/eval_jaxpr/ppermute | solution.py:21
  116.9 1.3 collective-permute-start
  118.2 1.0 constant_dynamic-slice_fusion.2
  120.1 8.6 %collective-permute-done = bf16[32,6144]{1,0:T(8,128)(2,1)} collective-permute-done((bf16[32,6144]{1,0:T(8,128)(2,1)}, bf16[32,6144]{1,0:T(8,128)(2,1)}, u32[]{:S(2)}, u32[]{:S(2)}) %collective-permute-start) | collective-permute-done | bytes 393248 | tf_op jit(solution)/shard_map/while/body/eval_jaxpr/ppermute | solution.py:21
  129.4 1.3 collective-permute-start
  130.7 1.0 constant_dynamic-slice_fusion.2
  132.6 7.7 %collective-permute-done = bf16[32,6144]{1,0:T(8,128)(2,1)} collective-permute-done((bf16[32,6144]{1,0:T(8,128)(2,1)}, bf16[32,6144]{1,0:T(8,128)(2,1)}, u32[]{:S(2)}, u32[]{:S(2)}) %collective-permute-start) | collective-permute-done | bytes 393248 | tf_op jit(solution)/shard_map/while/body/eval_jaxpr/ppermute | solution.py:21
  141.1 1.3 collective-permute-start
  144.2 8.7 %collective-permute-done = bf16[32,6144]{1,0:T(8,128)(2,1)} collective-permute-done((bf16[32,6144]{1,0:T(8,128)(2,1)}, bf16[32,6144]{1,0:T(8,128)(2,1)}, u32[]{:S(2)}, u32[]{:S(2)}) %collective-permute-start) | collective-permute-done | bytes 393248 | tf_op jit(solution)/shard_map/while/body/eval_jaxpr/ppermute | solution.py:21
  153.7 1.3 collective-permute-start
  155.0 1.0 constant_dynamic-slice_fusion.2
  156.8 8.1 %collective-permute-done = bf16[32,6144]{1,0:T(8,128)(2,1)} collective-permute-done((bf16[32,6144]{1,0:T(8,128)(2,1)}, bf16[32,6144]{1,0:T(8,128)(2,1)}, u32[]{:S(2)}, u32[]{:S(2)}) %collective-permute-start) | collective-permute-done | bytes 393248 | tf_op jit(solution)/shard_map/while/body/eval_jaxpr/ppermute | solution.py:21
  165.7 1.3 collective-permute-start
  168.9 63.9 %collective-permute-done = bf16[32,6144]{1,0:T(8,128)(2,1)} collective-permute-done((bf16[32,6144]{1,0:T(8,128)(2,1)}, bf16[32,6144]{1,0:T(8,128)(2,1)}, u32[]{:S(2)}, u32[]{:S(2)}) %collective-permute-start) | collective-permute-done | bytes 393248 | tf_op jit(solution)/shard_map/while/body/eval_jaxpr/ppermute | solution.py:21
  232.7 9.8 %conditional.2 = (bf16[32,6144]{1,0:T(8,128)(2,1)}) conditional(s32[]{:T(128)} %convert_element_type.14, () %tuple.47, (pred[]{:T(512)}, s32[]{:T(128)}, bf16[4,32,6144]{2,1,0:T(8,128)(2,1)}, bf16[32,6144]{1,0:T(8,128)(2,1)}, s32[384]{0:T(512)S(1)}, /*index=5*/s32[192]{0:T(256)S(1)}, f32[1,6144]{1,0:T(1,128)}, bf16[96,128,128]{2,1,0:T(8,128)(2,1)}, ...), branch_computations={%region_4.4_spmd, %region_5.5_spmd} | conditional | flops 196612 | bytes 1179707 | solution.py:201
  232.7 1.2 bitcast_select_fusion.x_ref
  233.9 8.6 %branch_1_fun.3 = bf16[32,6144]{1,0:T(8,128)(2,1)} custom-call(s32[384]{0:T(512)S(1)} %get-tuple-element.287.up_idx, s32[192]{0:T(256)S(1)} %get-tuple-element.288.dn_idx, bf16[32,6144]{1,0:T(8,128)(2,1)S(1)} %bitcast_select_fusion.x_ref, f32[1,6144]{1,0:T(1,128)} %get-tuple-element.293.g_ref, bf16[96,128,128]{2,1,0:T(8,128)(2,1)} %get-tuple-element.294.wu_hbm, ...), custom_call_target="tpu_custom_call" | custom-call | tf_op jit(solution)/shard_map/while/body/eval_jaxpr/cond/branch_1_fun/pallas_call | solution.py:141
  242.5 1.3 collective-permute-start
  243.8 1.0 constant_dynamic-slice_fusion.2
  244.9 1.8 bitcast_dynamic-update-slice_fusion.2
  246.7 7.1 %collective-permute-done = bf16[32,6144]{1,0:T(8,128)(2,1)} collective-permute-done((bf16[32,6144]{1,0:T(8,128)(2,1)}, bf16[32,6144]{1,0:T(8,128)(2,1)}, u32[]{:S(2)}, u32[]{:S(2)}) %collective-permute-start) | collective-permute-done | bytes 393248 | tf_op jit(solution)/shard_map/while/body/eval_jaxpr/ppermute | solution.py:21
  253.8 9.8 %conditional.2 = (bf16[32,6144]{1,0:T(8,128)(2,1)}) conditional(s32[]{:T(128)} %convert_element_type.14, () %tuple.47, (pred[]{:T(512)}, s32[]{:T(128)}, bf16[4,32,6144]{2,1,0:T(8,128)(2,1)}, bf16[32,6144]{1,0:T(8,128)(2,1)}, s32[384]{0:T(512)S(1)}, /*index=5*/s32[192]{0:T(256)S(1)}, f32[1,6144]{1,0:T(1,128)}, bf16[96,128,128]{2,1,0:T(8,128)(2,1)}, ...), branch_computations={%region_4.4_spmd, %region_5.5_spmd} | conditional | flops 196612 | bytes 1179707 | solution.py:201
  253.8 1.2 bitcast_select_fusion.x_ref
  254.9 8.6 %branch_1_fun.3 = bf16[32,6144]{1,0:T(8,128)(2,1)} custom-call(s32[384]{0:T(512)S(1)} %get-tuple-element.287.up_idx, s32[192]{0:T(256)S(1)} %get-tuple-element.288.dn_idx, bf16[32,6144]{1,0:T(8,128)(2,1)S(1)} %bitcast_select_fusion.x_ref, f32[1,6144]{1,0:T(1,128)} %get-tuple-element.293.g_ref, bf16[96,128,128]{2,1,0:T(8,128)(2,1)} %get-tuple-element.294.wu_hbm, ...), custom_call_target="tpu_custom_call" | custom-call | tf_op jit(solution)/shard_map/while/body/eval_jaxpr/cond/branch_1_fun/pallas_call | solution.py:141
  263.6 1.3 collective-permute-start
  264.9 1.0 constant_dynamic-slice_fusion.2
  265.9 1.8 bitcast_dynamic-update-slice_fusion.2
  267.7 7.6 %collective-permute-done = bf16[32,6144]{1,0:T(8,128)(2,1)} collective-permute-done((bf16[32,6144]{1,0:T(8,128)(2,1)}, bf16[32,6144]{1,0:T(8,128)(2,1)}, u32[]{:S(2)}, u32[]{:S(2)}) %collective-permute-start) | collective-permute-done | bytes 393248 | tf_op jit(solution)/shard_map/while/body/eval_jaxpr/ppermute | solution.py:21
  275.4 9.8 %conditional.2 = (bf16[32,6144]{1,0:T(8,128)(2,1)}) conditional(s32[]{:T(128)} %convert_element_type.14, () %tuple.47, (pred[]{:T(512)}, s32[]{:T(128)}, bf16[4,32,6144]{2,1,0:T(8,128)(2,1)}, bf16[32,6144]{1,0:T(8,128)(2,1)}, s32[384]{0:T(512)S(1)}, /*index=5*/s32[192]{0:T(256)S(1)}, f32[1,6144]{1,0:T(1,128)}, bf16[96,128,128]{2,1,0:T(8,128)(2,1)}, ...), branch_computations={%region_4.4_spmd, %region_5.5_spmd} | conditional | flops 196612 | bytes 1179707 | solution.py:201
  275.4 1.2 bitcast_select_fusion.x_ref
  276.5 8.6 %branch_1_fun.3 = bf16[32,6144]{1,0:T(8,128)(2,1)} custom-call(s32[384]{0:T(512)S(1)} %get-tuple-element.287.up_idx, s32[192]{0:T(256)S(1)} %get-tuple-element.288.dn_idx, bf16[32,6144]{1,0:T(8,128)(2,1)S(1)} %bitcast_select_fusion.x_ref, f32[1,6144]{1,0:T(1,128)} %get-tuple-element.293.g_ref, bf16[96,128,128]{2,1,0:T(8,128)(2,1)} %get-tuple-element.294.wu_hbm, ...), custom_call_target="tpu_custom_call" | custom-call | tf_op jit(solution)/shard_map/while/body/eval_jaxpr/cond/branch_1_fun/pallas_call | solution.py:141
  285.1 1.3 collective-permute-start
  286.5 1.0 constant_dynamic-slice_fusion.2
  287.5 1.8 bitcast_dynamic-update-slice_fusion.2
  289.3 7.9 %collective-permute-done = bf16[32,6144]{1,0:T(8,128)(2,1)} collective-permute-done((bf16[32,6144]{1,0:T(8,128)(2,1)}, bf16[32,6144]{1,0:T(8,128)(2,1)}, u32[]{:S(2)}, u32[]{:S(2)}) %collective-permute-start) | collective-permute-done | bytes 393248 | tf_op jit(solution)/shard_map/while/body/eval_jaxpr/ppermute | solution.py:21
  297.2 9.8 %conditional.2 = (bf16[32,6144]{1,0:T(8,128)(2,1)}) conditional(s32[]{:T(128)} %convert_element_type.14, () %tuple.47, (pred[]{:T(512)}, s32[]{:T(128)}, bf16[4,32,6144]{2,1,0:T(8,128)(2,1)}, bf16[32,6144]{1,0:T(8,128)(2,1)}, s32[384]{0:T(512)S(1)}, /*index=5*/s32[192]{0:T(256)S(1)}, f32[1,6144]{1,0:T(1,128)}, bf16[96,128,128]{2,1,0:T(8,128)(2,1)}, ...), branch_computations={%region_4.4_spmd, %region_5.5_spmd} | conditional | flops 196612 | bytes 1179707 | solution.py:201
  297.2 1.2 bitcast_select_fusion.x_ref
  298.4 8.6 %branch_1_fun.3 = bf16[32,6144]{1,0:T(8,128)(2,1)} custom-call(s32[384]{0:T(512)S(1)} %get-tuple-element.287.up_idx, s32[192]{0:T(256)S(1)} %get-tuple-element.288.dn_idx, bf16[32,6144]{1,0:T(8,128)(2,1)S(1)} %bitcast_select_fusion.x_ref, f32[1,6144]{1,0:T(1,128)} %get-tuple-element.293.g_ref, bf16[96,128,128]{2,1,0:T(8,128)(2,1)} %get-tuple-element.294.wu_hbm, ...), custom_call_target="tpu_custom_call" | custom-call | tf_op jit(solution)/shard_map/while/body/eval_jaxpr/cond/branch_1_fun/pallas_call | solution.py:141
  307.0 1.3 collective-permute-start
  308.3 1.0 constant_dynamic-slice_fusion.2
  309.4 1.8 bitcast_dynamic-update-slice_fusion.2
  311.2 5.8 %collective-permute-done = bf16[32,6144]{1,0:T(8,128)(2,1)} collective-permute-done((bf16[32,6144]{1,0:T(8,128)(2,1)}, bf16[32,6144]{1,0:T(8,128)(2,1)}, u32[]{:S(2)}, u32[]{:S(2)}) %collective-permute-start) | collective-permute-done | bytes 393248 | tf_op jit(solution)/shard_map/while/body/eval_jaxpr/ppermute | solution.py:21
  317.0 4.7 %scatter_fusion = bf16[160,6144]{1,0:T(8,128)(2,1)S(1)} fusion(bf16[160,6144]{1,0:T(8,128)(2,1)S(1)} %copy.40, s32[128]{0:T(128)S(1)} %compare_select_fusion.3, bf16[128,6144]{1,0:T(8,128)(2,1)} %bitcast.38), kind=kCustom, calls=%fused_computation.3 | custom fusion | bytes 4719104 | tf_op jit(solution)/shard_map/scatter | solution.py:217
  321.7 1.3 copy-done
  (69 shorter events, 23.9 us)
Async XLA Ops:
  6.5 1.9 copy-start.2
  6.5 1.6 copy-start.3
  6.5 76.2 %all-gather.2.cloned.1.call-start = ((), (), s32[]{:S(2)}) async-start(), calls=%async_computation | async-start | bytes 6684672 | tf_op jit(solution)/shard_map/all_gather | solution.py:48
  8.8 24.3 %copy-start.4 = (s32[160]{0:T(256)S(1)}, s32[160]{0:T(256)}, u32[]{:S(2)}) copy-start(s32[160]{0:T(256)} %param.12) | copy-start | bytes 1924
  8.9 18.0 %collective-permute-start.1 = (bf16[384,128]{1,0:T(8,128)(2,1)S(1)}, bf16[384,128]{1,0:T(8,128)(2,1)S(1)}, u32[]{:S(2)}, u32[]{:S(2)}) collective-permute-start(bf16[384,128]{1,0:T(8,128)(2,1)S(1)} %get-tuple-element.335), channel_id=1, source_target_pairs={{0,16},{16,32},{32,48},{48,0},{1,17},{17,33},{33,49},{49,1},{2,18}... | collective-permute-start | bytes 294920 | tf_op jit(solution)/shard_map/ppermute | solution.py:29
  15.0 13.0 %collective-permute-start.2 = (bf16[384,128]{1,0:T(8,128)(2,1)S(1)}, bf16[384,128]{1,0:T(8,128)(2,1)S(1)}, u32[]{:S(2)}, u32[]{:S(2)}) collective-permute-start(bf16[384,128]{1,0:T(8,128)(2,1)S(1)} %get-tuple-element.335), channel_id=1, source_target_pairs={{0,32},{16,48},{32,0},{48,16},{1,33},{17,49},{33,1},{49,17},{2,34}... | collective-permute-start | bytes 294920 | tf_op jit(solution)/shard_map/ppermute | solution.py:29
  23.2 8.4 %collective-permute-start.3 = (bf16[384,128]{1,0:T(8,128)(2,1)S(1)}, bf16[384,128]{1,0:T(8,128)(2,1)S(1)}, u32[]{:S(2)}, u32[]{:S(2)}) collective-permute-start(bf16[384,128]{1,0:T(8,128)(2,1)S(1)} %get-tuple-element.335), channel_id=1, source_target_pairs={{0,48},{16,0},{32,16},{48,32},{1,49},{17,1},{33,17},{49,33},{2,50}... | collective-permute-start | bytes 294920 | tf_op jit(solution)/shard_map/ppermute | solution.py:29
  36.4 2.0 copy-start.1
  37.3 1.2 copy-start.5
  37.3 3.0 copy-start.6
  89.3 13.5 %collective-permute-start = (bf16[32,6144]{1,0:T(8,128)(2,1)}, bf16[32,6144]{1,0:T(8,128)(2,1)}, u32[]{:S(2)}, u32[]{:S(2)}) collective-permute-start(bf16[32,6144]{1,0:T(8,128)(2,1)} %get-tuple-element.448), channel_id=1, source_target_pairs={{0,64},{64,128},{128,192},{192,256},{256,320},{320,384},{384,448},... | collective-permute-start | bytes 1179656 | tf_op jit(solution)/shard_map/while/body/eval_jaxpr/ppermute | solution.py:21
  103.5 12.6 %collective-permute-start = (bf16[32,6144]{1,0:T(8,128)(2,1)}, bf16[32,6144]{1,0:T(8,128)(2,1)}, u32[]{:S(2)}, u32[]{:S(2)}) collective-permute-start(bf16[32,6144]{1,0:T(8,128)(2,1)} %get-tuple-element.448), channel_id=1, source_target_pairs={{0,64},{64,128},{128,192},{192,256},{256,320},{320,384},{384,448},... | collective-permute-start | bytes 1179656 | tf_op jit(solution)/shard_map/while/body/eval_jaxpr/ppermute | solution.py:21
  116.9 11.7 %collective-permute-start = (bf16[32,6144]{1,0:T(8,128)(2,1)}, bf16[32,6144]{1,0:T(8,128)(2,1)}, u32[]{:S(2)}, u32[]{:S(2)}) collective-permute-start(bf16[32,6144]{1,0:T(8,128)(2,1)} %get-tuple-element.448), channel_id=1, source_target_pairs={{0,64},{64,128},{128,192},{192,256},{256,320},{320,384},{384,448},... | collective-permute-start | bytes 1179656 | tf_op jit(solution)/shard_map/while/body/eval_jaxpr/ppermute | solution.py:21
  129.4 10.9 %collective-permute-start = (bf16[32,6144]{1,0:T(8,128)(2,1)}, bf16[32,6144]{1,0:T(8,128)(2,1)}, u32[]{:S(2)}, u32[]{:S(2)}) collective-permute-start(bf16[32,6144]{1,0:T(8,128)(2,1)} %get-tuple-element.448), channel_id=1, source_target_pairs={{0,64},{64,128},{128,192},{192,256},{256,320},{320,384},{384,448},... | collective-permute-start | bytes 1179656 | tf_op jit(solution)/shard_map/while/body/eval_jaxpr/ppermute | solution.py:21
  141.1 11.8 %collective-permute-start = (bf16[32,6144]{1,0:T(8,128)(2,1)}, bf16[32,6144]{1,0:T(8,128)(2,1)}, u32[]{:S(2)}, u32[]{:S(2)}) collective-permute-start(bf16[32,6144]{1,0:T(8,128)(2,1)} %get-tuple-element.448), channel_id=1, source_target_pairs={{0,64},{64,128},{128,192},{192,256},{256,320},{320,384},{384,448},... | collective-permute-start | bytes 1179656 | tf_op jit(solution)/shard_map/while/body/eval_jaxpr/ppermute | solution.py:21
  153.7 11.3 %collective-permute-start = (bf16[32,6144]{1,0:T(8,128)(2,1)}, bf16[32,6144]{1,0:T(8,128)(2,1)}, u32[]{:S(2)}, u32[]{:S(2)}) collective-permute-start(bf16[32,6144]{1,0:T(8,128)(2,1)} %get-tuple-element.448), channel_id=1, source_target_pairs={{0,64},{64,128},{128,192},{192,256},{256,320},{320,384},{384,448},... | collective-permute-start | bytes 1179656 | tf_op jit(solution)/shard_map/while/body/eval_jaxpr/ppermute | solution.py:21
  165.7 67.0 %collective-permute-start = (bf16[32,6144]{1,0:T(8,128)(2,1)}, bf16[32,6144]{1,0:T(8,128)(2,1)}, u32[]{:S(2)}, u32[]{:S(2)}) collective-permute-start(bf16[32,6144]{1,0:T(8,128)(2,1)} %get-tuple-element.448), channel_id=1, source_target_pairs={{0,64},{64,128},{128,192},{192,256},{256,320},{320,384},{384,448},... | collective-permute-start | bytes 1179656 | tf_op jit(solution)/shard_map/while/body/eval_jaxpr/ppermute | solution.py:21
  242.5 11.3 %collective-permute-start = (bf16[32,6144]{1,0:T(8,128)(2,1)}, bf16[32,6144]{1,0:T(8,128)(2,1)}, u32[]{:S(2)}, u32[]{:S(2)}) collective-permute-start(bf16[32,6144]{1,0:T(8,128)(2,1)} %get-tuple-element.448), channel_id=1, source_target_pairs={{0,64},{64,128},{128,192},{192,256},{256,320},{320,384},{384,448},... | collective-permute-start | bytes 1179656 | tf_op jit(solution)/shard_map/while/body/eval_jaxpr/ppermute | solution.py:21
  263.6 11.8 %collective-permute-start = (bf16[32,6144]{1,0:T(8,128)(2,1)}, bf16[32,6144]{1,0:T(8,128)(2,1)}, u32[]{:S(2)}, u32[]{:S(2)}) collective-permute-start(bf16[32,6144]{1,0:T(8,128)(2,1)} %get-tuple-element.448), channel_id=1, source_target_pairs={{0,64},{64,128},{128,192},{192,256},{256,320},{320,384},{384,448},... | collective-permute-start | bytes 1179656 | tf_op jit(solution)/shard_map/while/body/eval_jaxpr/ppermute | solution.py:21
  285.1 12.1 %collective-permute-start = (bf16[32,6144]{1,0:T(8,128)(2,1)}, bf16[32,6144]{1,0:T(8,128)(2,1)}, u32[]{:S(2)}, u32[]{:S(2)}) collective-permute-start(bf16[32,6144]{1,0:T(8,128)(2,1)} %get-tuple-element.448), channel_id=1, source_target_pairs={{0,64},{64,128},{128,192},{192,256},{256,320},{320,384},{384,448},... | collective-permute-start | bytes 1179656 | tf_op jit(solution)/shard_map/while/body/eval_jaxpr/ppermute | solution.py:21
  307.0 10.0 %collective-permute-start = (bf16[32,6144]{1,0:T(8,128)(2,1)}, bf16[32,6144]{1,0:T(8,128)(2,1)}, u32[]{:S(2)}, u32[]{:S(2)}) collective-permute-start(bf16[32,6144]{1,0:T(8,128)(2,1)} %get-tuple-element.448), channel_id=1, source_target_pairs={{0,64},{64,128},{128,192},{192,256},{256,320},{320,384},{384,448},... | collective-permute-start | bytes 1179656 | tf_op jit(solution)/shard_map/while/body/eval_jaxpr/ppermute | solution.py:21
  321.7 1.3 copy-start
Sparse Core Ops, SparseCore 0:
  33.3 49.4 all-gather.1
